TPU v7x, 128 devices: a whole 4x4x4 slice. The times are simulated.
128 devices in a mesh: tm: 32 (over x, y, core), chan: 4 (over z).
Axes of the slice: x: 4, y: 4, z: 4, core: 2. Of those that a mesh axis runs over, the one named last changes fastest.
Arguments:
- streams: bfloat16 [262144, 1024], P('tm', 'chan'), may hold values from -6 to 6
- weights: bfloat16 [262144, 1024], P('tm', 'chan'), may hold values from 0.25 to 4
- pointing: int32 [262144], P('tm'), may hold values from 0 to 127
- touched: int32 [32, 32], replicated, may hold values from 0 to 3
- foreground_modes: float32 [1024, 16], P('chan'), as said below
Outputs:
- map_cube: float32 [16384, 1024], P('tm', 'chan')
- residual: float32 [16384, 1024], P('tm', 'chan')
Inputs may be any that keep to these rules, and one draw needn't show every extreme that they name: `foreground_modes`: the columns are mutually orthogonal over the 1024 channels, each of norm at most one.
All inputs are finite; a program needn't handle non-finite values.
Results may differ from a plain program's by a relative error of at most 0.0006.
Values may be sent and summed in bfloat16 or wider, within the bound.
No kernel may reach another device: no remote copies, remote signals or barrier semaphores. Data moves between devices by JAX's collectives and lax.ppermute only.
A program may use at most 128 MiB of HBM per device.

v0:
```python
import jax
import jax.numpy as jnp
from jax import lax
from jax.sharding import PartitionSpec as P

PIX_DEV = 512
BLK = 128
ITERS = 3


highest = lax.Precision.HIGHEST
ridge = 1.0


def per_device(streams, weights, pointing, touched, foreground_modes):
    group_count = lax.axis_size("tm")
    owner_index = lax.axis_index("tm")
    sample_count, channels = streams.shape
    run_length = sample_count // group_count
    blocks_each = PIX_DEV // BLK
    column = lax.dynamic_index_in_dim(touched, owner_index, axis=1, keepdims=False)
    owned_blocks = (column[:, None] == jnp.arange(blocks_each, dtype=jnp.int32)[None, :]).astype(
        jnp.float32
    )
    runs_in = streams.reshape(group_count, run_length, channels)
    weights_in = weights.reshape(group_count, run_length, channels)
    pixels_in = pointing.reshape(group_count, run_length)
    pixel_hits = (pixels_in[:, :, None] == jnp.arange(BLK, dtype=jnp.int32)[None, None, :]).astype(
        jnp.float32
    )
    noise_weights = weights_in.astype(jnp.float32).reshape(-1, channels)

    def filtered(samples):
        weighted = noise_weights * samples
        amplitudes = lax.psum(jnp.dot(weighted, foreground_modes, precision=highest), "chan")
        return noise_weights * (
            weighted - jnp.dot(amplitudes, foreground_modes.T, precision=highest)
        )

    def add_blocks(arrived):
        return jnp.einsum("cb,cpk->bpk", owned_blocks, arrived, precision=highest)

    def binned(samples):
        partial_value = jnp.einsum(
            "osp,osk->opk",
            pixel_hits,
            samples.reshape(group_count, run_length, channels),
            precision=highest,
        )
        summed = add_blocks(
            lax.all_to_all(partial_value, "tm", split_axis=0, concat_axis=0, tiled=True)
        )
        return summed.reshape(PIX_DEV, channels)

    def squares(vector):
        return lax.psum(jnp.sum(vector * vector), ("tm", "chan"))

    right_side = binned(filtered(runs_in.astype(jnp.float32).reshape(-1, channels)))
    map_cube = jnp.zeros_like(right_side)
    residual = right_side
    direction = right_side
    norm_now = squares(residual)
    for iteration in range(ITERS):
        picked = jnp.einsum(
            "cb,bpk->cpk",
            owned_blocks,
            direction.reshape(blocks_each, BLK, channels),
            precision=highest,
        )
        values = jnp.einsum(
            "osp,opk->osk",
            pixel_hits,
            lax.all_to_all(picked, "tm", split_axis=0, concat_axis=0, tiled=True),
            precision=highest,
        )
        applied = binned(filtered(values.reshape(-1, channels))) + ridge * direction
        step_size = norm_now / lax.psum(jnp.sum(direction * applied), ("tm", "chan"))
        map_cube = map_cube + step_size * direction
        residual = residual - step_size * applied
        norm_next = squares(residual)
        direction = residual + norm_next / norm_now * direction
        norm_now = norm_next
    return (map_cube, residual)


def solution(mesh):
    in_specs = (P("tm", "chan"), P("tm", "chan"), P("tm"), P(), P("chan", None))
    out_specs = (P("tm", "chan"), P("tm", "chan"))
    return jax.shard_map(
        per_device, mesh=mesh, in_specs=in_specs, out_specs=out_specs, check_vma=False
    )
```

profile of v0, /device:TPU:1, one launch (start us, length us, event | category | flops | bytes accessed | tf_op | source)
XLA Modules:
  0.0 1089.1 jit_solution(16559542014718959542)
XLA Ops:
  7.2 0.7 copy-done
  7.9 12.1 %fusion = f32[8192,16]{0,1:T(8,128)} fusion(f32[256,16]{0,1:T(8,128)S(1)} %copy-done, bf16[8192,256]{1,0:T(8,128)(2,1)} %param.6, bf16[8192,256]{1,0:T(8,128)(2,1)} %param.5), kind=kOutput, calls=%fused_computation.12 | convolution fusion | flops 408944640 | bytes 8929280 | tf_op jit(solution)/shard_map/dot_general | solution.py:35
  20.0 44.5 %all-reduce.6.cloned.1.call-done = f32[8192,16]{0,1:T(8,128)} async-done(((f32[8192,16]{0,1:T(8,128)}), f32[8192,16]{0,1:T(8,128)}) %all-reduce.6.cloned.1.call-update) | async-done | bytes 524304 | tf_op jit(solution)/shard_map/psum | solution.py:35
  64.5 10.8 convert_multiply_fusion.6
  75.3 5.8 fusion.15
  81.1 9.9 all-to-all-start
  91.0 0.2 all-reduce.8.cloned.1.call-start
  91.3 0.2 dynamic-slice_reduce_fusion
  91.5 51.7 %all-to-all-done = f32[32,128,256]{2,1,0:T(8,128)} async-done(((f32[32,128,256]{2,1,0:T(8,128)}), f32[32,128,256]{2,1,0:T(8,128)}, u32[]{:S(2)}, u32[]{:S(2)}) %all-to-all-start) | async-done | bytes 4194336 | tf_op jit(solution)/shard_map/all_to_all | solution.py:51
  143.2 5.8 fusion.7
  148.9 1.9 fusion.41
  150.8 2.4 copy.26
  153.3 57.7 %all_to_all.35 = f32[32,128,256]{2,1,0:T(8,128)S(1)} all-to-all(f32[32,128,256]{2,1,0:T(8,128)S(1)} %copy.26), channel_id=1, replica_groups=mesh['tm'=32,'chan'=4] {'tm'}, dimensions={0} | all-to-all | bytes 8388608 | tf_op jit(solution)/shard_map/all_to_all | solution.py:73
  210.9 6.1 fusion.14
  217.1 4.2 convert_multiply_fusion.5
  221.3 3.2 copy-done.4
  224.5 7.9 fusion.44
  232.4 0.4 all-reduce.10.cloned.1.call-start
  232.8 37.8 %all-reduce.8.cloned.1.call-done = f32[8192,16]{0,1:T(8,128)} async-done(((f32[8192,16]{0,1:T(8,128)}), f32[8192,16]{0,1:T(8,128)}) %all-reduce.8.cloned.1.call-update) | async-done | bytes 524304 | tf_op jit(solution)/shard_map/psum | solution.py:35
  270.7 10.4 convert_multiply_fusion.4
  281.1 4.3 fusion.13
  285.4 60.3 %all_to_all.36 = f32[32,128,256]{2,1,0:T(8,128)S(1)} all-to-all(f32[32,128,256]{2,1,0:T(8,128)S(1)} %fusion.13), channel_id=1, replica_groups=mesh['tm'=32,'chan'=4] {'tm'}, dimensions={0} | all-to-all | bytes 8388608 | tf_op jit(solution)/shard_map/all_to_all | solution.py:51
  345.7 5.4 multiply_reduce_fusion.3
  351.1 63.1 %all-reduce = (f32[]{:T(128)}, f32[]{:T(128)}) all-reduce(f32[]{:T(128)} %get-tuple-element.3, f32[]{:T(128)} %get-tuple-element.2), channel_id=1, replica_groups=mesh['tm'=32,'chan'=4] {'tm','chan'}, use_global_device_ids=true, to_apply=%region_2.3 | all-reduce | flops 2 | bytes 16 | tf_op jit(solution)/shard_map/psum | solution.py:56
  415.6 0.9 multiply_reduce_fusion.2
  416.4 62.9 %psum.74 = f32[]{:T(128)} all-reduce(f32[]{:T(128)} %get-tuple-element.8), channel_id=1, replica_groups=mesh['tm'=32,'chan'=4] {'tm','chan'}, use_global_device_ids=true, to_apply=%region_7.8 | all-reduce | flops 1 | bytes 8 | tf_op jit(solution)/shard_map/psum | solution.py:56
  480.7 0.1 multiply_add_fusion.2
  480.8 1.9 fusion.38
  482.7 2.4 copy.30
  485.1 55.6 %all_to_all.37 = f32[32,128,256]{2,1,0:T(8,128)S(1)} all-to-all(f32[32,128,256]{2,1,0:T(8,128)S(1)} %copy.30), channel_id=1, replica_groups=mesh['tm'=32,'chan'=4] {'tm'}, dimensions={0} | all-to-all | bytes 8388608 | tf_op jit(solution)/shard_map/all_to_all | solution.py:73
  540.8 6.1 fusion.12
  546.9 4.2 convert_multiply_fusion.3
  551.1 3.2 copy-done.5
  554.3 7.9 fusion.45
  562.2 0.4 all-reduce.12.cloned.1.call-start
  562.6 36.5 %all-reduce.10.cloned.1.call-done = f32[8192,16]{0,1:T(8,128)} async-done(((f32[8192,16]{0,1:T(8,128)}), f32[8192,16]{0,1:T(8,128)}) %all-reduce.10.cloned.1.call-update) | async-done | bytes 524304 | tf_op jit(solution)/shard_map/psum | solution.py:35
  599.1 10.4 convert_multiply_fusion.2
  609.6 4.3 fusion.11
  613.8 60.3 %all_to_all.38 = f32[32,128,256]{2,1,0:T(8,128)S(1)} all-to-all(f32[32,128,256]{2,1,0:T(8,128)S(1)} %fusion.11), channel_id=1, replica_groups=mesh['tm'=32,'chan'=4] {'tm'}, dimensions={0} | all-to-all | bytes 8388608 | tf_op jit(solution)/shard_map/all_to_all | solution.py:51
  674.2 5.4 multiply_reduce_fusion.1
  679.5 63.1 %psum.76 = f32[]{:T(128)} all-reduce(f32[]{:T(128)} %get-tuple-element.6), channel_id=1, replica_groups=mesh['tm'=32,'chan'=4] {'tm','chan'}, use_global_device_ids=true, to_apply=%region_10.11 | all-reduce | flops 1 | bytes 8 | tf_op jit(solution)/shard_map/psum | solution.py:77
  743.8 0.8 multiply_reduce_fusion
  744.7 62.9 %psum.77 = f32[]{:T(128)} all-reduce(f32[]{:T(128)} %multiply_reduce_fusion), channel_id=1, replica_groups=mesh['tm'=32,'chan'=4] {'tm','chan'}, use_global_device_ids=true, to_apply=%region_12.13 | all-reduce | flops 1 | bytes 8 | tf_op jit(solution)/shard_map/psum | solution.py:56
  808.8 0.1 multiply_add_fusion.1
  808.9 0.8 copy-done.7
  809.7 1.9 fusion.35
  811.6 2.4 copy.34
  814.1 55.6 %all_to_all.39 = f32[32,128,256]{2,1,0:T(8,128)S(1)} all-to-all(f32[32,128,256]{2,1,0:T(8,128)S(1)} %copy.34), channel_id=1, replica_groups=mesh['tm'=32,'chan'=4] {'tm'}, dimensions={0} | all-to-all | bytes 8388608 | tf_op jit(solution)/shard_map/all_to_all | solution.py:73
  869.7 6.1 fusion.10
  875.8 4.2 convert_multiply_fusion.1
  880.0 3.2 copy-done.6
  883.2 7.9 fusion.46
  891.1 36.9 %all-reduce.12.cloned.1.call-done = f32[8192,16]{0,1:T(8,128)} async-done(((f32[8192,16]{0,1:T(8,128)}), f32[8192,16]{0,1:T(8,128)}) %all-reduce.12.cloned.1.call-update) | async-done | bytes 524304 | tf_op jit(solution)/shard_map/psum | solution.py:35
  928.0 10.7 convert_multiply_fusion
  938.7 5.8 fusion.9
  944.6 10.4 all-to-all-start.6
  955.0 0.1 copy.29
  955.1 0.1 copy.33
  955.2 0.1 copy.37
  955.3 51.6 %all-to-all-done.6 = f32[32,128,256]{2,1,0:T(8,128)} async-done(((f32[32,128,256]{2,1,0:T(8,128)}), f32[32,128,256]{2,1,0:T(8,128)}, u32[]{:S(2)}, u32[]{:S(2)}) %all-to-all-start.6) | async-done | bytes 4194336 | tf_op jit(solution)/shard_map/all_to_all | solution.py:51
  1006.9 7.2 fusion.23
  1014.1 64.3 %psum.79 = f32[]{:T(128)} all-reduce(f32[]{:T(128)} %get-tuple-element.15), channel_id=1, replica_groups=mesh['tm'=32,'chan'=4] {'tm','chan'}, use_global_device_ids=true, to_apply=%region_15.16 | all-reduce | flops 1 | bytes 8 | tf_op jit(solution)/shard_map/psum | solution.py:77
  1079.6 1.1 copy.38
  1080.8 1.3 fusion.25
  (27 shorter events, 0.2 us)
Async XLA Ops:
  7.2 0.7 copy-start
  7.2 12.8 %copy-start.11 = (s32[8192]{0:T(1024)S(1)}, s32[8192]{0:T(1024)}, u32[]{:S(2)}) copy-start(s32[8192]{0:T(1024)} %param.7) | copy-start | bytes 98308
  7.2 57.3 %all-reduce.6.cloned.1.call-start = ((), (), s32[]{:S(2)}) async-start(), calls=%async_computation.7 | async-start | bytes 1048576 | tf_op jit(solution)/shard_map/psum | solution.py:35
  81.1 10.2 copy-start.12
  81.1 62.0 %all-to-all-start = ((f32[32,128,256]{2,1,0:T(8,128)}), f32[32,128,256]{2,1,0:T(8,128)}, u32[]{:S(2)}, u32[]{:S(2)}) async-start(f32[32,128,256]{2,1,0:T(8,128)} %fusion.15), calls=%async_computation | async-start | bytes 8388608 | tf_op jit(solution)/shard_map/all_to_all | solution.py:51
  91.0 179.6 %all-reduce.8.cloned.1.call-start = ((), (), s32[]{:S(2)}) async-start(), calls=%async_computation.8 | async-start | bytes 1048576 | tf_op jit(solution)/shard_map/psum | solution.py:35
  210.9 6.1 copy-start.1
  221.3 3.2 copy-start.4
  232.4 366.7 %all-reduce.10.cloned.1.call-start = ((), (), s32[]{:S(2)}) async-start(), calls=%async_computation.9 | async-start | bytes 1048576 | tf_op jit(solution)/shard_map/psum | solution.py:35
  540.8 6.1 copy-start.2
  551.1 3.2 copy-start.5
  562.2 365.9 %all-reduce.12.cloned.1.call-start = ((), (), s32[]{:S(2)}) async-start(), calls=%async_computation.10 | async-start | bytes 1048576 | tf_op jit(solution)/shard_map/psum | solution.py:35
  808.9 0.8 copy-start.7
  869.7 6.1 copy-start.3
  880.0 3.2 copy-start.6
  944.6 10.5 copy-start.9
  944.6 10.6 copy-start.10
  944.6 62.3 %copy-start.8 = (f32[8,64,256]{2,0,1:T(8,128)S(1)}, f32[8,64,256]{2,0,1:T(8,128)}, u32[]{:S(2)}) copy-start(f32[8,64,256]{2,0,1:T(8,128)} %copy-done.7) | copy-start | bytes 1572868
  944.6 62.3 %all-to-all-start.6 = ((f32[32,128,256]{2,1,0:T(8,128)}), f32[32,128,256]{2,1,0:T(8,128)}, u32[]{:S(2)}, u32[]{:S(2)}) async-start(f32[32,128,256]{2,1,0:T(8,128)} %fusion.9), calls=%async_computation.6 | async-start | bytes 8388608 | tf_op jit(solution)/shard_map/all_to_all | solution.py:51
Sparse Core Ops, SparseCore 0:
  20.1 44.3 all-reduce.5
  232.5 38.1 all-reduce.7
  562.3 36.7 all-reduce.9
  891.2 36.7 all-reduce.11
where the time goes:
time: 1100 us; the launch traced here: 1090 us
  blocking collectives  606 us (55%)
  waiting for transfers between devices  259 us (24%)
  matrix products  146 us (13%)
  starting transfers between devices  21.5 us (2%)
  between operations  21 us (2%)
  local copies, waits for them, and re-layouts  20.1 us (2%)
  other arithmetic  15.7 us (1%)
    psum x3, blocking collectives, squares(): return lax.psum(jnp.sum(vector * vector), ('tm', 'chan'))  189 us
    all_to_all x3, blocking collectives, per_device(): lax.all_to_all(picked, 'tm', split_axis=0, concat_axis=0, tiled=True)  169 us
    psum x4, waiting for transfers between devices, filtered(): lax.psum(jnp.dot(weighted, foreground_modes, precision=highest), 'chan')  156 us
    psum x2, blocking collectives, per_device(): lax.psum(jnp.sum(direction * applied), ('tm', 'chan'))  127 us
    all_to_all x2, blocking collectives, binned(): lax.all_to_all(partial_value, 'tm', split_axis=0, concat_axis=0, tiled=True)  121 us
    all_to_all x2, waiting for transfers between devices, binned(): lax.all_to_all(partial_value, 'tm', split_axis=0, concat_axis=0, tiled=True)  103 us
    dot_general x4, matrix products, filtered(): jnp.dot(amplitudes, foreground_modes.T, precision=highest)  42.3 us
    dot_general x4, matrix products, filtered(): jnp.dot(weighted, foreground_modes, precision=highest)  35.6 us
  transfers between devices with their start and end apart: 6, of which 6 were waited for; matrix products, arithmetic and copies ran while one was open for 0% of the time, Pallas kernels for 0%

commit v1 on v0

v1 whole, which is shorter than its diff:
```python
import jax
import jax.numpy as jnp
from jax import lax
from jax.sharding import PartitionSpec as P

PIX_DEV = 512
BLK = 128
ITERS = 3


highest = lax.Precision.HIGHEST
ridge = 1.0


def chan_sum(value):
    count = lax.axis_size("chan")
    total = value
    for shift in range(1, count):
        pairs = [(i, (i + shift) % count) for i in range(count)]
        total = total + lax.ppermute(value, "chan", pairs)
    return total


def global_sum(value):
    chans = lax.axis_size("chan")
    got = lax.all_to_all(jnp.broadcast_to(value, (chans, 1)), "chan", 0, 0, tiled=True)
    part = jnp.sum(got)
    groups = lax.axis_size("tm")
    got = lax.all_to_all(jnp.broadcast_to(part, (groups, 1)), "tm", 0, 0, tiled=True)
    return jnp.sum(got)


def per_device(streams, weights, pointing, touched, foreground_modes):
    group_count = lax.axis_size("tm")
    owner_index = lax.axis_index("tm")
    sample_count, channels = streams.shape
    run_length = sample_count // group_count
    blocks_each = PIX_DEV // BLK

    runs = streams.reshape(group_count, run_length, channels)
    scales = weights.reshape(group_count, run_length, channels)
    points = pointing.reshape(group_count, run_length)
    if run_length == channels:
        packed = jnp.concatenate(
            [runs, scales, points.astype(jnp.bfloat16)[:, None, :]], axis=1
        )
        packed = lax.all_to_all(packed, "tm", 0, 0, tiled=True)
        runs_in = packed[:, :run_length]
        weights_in = packed[:, run_length : 2 * run_length]
        points_in = packed[:, 2 * run_length].astype(jnp.int32)
    else:
        runs_in = lax.all_to_all(runs, "tm", 0, 0, tiled=True)
        weights_in = lax.all_to_all(scales, "tm", 0, 0, tiled=True)
        points_in = lax.all_to_all(points, "tm", 0, 0, tiled=True)

    column = lax.dynamic_index_in_dim(touched, owner_index, axis=1, keepdims=False)
    owned_blocks = (column[:, None] == jnp.arange(blocks_each, dtype=jnp.int32)[None, :]).astype(
        jnp.float32
    )
    pixel_hits = (points_in[:, :, None] == jnp.arange(BLK, dtype=jnp.int32)[None, None, :]).astype(
        jnp.float32
    )
    noise_weights = weights_in.astype(jnp.float32)

    def filtered(samples):
        weighted = noise_weights * samples
        amplitudes = jnp.einsum("csk,km->mcs", weighted, foreground_modes, precision=highest)
        amplitudes = chan_sum(amplitudes)
        return noise_weights * (
            weighted - jnp.einsum("mcs,km->csk", amplitudes, foreground_modes, precision=highest)
        )

    def binned(samples):
        partial_value = jnp.einsum("csp,csk->cpk", pixel_hits, samples, precision=highest)
        summed = jnp.einsum("cb,cpk->bpk", owned_blocks, partial_value, precision=highest)
        return summed.reshape(PIX_DEV, channels)

    def pointed(field):
        picked = jnp.einsum(
            "cb,bpk->cpk",
            owned_blocks,
            field.reshape(blocks_each, BLK, channels),
            precision=highest,
        )
        return jnp.einsum("csp,cpk->csk", pixel_hits, picked, precision=highest)

    def squares(vector):
        return global_sum(jnp.sum(vector * vector))

    right_side = binned(filtered(runs_in.astype(jnp.float32)))
    map_cube = jnp.zeros_like(right_side)
    residual = right_side
    direction = right_side
    norm_now = squares(residual)
    for iteration in range(ITERS):
        applied = binned(filtered(pointed(direction))) + ridge * direction
        step_size = norm_now / global_sum(jnp.sum(direction * applied))
        map_cube = map_cube + step_size * direction
        residual = residual - step_size * applied
        norm_next = squares(residual)
        direction = residual + norm_next / norm_now * direction
        norm_now = norm_next
    return (map_cube, residual)


def solution(mesh):
    in_specs = (P("tm", "chan"), P("tm", "chan"), P("tm"), P(), P("chan", None))
    out_specs = (P("tm", "chan"), P("tm", "chan"))
    return jax.shard_map(
        per_device, mesh=mesh, in_specs=in_specs, out_specs=out_specs, check_vma=False
    )
```

time: 1100 us -> 530 us (0.48)
  blocking collectives: 606 us -> 174 us
  waiting for transfers between devices: 259 us -> 120 us
  between operations: 21 us -> 7.77 us
    psum x5 -> x0, blocking collectives: 316 us -> none  [the longest x3 189 us: squares(): return lax.psum(jnp.sum(vector * vector), ('tm', 'chan'))]
    psum x4 -> x0, waiting for transfers between devices: 156 us -> none  [filtered(): lax.psum(jnp.dot(weighted, foreground_modes, precision=highest), 'chan')]
    all_to_all x5 -> x9, blocking collectives: 290 us -> 174 us  [the longest x1 106 us: per_device(): packed = lax.all_to_all(packed, 'tm', 0, 0, tiled=True)]
    ppermute x0 -> x12, waiting for transfers between devices: none -> 98.2 us  [chan_sum(): total = total + lax.ppermute(value, 'chan', pairs)]
    all_to_all x2 -> x4, waiting for transfers between devices: 103 us -> 21.9 us  [the longest x3 18.5 us: global_sum(): lax.all_to_all(jnp.broadcast_to(part, (groups, 1)), 'tm', 0, 0, tiled=True)]
    mul x3 -> x0, other arithmetic: 12.6 us -> none  [filtered(): weighted = noise_weights * samples]
  transfers between devices with their start and end apart: 6 -> 16, of which waited for: 6 -> 15; matrix products, arithmetic and copies ran while one was open for 0% -> 1% of each run, Pallas kernels for 0% -> 0%
where the time goes in v1:
time: 530 us; the launch traced here: 522 us
  blocking collectives  174 us (33%)
  matrix products  153 us (29%)
  waiting for transfers between devices  120 us (23%)
  starting transfers between devices  29.4 us (6%)
  local copies, waits for them, and re-layouts  20.4 us (4%)
  other arithmetic  17.5 us (3%)
  between operations  7.77 us (1%)
    all_to_all x1, blocking collectives, per_device(): packed = lax.all_to_all(packed, 'tm', 0, 0, tiled=True)  106 us
    ppermute x12, waiting for transfers between devices, chan_sum(): total = total + lax.ppermute(value, 'chan', pairs)  98.2 us
    dot_general x4, matrix products, binned(): jnp.einsum('csp,csk->cpk', pixel_hits, samples, precision=highest)  36.2 us
    all_to_all x3, blocking collectives, global_sum(): lax.all_to_all(jnp.broadcast_to(part, (groups, 1)), 'tm', 0, 0, tiled=True)  35.6 us
    dot_general x4, matrix products, filtered(): jnp.einsum('mcs,km->csk', amplitudes, foreground_modes, precision=highest)  34.1 us
    all_to_all x5, blocking collectives, global_sum(): lax.all_to_all(jnp.broadcast_to(value, (chans, 1)), 'chan', 0, 0, tiled=T...  32.4 us
    dot_general x4, matrix products, filtered(): jnp.einsum('csk,km->mcs', weighted, foreground_modes, precision=highest)  31.4 us
    dot_general x4, matrix products, binned(): jnp.einsum('cb,cpk->bpk', owned_blocks, partial_value, precision=highest)  25.8 us
  transfers between devices with their start and end apart: 16, of which 15 were waited for; matrix products, arithmetic and copies ran while one was open for 1% of the time, Pallas kernels for 0%

profile of v1, /device:TPU:1, one launch (start us, length us, event | category | flops | bytes accessed | tf_op | source)
XLA Modules:
  0.0 522.3 jit_solution(9073594417185988120)
XLA Ops:
  1.4 4.2 pad_maximum_fusion
  5.6 105.9 %all_to_all.77 = bf16[32,513,256]{2,1,0:T(8,128)(2,1)S(1)} all-to-all(bf16[32,513,256]{2,1,0:T(8,128)(2,1)S(1)} %pad_maximum_fusion), channel_id=1, replica_groups=mesh['tm'=32,'chan'=4] {'tm'}, dimensions={0} | all-to-all | bytes 16809984 | tf_op jit(solution)/shard_map/all_to_all | solution.py:47
  111.6 3.3 copy-done.1
  114.8 7.8 %fusion.38 = f32[16,32,256]{2,0,1:T(8,128)S(1)} fusion(bf16[32,513,256]{2,1,0:T(8,128)(2,1)S(1)} %all_to_all.77, f32[256,16]{0,1:T(8,128)S(1)} %copy-done), kind=kOutput, calls=%fused_computation.48 | convolution fusion | flops 408944640 | bytes 8929280 | tf_op jit(solution)/shard_map/csk,km->mcs/dot_general | solution.py:67
  122.6 3.8 collective-permute-start.2
  127.5 1.1 slice_convert_fusion
  128.6 19.9 %collective-permute-done.2 = f32[16,32,256]{2,0,1:T(8,128)S(1)} collective-permute-done((f32[16,32,256]{2,0,1:T(8,128)S(1)}, f32[16,32,256]{2,0,1:T(8,128)S(1)}, u32[]{:S(2)}, u32[]{:S(2)}) %collective-permute-start.2) | collective-permute-done | bytes 524320 | tf_op jit(solution)/shard_map/ppermute | solution.py:20
  148.5 4.3 collective-permute-done
  152.8 7.0 %fusion.69 = f32[32,256,256]{2,1,0:T(8,128)S(1)} fusion(f32[16,32,256]{2,0,1:T(8,128)S(1)} %collective-permute-done.2, f32[16,32,256]{2,0,1:T(8,128)S(1)} %collective-permute-done.1, f32[16,32,256]{2,0,1:T(8,128)S(1)} %fusion.38, f32[16,32,256]{2,0,1:T(8,128)S(1)} %collective-permute-done, f32[256,16]{0,1:T(8,128)S(1)} %copy-done), kind=kOutput, calls=%fused_computation.95 | convolution fusion | flops 403046400 | bytes 10502144 | tf_op jit(solution)/shard_map/mcs,km->csk/dot_general | solution.py:70
  159.8 6.9 %fusion = f32[32,128,256]{2,1,0:T(8,128)} fusion(f32[32,256,256]{2,1,0:T(8,128)S(1)} %fusion.69, bf16[32,513,256]{2,1,0:T(8,128)(2,1)S(1)} %copy-done.2, s32[32,256]{1,0:T(8,128)S(1)} %bitcast.119), kind=kOutput, calls=%fused_computation.9 | convolution fusion | flops 3232759808 | bytes 21004288 | tf_op jit(solution)/shard_map/csp,csk->cpk/dot_general | solution.py:74
  166.7 5.8 %fusion.24 = f32[4,128,256]{2,0,1:T(4,128)S(1)} fusion(f32[32,128,256]{2,1,0:T(8,128)} %fusion, s32[32]{0:T(128)S(1)} %dynamic-slice_reduce_fusion), kind=kOutput, calls=%fused_computation.33 | convolution fusion | flops 50331776 | bytes 4718720 | tf_op jit(solution)/shard_map/cb,cpk->bpk/dot_general | solution.py:75
  172.5 1.9 fusion.89
  174.3 6.9 %fusion.22 = f32[32,256,256]{2,1,0:T(8,128)S(1)} fusion(f32[32,128,256]{2,0,1:T(8,128)S(1)} %fusion.89, s32[32,256]{1,0:T(8,128)S(1)} %bitcast.120), kind=kOutput, calls=%fused_computation.31 | convolution fusion | flops 3222274048 | bytes 12615680 | tf_op jit(solution)/shard_map/csp,cpk->csk/dot_general | solution.py:85
  181.2 7.6 %fusion.37 = f32[16,32,256]{2,0,1:T(8,128)S(1)} fusion(f32[32,256,256]{2,1,0:T(8,128)S(1)} %fusion.22, bf16[32,513,256]{2,1,0:T(8,128)(2,1)S(1)} %copy-done.2, f32[256,16]{0,1:T(8,128)S(1)} %copy-done), kind=kOutput, calls=%fused_computation.47 | convolution fusion | flops 406847488 | bytes 13123584 | tf_op jit(solution)/shard_map/csk,km->mcs/dot_general | solution.py:67
  189.2 1.2 collective-permute-start.3
  190.4 11.4 %collective-permute-done.5 = f32[16,32,256]{2,0,1:T(8,128)S(1)} collective-permute-done((f32[16,32,256]{2,0,1:T(8,128)S(1)}, f32[16,32,256]{2,0,1:T(8,128)S(1)}, u32[]{:S(2)}, u32[]{:S(2)}) %collective-permute-start.5) | collective-permute-done | bytes 524320 | tf_op jit(solution)/shard_map/ppermute | solution.py:20
  201.8 1.0 collective-permute-done.4
  202.8 12.8 %collective-permute-done.3 = f32[16,32,256]{2,0,1:T(8,128)S(1)} collective-permute-done((f32[16,32,256]{2,0,1:T(8,128)S(1)}, f32[16,32,256]{2,0,1:T(8,128)S(1)}, u32[]{:S(2)}, u32[]{:S(2)}) %collective-permute-start.3) | collective-permute-done | bytes 524320 | tf_op jit(solution)/shard_map/ppermute | solution.py:20
  215.6 9.1 %fusion.65 = f32[32,256,256]{2,1,0:T(8,128)} fusion(f32[16,32,256]{2,0,1:T(8,128)S(1)} %collective-permute-done.5, f32[16,32,256]{2,0,1:T(8,128)S(1)} %collective-permute-done.4, f32[16,32,256]{2,0,1:T(8,128)S(1)} %fusion.37, f32[16,32,256]{2,0,1:T(8,128)S(1)} %collective-permute-done.3, f32[256,16]{0,1:T(8,128)S(1)} %copy-done), kind=kOutput, calls=%fused_computation.90 | convolution fusion | flops 403046400 | bytes 10502144 | tf_op jit(solution)/shard_map/mcs,km->csk/dot_general | solution.py:70
  224.7 10.4 %fusion.1 = f32[32,128,256]{2,1,0:T(8,128)} fusion(f32[32,256,256]{2,1,0:T(8,128)} %fusion.65, f32[32,256,256]{2,1,0:T(8,128)S(1)} %fusion.22, s32[32,256]{1,0:T(8,128)S(1)} %bitcast.121, bf16[32,513,256]{2,1,0:T(8,128)(2,1)S(1)} %copy-done.2), kind=kOutput, calls=%fused_computation.10 | convolution fusion | flops 3230662656 | bytes 25198592 | tf_op jit(solution)/shard_map/csp,csk->cpk/dot_general | solution.py:74
  235.0 7.4 %multiply_reduce_fusion.3 = (f32[]{:T(128)}, f32[]{:T(128)}, f32[4,128,256]{2,0,1:T(4,128)S(1)}, f32[4,128,256]{2,0,1:T(4,128)}) fusion(f32[4,128,256]{2,0,1:T(4,128)S(1)} %fusion.24, f32[32,128,256]{2,1,0:T(8,128)} %fusion.1, s32[32]{0:T(128)S(1)} %dynamic-slice_reduce_fusion), kind=kOutput, calls=%fused_computation.89 | convolution fusion | flops 50987136 | bytes 5767304 | tf_op jit(solution)/shard_map/cb,cpk->bpk/dot_general | solution.py:75
  243.1 6.5 %all_to_all.78 = f32[4,1,1]{2,1,0:T(1,128)S(1)} all-to-all(f32[4,1,1]{2,1,0:T(1,128)S(1)} %broadcast_in_dim.43), channel_id=1, replica_groups=mesh['tm'=32,'chan'=4] {'chan'}, dimensions={0} | all-to-all | bytes 32 | tf_op jit(solution)/shard_map/all_to_all | solution.py:26
  249.6 1.3 broadcast_in_dim.41
  250.9 3.2 all-to-all-start.1
  254.8 3.4 all-to-all-done.1
  258.1 1.3 broadcast_in_dim.44
  259.4 6.3 %all-to-all-start.4 = ((f32[32,1,1]{2,1,0:T(1,128)}), f32[32,1,1]{2,1,0:T(1,128)S(1)}, u32[]{:S(2)}, u32[]{:S(2)}) async-start(f32[32,1,1]{2,1,0:T(1,128)} %broadcast_in_dim.44), calls=%async_computation.4 | async-start | bytes 32768 | tf_op jit(solution)/shard_map/all_to_all | solution.py:29
  266.3 6.3 %all-to-all-done.4 = f32[32,1,1]{2,1,0:T(1,128)S(1)} async-done(((f32[32,1,1]{2,1,0:T(1,128)}), f32[32,1,1]{2,1,0:T(1,128)S(1)}, u32[]{:S(2)}, u32[]{:S(2)}) %all-to-all-start.4) | async-done | bytes 160 | tf_op jit(solution)/shard_map/all_to_all | solution.py:29
  272.7 1.3 broadcast_in_dim.42
  274.0 4.1 all-to-all-start.2
  278.8 6.3 %all-to-all-done.2 = f32[32,1,1]{2,1,0:T(1,128)S(1)} async-done(((f32[32,1,1]{2,1,0:T(1,128)}), f32[32,1,1]{2,1,0:T(1,128)S(1)}, u32[]{:S(2)}, u32[]{:S(2)}) %all-to-all-start.2) | async-done | bytes 160 | tf_op jit(solution)/shard_map/all_to_all | solution.py:29
  288.8 6.5 %all_to_all.79 = f32[4,1,1]{2,1,0:T(1,128)S(1)} all-to-all(f32[4,1,1]{2,1,0:T(1,128)S(1)} %broadcast_in_dim.45), channel_id=1, replica_groups=mesh['tm'=32,'chan'=4] {'chan'}, dimensions={0} | all-to-all | bytes 32 | tf_op jit(solution)/shard_map/all_to_all | solution.py:26
  296.6 11.8 %all_to_all.80 = f32[32,1,1]{2,1,0:T(1,128)S(1)} all-to-all(f32[32,1,1]{2,1,0:T(1,128)S(1)} %broadcast_in_dim.46), channel_id=1, replica_groups=mesh['tm'=32,'chan'=4] {'tm'}, dimensions={0} | all-to-all | bytes 256 | tf_op jit(solution)/shard_map/all_to_all | solution.py:29
  310.6 1.9 fusion.86
  312.5 6.7 %fusion.18 = f32[32,256,256]{2,1,0:T(8,128)S(1)} fusion(f32[32,128,256]{2,0,1:T(8,128)S(1)} %fusion.86, s32[32,256]{1,0:T(8,128)S(1)} %bitcast.122), kind=kOutput, calls=%fused_computation.27 | convolution fusion | flops 3222274048 | bytes 12615680 | tf_op jit(solution)/shard_map/csp,cpk->csk/dot_general | solution.py:85
  319.2 3.2 copy-done.3
  322.4 7.9 %fusion.36 = f32[16,32,256]{2,0,1:T(8,128)S(1)} fusion(f32[32,256,256]{2,1,0:T(8,128)S(1)} %fusion.18, bf16[32,513,256]{2,1,0:T(8,128)(2,1)S(1)} %bitcast.106, f32[256,16]{0,1:T(8,128)S(1)} %copy-done), kind=kOutput, calls=%fused_computation.46 | convolution fusion | flops 406847488 | bytes 13123584 | tf_op jit(solution)/shard_map/csk,km->mcs/dot_general | solution.py:67
  331.3 1.2 collective-permute-start.7
  332.5 10.7 %collective-permute-done.8 = f32[16,32,256]{2,0,1:T(8,128)S(1)} collective-permute-done((f32[16,32,256]{2,0,1:T(8,128)S(1)}, f32[16,32,256]{2,0,1:T(8,128)S(1)}, u32[]{:S(2)}, u32[]{:S(2)}) %collective-permute-start.8) | collective-permute-done | bytes 524320 | tf_op jit(solution)/shard_map/ppermute | solution.py:20
  343.2 2.2 collective-permute-done.7
  345.4 12.5 %collective-permute-done.6 = f32[16,32,256]{2,0,1:T(8,128)S(1)} collective-permute-done((f32[16,32,256]{2,0,1:T(8,128)S(1)}, f32[16,32,256]{2,0,1:T(8,128)S(1)}, u32[]{:S(2)}, u32[]{:S(2)}) %collective-permute-start.6) | collective-permute-done | bytes 524320 | tf_op jit(solution)/shard_map/ppermute | solution.py:20
  357.9 8.9 %fusion.61 = f32[32,256,256]{2,1,0:T(8,128)} fusion(f32[16,32,256]{2,0,1:T(8,128)S(1)} %collective-permute-done.8, f32[16,32,256]{2,0,1:T(8,128)S(1)} %collective-permute-done.7, f32[16,32,256]{2,0,1:T(8,128)S(1)} %fusion.36, f32[16,32,256]{2,0,1:T(8,128)S(1)} %collective-permute-done.6, f32[256,16]{0,1:T(8,128)S(1)} %copy-done), kind=kOutput, calls=%fused_computation.82 | convolution fusion | flops 403046400 | bytes 10502144 | tf_op jit(solution)/shard_map/mcs,km->csk/dot_general | solution.py:70
  366.8 8.5 %fusion.2 = f32[32,128,256]{2,1,0:T(8,128)S(1)} fusion(f32[32,256,256]{2,1,0:T(8,128)} %fusion.61, f32[32,256,256]{2,1,0:T(8,128)} %copy-done.3, s32[32,256]{1,0:T(8,128)S(1)} %bitcast.123, bf16[32,513,256]{2,1,0:T(8,128)(2,1)S(1)} %bitcast.106), kind=kOutput, calls=%fused_computation.11 | convolution fusion | flops 3230662656 | bytes 25198592 | tf_op jit(solution)/shard_map/csp,csk->cpk/dot_general | solution.py:74
  375.3 5.3 %multiply_reduce_fusion.1 = (f32[]{:T(128)}, f32[4,128,256]{2,0,1:T(4,128)S(1)}, f32[4,128,256]{2,0,1:T(4,128)}) fusion(f32[4,128,256]{2,0,1:T(4,128)S(1)} %bitcast.111, f32[32,128,256]{2,1,0:T(8,128)S(1)} %fusion.2, s32[32]{0:T(128)S(1)} %dynamic-slice_reduce_fusion), kind=kOutput, calls=%fused_computation.81 | convolution fusion | flops 50724992 | bytes 5767300 | tf_op jit(solution)/shard_map/cb,cpk->bpk/dot_general | solution.py:75
  381.3 6.5 %all_to_all.81 = f32[4,1,1]{2,1,0:T(1,128)S(1)} all-to-all(f32[4,1,1]{2,1,0:T(1,128)S(1)} %broadcast_in_dim.47), channel_id=1, replica_groups=mesh['tm'=32,'chan'=4] {'chan'}, dimensions={0} | all-to-all | bytes 32 | tf_op jit(solution)/shard_map/all_to_all | solution.py:26
  389.1 11.9 %all_to_all.82 = f32[32,1,1]{2,1,0:T(1,128)S(1)} all-to-all(f32[32,1,1]{2,1,0:T(1,128)S(1)} %broadcast_in_dim.48), channel_id=1, replica_groups=mesh['tm'=32,'chan'=4] {'tm'}, dimensions={0} | all-to-all | bytes 256 | tf_op jit(solution)/shard_map/all_to_all | solution.py:29
  404.7 6.5 %all_to_all.83 = f32[4,1,1]{2,1,0:T(1,128)S(1)} all-to-all(f32[4,1,1]{2,1,0:T(1,128)S(1)} %broadcast_in_dim.49), channel_id=1, replica_groups=mesh['tm'=32,'chan'=4] {'chan'}, dimensions={0} | all-to-all | bytes 32 | tf_op jit(solution)/shard_map/all_to_all | solution.py:26
  412.5 11.8 %all_to_all.84 = f32[32,1,1]{2,1,0:T(1,128)S(1)} all-to-all(f32[32,1,1]{2,1,0:T(1,128)S(1)} %broadcast_in_dim.50), channel_id=1, replica_groups=mesh['tm'=32,'chan'=4] {'tm'}, dimensions={0} | all-to-all | bytes 256 | tf_op jit(solution)/shard_map/all_to_all | solution.py:29
  426.3 1.9 fusion.83
  428.3 6.7 %fusion.14 = f32[32,256,256]{2,1,0:T(8,128)S(1)} fusion(f32[32,128,256]{2,0,1:T(8,128)S(1)} %fusion.83, s32[32,256]{1,0:T(8,128)S(1)} %bitcast.124), kind=kOutput, calls=%fused_computation.23 | convolution fusion | flops 3222274048 | bytes 12615680 | tf_op jit(solution)/shard_map/csp,cpk->csk/dot_general | solution.py:85
  435.0 8.0 %fusion.35 = f32[16,32,256]{2,0,1:T(8,128)S(1)} fusion(f32[32,256,256]{2,1,0:T(8,128)S(1)} %fusion.14, bf16[32,513,256]{2,1,0:T(8,128)(2,1)S(1)} %bitcast.108, f32[256,16]{0,1:T(8,128)S(1)} %copy-done), kind=kOutput, calls=%fused_computation.45 | convolution fusion | flops 406847488 | bytes 13123584 | tf_op jit(solution)/shard_map/csk,km->mcs/dot_general | solution.py:67
  444.0 1.2 collective-permute-start.10
  447.1 8.8 %collective-permute-done.11 = f32[16,32,256]{2,0,1:T(8,128)S(1)} collective-permute-done((f32[16,32,256]{2,0,1:T(8,128)S(1)}, f32[16,32,256]{2,0,1:T(8,128)S(1)}, u32[]{:S(2)}, u32[]{:S(2)}) %collective-permute-start.11) | collective-permute-done | bytes 524320 | tf_op jit(solution)/shard_map/ppermute | solution.py:20
  455.9 2.1 collective-permute-done.10
  458.1 12.5 %collective-permute-done.9 = f32[16,32,256]{2,0,1:T(8,128)S(1)} collective-permute-done((f32[16,32,256]{2,0,1:T(8,128)S(1)}, f32[16,32,256]{2,0,1:T(8,128)S(1)}, u32[]{:S(2)}, u32[]{:S(2)}) %collective-permute-start.9) | collective-permute-done | bytes 524320 | tf_op jit(solution)/shard_map/ppermute | solution.py:20
  470.6 9.0 %fusion.57 = f32[32,256,256]{2,1,0:T(8,128)} fusion(f32[16,32,256]{2,0,1:T(8,128)S(1)} %collective-permute-done.11, f32[16,32,256]{2,0,1:T(8,128)S(1)} %collective-permute-done.10, f32[16,32,256]{2,0,1:T(8,128)S(1)} %fusion.35, f32[16,32,256]{2,0,1:T(8,128)S(1)} %collective-permute-done.9, f32[256,16]{0,1:T(8,128)S(1)} %copy-done), kind=kOutput, calls=%fused_computation.74 | convolution fusion | flops 403046400 | bytes 10502144 | tf_op jit(solution)/shard_map/mcs,km->csk/dot_general | solution.py:70
  479.6 10.5 %fusion.3 = f32[32,128,256]{2,1,0:T(8,128)} fusion(f32[32,256,256]{2,1,0:T(8,128)} %fusion.57, f32[32,256,256]{2,1,0:T(8,128)S(1)} %fusion.14, s32[32,256]{1,0:T(8,128)S(1)} %bitcast.125, bf16[32,513,256]{2,1,0:T(8,128)(2,1)S(1)} %bitcast.108), kind=kOutput, calls=%fused_computation.12 | convolution fusion | flops 3230662656 | bytes 25198592 | tf_op jit(solution)/shard_map/csp,csk->cpk/dot_general | solution.py:74
  490.1 7.3 %fusion.47 = (f32[]{:T(128)}, f32[4,128,256]{2,0,1:T(4,128)}) fusion(f32[4,128,256]{2,0,1:T(4,128)S(1)} %bitcast.116, f32[32,128,256]{2,1,0:T(8,128)} %fusion.3, s32[32]{0:T(128)S(1)} %dynamic-slice_reduce_fusion), kind=kOutput, calls=%fused_computation.58 | convolution fusion | flops 50724992 | bytes 5243012 | tf_op jit(solution)/shard_map/cb,cpk->bpk/dot_general | solution.py:75
  498.0 6.5 %all_to_all.85 = f32[4,1,1]{2,1,0:T(1,128)S(1)} all-to-all(f32[4,1,1]{2,1,0:T(1,128)S(1)} %broadcast_in_dim.51), channel_id=1, replica_groups=mesh['tm'=32,'chan'=4] {'chan'}, dimensions={0} | all-to-all | bytes 32 | tf_op jit(solution)/shard_map/all_to_all | solution.py:26
  505.2 1.3 broadcast_in_dim.52
  506.5 5.3 %all-to-all-start.12 = ((f32[32,1,1]{2,1,0:T(1,128)}), f32[32,1,1]{2,1,0:T(1,128)S(1)}, u32[]{:S(2)}, u32[]{:S(2)}) async-start(f32[32,1,1]{2,1,0:T(1,128)} %broadcast_in_dim.52), calls=%async_computation.12 | async-start | bytes 32768 | tf_op jit(solution)/shard_map/all_to_all | solution.py:29
  511.8 1.1 copy.53
  513.0 5.9 %all-to-all-done.12 = f32[32,1,1]{2,1,0:T(1,128)S(1)} async-done(((f32[32,1,1]{2,1,0:T(1,128)}), f32[32,1,1]{2,1,0:T(1,128)S(1)}, u32[]{:S(2)}, u32[]{:S(2)}) %all-to-all-start.12) | async-done | bytes 160 | tf_op jit(solution)/shard_map/all_to_all | solution.py:29
  520.7 1.3 fusion.49
  (70 shorter events, 21.6 us)
Async XLA Ops:
  0.6 114.2 %copy-start = (f32[256,16]{0,1:T(8,128)S(1)}, f32[256,16]{0,1:T(8,128)}, u32[]{:S(2)}) copy-start(f32[256,16]{0,1:T(8,128)} %param.9) | copy-start | bytes 49156
  5.6 121.7 %copy-start.8 = (s32[32,32]{1,0:T(8,128)S(1)}, s32[32,32]{1,0:T(8,128)}, u32[]{:S(2)}) copy-start(s32[32,32]{1,0:T(8,128)} %param.8) | copy-start | bytes 12292
  111.6 3.3 copy-start.1
  122.6 25.9 %collective-permute-start.2 = (f32[16,32,256]{2,0,1:T(8,128)S(1)}, f32[16,32,256]{2,0,1:T(8,128)S(1)}, u32[]{:S(2)}, u32[]{:S(2)}) collective-permute-start(f32[16,32,256]{2,0,1:T(8,128)S(1)} %fusion.38), channel_id=1, source_target_pairs={{0,3},{1,0},{2,1},{3,2},{4,7},{5,4},{6,5},{7,6},{8,11},{9,8},{10,9... | collective-permute-start | bytes 1572872 | tf_op jit(solution)/shard_map/ppermute | solution.py:20
  126.4 22.1 %collective-permute-start.1 = (f32[16,32,256]{2,0,1:T(8,128)S(1)}, f32[16,32,256]{2,0,1:T(8,128)S(1)}, u32[]{:S(2)}, u32[]{:S(2)}) collective-permute-start(f32[16,32,256]{2,0,1:T(8,128)S(1)} %fusion.38), channel_id=1, source_target_pairs={{0,2},{1,3},{2,0},{3,1},{4,6},{5,7},{6,4},{7,5},{8,10},{9,11},{10,... | collective-permute-start | bytes 1572872 | tf_op jit(solution)/shard_map/ppermute | solution.py:20
  126.4 26.4 %collective-permute-start = (f32[16,32,256]{2,0,1:T(8,128)S(1)}, f32[16,32,256]{2,0,1:T(8,128)S(1)}, u32[]{:S(2)}, u32[]{:S(2)}) collective-permute-start(f32[16,32,256]{2,0,1:T(8,128)S(1)} %fusion.38), channel_id=1, source_target_pairs={{0,1},{1,2},{2,3},{3,0},{4,5},{5,6},{6,7},{7,4},{8,9},{9,10},{10,1... | collective-permute-start | bytes 1572872 | tf_op jit(solution)/shard_map/ppermute | solution.py:20
  127.3 32.5 %copy-start.2 = (bf16[32,513,256]{2,1,0:T(8,128)(2,1)S(1)}, bf16[32,513,256]{2,1,0:T(8,128)(2,1)}, u32[]{:S(2)}) copy-start(bf16[32,513,256]{2,1,0:T(8,128)(2,1)} %copy-done.1) | copy-start | bytes 25214980
  188.8 12.9 %collective-permute-start.5 = (f32[16,32,256]{2,0,1:T(8,128)S(1)}, f32[16,32,256]{2,0,1:T(8,128)S(1)}, u32[]{:S(2)}, u32[]{:S(2)}) collective-permute-start(f32[16,32,256]{2,0,1:T(8,128)S(1)} %fusion.37), channel_id=1, source_target_pairs={{0,3},{1,0},{2,1},{3,2},{4,7},{5,4},{6,5},{7,6},{8,11},{9,8},{10,9... | collective-permute-start | bytes 1572872 | tf_op jit(solution)/shard_map/ppermute | solution.py:20
  188.9 13.9 %collective-permute-start.4 = (f32[16,32,256]{2,0,1:T(8,128)S(1)}, f32[16,32,256]{2,0,1:T(8,128)S(1)}, u32[]{:S(2)}, u32[]{:S(2)}) collective-permute-start(f32[16,32,256]{2,0,1:T(8,128)S(1)} %fusion.37), channel_id=1, source_target_pairs={{0,2},{1,3},{2,0},{3,1},{4,6},{5,7},{6,4},{7,5},{8,10},{9,11},{10,... | collective-permute-start | bytes 1572872 | tf_op jit(solution)/shard_map/ppermute | solution.py:20
  189.2 26.4 %collective-permute-start.3 = (f32[16,32,256]{2,0,1:T(8,128)S(1)}, f32[16,32,256]{2,0,1:T(8,128)S(1)}, u32[]{:S(2)}, u32[]{:S(2)}) collective-permute-start(f32[16,32,256]{2,0,1:T(8,128)S(1)} %fusion.37), channel_id=1, source_target_pairs={{0,1},{1,2},{2,3},{3,0},{4,5},{5,6},{6,7},{7,4},{8,9},{9,10},{10,1... | collective-permute-start | bytes 1572872 | tf_op jit(solution)/shard_map/ppermute | solution.py:20
  250.9 7.3 %all-to-all-start.1 = ((f32[4,1,1]{2,1,0:T(1,128)}), f32[4,1,1]{2,1,0:T(1,128)S(1)}, u32[]{:S(2)}, u32[]{:S(2)}) async-start(f32[4,1,1]{2,1,0:T(1,128)} %broadcast_in_dim.41), calls=%async_computation.1 | async-start | bytes 4096 | tf_op jit(solution)/shard_map/all_to_all | solution.py:26
  259.4 13.3 %all-to-all-start.4 = ((f32[32,1,1]{2,1,0:T(1,128)}), f32[32,1,1]{2,1,0:T(1,128)S(1)}, u32[]{:S(2)}, u32[]{:S(2)}) async-start(f32[32,1,1]{2,1,0:T(1,128)} %broadcast_in_dim.44), calls=%async_computation.4 | async-start | bytes 32768 | tf_op jit(solution)/shard_map/all_to_all | solution.py:29
  274.0 11.2 %all-to-all-start.2 = ((f32[32,1,1]{2,1,0:T(1,128)}), f32[32,1,1]{2,1,0:T(1,128)S(1)}, u32[]{:S(2)}, u32[]{:S(2)}) async-start(f32[32,1,1]{2,1,0:T(1,128)} %broadcast_in_dim.42), calls=%async_computation.2 | async-start | bytes 32768 | tf_op jit(solution)/shard_map/all_to_all | solution.py:29
  287.1 35.3 %slice-start = ((s8[8519680]{0:T(1024)(128)(4,1)}), s8[131072]{0:T(1024)(128)(4,1)S(1)}, s32[]{:S(2)}) async-start(s8[8519680]{0:T(1024)(128)(4,1)} %bitcast.105), calls=%async_computation.13 | async-start | bytes 262144
  310.5 11.9 %slice-start.1 = ((s8[8519680]{0:T(1024)(128)(4,1)}), s8[4194304]{0:T(1024)(128)(4,1)S(1)}, s32[]{:S(2)}) async-start(s8[8519680]{0:T(1024)(128)(4,1)} %bitcast.105), calls=%async_computation.14 | async-start | bytes 8388608
  312.5 10.0 %slice-start.2 = ((s8[8519680]{0:T(1024)(128)(4,1)}), s8[4194304]{0:T(1024)(128)(4,1)S(1)}, s32[]{:S(2)}) async-start(s8[8519680]{0:T(1024)(128)(4,1)} %bitcast.105), calls=%async_computation.15 | async-start | bytes 8388608
  319.2 3.2 copy-start.3
  330.3 12.9 %collective-permute-start.8 = (f32[16,32,256]{2,0,1:T(8,128)S(1)}, f32[16,32,256]{2,0,1:T(8,128)S(1)}, u32[]{:S(2)}, u32[]{:S(2)}) collective-permute-start(f32[16,32,256]{2,0,1:T(8,128)S(1)} %fusion.36), channel_id=1, source_target_pairs={{0,3},{1,0},{2,1},{3,2},{4,7},{5,4},{6,5},{7,6},{8,11},{9,8},{10,9... | collective-permute-start | bytes 1572872 | tf_op jit(solution)/shard_map/ppermute | solution.py:20
  331.3 14.1 %collective-permute-start.7 = (f32[16,32,256]{2,0,1:T(8,128)S(1)}, f32[16,32,256]{2,0,1:T(8,128)S(1)}, u32[]{:S(2)}, u32[]{:S(2)}) collective-permute-start(f32[16,32,256]{2,0,1:T(8,128)S(1)} %fusion.36), channel_id=1, source_target_pairs={{0,2},{1,3},{2,0},{3,1},{4,6},{5,7},{6,4},{7,5},{8,10},{9,11},{10,... | collective-permute-start | bytes 1572872 | tf_op jit(solution)/shard_map/ppermute | solution.py:20
  332.5 25.4 %collective-permute-start.6 = (f32[16,32,256]{2,0,1:T(8,128)S(1)}, f32[16,32,256]{2,0,1:T(8,128)S(1)}, u32[]{:S(2)}, u32[]{:S(2)}) collective-permute-start(f32[16,32,256]{2,0,1:T(8,128)S(1)} %fusion.36), channel_id=1, source_target_pairs={{0,1},{1,2},{2,3},{3,0},{4,5},{5,6},{6,7},{7,4},{8,9},{9,10},{10,1... | collective-permute-start | bytes 1572872 | tf_op jit(solution)/shard_map/ppermute | solution.py:20
  426.2 8.7 %slice-start.3 = ((s8[8519680]{0:T(1024)(128)(4,1)}), s8[4194304]{0:T(1024)(128)(4,1)S(1)}, s32[]{:S(2)}) async-start(s8[8519680]{0:T(1024)(128)(4,1)} %bitcast.107), calls=%async_computation.16 | async-start | bytes 8388608
  426.3 8.6 %slice-start.4 = ((s8[8519680]{0:T(1024)(128)(4,1)}), s8[4194304]{0:T(1024)(128)(4,1)S(1)}, s32[]{:S(2)}) async-start(s8[8519680]{0:T(1024)(128)(4,1)} %bitcast.107), calls=%async_computation.17 | async-start | bytes 8388608
  428.2 6.7 %slice-start.5 = ((s8[8519680]{0:T(1024)(128)(4,1)}), s8[131072]{0:T(1024)(128)(4,1)S(1)}, s32[]{:S(2)}) async-start(s8[8519680]{0:T(1024)(128)(4,1)} %bitcast.107), calls=%async_computation.18 | async-start | bytes 262144
  435.0 11.1 %copy-start.4 = (f32[4,128,256]{2,0,1:T(4,128)S(1)}, f32[4,128,256]{2,0,1:T(4,128)}, u32[]{:S(2)}) copy-start(f32[4,128,256]{2,0,1:T(4,128)} %get-tuple-element.11) | copy-start | bytes 1572868
  435.0 12.0 %copy-start.5 = (f32[4,128,256]{2,0,1:T(4,128)S(1)}, f32[4,128,256]{2,0,1:T(4,128)}, u32[]{:S(2)}) copy-start(f32[4,128,256]{2,0,1:T(4,128)} %get-tuple-element.12) | copy-start | bytes 1572868
  443.1 12.9 %collective-permute-start.11 = (f32[16,32,256]{2,0,1:T(8,128)S(1)}, f32[16,32,256]{2,0,1:T(8,128)S(1)}, u32[]{:S(2)}, u32[]{:S(2)}) collective-permute-start(f32[16,32,256]{2,0,1:T(8,128)S(1)} %fusion.35), channel_id=1, source_target_pairs={{0,3},{1,0},{2,1},{3,2},{4,7},{5,4},{6,5},{7,6},{8,11},{9,8},{10,9... | collective-permute-start | bytes 1572872 | tf_op jit(solution)/shard_map/ppermute | solution.py:20
  444.0 14.1 %collective-permute-start.10 = (f32[16,32,256]{2,0,1:T(8,128)S(1)}, f32[16,32,256]{2,0,1:T(8,128)S(1)}, u32[]{:S(2)}, u32[]{:S(2)}) collective-permute-start(f32[16,32,256]{2,0,1:T(8,128)S(1)} %fusion.35), channel_id=1, source_target_pairs={{0,2},{1,3},{2,0},{3,1},{4,6},{5,7},{6,4},{7,5},{8,10},{9,11},{10,... | collective-permute-start | bytes 1572872 | tf_op jit(solution)/shard_map/ppermute | solution.py:20
  445.2 25.4 %collective-permute-start.9 = (f32[16,32,256]{2,0,1:T(8,128)S(1)}, f32[16,32,256]{2,0,1:T(8,128)S(1)}, u32[]{:S(2)}, u32[]{:S(2)}) collective-permute-start(f32[16,32,256]{2,0,1:T(8,128)S(1)} %fusion.35), channel_id=1, source_target_pairs={{0,1},{1,2},{2,3},{3,0},{4,5},{5,6},{6,7},{7,4},{8,9},{9,10},{10,1... | collective-permute-start | bytes 1572872 | tf_op jit(solution)/shard_map/ppermute | solution.py:20
  479.6 41.1 %copy-start.6 = (f32[4,128,256]{2,1,0:T(8,128)S(1)}, f32[4,128,256]{2,1,0:T(8,128)}, u32[]{:S(2)}) copy-start(f32[4,128,256]{2,1,0:T(8,128)} %copy.36) | copy-start | bytes 1572868
  479.6 41.1 %copy-start.7 = (f32[4,128,256]{2,1,0:T(8,128)S(1)}, f32[4,128,256]{2,1,0:T(8,128)}, u32[]{:S(2)}) copy-start(f32[4,128,256]{2,1,0:T(8,128)} %copy.44) | copy-start | bytes 1572868
  506.5 12.3 %all-to-all-start.12 = ((f32[32,1,1]{2,1,0:T(1,128)}), f32[32,1,1]{2,1,0:T(1,128)S(1)}, u32[]{:S(2)}, u32[]{:S(2)}) async-start(f32[32,1,1]{2,1,0:T(1,128)} %broadcast_in_dim.52), calls=%async_computation.12 | async-start | bytes 32768 | tf_op jit(solution)/shard_map/all_to_all | solution.py:29

commit v2 on v1

--- a/solution.py
+++ b/solution.py
@@ -9,6 +9,7 @@
 
 
 highest = lax.Precision.HIGHEST
+high = lax.Precision.HIGH
 ridge = 1.0
 
 
@@ -22,11 +23,10 @@
 
 
 def global_sum(value):
-    chans = lax.axis_size("chan")
-    got = lax.all_to_all(jnp.broadcast_to(value, (chans, 1)), "chan", 0, 0, tiled=True)
-    part = jnp.sum(got)
-    groups = lax.axis_size("tm")
-    got = lax.all_to_all(jnp.broadcast_to(part, (groups, 1)), "tm", 0, 0, tiled=True)
+    everyone = lax.axis_size("tm") * lax.axis_size("chan")
+    got = lax.all_to_all(
+        jnp.broadcast_to(value, (everyone, 1)), ("tm", "chan"), 0, 0, tiled=True
+    )
     return jnp.sum(got)
 
 
@@ -71,8 +71,8 @@
         )
 
     def binned(samples):
-        partial_value = jnp.einsum("csp,csk->cpk", pixel_hits, samples, precision=highest)
-        summed = jnp.einsum("cb,cpk->bpk", owned_blocks, partial_value, precision=highest)
+        partial_value = jnp.einsum("csp,csk->cpk", pixel_hits, samples, precision=high)
+        summed = jnp.einsum("cb,cpk->bpk", owned_blocks, partial_value, precision=high)
         return summed.reshape(PIX_DEV, channels)
 
     def pointed(field):
@@ -80,9 +80,9 @@
             "cb,bpk->cpk",
             owned_blocks,
             field.reshape(blocks_each, BLK, channels),
-            precision=highest,
+            precision=high,
         )
-        return jnp.einsum("csp,cpk->csk", pixel_hits, picked, precision=highest)
+        return jnp.einsum("csp,cpk->csk", pixel_hits, picked, precision=high)
 
     def squares(vector):
         return global_sum(jnp.sum(vector * vector))

time: 530 us -> 477 us (0.900)
  matrix products: 153 us -> 138 us
  blocking collectives: 174 us -> 160 us
  starting transfers between devices: 29.4 us -> 19.7 us
  local copies, waits for them, and re-layouts: 20.4 us -> 13.7 us
    dot_general x11, matrix products: 82.2 us -> 68.4 us  [the longest x4 30.7 us: binned(): jnp.einsum('csp,csk->cpk', pixel_hits, samples, precision=high)]
    all_to_all x8 -> x4, blocking collectives: 67.9 us -> 54.5 us  [global_sum(): lax.all_to_all(jnp.broadcast_to(value, (everyone, 1)), ('tm', 'chan'), 0,...]
    all_to_all x4 -> x2, starting transfers between devices: 19 us -> 8.5 us  [global_sum(): lax.all_to_all(jnp.broadcast_to(value, (everyone, 1)), ('tm', 'chan'), 0,...]
    all_to_all x4 -> x2, waiting for transfers between devices: 21.9 us -> 17 us  [global_sum(): lax.all_to_all(jnp.broadcast_to(value, (everyone, 1)), ('tm', 'chan'), 0,...]
  transfers between devices with their start and end apart: 16 -> 14, of which waited for: 15 -> 13; matrix products, arithmetic and copies ran while one was open for 1% -> 1% of each run, Pallas kernels for 0% -> 0%
where the time goes in v2:
time: 477 us; the launch traced here: 470 us
  blocking collectives  160 us (34%)
  matrix products  138 us (29%)
  waiting for transfers between devices  116 us (24%)
  starting transfers between devices  19.7 us (4%)
  other arithmetic  14.1 us (3%)
  local copies, waits for them, and re-layouts  13.7 us (3%)
  between operations  7.8 us (2%)
    all_to_all x1, blocking collectives, per_device(): packed = lax.all_to_all(packed, 'tm', 0, 0, tiled=True)  106 us
    ppermute x12, waiting for transfers between devices, chan_sum(): total = total + lax.ppermute(value, 'chan', pairs)  99.4 us
    all_to_all x4, blocking collectives, global_sum(): lax.all_to_all(jnp.broadcast_to(value, (everyone, 1)), ('tm', 'chan'), 0,...  54.5 us
    dot_general x4, matrix products, filtered(): jnp.einsum('mcs,km->csk', amplitudes, foreground_modes, precision=highest)  34.1 us
    dot_general x4, matrix products, filtered(): jnp.einsum('csk,km->mcs', weighted, foreground_modes, precision=highest)  31.2 us
    dot_general x4, matrix products, binned(): jnp.einsum('csp,csk->cpk', pixel_hits, samples, precision=high)  30.7 us
    dot_general x4, matrix products, binned(): jnp.einsum('cb,cpk->bpk', owned_blocks, partial_value, precision=high)  23 us
    all_to_all x2, waiting for transfers between devices, global_sum(): lax.all_to_all(jnp.broadcast_to(value, (everyone, 1)), ('tm', 'chan'), 0,...  17 us
  transfers between devices with their start and end apart: 14, of which 13 were waited for; matrix products, arithmetic and copies ran while one was open for 1% of the time, Pallas kernels for 0%

profile of v2, /device:TPU:1, one launch (start us, length us, event | category | flops | bytes accessed | tf_op | source)
XLA Modules:
  0.0 470.0 jit_solution(16861522089110190907)
XLA Ops:
  0.6 0.8 convert_element_type.31
  1.4 4.2 pad_maximum_fusion
  5.6 105.9 %all_to_all.41 = bf16[32,513,256]{2,1,0:T(8,128)(2,1)S(1)} all-to-all(bf16[32,513,256]{2,1,0:T(8,128)(2,1)S(1)} %pad_maximum_fusion), channel_id=1, replica_groups=mesh['tm'=32,'chan'=4] {'tm'}, dimensions={0} | all-to-all | bytes 16809984 | tf_op jit(solution)/shard_map/all_to_all | solution.py:47
  111.6 3.3 copy-done.1
  114.8 7.8 %fusion.38 = f32[16,32,256]{2,0,1:T(8,128)S(1)} fusion(bf16[32,513,256]{2,1,0:T(8,128)(2,1)S(1)} %all_to_all.41, f32[256,16]{0,1:T(8,128)S(1)} %copy-done), kind=kOutput, calls=%fused_computation.48 | convolution fusion | flops 408944640 | bytes 8929280 | tf_op jit(solution)/shard_map/csk,km->mcs/dot_general | solution.py:67
  122.6 3.8 collective-permute-start.2
  126.4 1.1 collective-permute-start
  127.7 1.1 slice_convert_fusion
  128.8 19.7 %collective-permute-done.2 = f32[16,32,256]{2,0,1:T(8,128)S(1)} collective-permute-done((f32[16,32,256]{2,0,1:T(8,128)S(1)}, f32[16,32,256]{2,0,1:T(8,128)S(1)}, u32[]{:S(2)}, u32[]{:S(2)}) %collective-permute-start.2) | collective-permute-done | bytes 524320 | tf_op jit(solution)/shard_map/ppermute | solution.py:21
  148.5 4.5 collective-permute-done
  153.0 7.0 %fusion.69 = f32[32,256,256]{2,1,0:T(8,128)S(1)} fusion(f32[16,32,256]{2,0,1:T(8,128)S(1)} %collective-permute-done.2, f32[16,32,256]{2,0,1:T(8,128)S(1)} %collective-permute-done.1, f32[16,32,256]{2,0,1:T(8,128)S(1)} %fusion.38, f32[16,32,256]{2,0,1:T(8,128)S(1)} %collective-permute-done, f32[256,16]{0,1:T(8,128)S(1)} %copy-done), kind=kOutput, calls=%fused_computation.95 | convolution fusion | flops 403046400 | bytes 10502144 | tf_op jit(solution)/shard_map/mcs,km->csk/dot_general | solution.py:70
  160.0 5.2 %fusion = f32[32,128,256]{2,1,0:T(8,128)} fusion(f32[32,256,256]{2,1,0:T(8,128)S(1)} %fusion.69, bf16[32,513,256]{2,1,0:T(8,128)(2,1)S(1)} %copy-done.2, s32[32,256]{1,0:T(8,128)S(1)} %bitcast.119), kind=kOutput, calls=%fused_computation.9 | convolution fusion | flops 1622147072 | bytes 21004288 | tf_op jit(solution)/shard_map/csp,csk->cpk/dot_general | solution.py:74
  165.2 5.1 %fusion.24 = f32[4,128,256]{2,0,1:T(4,128)S(1)} fusion(f32[32,128,256]{2,1,0:T(8,128)} %fusion, s32[32]{0:T(128)S(1)} %dynamic-slice_reduce_fusion), kind=kOutput, calls=%fused_computation.33 | convolution fusion | flops 25165952 | bytes 4718720 | tf_op jit(solution)/shard_map/cb,cpk->bpk/dot_general | solution.py:75
  170.3 1.4 fusion.89
  171.7 4.9 %fusion.22 = f32[32,256,256]{2,1,0:T(8,128)S(1)} fusion(f32[32,128,256]{2,0,1:T(8,128)S(1)} %fusion.89, s32[32,256]{1,0:T(8,128)S(1)} %bitcast.120), kind=kOutput, calls=%fused_computation.31 | convolution fusion | flops 1611661312 | bytes 12615680 | tf_op jit(solution)/shard_map/csp,cpk->csk/dot_general | solution.py:85
  176.5 7.6 %fusion.37 = f32[16,32,256]{2,0,1:T(8,128)S(1)} fusion(f32[32,256,256]{2,1,0:T(8,128)S(1)} %fusion.22, bf16[32,513,256]{2,1,0:T(8,128)(2,1)S(1)} %copy-done.2, f32[256,16]{0,1:T(8,128)S(1)} %copy-done), kind=kOutput, calls=%fused_computation.47 | convolution fusion | flops 406847488 | bytes 13123584 | tf_op jit(solution)/shard_map/csk,km->mcs/dot_general | solution.py:67
  184.3 1.4 collective-permute-start.3
  185.7 11.5 %collective-permute-done.5 = f32[16,32,256]{2,0,1:T(8,128)S(1)} collective-permute-done((f32[16,32,256]{2,0,1:T(8,128)S(1)}, f32[16,32,256]{2,0,1:T(8,128)S(1)}, u32[]{:S(2)}, u32[]{:S(2)}) %collective-permute-start.5) | collective-permute-done | bytes 524320 | tf_op jit(solution)/shard_map/ppermute | solution.py:21
  197.2 1.1 collective-permute-done.4
  198.3 12.6 %collective-permute-done.3 = f32[16,32,256]{2,0,1:T(8,128)S(1)} collective-permute-done((f32[16,32,256]{2,0,1:T(8,128)S(1)}, f32[16,32,256]{2,0,1:T(8,128)S(1)}, u32[]{:S(2)}, u32[]{:S(2)}) %collective-permute-start.3) | collective-permute-done | bytes 524320 | tf_op jit(solution)/shard_map/ppermute | solution.py:21
  210.9 9.3 %fusion.65 = f32[32,256,256]{2,1,0:T(8,128)} fusion(f32[16,32,256]{2,0,1:T(8,128)S(1)} %collective-permute-done.5, f32[16,32,256]{2,0,1:T(8,128)S(1)} %collective-permute-done.4, f32[16,32,256]{2,0,1:T(8,128)S(1)} %fusion.37, f32[16,32,256]{2,0,1:T(8,128)S(1)} %collective-permute-done.3, f32[256,16]{0,1:T(8,128)S(1)} %copy-done), kind=kOutput, calls=%fused_computation.90 | convolution fusion | flops 403046400 | bytes 10502144 | tf_op jit(solution)/shard_map/mcs,km->csk/dot_general | solution.py:70
  220.2 8.9 %fusion.1 = f32[32,128,256]{2,1,0:T(8,128)} fusion(f32[32,256,256]{2,1,0:T(8,128)} %fusion.65, f32[32,256,256]{2,1,0:T(8,128)S(1)} %fusion.22, s32[32,256]{1,0:T(8,128)S(1)} %bitcast.121, bf16[32,513,256]{2,1,0:T(8,128)(2,1)S(1)} %copy-done.2), kind=kOutput, calls=%fused_computation.10 | convolution fusion | flops 1620049920 | bytes 25198592 | tf_op jit(solution)/shard_map/csp,csk->cpk/dot_general | solution.py:74
  229.1 6.8 %multiply_reduce_fusion.3 = (f32[]{:T(128)}, f32[]{:T(128)}, f32[4,128,256]{2,0,1:T(4,128)S(1)}, f32[4,128,256]{2,0,1:T(4,128)}) fusion(f32[4,128,256]{2,0,1:T(4,128)S(1)} %fusion.24, f32[32,128,256]{2,1,0:T(8,128)} %fusion.1, s32[32]{0:T(128)S(1)} %dynamic-slice_reduce_fusion), kind=kOutput, calls=%fused_computation.89 | convolution fusion | flops 25821310 | bytes 5767304 | tf_op jit(solution)/shard_map/cb,cpk->bpk/dot_general | solution.py:75
  236.6 13.2 %all_to_all.42 = f32[128,1,1]{2,1,0:T(1,128)S(1)} all-to-all(f32[128,1,1]{2,1,0:T(1,128)S(1)} %broadcast_in_dim.24), channel_id=1, replica_groups=mesh['tm'=32,'chan'=4] {'tm','chan'}, dimensions={0} | all-to-all | bytes 1024 | tf_op jit(solution)/shard_map/all_to_all | solution.py:27
  249.8 1.3 broadcast_in_dim.23
  251.1 4.3 all-to-all-start.1
  255.4 0.8 reduce_sum.111
  256.2 8.8 %all-to-all-done.1 = f32[128,1,1]{2,1,0:T(1,128)S(1)} async-done(((f32[128,1,1]{2,1,0:T(1,128)}), f32[128,1,1]{2,1,0:T(1,128)S(1)}, u32[]{:S(2)}, u32[]{:S(2)}) %all-to-all-start.1) | async-done | bytes 544 | tf_op jit(solution)/shard_map/all_to_all | solution.py:27
  267.1 1.0 multiply_reduce_fusion.2
  268.8 13.8 %all_to_all.43 = f32[128,1,1]{2,1,0:T(1,128)S(1)} all-to-all(f32[128,1,1]{2,1,0:T(1,128)S(1)} %broadcast_in_dim.25), channel_id=1, replica_groups=mesh['tm'=32,'chan'=4] {'tm','chan'}, dimensions={0} | all-to-all | bytes 1024 | tf_op jit(solution)/shard_map/all_to_all | solution.py:27
  282.6 0.8 reduce_sum.113
  284.8 1.4 fusion.86
  286.2 4.9 %fusion.18 = f32[32,256,256]{2,1,0:T(8,128)S(1)} fusion(f32[32,128,256]{2,0,1:T(8,128)S(1)} %fusion.86, s32[32,256]{1,0:T(8,128)S(1)} %bitcast.122), kind=kOutput, calls=%fused_computation.27 | convolution fusion | flops 1611661312 | bytes 12615680 | tf_op jit(solution)/shard_map/csp,cpk->csk/dot_general | solution.py:85
  291.1 3.2 copy-done.3
  294.3 7.9 %fusion.36 = f32[16,32,256]{2,0,1:T(8,128)S(1)} fusion(f32[32,256,256]{2,1,0:T(8,128)S(1)} %fusion.18, bf16[32,513,256]{2,1,0:T(8,128)(2,1)S(1)} %bitcast.106, f32[256,16]{0,1:T(8,128)S(1)} %copy-done), kind=kOutput, calls=%fused_computation.46 | convolution fusion | flops 406847488 | bytes 13123584 | tf_op jit(solution)/shard_map/csk,km->mcs/dot_general | solution.py:67
  302.3 0.8 collective-permute-start.8
  303.1 1.6 collective-permute-start.7
  304.6 10.7 %collective-permute-done.8 = f32[16,32,256]{2,0,1:T(8,128)S(1)} collective-permute-done((f32[16,32,256]{2,0,1:T(8,128)S(1)}, f32[16,32,256]{2,0,1:T(8,128)S(1)}, u32[]{:S(2)}, u32[]{:S(2)}) %collective-permute-start.8) | collective-permute-done | bytes 524320 | tf_op jit(solution)/shard_map/ppermute | solution.py:21
  315.4 2.0 collective-permute-done.7
  317.3 12.4 %collective-permute-done.6 = f32[16,32,256]{2,0,1:T(8,128)S(1)} collective-permute-done((f32[16,32,256]{2,0,1:T(8,128)S(1)}, f32[16,32,256]{2,0,1:T(8,128)S(1)}, u32[]{:S(2)}, u32[]{:S(2)}) %collective-permute-start.6) | collective-permute-done | bytes 524320 | tf_op jit(solution)/shard_map/ppermute | solution.py:21
  329.7 8.9 %fusion.61 = f32[32,256,256]{2,1,0:T(8,128)} fusion(f32[16,32,256]{2,0,1:T(8,128)S(1)} %collective-permute-done.8, f32[16,32,256]{2,0,1:T(8,128)S(1)} %collective-permute-done.7, f32[16,32,256]{2,0,1:T(8,128)S(1)} %fusion.36, f32[16,32,256]{2,0,1:T(8,128)S(1)} %collective-permute-done.6, f32[256,16]{0,1:T(8,128)S(1)} %copy-done), kind=kOutput, calls=%fused_computation.82 | convolution fusion | flops 403046400 | bytes 10502144 | tf_op jit(solution)/shard_map/mcs,km->csk/dot_general | solution.py:70
  338.6 7.7 %fusion.2 = f32[32,128,256]{2,1,0:T(8,128)S(1)} fusion(f32[32,256,256]{2,1,0:T(8,128)} %fusion.61, f32[32,256,256]{2,1,0:T(8,128)} %copy-done.3, s32[32,256]{1,0:T(8,128)S(1)} %bitcast.123, bf16[32,513,256]{2,1,0:T(8,128)(2,1)S(1)} %bitcast.106), kind=kOutput, calls=%fused_computation.11 | convolution fusion | flops 1620049920 | bytes 25198592 | tf_op jit(solution)/shard_map/csp,csk->cpk/dot_general | solution.py:74
  346.2 4.6 multiply_reduce_fusion.1
  351.5 13.8 %all_to_all.44 = f32[128,1,1]{2,1,0:T(1,128)S(1)} all-to-all(f32[128,1,1]{2,1,0:T(1,128)S(1)} %broadcast_in_dim.26), channel_id=1, replica_groups=mesh['tm'=32,'chan'=4] {'tm','chan'}, dimensions={0} | all-to-all | bytes 1024 | tf_op jit(solution)/shard_map/all_to_all | solution.py:27
  365.3 0.8 reduce_sum.115
  367.4 0.9 multiply_reduce_fusion
  369.1 13.8 %all_to_all.45 = f32[128,1,1]{2,1,0:T(1,128)S(1)} all-to-all(f32[128,1,1]{2,1,0:T(1,128)S(1)} %broadcast_in_dim.27), channel_id=1, replica_groups=mesh['tm'=32,'chan'=4] {'tm','chan'}, dimensions={0} | all-to-all | bytes 1024 | tf_op jit(solution)/shard_map/all_to_all | solution.py:27
  382.9 0.8 reduce_sum.117
  385.1 1.4 fusion.83
  386.5 4.9 %fusion.14 = f32[32,256,256]{2,1,0:T(8,128)S(1)} fusion(f32[32,128,256]{2,0,1:T(8,128)S(1)} %fusion.83, s32[32,256]{1,0:T(8,128)S(1)} %bitcast.124), kind=kOutput, calls=%fused_computation.23 | convolution fusion | flops 1611661312 | bytes 12615680 | tf_op jit(solution)/shard_map/csp,cpk->csk/dot_general | solution.py:85
  391.4 7.8 %fusion.35 = f32[16,32,256]{2,0,1:T(8,128)S(1)} fusion(f32[32,256,256]{2,1,0:T(8,128)S(1)} %fusion.14, bf16[32,513,256]{2,1,0:T(8,128)(2,1)S(1)} %bitcast.108, f32[256,16]{0,1:T(8,128)S(1)} %copy-done), kind=kOutput, calls=%fused_computation.45 | convolution fusion | flops 406847488 | bytes 13123584 | tf_op jit(solution)/shard_map/csk,km->mcs/dot_general | solution.py:67
  399.2 0.8 collective-permute-start.11
  400.0 1.6 collective-permute-start.10
  401.6 10.7 %collective-permute-done.11 = f32[16,32,256]{2,0,1:T(8,128)S(1)} collective-permute-done((f32[16,32,256]{2,0,1:T(8,128)S(1)}, f32[16,32,256]{2,0,1:T(8,128)S(1)}, u32[]{:S(2)}, u32[]{:S(2)}) %collective-permute-start.11) | collective-permute-done | bytes 524320 | tf_op jit(solution)/shard_map/ppermute | solution.py:21
  412.3 2.0 collective-permute-done.10
  414.3 12.4 %collective-permute-done.9 = f32[16,32,256]{2,0,1:T(8,128)S(1)} collective-permute-done((f32[16,32,256]{2,0,1:T(8,128)S(1)}, f32[16,32,256]{2,0,1:T(8,128)S(1)}, u32[]{:S(2)}, u32[]{:S(2)}) %collective-permute-start.9) | collective-permute-done | bytes 524320 | tf_op jit(solution)/shard_map/ppermute | solution.py:21
  426.6 8.9 %fusion.57 = f32[32,256,256]{2,1,0:T(8,128)} fusion(f32[16,32,256]{2,0,1:T(8,128)S(1)} %collective-permute-done.11, f32[16,32,256]{2,0,1:T(8,128)S(1)} %collective-permute-done.10, f32[16,32,256]{2,0,1:T(8,128)S(1)} %fusion.35, f32[16,32,256]{2,0,1:T(8,128)S(1)} %collective-permute-done.9, f32[256,16]{0,1:T(8,128)S(1)} %copy-done), kind=kOutput, calls=%fused_computation.74 | convolution fusion | flops 403046400 | bytes 10502144 | tf_op jit(solution)/shard_map/mcs,km->csk/dot_general | solution.py:70
  435.6 9.0 %fusion.3 = f32[32,128,256]{2,1,0:T(8,128)} fusion(f32[32,256,256]{2,1,0:T(8,128)} %fusion.57, f32[32,256,256]{2,1,0:T(8,128)S(1)} %fusion.14, s32[32,256]{1,0:T(8,128)S(1)} %bitcast.125, bf16[32,513,256]{2,1,0:T(8,128)(2,1)S(1)} %bitcast.108), kind=kOutput, calls=%fused_computation.12 | convolution fusion | flops 1620049920 | bytes 25198592 | tf_op jit(solution)/shard_map/csp,csk->cpk/dot_general | solution.py:74
  444.6 6.6 %fusion.47 = (f32[]{:T(128)}, f32[4,128,256]{2,0,1:T(4,128)}) fusion(f32[4,128,256]{2,0,1:T(4,128)S(1)} %bitcast.116, f32[32,128,256]{2,1,0:T(8,128)} %fusion.3, s32[32]{0:T(128)S(1)} %dynamic-slice_reduce_fusion), kind=kOutput, calls=%fused_computation.58 | convolution fusion | flops 25559168 | bytes 5243012 | tf_op jit(solution)/shard_map/cb,cpk->bpk/dot_general | solution.py:75
  451.2 1.3 broadcast_in_dim.28
  452.5 4.2 all-to-all-start.6
  457.1 1.1 copy.47
  458.3 8.2 %all-to-all-done.6 = f32[128,1,1]{2,1,0:T(1,128)S(1)} async-done(((f32[128,1,1]{2,1,0:T(1,128)}), f32[128,1,1]{2,1,0:T(1,128)S(1)}, u32[]{:S(2)}, u32[]{:S(2)}) %all-to-all-start.6) | async-done | bytes 544 | tf_op jit(solution)/shard_map/all_to_all | solution.py:27
  468.5 1.3 fusion.49
  (46 shorter events, 5.2 us)
Async XLA Ops:
  0.6 114.2 %copy-start = (f32[256,16]{0,1:T(8,128)S(1)}, f32[256,16]{0,1:T(8,128)}, u32[]{:S(2)}) copy-start(f32[256,16]{0,1:T(8,128)} %param.9) | copy-start | bytes 49156
  5.6 121.9 %copy-start.6 = (s32[32,32]{1,0:T(8,128)S(1)}, s32[32,32]{1,0:T(8,128)}, u32[]{:S(2)}) copy-start(s32[32,32]{1,0:T(8,128)} %param.8) | copy-start | bytes 12292
  111.6 3.3 copy-start.1
  122.6 25.9 %collective-permute-start.2 = (f32[16,32,256]{2,0,1:T(8,128)S(1)}, f32[16,32,256]{2,0,1:T(8,128)S(1)}, u32[]{:S(2)}, u32[]{:S(2)}) collective-permute-start(f32[16,32,256]{2,0,1:T(8,128)S(1)} %fusion.38), channel_id=1, source_target_pairs={{0,3},{1,0},{2,1},{3,2},{4,7},{5,4},{6,5},{7,6},{8,11},{9,8},{10,9... | collective-permute-start | bytes 1572872 | tf_op jit(solution)/shard_map/ppermute | solution.py:21
  126.4 22.1 %collective-permute-start.1 = (f32[16,32,256]{2,0,1:T(8,128)S(1)}, f32[16,32,256]{2,0,1:T(8,128)S(1)}, u32[]{:S(2)}, u32[]{:S(2)}) collective-permute-start(f32[16,32,256]{2,0,1:T(8,128)S(1)} %fusion.38), channel_id=1, source_target_pairs={{0,2},{1,3},{2,0},{3,1},{4,6},{5,7},{6,4},{7,5},{8,10},{9,11},{10,... | collective-permute-start | bytes 1572872 | tf_op jit(solution)/shard_map/ppermute | solution.py:21
  126.4 26.6 %collective-permute-start = (f32[16,32,256]{2,0,1:T(8,128)S(1)}, f32[16,32,256]{2,0,1:T(8,128)S(1)}, u32[]{:S(2)}, u32[]{:S(2)}) collective-permute-start(f32[16,32,256]{2,0,1:T(8,128)S(1)} %fusion.38), channel_id=1, source_target_pairs={{0,1},{1,2},{2,3},{3,0},{4,5},{5,6},{6,7},{7,4},{8,9},{9,10},{10,1... | collective-permute-start | bytes 1572872 | tf_op jit(solution)/shard_map/ppermute | solution.py:21
  127.6 32.5 %copy-start.2 = (bf16[32,513,256]{2,1,0:T(8,128)(2,1)S(1)}, bf16[32,513,256]{2,1,0:T(8,128)(2,1)}, u32[]{:S(2)}) copy-start(bf16[32,513,256]{2,1,0:T(8,128)(2,1)} %copy-done.1) | copy-start | bytes 25214980
  184.2 13.0 %collective-permute-start.5 = (f32[16,32,256]{2,0,1:T(8,128)S(1)}, f32[16,32,256]{2,0,1:T(8,128)S(1)}, u32[]{:S(2)}, u32[]{:S(2)}) collective-permute-start(f32[16,32,256]{2,0,1:T(8,128)S(1)} %fusion.37), channel_id=1, source_target_pairs={{0,3},{1,0},{2,1},{3,2},{4,7},{5,4},{6,5},{7,6},{8,11},{9,8},{10,9... | collective-permute-start | bytes 1572872 | tf_op jit(solution)/shard_map/ppermute | solution.py:21
  184.2 14.1 %collective-permute-start.4 = (f32[16,32,256]{2,0,1:T(8,128)S(1)}, f32[16,32,256]{2,0,1:T(8,128)S(1)}, u32[]{:S(2)}, u32[]{:S(2)}) collective-permute-start(f32[16,32,256]{2,0,1:T(8,128)S(1)} %fusion.37), channel_id=1, source_target_pairs={{0,2},{1,3},{2,0},{3,1},{4,6},{5,7},{6,4},{7,5},{8,10},{9,11},{10,... | collective-permute-start | bytes 1572872 | tf_op jit(solution)/shard_map/ppermute | solution.py:21
  184.3 26.6 %collective-permute-start.3 = (f32[16,32,256]{2,0,1:T(8,128)S(1)}, f32[16,32,256]{2,0,1:T(8,128)S(1)}, u32[]{:S(2)}, u32[]{:S(2)}) collective-permute-start(f32[16,32,256]{2,0,1:T(8,128)S(1)} %fusion.37), channel_id=1, source_target_pairs={{0,1},{1,2},{2,3},{3,0},{4,5},{5,6},{6,7},{7,4},{8,9},{9,10},{10,1... | collective-permute-start | bytes 1572872 | tf_op jit(solution)/shard_map/ppermute | solution.py:21
  251.1 13.9 %all-to-all-start.1 = ((f32[128,1,1]{2,1,0:T(1,128)}), f32[128,1,1]{2,1,0:T(1,128)S(1)}, u32[]{:S(2)}, u32[]{:S(2)}) async-start(f32[128,1,1]{2,1,0:T(1,128)} %broadcast_in_dim.23), calls=%async_computation.1 | async-start | bytes 131072 | tf_op jit(solution)/shard_map/all_to_all | solution.py:27
  267.1 27.2 %slice-start = ((s8[8519680]{0:T(1024)(128)(4,1)}), s8[131072]{0:T(1024)(128)(4,1)S(1)}, s32[]{:S(2)}) async-start(s8[8519680]{0:T(1024)(128)(4,1)} %bitcast.105), calls=%async_computation.7 | async-start | bytes 262144
  284.8 9.5 %slice-start.1 = ((s8[8519680]{0:T(1024)(128)(4,1)}), s8[4194304]{0:T(1024)(128)(4,1)S(1)}, s32[]{:S(2)}) async-start(s8[8519680]{0:T(1024)(128)(4,1)} %bitcast.105), calls=%async_computation.8 | async-start | bytes 8388608
  286.2 8.1 %slice-start.2 = ((s8[8519680]{0:T(1024)(128)(4,1)}), s8[4194304]{0:T(1024)(128)(4,1)S(1)}, s32[]{:S(2)}) async-start(s8[8519680]{0:T(1024)(128)(4,1)} %bitcast.105), calls=%async_computation.9 | async-start | bytes 8388608
  291.1 3.2 copy-start.3
  302.3 13.1 %collective-permute-start.8 = (f32[16,32,256]{2,0,1:T(8,128)S(1)}, f32[16,32,256]{2,0,1:T(8,128)S(1)}, u32[]{:S(2)}, u32[]{:S(2)}) collective-permute-start(f32[16,32,256]{2,0,1:T(8,128)S(1)} %fusion.36), channel_id=1, source_target_pairs={{0,3},{1,0},{2,1},{3,2},{4,7},{5,4},{6,5},{7,6},{8,11},{9,8},{10,9... | collective-permute-start | bytes 1572872 | tf_op jit(solution)/shard_map/ppermute | solution.py:21
  303.1 14.2 %collective-permute-start.7 = (f32[16,32,256]{2,0,1:T(8,128)S(1)}, f32[16,32,256]{2,0,1:T(8,128)S(1)}, u32[]{:S(2)}, u32[]{:S(2)}) collective-permute-start(f32[16,32,256]{2,0,1:T(8,128)S(1)} %fusion.36), channel_id=1, source_target_pairs={{0,2},{1,3},{2,0},{3,1},{4,6},{5,7},{6,4},{7,5},{8,10},{9,11},{10,... | collective-permute-start | bytes 1572872 | tf_op jit(solution)/shard_map/ppermute | solution.py:21
  304.6 25.0 %collective-permute-start.6 = (f32[16,32,256]{2,0,1:T(8,128)S(1)}, f32[16,32,256]{2,0,1:T(8,128)S(1)}, u32[]{:S(2)}, u32[]{:S(2)}) collective-permute-start(f32[16,32,256]{2,0,1:T(8,128)S(1)} %fusion.36), channel_id=1, source_target_pairs={{0,1},{1,2},{2,3},{3,0},{4,5},{5,6},{6,7},{7,4},{8,9},{9,10},{10,1... | collective-permute-start | bytes 1572872 | tf_op jit(solution)/shard_map/ppermute | solution.py:21
  385.0 6.4 %slice-start.3 = ((s8[8519680]{0:T(1024)(128)(4,1)}), s8[4194304]{0:T(1024)(128)(4,1)S(1)}, s32[]{:S(2)}) async-start(s8[8519680]{0:T(1024)(128)(4,1)} %bitcast.107), calls=%async_computation.10 | async-start | bytes 8388608
  385.1 6.3 %slice-start.4 = ((s8[8519680]{0:T(1024)(128)(4,1)}), s8[4194304]{0:T(1024)(128)(4,1)S(1)}, s32[]{:S(2)}) async-start(s8[8519680]{0:T(1024)(128)(4,1)} %bitcast.107), calls=%async_computation.11 | async-start | bytes 8388608
  386.5 4.9 %slice-start.5 = ((s8[8519680]{0:T(1024)(128)(4,1)}), s8[131072]{0:T(1024)(128)(4,1)S(1)}, s32[]{:S(2)}) async-start(s8[8519680]{0:T(1024)(128)(4,1)} %bitcast.107), calls=%async_computation.12 | async-start | bytes 262144
  399.2 13.1 %collective-permute-start.11 = (f32[16,32,256]{2,0,1:T(8,128)S(1)}, f32[16,32,256]{2,0,1:T(8,128)S(1)}, u32[]{:S(2)}, u32[]{:S(2)}) collective-permute-start(f32[16,32,256]{2,0,1:T(8,128)S(1)} %fusion.35), channel_id=1, source_target_pairs={{0,3},{1,0},{2,1},{3,2},{4,7},{5,4},{6,5},{7,6},{8,11},{9,8},{10,9... | collective-permute-start | bytes 1572872 | tf_op jit(solution)/shard_map/ppermute | solution.py:21
  400.0 14.2 %collective-permute-start.10 = (f32[16,32,256]{2,0,1:T(8,128)S(1)}, f32[16,32,256]{2,0,1:T(8,128)S(1)}, u32[]{:S(2)}, u32[]{:S(2)}) collective-permute-start(f32[16,32,256]{2,0,1:T(8,128)S(1)} %fusion.35), channel_id=1, source_target_pairs={{0,2},{1,3},{2,0},{3,1},{4,6},{5,7},{6,4},{7,5},{8,10},{9,11},{10,... | collective-permute-start | bytes 1572872 | tf_op jit(solution)/shard_map/ppermute | solution.py:21
  401.6 25.0 %collective-permute-start.9 = (f32[16,32,256]{2,0,1:T(8,128)S(1)}, f32[16,32,256]{2,0,1:T(8,128)S(1)}, u32[]{:S(2)}, u32[]{:S(2)}) collective-permute-start(f32[16,32,256]{2,0,1:T(8,128)S(1)} %fusion.35), channel_id=1, source_target_pairs={{0,1},{1,2},{2,3},{3,0},{4,5},{5,6},{6,7},{7,4},{8,9},{9,10},{10,1... | collective-permute-start | bytes 1572872 | tf_op jit(solution)/shard_map/ppermute | solution.py:21
  435.6 21.3 %copy-start.4 = (f32[4,128,256]{2,0,1:T(4,128)S(1)}, f32[4,128,256]{2,0,1:T(4,128)}, u32[]{:S(2)}) copy-start(f32[4,128,256]{2,0,1:T(4,128)} %get-tuple-element.11) | copy-start | bytes 1572868
  435.6 21.5 %copy-start.5 = (f32[4,128,256]{2,0,1:T(4,128)S(1)}, f32[4,128,256]{2,0,1:T(4,128)}, u32[]{:S(2)}) copy-start(f32[4,128,256]{2,0,1:T(4,128)} %get-tuple-element.12) | copy-start | bytes 1572868
  452.5 14.0 %all-to-all-start.6 = ((f32[128,1,1]{2,1,0:T(1,128)}), f32[128,1,1]{2,1,0:T(1,128)S(1)}, u32[]{:S(2)}, u32[]{:S(2)}) async-start(f32[128,1,1]{2,1,0:T(1,128)} %broadcast_in_dim.28), calls=%async_computation.6 | async-start | bytes 131072 | tf_op jit(solution)/shard_map/all_to_all | solution.py:27

commit v3 on v2

--- a/solution.py
+++ b/solution.py
@@ -87,18 +87,26 @@
     def squares(vector):
         return global_sum(jnp.sum(vector * vector))
 
+    def operate(field):
+        return binned(filtered(pointed(field))) + ridge * field
+
     right_side = binned(filtered(runs_in.astype(jnp.float32)))
     map_cube = jnp.zeros_like(right_side)
     residual = right_side
     direction = right_side
     norm_now = squares(residual)
+    applied = operate(direction)
     for iteration in range(ITERS):
-        applied = binned(filtered(pointed(direction))) + ridge * direction
         step_size = norm_now / global_sum(jnp.sum(direction * applied))
         map_cube = map_cube + step_size * direction
         residual = residual - step_size * applied
+        if iteration == ITERS - 1:
+            break
         norm_next = squares(residual)
-        direction = residual + norm_next / norm_now * direction
+        applied_residual = operate(residual)
+        ratio = norm_next / norm_now
+        direction = residual + ratio * direction
+        applied = applied_residual + ratio * applied
         norm_now = norm_next
     return (map_cube, residual)
 

time: 477 us -> 459 us (0.962)
  waiting for transfers between devices: 116 us -> 59.8 us
  blocking collectives: 160 us -> 183 us
  matrix products: 138 us -> 144 us
  starting transfers between devices: 19.7 us -> 25 us
    ppermute x12, waiting for transfers between devices: 99.4 us -> 43.1 us  [chan_sum(): total = total + lax.ppermute(value, 'chan', pairs)]
    all_to_all x4, blocking collectives: 54.5 us -> 76.7 us  [global_sum(): lax.all_to_all(jnp.broadcast_to(value, (everyone, 1)), ('tm', 'chan'), 0,...]
    ppermute x12, starting transfers between devices: 11.2 us -> 16.3 us  [chan_sum(): total = total + lax.ppermute(value, 'chan', pairs)]
    unnamed x27 -> x25, local copies, waits for them, and re-layouts: 6.54 us -> 11.3 us
  transfers between devices with their start and end apart: 14 -> 14, of which waited for: 13 -> 6; matrix products, arithmetic and copies ran while one was open for 1% -> 2% of each run, Pallas kernels for 0% -> 0%
where the time goes in v3:
time: 459 us; the launch traced here: 451 us
  blocking collectives  183 us (40%)
  matrix products  144 us (31%)
  waiting for transfers between devices  59.8 us (13%)
  starting transfers between devices  25 us (5%)
  local copies, waits for them, and re-layouts  18.3 us (4%)
  other arithmetic  13.8 us (3%)
  between operations  7.87 us (2%)
    all_to_all x1, blocking collectives, per_device(): packed = lax.all_to_all(packed, 'tm', 0, 0, tiled=True)  106 us
    all_to_all x4, blocking collectives, global_sum(): lax.all_to_all(jnp.broadcast_to(value, (everyone, 1)), ('tm', 'chan'), 0,...  76.7 us
    ppermute x12, waiting for transfers between devices, chan_sum(): total = total + lax.ppermute(value, 'chan', pairs)  43.1 us
    dot_general x4, matrix products, filtered(): jnp.einsum('csk,km->mcs', weighted, foreground_modes, precision=highest)  35.4 us
    dot_general x4, matrix products, filtered(): jnp.einsum('mcs,km->csk', amplitudes, foreground_modes, precision=highest)  33.9 us
    dot_general x4, matrix products, binned(): jnp.einsum('csp,csk->cpk', pixel_hits, samples, precision=high)  29.8 us
    dot_general x4, matrix products, binned(): jnp.einsum('cb,cpk->bpk', owned_blocks, partial_value, precision=high)  26.2 us
    all_to_all x2, waiting for transfers between devices, global_sum(): lax.all_to_all(jnp.broadcast_to(value, (everyone, 1)), ('tm', 'chan'), 0,...  16.7 us
  transfers between devices with their start and end apart: 14, of which 6 were waited for; matrix products, arithmetic and copies ran while one was open for 2% of the time, Pallas kernels for 0%

profile of v3, /device:TPU:1, one launch (start us, length us, event | category | flops | bytes accessed | tf_op | source)
XLA Modules:
  0.0 451.5 jit_solution(7239104266014323390)
XLA Ops:
  0.6 0.8 convert_element_type.31
  1.4 4.2 pad_maximum_fusion
  5.6 105.9 %all_to_all.41 = bf16[32,513,256]{2,1,0:T(8,128)(2,1)S(1)} all-to-all(bf16[32,513,256]{2,1,0:T(8,128)(2,1)S(1)} %pad_maximum_fusion), channel_id=1, replica_groups=mesh['tm'=32,'chan'=4] {'tm'}, dimensions={0} | all-to-all | bytes 16809984 | tf_op jit(solution)/shard_map/all_to_all | solution.py:47
  111.6 3.3 copy-done.1
  114.8 7.8 %fusion.38 = f32[16,32,256]{2,0,1:T(8,128)S(1)} fusion(bf16[32,513,256]{2,1,0:T(8,128)(2,1)S(1)} %all_to_all.41, f32[256,16]{0,1:T(8,128)S(1)} %copy-done), kind=kOutput, calls=%fused_computation.48 | convolution fusion | flops 408944640 | bytes 8929280 | tf_op jit(solution)/shard_map/csk,km->mcs/dot_general | solution.py:67
  122.6 1.7 collective-permute-start
  124.3 3.3 collective-permute-start.1
  127.6 0.9 collective-permute-start.2
  128.7 1.1 slice_convert_fusion
  129.8 8.6 %collective-permute-done = f32[16,32,256]{2,0,1:T(8,128)S(1)} collective-permute-done((f32[16,32,256]{2,0,1:T(8,128)S(1)}, f32[16,32,256]{2,0,1:T(8,128)S(1)}, u32[]{:S(2)}, u32[]{:S(2)}) %collective-permute-start) | collective-permute-done | bytes 524320 | tf_op jit(solution)/shard_map/ppermute | solution.py:21
  138.3 12.1 %collective-permute-done.1 = f32[16,32,256]{2,0,1:T(8,128)S(1)} collective-permute-done((f32[16,32,256]{2,0,1:T(8,128)S(1)}, f32[16,32,256]{2,0,1:T(8,128)S(1)}, u32[]{:S(2)}, u32[]{:S(2)}) %collective-permute-start.1) | collective-permute-done | bytes 524320 | tf_op jit(solution)/shard_map/ppermute | solution.py:21
  150.5 7.0 %fusion.66 = f32[32,256,256]{2,1,0:T(8,128)S(1)} fusion(f32[16,32,256]{2,0,1:T(8,128)S(1)} %collective-permute-done.2, f32[16,32,256]{2,0,1:T(8,128)S(1)} %collective-permute-done.1, f32[16,32,256]{2,0,1:T(8,128)S(1)} %fusion.38, f32[16,32,256]{2,0,1:T(8,128)S(1)} %collective-permute-done, f32[256,16]{0,1:T(8,128)S(1)} %copy-done), kind=kOutput, calls=%fused_computation.93 | convolution fusion | flops 403046400 | bytes 10502144 | tf_op jit(solution)/shard_map/mcs,km->csk/dot_general | solution.py:70
  157.5 5.4 %fusion = f32[32,128,256]{2,1,0:T(8,128)} fusion(f32[32,256,256]{2,1,0:T(8,128)S(1)} %fusion.66, bf16[32,513,256]{2,1,0:T(8,128)(2,1)S(1)} %copy-done.2, s32[32,256]{1,0:T(8,128)S(1)} %bitcast.98), kind=kOutput, calls=%fused_computation.9 | convolution fusion | flops 1622147072 | bytes 21004288 | tf_op jit(solution)/shard_map/csp,csk->cpk/dot_general | solution.py:74
  162.9 5.1 %fusion.24 = f32[4,128,256]{2,0,1:T(4,128)S(1)} fusion(f32[32,128,256]{2,1,0:T(8,128)} %fusion, s32[32]{0:T(128)S(1)} %dynamic-slice_reduce_fusion), kind=kOutput, calls=%fused_computation.33 | convolution fusion | flops 25165952 | bytes 4718720 | tf_op jit(solution)/shard_map/cb,cpk->bpk/dot_general | solution.py:75
  168.0 1.4 fusion.86
  169.3 4.9 %fusion.22 = f32[32,256,256]{2,1,0:T(8,128)S(1)} fusion(f32[32,128,256]{2,0,1:T(8,128)S(1)} %fusion.86, s32[32,256]{1,0:T(8,128)S(1)} %bitcast.99), kind=kOutput, calls=%fused_computation.31 | convolution fusion | flops 1611661312 | bytes 12615680 | tf_op jit(solution)/shard_map/csp,cpk->csk/dot_general | solution.py:85
  174.2 7.8 %fusion.37 = f32[16,32,256]{2,0,1:T(8,128)S(1)} fusion(f32[32,256,256]{2,1,0:T(8,128)S(1)} %fusion.22, bf16[32,513,256]{2,1,0:T(8,128)(2,1)S(1)} %copy-done.2, f32[256,16]{0,1:T(8,128)S(1)} %copy-done), kind=kOutput, calls=%fused_computation.47 | convolution fusion | flops 406847488 | bytes 13123584 | tf_op jit(solution)/shard_map/csk,km->mcs/dot_general | solution.py:67
  182.0 1.7 collective-permute-start.3
  183.8 2.1 collective-permute-start.4
  186.2 9.3 %collective-permute-done.3 = f32[16,32,256]{2,0,1:T(8,128)S(1)} collective-permute-done((f32[16,32,256]{2,0,1:T(8,128)S(1)}, f32[16,32,256]{2,0,1:T(8,128)S(1)}, u32[]{:S(2)}, u32[]{:S(2)}) %collective-permute-start.3) | collective-permute-done | bytes 524320 | tf_op jit(solution)/shard_map/ppermute | solution.py:21
  195.5 13.1 %collective-permute-done.4 = f32[16,32,256]{2,0,1:T(8,128)S(1)} collective-permute-done((f32[16,32,256]{2,0,1:T(8,128)S(1)}, f32[16,32,256]{2,0,1:T(8,128)S(1)}, u32[]{:S(2)}, u32[]{:S(2)}) %collective-permute-start.4) | collective-permute-done | bytes 524320 | tf_op jit(solution)/shard_map/ppermute | solution.py:21
  208.7 8.9 %fusion.62 = f32[32,256,256]{2,1,0:T(8,128)} fusion(f32[16,32,256]{2,0,1:T(8,128)S(1)} %collective-permute-done.5, f32[16,32,256]{2,0,1:T(8,128)S(1)} %collective-permute-done.4, f32[16,32,256]{2,0,1:T(8,128)S(1)} %fusion.37, f32[16,32,256]{2,0,1:T(8,128)S(1)} %collective-permute-done.3, f32[256,16]{0,1:T(8,128)S(1)} %copy-done), kind=kOutput, calls=%fused_computation.88 | convolution fusion | flops 403046400 | bytes 10502144 | tf_op jit(solution)/shard_map/mcs,km->csk/dot_general | solution.py:70
  217.6 8.9 %fusion.1 = f32[32,128,256]{2,1,0:T(8,128)} fusion(f32[32,256,256]{2,1,0:T(8,128)} %fusion.62, f32[32,256,256]{2,1,0:T(8,128)S(1)} %fusion.22, s32[32,256]{1,0:T(8,128)S(1)} %bitcast.100, bf16[32,513,256]{2,1,0:T(8,128)(2,1)S(1)} %copy-done.2), kind=kOutput, calls=%fused_computation.10 | convolution fusion | flops 1620049920 | bytes 25198592 | tf_op jit(solution)/shard_map/csp,csk->cpk/dot_general | solution.py:74
  226.5 6.8 %multiply_reduce_fusion.4 = (f32[]{:T(128)}, f32[]{:T(128)}, f32[4,128,256]{2,0,1:T(4,128)S(1)}, f32[4,128,256]{2,0,1:T(4,128)}) fusion(f32[4,128,256]{2,0,1:T(4,128)S(1)} %fusion.24, f32[32,128,256]{2,1,0:T(8,128)} %fusion.1, s32[32]{0:T(128)S(1)} %dynamic-slice_reduce_fusion), kind=kOutput, calls=%fused_computation.87 | convolution fusion | flops 25821310 | bytes 5767304 | tf_op jit(solution)/shard_map/cb,cpk->bpk/dot_general | solution.py:75
  233.9 15.1 %all_to_all.42 = f32[128,1,1]{2,1,0:T(1,128)S(1)} all-to-all(f32[128,1,1]{2,1,0:T(1,128)S(1)} %broadcast_in_dim.23), channel_id=1, replica_groups=mesh['tm'=32,'chan'=4] {'tm','chan'}, dimensions={0} | all-to-all | bytes 1024 | tf_op jit(solution)/shard_map/all_to_all | solution.py:27
  249.0 1.3 broadcast_in_dim.24
  250.4 4.7 %all-to-all-start.2 = ((f32[128,1,1]{2,1,0:T(1,128)}), f32[128,1,1]{2,1,0:T(1,128)S(1)}, u32[]{:S(2)}, u32[]{:S(2)}) async-start(f32[128,1,1]{2,1,0:T(1,128)} %broadcast_in_dim.24), calls=%async_computation.2 | async-start | bytes 131072 | tf_op jit(solution)/shard_map/all_to_all | solution.py:27
  255.1 0.8 reduce_sum.109
  255.8 8.4 %all-to-all-done.2 = f32[128,1,1]{2,1,0:T(1,128)S(1)} async-done(((f32[128,1,1]{2,1,0:T(1,128)}), f32[128,1,1]{2,1,0:T(1,128)S(1)}, u32[]{:S(2)}, u32[]{:S(2)}) %all-to-all-start.2) | async-done | bytes 544 | tf_op jit(solution)/shard_map/all_to_all | solution.py:27
  264.3 0.7 reduce_sum.111
  266.3 0.9 multiply_reduce_fusion.3
  267.2 1.4 fusion.83
  268.6 4.9 %fusion.18 = f32[32,256,256]{2,1,0:T(8,128)S(1)} fusion(f32[32,128,256]{2,0,1:T(8,128)S(1)} %fusion.83, s32[32,256]{1,0:T(8,128)S(1)} %bitcast.101), kind=kOutput, calls=%fused_computation.27 | convolution fusion | flops 1611661312 | bytes 12615680 | tf_op jit(solution)/shard_map/csp,cpk->csk/dot_general | solution.py:85
  273.5 3.2 copy-done.5
  276.7 9.9 %fusion.36 = f32[16,32,256]{2,0,1:T(8,128)S(1)} fusion(f32[32,256,256]{2,1,0:T(8,128)S(1)} %fusion.18, bf16[32,513,256]{2,1,0:T(8,128)(2,1)} %copy-done.1, f32[256,16]{0,1:T(8,128)S(1)} %copy-done), kind=kOutput, calls=%fused_computation.46 | convolution fusion | flops 406847488 | bytes 13123584 | tf_op jit(solution)/shard_map/csk,km->mcs/dot_general | solution.py:67
  287.2 1.4 collective-permute-start.7
  288.7 1.2 collective-permute-start.8
  290.5 24.0 %all_to_all.43 = f32[128,1,1]{2,1,0:T(1,128)S(1)} all-to-all(f32[128,1,1]{2,1,0:T(1,128)S(1)} %broadcast_in_dim.25), channel_id=1, replica_groups=mesh['tm'=32,'chan'=4] {'tm','chan'}, dimensions={0} | all-to-all | bytes 1024 | tf_op jit(solution)/shard_map/all_to_all | solution.py:27
  314.5 0.8 reduce_sum.113
  316.6 0.8 copy-done.9
  317.4 9.0 %fusion.58 = f32[32,256,256]{2,1,0:T(8,128)S(1)} fusion(f32[16,32,256]{2,0,1:T(8,128)} %collective-permute-done.8, f32[16,32,256]{2,0,1:T(8,128)} %collective-permute-done.7, f32[16,32,256]{2,0,1:T(8,128)S(1)} %fusion.36, f32[16,32,256]{2,0,1:T(8,128)} %copy-done.9, f32[256,16]{0,1:T(8,128)S(1)} %copy-done), kind=kOutput, calls=%fused_computation.80 | convolution fusion | flops 403046400 | bytes 10502144 | tf_op jit(solution)/shard_map/mcs,km->csk/dot_general | solution.py:70
  326.4 7.7 %fusion.2 = f32[32,128,256]{2,1,0:T(8,128)} fusion(f32[32,256,256]{2,1,0:T(8,128)S(1)} %fusion.58, f32[32,256,256]{2,1,0:T(8,128)S(1)} %copy-done.6, s32[32,256]{1,0:T(8,128)S(1)} %bitcast.102, bf16[32,513,256]{2,1,0:T(8,128)(2,1)} %copy-done.1), kind=kOutput, calls=%fused_computation.11 | convolution fusion | flops 1620049920 | bytes 25198592 | tf_op jit(solution)/shard_map/csp,csk->cpk/dot_general | solution.py:74
  334.1 7.2 %multiply_reduce_fusion.2 = (f32[]{:T(128)}, f32[4,128,256]{2,0,1:T(4,128)S(1)}, f32[4,128,256]{2,0,1:T(4,128)}) fusion(f32[4,128,256]{2,0,1:T(4,128)S(1)} %get-tuple-element.7, f32[4,128,256]{2,0,1:T(4,128)S(1)} %fusion.24, f32[]{:T(128)S(6)} %div.16, f32[4,128,256]{2,0,1:T(4,128)S(1)} %get-tuple-element.8, f32[32,128,256]{2,1,0:T(8,128)} %fusion.2, ...), kind=kOutput, calls=%fused_computation.78 | convolution fusion | flops 26083456 | bytes 6815880 | tf_op jit(solution)/shard_map/cb,cpk->bpk/dot_general | solution.py:75
  342.0 14.7 %all_to_all.44 = f32[128,1,1]{2,1,0:T(1,128)S(1)} all-to-all(f32[128,1,1]{2,1,0:T(1,128)S(1)} %broadcast_in_dim.26), channel_id=1, replica_groups=mesh['tm'=32,'chan'=4] {'tm','chan'}, dimensions={0} | all-to-all | bytes 1024 | tf_op jit(solution)/shard_map/all_to_all | solution.py:27
  356.7 0.8 reduce_sum.115
  358.8 1.4 fusion.78
  360.2 4.9 %fusion.14 = f32[32,256,256]{2,1,0:T(8,128)S(1)} fusion(f32[32,128,256]{2,0,1:T(8,128)S(1)} %fusion.78, s32[32,256]{1,0:T(8,128)S(1)} %bitcast.103), kind=kOutput, calls=%fused_computation.23 | convolution fusion | flops 1611661312 | bytes 12615680 | tf_op jit(solution)/shard_map/csp,cpk->csk/dot_general | solution.py:85
  365.1 3.2 copy-done.3
  368.3 9.9 %fusion.35 = f32[16,32,256]{2,0,1:T(8,128)S(1)} fusion(f32[32,256,256]{2,1,0:T(8,128)S(1)} %fusion.14, bf16[32,513,256]{2,1,0:T(8,128)(2,1)} %copy-done.1, f32[256,16]{0,1:T(8,128)S(1)} %copy-done), kind=kOutput, calls=%fused_computation.45 | convolution fusion | flops 406847488 | bytes 13123584 | tf_op jit(solution)/shard_map/csk,km->mcs/dot_general | solution.py:67
  378.2 1.2 collective-permute-start.10
  379.4 1.9 collective-permute-start.11
  381.3 0.9 multiply_reduce_fusion.1
  382.8 22.9 %all_to_all.45 = f32[128,1,1]{2,1,0:T(1,128)S(1)} all-to-all(f32[128,1,1]{2,1,0:T(1,128)S(1)} %broadcast_in_dim.27), channel_id=1, replica_groups=mesh['tm'=32,'chan'=4] {'tm','chan'}, dimensions={0} | all-to-all | bytes 1024 | tf_op jit(solution)/shard_map/all_to_all | solution.py:27
  405.8 0.8 reduce_sum.117
  408.0 0.8 copy-done.10
  408.8 9.0 %fusion.54 = f32[32,256,256]{2,1,0:T(8,128)S(1)} fusion(f32[16,32,256]{2,0,1:T(8,128)} %collective-permute-done.11, f32[16,32,256]{2,0,1:T(8,128)} %copy-done.10, f32[16,32,256]{2,0,1:T(8,128)S(1)} %fusion.35, f32[16,32,256]{2,0,1:T(8,128)} %collective-permute-done.9, f32[256,16]{0,1:T(8,128)S(1)} %copy-done), kind=kOutput, calls=%fused_computation.72 | convolution fusion | flops 403046400 | bytes 10502144 | tf_op jit(solution)/shard_map/mcs,km->csk/dot_general | solution.py:70
  417.8 7.8 %fusion.3 = f32[32,128,256]{2,1,0:T(8,128)} fusion(f32[32,256,256]{2,1,0:T(8,128)S(1)} %fusion.54, f32[32,256,256]{2,1,0:T(8,128)S(1)} %copy-done.4, s32[32,256]{1,0:T(8,128)S(1)} %bitcast.104, bf16[32,513,256]{2,1,0:T(8,128)(2,1)} %copy-done.1), kind=kOutput, calls=%fused_computation.12 | convolution fusion | flops 1620049920 | bytes 25198592 | tf_op jit(solution)/shard_map/csp,csk->cpk/dot_general | solution.py:74
  425.5 7.2 %multiply_reduce_fusion = (f32[]{:T(128)}, f32[4,128,256]{2,0,1:T(4,128)}) fusion(f32[4,128,256]{2,0,1:T(4,128)S(1)} %get-tuple-element.5, f32[]{:T(128)S(6)} %div.18, f32[4,128,256]{2,0,1:T(4,128)S(1)} %get-tuple-element.7, f32[4,128,256]{2,0,1:T(4,128)S(1)} %fusion.24, f32[]{:T(128)S(6)} %div.16, f32[]{:T(128)S(6)} %div.17, f32[32,128,256]{2,1,0:T(8,128)} %fusion.3, ...), kind=kOutput, calls=%fused_computation.71 | convolution fusion | flops 26607744 | bytes 6291600 | tf_op jit(solution)/shard_map/cb,cpk->bpk/dot_general | solution.py:75
  432.7 1.3 broadcast_in_dim.28
  434.0 4.1 all-to-all-start.6
  438.4 1.1 copy.47
  439.6 8.2 %all-to-all-done.6 = f32[128,1,1]{2,1,0:T(1,128)S(1)} async-done(((f32[128,1,1]{2,1,0:T(1,128)}), f32[128,1,1]{2,1,0:T(1,128)S(1)}, u32[]{:S(2)}, u32[]{:S(2)}) %all-to-all-start.6) | async-done | bytes 544 | tf_op jit(solution)/shard_map/all_to_all | solution.py:27
  447.8 0.7 reduce_sum.119
  449.9 1.4 fusion.49
  (40 shorter events, 4.2 us)
Async XLA Ops:
  0.6 114.2 %copy-start = (f32[256,16]{0,1:T(8,128)S(1)}, f32[256,16]{0,1:T(8,128)}, u32[]{:S(2)}) copy-start(f32[256,16]{0,1:T(8,128)} %param.9) | copy-start | bytes 49156
  5.6 122.9 %copy-start.11 = (s32[32,32]{1,0:T(8,128)S(1)}, s32[32,32]{1,0:T(8,128)}, u32[]{:S(2)}) copy-start(s32[32,32]{1,0:T(8,128)} %param.8) | copy-start | bytes 12292
  111.6 3.3 copy-start.1
  122.6 15.7 %collective-permute-start = (f32[16,32,256]{2,0,1:T(8,128)S(1)}, f32[16,32,256]{2,0,1:T(8,128)S(1)}, u32[]{:S(2)}, u32[]{:S(2)}) collective-permute-start(f32[16,32,256]{2,0,1:T(8,128)S(1)} %fusion.38), channel_id=1, source_target_pairs={{0,1},{1,2},{2,3},{3,0},{4,5},{5,6},{6,7},{7,4},{8,9},{9,10},{10,1... | collective-permute-start | bytes 1572872 | tf_op jit(solution)/shard_map/ppermute | solution.py:21
  124.3 26.2 %collective-permute-start.1 = (f32[16,32,256]{2,0,1:T(8,128)S(1)}, f32[16,32,256]{2,0,1:T(8,128)S(1)}, u32[]{:S(2)}, u32[]{:S(2)}) collective-permute-start(f32[16,32,256]{2,0,1:T(8,128)S(1)} %fusion.38), channel_id=1, source_target_pairs={{0,2},{1,3},{2,0},{3,1},{4,6},{5,7},{6,4},{7,5},{8,10},{9,11},{10,... | collective-permute-start | bytes 1572872 | tf_op jit(solution)/shard_map/ppermute | solution.py:21
  127.6 22.9 %collective-permute-start.2 = (f32[16,32,256]{2,0,1:T(8,128)S(1)}, f32[16,32,256]{2,0,1:T(8,128)S(1)}, u32[]{:S(2)}, u32[]{:S(2)}) collective-permute-start(f32[16,32,256]{2,0,1:T(8,128)S(1)} %fusion.38), channel_id=1, source_target_pairs={{0,3},{1,0},{2,1},{3,2},{4,7},{5,4},{6,5},{7,6},{8,11},{9,8},{10,9... | collective-permute-start | bytes 1572872 | tf_op jit(solution)/shard_map/ppermute | solution.py:21
  128.5 29.0 %copy-start.2 = (bf16[32,513,256]{2,1,0:T(8,128)(2,1)S(1)}, bf16[32,513,256]{2,1,0:T(8,128)(2,1)}, u32[]{:S(2)}) copy-start(bf16[32,513,256]{2,1,0:T(8,128)(2,1)} %copy-done.1) | copy-start | bytes 25214980
  182.0 13.5 %collective-permute-start.3 = (f32[16,32,256]{2,0,1:T(8,128)S(1)}, f32[16,32,256]{2,0,1:T(8,128)S(1)}, u32[]{:S(2)}, u32[]{:S(2)}) collective-permute-start(f32[16,32,256]{2,0,1:T(8,128)S(1)} %fusion.37), channel_id=1, source_target_pairs={{0,1},{1,2},{2,3},{3,0},{4,5},{5,6},{6,7},{7,4},{8,9},{9,10},{10,1... | collective-permute-start | bytes 1572872 | tf_op jit(solution)/shard_map/ppermute | solution.py:21
  183.8 24.9 %collective-permute-start.4 = (f32[16,32,256]{2,0,1:T(8,128)S(1)}, f32[16,32,256]{2,0,1:T(8,128)S(1)}, u32[]{:S(2)}, u32[]{:S(2)}) collective-permute-start(f32[16,32,256]{2,0,1:T(8,128)S(1)} %fusion.37), channel_id=1, source_target_pairs={{0,2},{1,3},{2,0},{3,1},{4,6},{5,7},{6,4},{7,5},{8,10},{9,11},{10,... | collective-permute-start | bytes 1572872 | tf_op jit(solution)/shard_map/ppermute | solution.py:21
  185.9 22.8 %collective-permute-start.5 = (f32[16,32,256]{2,0,1:T(8,128)S(1)}, f32[16,32,256]{2,0,1:T(8,128)S(1)}, u32[]{:S(2)}, u32[]{:S(2)}) collective-permute-start(f32[16,32,256]{2,0,1:T(8,128)S(1)} %fusion.37), channel_id=1, source_target_pairs={{0,3},{1,0},{2,1},{3,2},{4,7},{5,4},{6,5},{7,6},{8,11},{9,8},{10,9... | collective-permute-start | bytes 1572872 | tf_op jit(solution)/shard_map/ppermute | solution.py:21
  250.4 13.9 %all-to-all-start.2 = ((f32[128,1,1]{2,1,0:T(1,128)}), f32[128,1,1]{2,1,0:T(1,128)S(1)}, u32[]{:S(2)}, u32[]{:S(2)}) async-start(f32[128,1,1]{2,1,0:T(1,128)} %broadcast_in_dim.24), calls=%async_computation.2 | async-start | bytes 131072 | tf_op jit(solution)/shard_map/all_to_all | solution.py:27
  273.5 3.2 copy-start.5
  286.6 29.9 %collective-permute-start.6 = (f32[16,32,256]{2,0,1:T(8,128)S(1)}, f32[16,32,256]{2,0,1:T(8,128)S(1)}, u32[]{:S(2)}, u32[]{:S(2)}) collective-permute-start(f32[16,32,256]{2,0,1:T(8,128)S(1)} %fusion.36), channel_id=1, source_target_pairs={{0,1},{1,2},{2,3},{3,0},{4,5},{5,6},{6,7},{7,4},{8,9},{9,10},{10,1... | collective-permute-start | bytes 1572872 | tf_op jit(solution)/shard_map/ppermute | solution.py:21
  287.2 29.3 %collective-permute-start.7 = (f32[16,32,256]{2,0,1:T(8,128)S(1)}, f32[16,32,256]{2,0,1:T(8,128)}, u32[]{:S(2)}, u32[]{:S(2)}) collective-permute-start(f32[16,32,256]{2,0,1:T(8,128)S(1)} %fusion.36), channel_id=1, source_target_pairs={{0,2},{1,3},{2,0},{3,1},{4,6},{5,7},{6,4},{7,5},{8,10},{9,11},{10,... | collective-permute-start | bytes 1572872 | tf_op jit(solution)/shard_map/ppermute | solution.py:21
  288.7 28.7 %collective-permute-start.8 = (f32[16,32,256]{2,0,1:T(8,128)S(1)}, f32[16,32,256]{2,0,1:T(8,128)}, u32[]{:S(2)}, u32[]{:S(2)}) collective-permute-start(f32[16,32,256]{2,0,1:T(8,128)S(1)} %fusion.36), channel_id=1, source_target_pairs={{0,3},{1,0},{2,1},{3,2},{4,7},{5,4},{6,5},{7,6},{8,11},{9,8},{10,9... | collective-permute-start | bytes 1572872 | tf_op jit(solution)/shard_map/ppermute | solution.py:21
  316.6 9.8 %copy-start.6 = (f32[32,256,256]{2,1,0:T(8,128)S(1)}, f32[32,256,256]{2,1,0:T(8,128)}, u32[]{:S(2)}) copy-start(f32[32,256,256]{2,1,0:T(8,128)} %copy-done.5) | copy-start | bytes 25165828
  316.6 0.8 copy-start.9
  365.1 3.2 copy-start.3
  378.2 29.7 %collective-permute-start.10 = (f32[16,32,256]{2,0,1:T(8,128)S(1)}, f32[16,32,256]{2,0,1:T(8,128)S(1)}, u32[]{:S(2)}, u32[]{:S(2)}) collective-permute-start(f32[16,32,256]{2,0,1:T(8,128)S(1)} %fusion.35), channel_id=1, source_target_pairs={{0,2},{1,3},{2,0},{3,1},{4,6},{5,7},{6,4},{7,5},{8,10},{9,11},{10,... | collective-permute-start | bytes 1572872 | tf_op jit(solution)/shard_map/ppermute | solution.py:21
  379.4 28.6 %collective-permute-start.11 = (f32[16,32,256]{2,0,1:T(8,128)S(1)}, f32[16,32,256]{2,0,1:T(8,128)}, u32[]{:S(2)}, u32[]{:S(2)}) collective-permute-start(f32[16,32,256]{2,0,1:T(8,128)S(1)} %fusion.35), channel_id=1, source_target_pairs={{0,3},{1,0},{2,1},{3,2},{4,7},{5,4},{6,5},{7,6},{8,11},{9,8},{10,9... | collective-permute-start | bytes 1572872 | tf_op jit(solution)/shard_map/ppermute | solution.py:21
  381.2 27.5 %collective-permute-start.9 = (f32[16,32,256]{2,0,1:T(8,128)S(1)}, f32[16,32,256]{2,0,1:T(8,128)}, u32[]{:S(2)}, u32[]{:S(2)}) collective-permute-start(f32[16,32,256]{2,0,1:T(8,128)S(1)} %fusion.35), channel_id=1, source_target_pairs={{0,1},{1,2},{2,3},{3,0},{4,5},{5,6},{6,7},{7,4},{8,9},{9,10},{10,1... | collective-permute-start | bytes 1572872 | tf_op jit(solution)/shard_map/ppermute | solution.py:21
  407.9 9.8 %copy-start.4 = (f32[32,256,256]{2,1,0:T(8,128)S(1)}, f32[32,256,256]{2,1,0:T(8,128)}, u32[]{:S(2)}) copy-start(f32[32,256,256]{2,1,0:T(8,128)} %copy-done.3) | copy-start | bytes 25165828
  407.9 0.8 copy-start.10
  417.7 20.4 %copy-start.7 = (f32[4,128,256]{2,0,1:T(4,128)S(1)}, f32[4,128,256]{2,0,1:T(4,128)}, u32[]{:S(2)}) copy-start(f32[4,128,256]{2,0,1:T(4,128)} %get-tuple-element.11) | copy-start | bytes 1572868
  425.5 12.8 %copy-start.8 = (f32[4,128,256]{2,0,1:T(4,128)S(1)}, f32[4,128,256]{2,0,1:T(4,128)}, u32[]{:S(2)}) copy-start(f32[4,128,256]{2,0,1:T(4,128)} %get-tuple-element.12) | copy-start | bytes 1572868
  434.0 13.8 %all-to-all-start.6 = ((f32[128,1,1]{2,1,0:T(1,128)}), f32[128,1,1]{2,1,0:T(1,128)S(1)}, u32[]{:S(2)}, u32[]{:S(2)}) async-start(f32[128,1,1]{2,1,0:T(1,128)} %broadcast_in_dim.28), calls=%async_computation.6 | async-start | bytes 131072 | tf_op jit(solution)/shard_map/all_to_all | solution.py:27

commit v4 on v3

--- a/solution.py
+++ b/solution.py
@@ -37,19 +37,14 @@
     run_length = sample_count // group_count
     blocks_each = PIX_DEV // BLK
 
-    runs = streams.reshape(group_count, run_length, channels)
     scales = weights.reshape(group_count, run_length, channels)
     points = pointing.reshape(group_count, run_length)
     if run_length == channels:
-        packed = jnp.concatenate(
-            [runs, scales, points.astype(jnp.bfloat16)[:, None, :]], axis=1
-        )
+        packed = jnp.concatenate([scales, points.astype(jnp.bfloat16)[:, None, :]], axis=1)
         packed = lax.all_to_all(packed, "tm", 0, 0, tiled=True)
-        runs_in = packed[:, :run_length]
-        weights_in = packed[:, run_length : 2 * run_length]
-        points_in = packed[:, 2 * run_length].astype(jnp.int32)
+        weights_in = packed[:, :run_length]
+        points_in = packed[:, run_length].astype(jnp.int32)
     else:
-        runs_in = lax.all_to_all(runs, "tm", 0, 0, tiled=True)
         weights_in = lax.all_to_all(scales, "tm", 0, 0, tiled=True)
         points_in = lax.all_to_all(points, "tm", 0, 0, tiled=True)
 
@@ -62,7 +57,7 @@
     )
     noise_weights = weights_in.astype(jnp.float32)
 
-    def filtered(samples):
+    def filtered(samples, noise_weights):
         weighted = noise_weights * samples
         amplitudes = jnp.einsum("csk,km->mcs", weighted, foreground_modes, precision=highest)
         amplitudes = chan_sum(amplitudes)
@@ -88,9 +83,20 @@
         return global_sum(jnp.sum(vector * vector))
 
     def operate(field):
-        return binned(filtered(pointed(field))) + ridge * field
+        return binned(filtered(pointed(field), noise_weights)) + ridge * field
 
-    right_side = binned(filtered(runs_in.astype(jnp.float32)))
+    local_hits = (points[:, :, None] == jnp.arange(BLK, dtype=jnp.int32)[None, None, :]).astype(
+        jnp.float32
+    )
+    local_noise = filtered(
+        streams.astype(jnp.float32).reshape(group_count, run_length, channels),
+        scales.astype(jnp.float32),
+    )
+    local_partial = jnp.einsum("csp,csk->cpk", local_hits, local_noise, precision=high)
+    arrived = lax.all_to_all(local_partial, "tm", 0, 0, tiled=True)
+    right_side = jnp.einsum("cb,cpk->bpk", owned_blocks, arrived, precision=high).reshape(
+        PIX_DEV, channels
+    )
     map_cube = jnp.zeros_like(right_side)
     residual = right_side
     direction = right_side

time: 459 us -> 424 us (0.924)
  blocking collectives: 183 us -> 79.8 us
  waiting for transfers between devices: 59.8 us -> 115 us
  starting transfers between devices: 25 us -> 43.2 us
  local copies, waits for them, and re-layouts: 18.3 us -> 7.5 us
  matrix products: 144 us -> 150 us
    all_to_all x1 -> x0, blocking collectives: 106 us -> none  [per_device(): packed = lax.all_to_all(packed, 'tm', 0, 0, tiled=True)]
    all_to_all x0 -> x2, waiting for transfers between devices: none -> 53.3 us  [the longest x1 50.5 us: per_device(): arrived = lax.all_to_all(local_partial, 'tm', 0, 0, tiled=True)]
    all_to_all x0 -> x2, starting transfers between devices: none -> 16.3 us  [the longest x1 8.62 us: per_device(): packed = lax.all_to_all(packed, 'tm', 0, 0, tiled=True)]
    dot_general x0 -> x2, matrix products: none -> 10.6 us  [the longest x1 5.56 us: per_device(): jnp.einsum('csp,csk->cpk', local_hits, local_noise, precision=high)]
    dot_general x4, matrix products: 35.4 us -> 46 us  [filtered(): jnp.einsum('csk,km->mcs', weighted, foreground_modes, precision=highest)]
    unnamed x25 -> x29, local copies, waits for them, and re-layouts: 11.3 us -> 1.63 us
    dot_general x4 -> x3, matrix products: 29.8 us -> 23.2 us  [binned(): jnp.einsum('csp,csk->cpk', pixel_hits, samples, precision=high)]
    dot_general x4 -> x3, matrix products: 26.2 us -> 19.9 us  [binned(): jnp.einsum('cb,cpk->bpk', owned_blocks, partial_value, precision=high)]
  transfers between devices with their start and end apart: 14 -> 16, of which waited for: 6 -> 8; matrix products, arithmetic and copies ran while one was open for 2% -> 7% of each run, Pallas kernels for 0% -> 0%
where the time goes in v4:
time: 424 us; the launch traced here: 419 us
  matrix products  150 us (35%)
  waiting for transfers between devices  115 us (27%)
  blocking collectives  79.8 us (19%)
  starting transfers between devices  43.2 us (10%)
  other arithmetic  14.7 us (3%)
  between operations  7.82 us (2%)
  local copies, waits for them, and re-layouts  7.5 us (2%)
    all_to_all x4, blocking collectives, global_sum(): lax.all_to_all(jnp.broadcast_to(value, (everyone, 1)), ('tm', 'chan'), 0,...  79.8 us
    all_to_all x1, waiting for transfers between devices, per_device(): arrived = lax.all_to_all(local_partial, 'tm', 0, 0, tiled=True)  50.5 us
    dot_general x4, matrix products, filtered(): jnp.einsum('csk,km->mcs', weighted, foreground_modes, precision=highest)  46 us
    ppermute x12, waiting for transfers between devices, chan_sum(): total = total + lax.ppermute(value, 'chan', pairs)  44 us
    dot_general x4, matrix products, filtered(): jnp.einsum('mcs,km->csk', amplitudes, foreground_modes, precision=highest)  32 us
    dot_general x3, matrix products, binned(): jnp.einsum('csp,csk->cpk', pixel_hits, samples, precision=high)  23.2 us
    dot_general x3, matrix products, binned(): jnp.einsum('cb,cpk->bpk', owned_blocks, partial_value, precision=high)  19.9 us
    all_to_all x2, waiting for transfers between devices, global_sum(): lax.all_to_all(jnp.broadcast_to(value, (everyone, 1)), ('tm', 'chan'), 0,...  18.2 us
  transfers between devices with their start and end apart: 16, of which 8 were waited for; matrix products, arithmetic and copies ran while one was open for 7% of the time, Pallas kernels for 0%

profile of v4, /device:TPU:1, one launch (start us, length us, event | category | flops | bytes accessed | tf_op | source)
XLA Modules:
  0.0 418.9 jit_solution(15102131986780431655)
XLA Ops:
  0.6 0.8 convert_element_type.34
  1.4 4.5 %pad_maximum_fusion = bf16[32,257,256]{2,1,0:T(8,128)(2,1)} fusion(bf16[32,1,256]{2,1,0:T(2,128)(2,1)S(1)} %convert_element_type.40, bf16[32,256,256]{2,1,0:T(8,128)(2,1)} %bitcast.97), kind=kLoop, calls=%fused_computation.20 | loop fusion | flops 8421376 | bytes 8421376 | tf_op jit(solution)/shard_map/concatenate | solution.py:43
  6.0 8.6 %all-to-all-start.2 = ((bf16[32,257,256]{2,1,0:T(8,128)(2,1)}), bf16[32,257,256]{2,1,0:T(8,128)(2,1)}, u32[]{:S(2)}, u32[]{:S(2)}) async-start(bf16[32,257,256]{2,1,0:T(8,128)(2,1)} %pad_maximum_fusion), calls=%async_computation.2 | async-start | bytes 8650752 | tf_op jit(solution)/shard_map/all_to_all | solution.py:44
  14.6 10.2 %fusion.42 = f32[16,32,256]{2,0,1:T(8,128)S(1)} fusion(bf16[32,256,256]{2,1,0:T(8,128)(2,1)} %bitcast.98, bf16[32,256,256]{2,1,0:T(8,128)(2,1)} %bitcast.100, f32[256,16]{0,1:T(8,128)S(1)} %copy-done), kind=kOutput, calls=%fused_computation.53 | convolution fusion | flops 408944640 | bytes 8929280 | tf_op jit(solution)/shard_map/csk,km->mcs/dot_general | solution.py:62
  24.8 1.7 collective-permute-start
  26.5 3.3 collective-permute-start.1
  29.8 0.9 collective-permute-start.2
  30.7 10.0 %collective-permute-done = f32[16,32,256]{2,0,1:T(8,128)S(1)} collective-permute-done((f32[16,32,256]{2,0,1:T(8,128)S(1)}, f32[16,32,256]{2,0,1:T(8,128)S(1)}, u32[]{:S(2)}, u32[]{:S(2)}) %collective-permute-start) | collective-permute-done | bytes 524320 | tf_op jit(solution)/shard_map/ppermute | solution.py:21
  40.7 12.1 %collective-permute-done.1 = f32[16,32,256]{2,0,1:T(8,128)S(1)} collective-permute-done((f32[16,32,256]{2,0,1:T(8,128)S(1)}, f32[16,32,256]{2,0,1:T(8,128)S(1)}, u32[]{:S(2)}, u32[]{:S(2)}) %collective-permute-start.1) | collective-permute-done | bytes 524320 | tf_op jit(solution)/shard_map/ppermute | solution.py:21
  52.8 7.1 %fusion.62 = f32[32,256,256]{2,1,0:T(8,128)S(1)} fusion(f32[16,32,256]{2,0,1:T(8,128)S(1)} %collective-permute-done.2, f32[16,32,256]{2,0,1:T(8,128)S(1)} %collective-permute-done.1, f32[16,32,256]{2,0,1:T(8,128)S(1)} %fusion.42, f32[16,32,256]{2,0,1:T(8,128)S(1)} %collective-permute-done, f32[256,16]{0,1:T(8,128)S(1)} %copy-done), kind=kOutput, calls=%fused_computation.90 | convolution fusion | flops 403046400 | bytes 10502144 | tf_op jit(solution)/shard_map/mcs,km->csk/dot_general | solution.py:65
  59.9 5.6 %fusion = f32[32,128,256]{2,1,0:T(8,128)} fusion(bf16[32,256,256]{2,1,0:T(8,128)(2,1)S(1)} %bitcast.99, f32[32,256,256]{2,1,0:T(8,128)S(1)} %fusion.62, bf16[32,256,256]{2,1,0:T(8,128)(2,1)S(1)} %bitcast.101, s32[32,256]{1,0:T(8,128)S(1)} %eq.47), kind=kOutput, calls=%fused_computation.8 | convolution fusion | flops 1622147072 | bytes 21004288 | tf_op jit(solution)/shard_map/csp,csk->cpk/dot_general | solution.py:95
  65.5 2.8 all-to-all-done.2
  68.2 7.6 %all-to-all-start = ((f32[32,128,256]{2,1,0:T(8,128)}), f32[32,128,256]{2,1,0:T(8,128)}, u32[]{:S(2)}, u32[]{:S(2)}) async-start(f32[32,128,256]{2,1,0:T(8,128)} %fusion), calls=%async_computation | async-start | bytes 8388608 | tf_op jit(solution)/shard_map/all_to_all | solution.py:96
  76.1 0.9 slice_convert_fusion
  77.0 50.5 %all-to-all-done = f32[32,128,256]{2,1,0:T(8,128)} async-done(((f32[32,128,256]{2,1,0:T(8,128)}), f32[32,128,256]{2,1,0:T(8,128)}, u32[]{:S(2)}, u32[]{:S(2)}) %all-to-all-start) | async-done | bytes 4194336 | tf_op jit(solution)/shard_map/all_to_all | solution.py:96
  127.5 5.1 %fusion.24 = f32[4,128,256]{2,0,1:T(4,128)S(1)} fusion(f32[32,128,256]{2,1,0:T(8,128)} %all-to-all-done, s32[32]{0:T(128)S(1)} %dynamic-slice_reduce_fusion), kind=kOutput, calls=%fused_computation.33 | convolution fusion | flops 25165952 | bytes 4718720 | tf_op jit(solution)/shard_map/cb,cpk->bpk/dot_general | solution.py:97
  132.6 1.4 fusion.82
  134.0 4.9 %fusion.22 = f32[32,256,256]{2,1,0:T(8,128)S(1)} fusion(f32[32,128,256]{2,0,1:T(8,128)S(1)} %fusion.82, s32[32,256]{1,0:T(8,128)S(1)} %bitcast.102), kind=kOutput, calls=%fused_computation.31 | convolution fusion | flops 1611661312 | bytes 12615680 | tf_op jit(solution)/shard_map/csp,cpk->csk/dot_general | solution.py:80
  138.9 10.0 %fusion.41 = f32[16,32,256]{2,0,1:T(8,128)S(1)} fusion(f32[32,256,256]{2,1,0:T(8,128)S(1)} %fusion.22, bf16[32,257,256]{2,1,0:T(8,128)(2,1)} %all-to-all-done.2, f32[256,16]{0,1:T(8,128)S(1)} %copy-done), kind=kOutput, calls=%fused_computation.52 | convolution fusion | flops 406847488 | bytes 13123584 | tf_op jit(solution)/shard_map/csk,km->mcs/dot_general | solution.py:62
  148.9 1.7 collective-permute-start.3
  150.5 3.3 collective-permute-start.4
  153.8 0.7 collective-permute-start.5
  154.6 9.7 %collective-permute-done.3 = f32[16,32,256]{2,0,1:T(8,128)S(1)} collective-permute-done((f32[16,32,256]{2,0,1:T(8,128)S(1)}, f32[16,32,256]{2,0,1:T(8,128)S(1)}, u32[]{:S(2)}, u32[]{:S(2)}) %collective-permute-start.3) | collective-permute-done | bytes 524320 | tf_op jit(solution)/shard_map/ppermute | solution.py:21
  164.3 12.1 %collective-permute-done.4 = f32[16,32,256]{2,0,1:T(8,128)S(1)} collective-permute-done((f32[16,32,256]{2,0,1:T(8,128)S(1)}, f32[16,32,256]{2,0,1:T(8,128)S(1)}, u32[]{:S(2)}, u32[]{:S(2)}) %collective-permute-start.4) | collective-permute-done | bytes 524320 | tf_op jit(solution)/shard_map/ppermute | solution.py:21
  176.5 7.0 %fusion.58 = f32[32,256,256]{2,1,0:T(8,128)S(1)} fusion(f32[16,32,256]{2,0,1:T(8,128)S(1)} %collective-permute-done.5, f32[16,32,256]{2,0,1:T(8,128)S(1)} %collective-permute-done.4, f32[16,32,256]{2,0,1:T(8,128)S(1)} %fusion.41, f32[16,32,256]{2,0,1:T(8,128)S(1)} %collective-permute-done.3, f32[256,16]{0,1:T(8,128)S(1)} %copy-done), kind=kOutput, calls=%fused_computation.85 | convolution fusion | flops 403046400 | bytes 10502144 | tf_op jit(solution)/shard_map/mcs,km->csk/dot_general | solution.py:65
  183.5 7.7 %fusion.1 = f32[32,128,256]{2,1,0:T(8,128)} fusion(f32[32,256,256]{2,1,0:T(8,128)S(1)} %fusion.58, f32[32,256,256]{2,1,0:T(8,128)S(1)} %fusion.22, s32[32,256]{1,0:T(8,128)S(1)} %bitcast.103, bf16[32,257,256]{2,1,0:T(8,128)(2,1)} %all-to-all-done.2), kind=kOutput, calls=%fused_computation.9 | convolution fusion | flops 1620049920 | bytes 25198592 | tf_op jit(solution)/shard_map/csp,csk->cpk/dot_general | solution.py:69
  191.2 6.3 %multiply_reduce_fusion.4 = (f32[]{:T(128)}, f32[]{:T(128)}, f32[4,128,256]{2,0,1:T(4,128)S(1)}, f32[4,128,256]{2,0,1:T(4,128)S(1)}) fusion(f32[4,128,256]{2,0,1:T(4,128)S(1)} %fusion.24, f32[32,128,256]{2,1,0:T(8,128)} %fusion.1, s32[32]{0:T(128)S(1)} %dynamic-slice_reduce_fusion), kind=kOutput, calls=%fused_computation.84 | convolution fusion | flops 25821310 | bytes 5767304 | tf_op jit(solution)/shard_map/cb,cpk->bpk/dot_general | solution.py:70
  198.2 18.2 %all_to_all.46 = f32[128,1,1]{2,1,0:T(1,128)S(1)} all-to-all(f32[128,1,1]{2,1,0:T(1,128)S(1)} %broadcast_in_dim.24), channel_id=1, replica_groups=mesh['tm'=32,'chan'=4] {'tm','chan'}, dimensions={0} | all-to-all | bytes 1024 | tf_op jit(solution)/shard_map/all_to_all | solution.py:27
  216.4 1.3 broadcast_in_dim.25
  217.7 4.3 %all-to-all-start.3 = ((f32[128,1,1]{2,1,0:T(1,128)}), f32[128,1,1]{2,1,0:T(1,128)S(1)}, u32[]{:S(2)}, u32[]{:S(2)}) async-start(f32[128,1,1]{2,1,0:T(1,128)} %broadcast_in_dim.25), calls=%async_computation.3 | async-start | bytes 131072 | tf_op jit(solution)/shard_map/all_to_all | solution.py:27
  222.0 0.7 reduce_sum.109
  222.7 8.9 %all-to-all-done.3 = f32[128,1,1]{2,1,0:T(1,128)S(1)} async-done(((f32[128,1,1]{2,1,0:T(1,128)}), f32[128,1,1]{2,1,0:T(1,128)S(1)}, u32[]{:S(2)}, u32[]{:S(2)}) %all-to-all-start.3) | async-done | bytes 544 | tf_op jit(solution)/shard_map/all_to_all | solution.py:27
  231.6 0.7 reduce_sum.111
  233.7 0.9 multiply_reduce_fusion.3
  234.6 1.4 fusion.79
  235.9 4.9 %fusion.18 = f32[32,256,256]{2,1,0:T(8,128)S(1)} fusion(f32[32,128,256]{2,0,1:T(8,128)S(1)} %fusion.79, s32[32,256]{1,0:T(8,128)S(1)} %bitcast.104), kind=kOutput, calls=%fused_computation.27 | convolution fusion | flops 1611661312 | bytes 12615680 | tf_op jit(solution)/shard_map/csp,cpk->csk/dot_general | solution.py:80
  240.8 12.9 %fusion.40 = f32[16,32,256]{2,0,1:T(8,128)S(1)} fusion(f32[32,256,256]{2,1,0:T(8,128)S(1)} %fusion.18, bf16[32,257,256]{2,1,0:T(8,128)(2,1)} %all-to-all-done.2, f32[256,16]{0,1:T(8,128)S(1)} %copy-done), kind=kOutput, calls=%fused_computation.51 | convolution fusion | flops 406847488 | bytes 13123584 | tf_op jit(solution)/shard_map/csk,km->mcs/dot_general | solution.py:62
  254.4 1.4 collective-permute-start.7
  255.9 1.2 collective-permute-start.8
  257.7 24.0 %all_to_all.47 = f32[128,1,1]{2,1,0:T(1,128)S(1)} all-to-all(f32[128,1,1]{2,1,0:T(1,128)S(1)} %broadcast_in_dim.26), channel_id=1, replica_groups=mesh['tm'=32,'chan'=4] {'tm','chan'}, dimensions={0} | all-to-all | bytes 1024 | tf_op jit(solution)/shard_map/all_to_all | solution.py:27
  281.7 0.7 reduce_sum.113
  283.7 0.8 copy-done.10
  284.5 9.0 %fusion.54 = f32[32,256,256]{2,1,0:T(8,128)S(1)} fusion(f32[16,32,256]{2,0,1:T(8,128)} %collective-permute-done.8, f32[16,32,256]{2,0,1:T(8,128)} %collective-permute-done.7, f32[16,32,256]{2,0,1:T(8,128)S(1)} %fusion.40, f32[16,32,256]{2,0,1:T(8,128)} %copy-done.10, f32[256,16]{0,1:T(8,128)S(1)} %copy-done), kind=kOutput, calls=%fused_computation.77 | convolution fusion | flops 403046400 | bytes 10502144 | tf_op jit(solution)/shard_map/mcs,km->csk/dot_general | solution.py:65
  293.5 7.7 %fusion.2 = f32[32,128,256]{2,1,0:T(8,128)} fusion(f32[32,256,256]{2,1,0:T(8,128)S(1)} %fusion.54, f32[32,256,256]{2,1,0:T(8,128)S(1)} %copy-done.4, s32[32,256]{1,0:T(8,128)} %bitcast.105, bf16[32,257,256]{2,1,0:T(8,128)(2,1)} %all-to-all-done.2), kind=kOutput, calls=%fused_computation.10 | convolution fusion | flops 1620049920 | bytes 25198592 | tf_op jit(solution)/shard_map/csp,csk->cpk/dot_general | solution.py:69
  301.2 7.2 %multiply_reduce_fusion.2 = (f32[]{:T(128)}, f32[4,128,256]{2,0,1:T(4,128)S(1)}, f32[4,128,256]{2,0,1:T(4,128)}) fusion(f32[4,128,256]{2,0,1:T(4,128)S(1)} %get-tuple-element.7, f32[4,128,256]{2,0,1:T(4,128)S(1)} %fusion.24, f32[]{:T(128)S(6)} %div.16, f32[4,128,256]{2,0,1:T(4,128)S(1)} %get-tuple-element.8, f32[32,128,256]{2,1,0:T(8,128)} %fusion.2, ...), kind=kOutput, calls=%fused_computation.75 | convolution fusion | flops 26083456 | bytes 6815880 | tf_op jit(solution)/shard_map/cb,cpk->bpk/dot_general | solution.py:70
  309.1 14.7 %all_to_all.48 = f32[128,1,1]{2,1,0:T(1,128)S(1)} all-to-all(f32[128,1,1]{2,1,0:T(1,128)S(1)} %broadcast_in_dim.27), channel_id=1, replica_groups=mesh['tm'=32,'chan'=4] {'tm','chan'}, dimensions={0} | all-to-all | bytes 1024 | tf_op jit(solution)/shard_map/all_to_all | solution.py:27
  323.8 0.7 reduce_sum.115
  325.8 1.4 fusion.74
  327.2 4.9 %fusion.14 = f32[32,256,256]{2,1,0:T(8,128)S(1)} fusion(f32[32,128,256]{2,0,1:T(8,128)S(1)} %fusion.74, s32[32,256]{1,0:T(8,128)S(1)} %bitcast.107), kind=kOutput, calls=%fused_computation.23 | convolution fusion | flops 1611661312 | bytes 12615680 | tf_op jit(solution)/shard_map/csp,cpk->csk/dot_general | solution.py:80
  332.1 12.9 %fusion.39 = f32[16,32,256]{2,0,1:T(8,128)S(1)} fusion(f32[32,256,256]{2,1,0:T(8,128)S(1)} %fusion.14, bf16[32,257,256]{2,1,0:T(8,128)(2,1)} %all-to-all-done.2, f32[256,16]{0,1:T(8,128)S(1)} %copy-done), kind=kOutput, calls=%fused_computation.50 | convolution fusion | flops 406847488 | bytes 13123584 | tf_op jit(solution)/shard_map/csk,km->mcs/dot_general | solution.py:62
  345.1 1.2 collective-permute-start.10
  346.3 1.9 collective-permute-start.11
  348.1 0.9 multiply_reduce_fusion.1
  349.7 23.0 %all_to_all.49 = f32[128,1,1]{2,1,0:T(1,128)S(1)} all-to-all(f32[128,1,1]{2,1,0:T(1,128)S(1)} %broadcast_in_dim.28), channel_id=1, replica_groups=mesh['tm'=32,'chan'=4] {'tm','chan'}, dimensions={0} | all-to-all | bytes 1024 | tf_op jit(solution)/shard_map/all_to_all | solution.py:27
  372.6 0.8 reduce_sum.117
  374.8 0.8 copy-done.11
  375.5 9.0 %fusion.50 = f32[32,256,256]{2,1,0:T(8,128)S(1)} fusion(f32[16,32,256]{2,0,1:T(8,128)} %collective-permute-done.11, f32[16,32,256]{2,0,1:T(8,128)} %copy-done.11, f32[16,32,256]{2,0,1:T(8,128)S(1)} %fusion.39, f32[16,32,256]{2,0,1:T(8,128)} %collective-permute-done.9, f32[256,16]{0,1:T(8,128)S(1)} %copy-done), kind=kOutput, calls=%fused_computation.69 | convolution fusion | flops 403046400 | bytes 10502144 | tf_op jit(solution)/shard_map/mcs,km->csk/dot_general | solution.py:65
  384.5 7.7 %fusion.3 = f32[32,128,256]{2,1,0:T(8,128)} fusion(f32[32,256,256]{2,1,0:T(8,128)S(1)} %fusion.50, f32[32,256,256]{2,1,0:T(8,128)S(1)} %copy-done.2, s32[32,256]{1,0:T(8,128)} %bitcast.106, bf16[32,257,256]{2,1,0:T(8,128)(2,1)} %all-to-all-done.2), kind=kOutput, calls=%fused_computation.11 | convolution fusion | flops 1620049920 | bytes 25198592 | tf_op jit(solution)/shard_map/csp,csk->cpk/dot_general | solution.py:69
  392.3 6.4 %multiply_reduce_fusion = (f32[]{:T(128)}, f32[4,128,256]{2,0,1:T(4,128)S(1)}) fusion(f32[4,128,256]{2,0,1:T(4,128)S(1)} %get-tuple-element.5, f32[]{:T(128)S(6)} %div.18, f32[4,128,256]{2,0,1:T(4,128)S(1)} %get-tuple-element.7, f32[4,128,256]{2,0,1:T(4,128)S(1)} %fusion.24, f32[]{:T(128)S(6)} %div.16, f32[]{:T(128)S(6)} %div.17, ...), kind=kOutput, calls=%fused_computation.68 | convolution fusion | flops 26607744 | bytes 6291600 | tf_op jit(solution)/shard_map/cb,cpk->bpk/dot_general | solution.py:70
  398.6 1.2 broadcast_in_dim.29
  399.8 4.7 %all-to-all-start.7 = ((f32[128,1,1]{2,1,0:T(1,128)}), f32[128,1,1]{2,1,0:T(1,128)}, u32[]{:S(2)}, u32[]{:S(2)}) async-start(f32[128,1,1]{2,1,0:T(1,128)} %broadcast_in_dim.29), calls=%async_computation.7 | async-start | bytes 131072 | tf_op jit(solution)/shard_map/all_to_all | solution.py:27
  405.0 9.3 %all-to-all-done.7 = f32[128,1,1]{2,1,0:T(1,128)} async-done(((f32[128,1,1]{2,1,0:T(1,128)}), f32[128,1,1]{2,1,0:T(1,128)}, u32[]{:S(2)}, u32[]{:S(2)}) %all-to-all-start.7) | async-done | bytes 544 | tf_op jit(solution)/shard_map/all_to_all | solution.py:27
  414.3 1.6 reduce_sum.119
  417.3 1.4 fusion.45
  (48 shorter events, 4.1 us)
Async XLA Ops:
  0.6 14.0 %copy-start = (f32[256,16]{0,1:T(8,128)S(1)}, f32[256,16]{0,1:T(8,128)}, u32[]{:S(2)}) copy-start(f32[256,16]{0,1:T(8,128)} %param.9) | copy-start | bytes 49156
  6.0 62.3 %all-to-all-start.2 = ((bf16[32,257,256]{2,1,0:T(8,128)(2,1)}), bf16[32,257,256]{2,1,0:T(8,128)(2,1)}, u32[]{:S(2)}, u32[]{:S(2)}) async-start(bf16[32,257,256]{2,1,0:T(8,128)(2,1)} %pad_maximum_fusion), calls=%async_computation.2 | async-start | bytes 8650752 | tf_op jit(solution)/shard_map/all_to_all | solution.py:44
  14.6 16.1 %copy-start.12 = (s32[8192]{0:T(1024)S(1)}, s32[8192]{0:T(1024)}, u32[]{:S(2)}) copy-start(s32[8192]{0:T(1024)} %param.7) | copy-start | bytes 98308
  24.8 15.9 %collective-permute-start = (f32[16,32,256]{2,0,1:T(8,128)S(1)}, f32[16,32,256]{2,0,1:T(8,128)S(1)}, u32[]{:S(2)}, u32[]{:S(2)}) collective-permute-start(f32[16,32,256]{2,0,1:T(8,128)S(1)} %fusion.42), channel_id=1, source_target_pairs={{0,1},{1,2},{2,3},{3,0},{4,5},{5,6},{6,7},{7,4},{8,9},{9,10},{10,1... | collective-permute-start | bytes 1572872 | tf_op jit(solution)/shard_map/ppermute | solution.py:21
  26.5 26.4 %collective-permute-start.1 = (f32[16,32,256]{2,0,1:T(8,128)S(1)}, f32[16,32,256]{2,0,1:T(8,128)S(1)}, u32[]{:S(2)}, u32[]{:S(2)}) collective-permute-start(f32[16,32,256]{2,0,1:T(8,128)S(1)} %fusion.42), channel_id=1, source_target_pairs={{0,2},{1,3},{2,0},{3,1},{4,6},{5,7},{6,4},{7,5},{8,10},{9,11},{10,... | collective-permute-start | bytes 1572872 | tf_op jit(solution)/shard_map/ppermute | solution.py:21
  29.8 23.1 %collective-permute-start.2 = (f32[16,32,256]{2,0,1:T(8,128)S(1)}, f32[16,32,256]{2,0,1:T(8,128)S(1)}, u32[]{:S(2)}, u32[]{:S(2)}) collective-permute-start(f32[16,32,256]{2,0,1:T(8,128)S(1)} %fusion.42), channel_id=1, source_target_pairs={{0,3},{1,0},{2,1},{3,2},{4,7},{5,4},{6,5},{7,6},{8,11},{9,8},{10,9... | collective-permute-start | bytes 1572872 | tf_op jit(solution)/shard_map/ppermute | solution.py:21
  30.7 29.2 %copy-start.5 = (bf16[8192,256]{1,0:T(8,128)(2,1)S(1)}, bf16[8192,256]{1,0:T(8,128)(2,1)}, u32[]{:S(2)}) copy-start(bf16[8192,256]{1,0:T(8,128)(2,1)} %param.6) | copy-start | bytes 12582916
  30.7 29.2 %copy-start.6 = (bf16[8192,256]{1,0:T(8,128)(2,1)S(1)}, bf16[8192,256]{1,0:T(8,128)(2,1)}, u32[]{:S(2)}) copy-start(bf16[8192,256]{1,0:T(8,128)(2,1)} %param.5) | copy-start | bytes 12582916
  65.5 10.4 %copy-start.13 = (s32[32,32]{1,0:T(8,128)S(1)}, s32[32,32]{1,0:T(8,128)}, u32[]{:S(2)}) copy-start(s32[32,32]{1,0:T(8,128)} %param.8) | copy-start | bytes 12292
  68.2 59.3 %all-to-all-start = ((f32[32,128,256]{2,1,0:T(8,128)}), f32[32,128,256]{2,1,0:T(8,128)}, u32[]{:S(2)}, u32[]{:S(2)}) async-start(f32[32,128,256]{2,1,0:T(8,128)} %fusion), calls=%async_computation | async-start | bytes 8388608 | tf_op jit(solution)/shard_map/all_to_all | solution.py:96
  77.0 158.9 %copy-start.8 = (s32[32,1,256]{2,0,1:T(8,128)}, s32[32,1,256]{2,0,1:T(8,128)S(1)}, u32[]{:S(2)}) copy-start(s32[32,1,256]{2,0,1:T(8,128)S(1)} %copy.94) | copy-start | bytes 98308
  148.9 15.5 %collective-permute-start.3 = (f32[16,32,256]{2,0,1:T(8,128)S(1)}, f32[16,32,256]{2,0,1:T(8,128)S(1)}, u32[]{:S(2)}, u32[]{:S(2)}) collective-permute-start(f32[16,32,256]{2,0,1:T(8,128)S(1)} %fusion.41), channel_id=1, source_target_pairs={{0,1},{1,2},{2,3},{3,0},{4,5},{5,6},{6,7},{7,4},{8,9},{9,10},{10,1... | collective-permute-start | bytes 1572872 | tf_op jit(solution)/shard_map/ppermute | solution.py:21
  150.5 25.9 %collective-permute-start.4 = (f32[16,32,256]{2,0,1:T(8,128)S(1)}, f32[16,32,256]{2,0,1:T(8,128)S(1)}, u32[]{:S(2)}, u32[]{:S(2)}) collective-permute-start(f32[16,32,256]{2,0,1:T(8,128)S(1)} %fusion.41), channel_id=1, source_target_pairs={{0,2},{1,3},{2,0},{3,1},{4,6},{5,7},{6,4},{7,5},{8,10},{9,11},{10,... | collective-permute-start | bytes 1572872 | tf_op jit(solution)/shard_map/ppermute | solution.py:21
  153.8 22.6 %collective-permute-start.5 = (f32[16,32,256]{2,0,1:T(8,128)S(1)}, f32[16,32,256]{2,0,1:T(8,128)S(1)}, u32[]{:S(2)}, u32[]{:S(2)}) collective-permute-start(f32[16,32,256]{2,0,1:T(8,128)S(1)} %fusion.41), channel_id=1, source_target_pairs={{0,3},{1,0},{2,1},{3,2},{4,7},{5,4},{6,5},{7,6},{8,11},{9,8},{10,9... | collective-permute-start | bytes 1572872 | tf_op jit(solution)/shard_map/ppermute | solution.py:21
  217.7 13.9 %all-to-all-start.3 = ((f32[128,1,1]{2,1,0:T(1,128)}), f32[128,1,1]{2,1,0:T(1,128)S(1)}, u32[]{:S(2)}, u32[]{:S(2)}) async-start(f32[128,1,1]{2,1,0:T(1,128)} %broadcast_in_dim.25), calls=%async_computation.3 | async-start | bytes 131072 | tf_op jit(solution)/shard_map/all_to_all | solution.py:27
  240.8 13.0 %copy-start.3 = (f32[32,256,256]{2,1,0:T(8,128)}, f32[32,256,256]{2,1,0:T(8,128)S(1)}, u32[]{:S(2)}) copy-start(f32[32,256,256]{2,1,0:T(8,128)S(1)} %fusion.18) | copy-start | bytes 25165828
  253.8 29.9 %collective-permute-start.6 = (f32[16,32,256]{2,0,1:T(8,128)S(1)}, f32[16,32,256]{2,0,1:T(8,128)S(1)}, u32[]{:S(2)}, u32[]{:S(2)}) collective-permute-start(f32[16,32,256]{2,0,1:T(8,128)S(1)} %fusion.40), channel_id=1, source_target_pairs={{0,1},{1,2},{2,3},{3,0},{4,5},{5,6},{6,7},{7,4},{8,9},{9,10},{10,1... | collective-permute-start | bytes 1572872 | tf_op jit(solution)/shard_map/ppermute | solution.py:21
  254.4 29.3 %collective-permute-start.7 = (f32[16,32,256]{2,0,1:T(8,128)S(1)}, f32[16,32,256]{2,0,1:T(8,128)}, u32[]{:S(2)}, u32[]{:S(2)}) collective-permute-start(f32[16,32,256]{2,0,1:T(8,128)S(1)} %fusion.40), channel_id=1, source_target_pairs={{0,2},{1,3},{2,0},{3,1},{4,6},{5,7},{6,4},{7,5},{8,10},{9,11},{10,... | collective-permute-start | bytes 1572872 | tf_op jit(solution)/shard_map/ppermute | solution.py:21
  255.9 28.7 %collective-permute-start.8 = (f32[16,32,256]{2,0,1:T(8,128)S(1)}, f32[16,32,256]{2,0,1:T(8,128)}, u32[]{:S(2)}, u32[]{:S(2)}) collective-permute-start(f32[16,32,256]{2,0,1:T(8,128)S(1)} %fusion.40), channel_id=1, source_target_pairs={{0,3},{1,0},{2,1},{3,2},{4,7},{5,4},{6,5},{7,6},{8,11},{9,8},{10,9... | collective-permute-start | bytes 1572872 | tf_op jit(solution)/shard_map/ppermute | solution.py:21
  283.7 9.8 %copy-start.4 = (f32[32,256,256]{2,1,0:T(8,128)S(1)}, f32[32,256,256]{2,1,0:T(8,128)}, u32[]{:S(2)}) copy-start(f32[32,256,256]{2,1,0:T(8,128)} %copy-done.3) | copy-start | bytes 25165828
  283.7 0.8 copy-start.10
  308.4 18.8 %copy-start.9 = (s32[32,1,256]{2,0,1:T(8,128)S(1)}, s32[32,1,256]{2,0,1:T(8,128)}, u32[]{:S(2)}) copy-start(s32[32,1,256]{2,0,1:T(8,128)} %copy-done.8) | copy-start | bytes 98308
  332.1 13.0 %copy-start.1 = (f32[32,256,256]{2,1,0:T(8,128)}, f32[32,256,256]{2,1,0:T(8,128)S(1)}, u32[]{:S(2)}) copy-start(f32[32,256,256]{2,1,0:T(8,128)S(1)} %fusion.14) | copy-start | bytes 25165828
  345.1 29.7 %collective-permute-start.10 = (f32[16,32,256]{2,0,1:T(8,128)S(1)}, f32[16,32,256]{2,0,1:T(8,128)S(1)}, u32[]{:S(2)}, u32[]{:S(2)}) collective-permute-start(f32[16,32,256]{2,0,1:T(8,128)S(1)} %fusion.39), channel_id=1, source_target_pairs={{0,2},{1,3},{2,0},{3,1},{4,6},{5,7},{6,4},{7,5},{8,10},{9,11},{10,... | collective-permute-start | bytes 1572872 | tf_op jit(solution)/shard_map/ppermute | solution.py:21
  346.3 28.5 %collective-permute-start.11 = (f32[16,32,256]{2,0,1:T(8,128)S(1)}, f32[16,32,256]{2,0,1:T(8,128)}, u32[]{:S(2)}, u32[]{:S(2)}) collective-permute-start(f32[16,32,256]{2,0,1:T(8,128)S(1)} %fusion.39), channel_id=1, source_target_pairs={{0,3},{1,0},{2,1},{3,2},{4,7},{5,4},{6,5},{7,6},{8,11},{9,8},{10,9... | collective-permute-start | bytes 1572872 | tf_op jit(solution)/shard_map/ppermute | solution.py:21
  348.1 27.4 %collective-permute-start.9 = (f32[16,32,256]{2,0,1:T(8,128)S(1)}, f32[16,32,256]{2,0,1:T(8,128)}, u32[]{:S(2)}, u32[]{:S(2)}) collective-permute-start(f32[16,32,256]{2,0,1:T(8,128)S(1)} %fusion.39), channel_id=1, source_target_pairs={{0,1},{1,2},{2,3},{3,0},{4,5},{5,6},{6,7},{7,4},{8,9},{9,10},{10,1... | collective-permute-start | bytes 1572872 | tf_op jit(solution)/shard_map/ppermute | solution.py:21
  374.7 9.8 %copy-start.2 = (f32[32,256,256]{2,1,0:T(8,128)S(1)}, f32[32,256,256]{2,1,0:T(8,128)}, u32[]{:S(2)}) copy-start(f32[32,256,256]{2,1,0:T(8,128)} %copy-done.1) | copy-start | bytes 25165828
  374.7 0.8 copy-start.11
  392.3 12.6 %copy-start.7 = (f32[4,128,256]{2,0,1:T(4,128)S(1)}, f32[4,128,256]{2,0,1:T(4,128)}, u32[]{:S(2)}) copy-start(f32[4,128,256]{2,0,1:T(4,128)} %get-tuple-element.12) | copy-start | bytes 1572868
  399.8 14.5 %all-to-all-start.7 = ((f32[128,1,1]{2,1,0:T(1,128)}), f32[128,1,1]{2,1,0:T(1,128)}, u32[]{:S(2)}, u32[]{:S(2)}) async-start(f32[128,1,1]{2,1,0:T(1,128)} %broadcast_in_dim.29), calls=%async_computation.7 | async-start | bytes 131072 | tf_op jit(solution)/shard_map/all_to_all | solution.py:27

commit v5 on v4

--- a/solution.py
+++ b/solution.py
@@ -1,6 +1,10 @@
+import functools
+
 import jax
 import jax.numpy as jnp
 from jax import lax
+from jax.experimental import pallas as pl
+from jax.experimental.pallas import tpu as pltpu
 from jax.sharding import PartitionSpec as P
 
 PIX_DEV = 512
@@ -11,6 +15,106 @@
 highest = lax.Precision.HIGHEST
 high = lax.Precision.HIGH
 ridge = 1.0
+RUNS = 4
+
+
+def gathered(field_ref, block, points):
+    start = pl.multiple_of(block * BLK, BLK)
+    rest = field_ref[pl.ds(start, BLK), :]
+    hits = (points == lax.broadcasted_iota(jnp.int32, (points.shape[0], BLK), 1)).astype(
+        jnp.bfloat16
+    )
+    total = None
+    for _ in range(3):
+        part = rest.astype(jnp.bfloat16)
+        rest = rest - part.astype(jnp.float32)
+        term = jnp.dot(hits, part, preferred_element_type=jnp.float32)
+        total = term if total is None else total + term
+    return total
+
+
+def amp_kernel(blocks_ref, field_ref, points_ref, weights_ref, modes_t_ref, amp_ref):
+    step = pl.program_id(0)
+    for j in range(RUNS):
+        x = gathered(field_ref, blocks_ref[step * RUNS + j], points_ref[j])
+        y = weights_ref[j].astype(jnp.float32) * x
+        amp_ref[j] = lax.dot_general(
+            modes_t_ref[...], y, (((1,), (1,)), ((), ())),
+            precision=highest, preferred_element_type=jnp.float32,
+        )
+
+
+def bin_kernel(blocks_ref, field_ref, points_ref, rows_ref, weights_ref, amp_ref, modes_t_ref, out_ref):
+    step = pl.program_id(0)
+
+    @pl.when(step == 0)
+    def _():
+        out_ref[...] = jnp.zeros_like(out_ref)
+
+    for j in range(RUNS):
+        block = blocks_ref[step * RUNS + j]
+        x = gathered(field_ref, block, points_ref[j])
+        w = weights_ref[j].astype(jnp.float32)
+        y = w * x
+        correction = lax.dot_general(
+            amp_ref[j], modes_t_ref[...], (((0,), (0,)), ((), ())),
+            precision=highest, preferred_element_type=jnp.float32,
+        )
+        rest = w * (y - correction)
+        hits = (rows_ref[j] == lax.broadcasted_iota(jnp.int32, (BLK, rest.shape[0]), 0)).astype(
+            jnp.bfloat16
+        )
+        total = None
+        for _ in range(3):
+            part = rest.astype(jnp.bfloat16)
+            rest = rest - part.astype(jnp.float32)
+            term = jnp.dot(hits, part, preferred_element_type=jnp.float32)
+            total = term if total is None else total + term
+        start = pl.multiple_of(block * BLK, BLK)
+        out_ref[pl.ds(start, BLK), :] += total
+
+
+def owner_operator(blocks, field, points_col, points_row, noise_weights, modes_t):
+    groups, run_length, channels = noise_weights.shape
+    modes = modes_t.shape[0]
+    steps = groups // RUNS
+    full = pl.BlockSpec(field.shape, lambda i, b: (0, 0))
+    per_run = lambda *shape: pl.BlockSpec((RUNS,) + shape, lambda i, b: (i, 0, 0))
+    gather_flops = groups * 3 * 2 * run_length * BLK * channels
+    amps = pl.pallas_call(
+        amp_kernel,
+        grid_spec=pltpu.PrefetchScalarGridSpec(
+            num_scalar_prefetch=1,
+            grid=(steps,),
+            in_specs=[full, per_run(run_length, 1), per_run(run_length, channels),
+                      pl.BlockSpec(modes_t.shape, lambda i, b: (0, 0))],
+            out_specs=per_run(modes, run_length),
+        ),
+        out_shape=jax.ShapeDtypeStruct((groups, modes, run_length), jnp.float32),
+        cost_estimate=pl.CostEstimate(
+            flops=gather_flops + groups * 12 * run_length * channels * modes,
+            bytes_accessed=noise_weights.size * 2 + field.size * 4,
+            transcendentals=0,
+        ),
+    )(blocks, field, points_col, noise_weights, modes_t)
+    amps = chan_sum(amps)
+    return pl.pallas_call(
+        bin_kernel,
+        grid_spec=pltpu.PrefetchScalarGridSpec(
+            num_scalar_prefetch=1,
+            grid=(steps,),
+            in_specs=[full, per_run(run_length, 1), per_run(1, run_length),
+                      per_run(run_length, channels), per_run(modes, run_length),
+                      pl.BlockSpec(modes_t.shape, lambda i, b: (0, 0))],
+            out_specs=full,
+        ),
+        out_shape=jax.ShapeDtypeStruct(field.shape, jnp.float32),
+        cost_estimate=pl.CostEstimate(
+            flops=2 * gather_flops + groups * 12 * run_length * channels * modes,
+            bytes_accessed=noise_weights.size * 2 + field.size * 8,
+            transcendentals=0,
+        ),
+    )(blocks, field, points_col, points_row, noise_weights, amps, modes_t)
 
 
 def chan_sum(value):
@@ -82,8 +186,15 @@
     def squares(vector):
         return global_sum(jnp.sum(vector * vector))
 
+    points_col = points_in[:, :, None]
+    points_row = points_in[:, None, :]
+    modes_t = foreground_modes.T
+
     def operate(field):
-        return binned(filtered(pointed(field), noise_weights)) + ridge * field
+        return (
+            owner_operator(column, field, points_col, points_row, weights_in, modes_t)
+            + ridge * field
+        )
 
     local_hits = (points[:, :, None] == jnp.arange(BLK, dtype=jnp.int32)[None, None, :]).astype(
         jnp.float32

time: 424 us -> 427 us (level)
  Pallas kernels: 0 us -> 123 us
  matrix products: 150 us -> 28.6 us
  waiting for transfers between devices: 115 us -> 93.7 us
  other arithmetic: 14.7 us -> 29.4 us
  local copies, waits for them, and re-layouts: 7.5 us -> 13.7 us
    pallas_call x0 -> x6, Pallas kernels: none -> 123 us  [the longest x3 74.9 us: owner_operator(): pl.pallas_call(bin_kernel, grid_spec=pltpu.PrefetchScalarGridSpec(num_sca...]
    dot_general x12 -> x0, matrix products: 61.8 us -> none  [the longest x3 23.2 us: binned(): jnp.einsum('csp,csk->cpk', pixel_hits, samples, precision=high)]
    dot_general x4 -> x1, matrix products: 46 us -> 10.2 us  [filtered(): jnp.einsum('csk,km->mcs', weighted, foreground_modes, precision=highest)]
    dot_general x4 -> x1, matrix products: 32 us -> 7.05 us  [filtered(): jnp.einsum('mcs,km->csk', amplitudes, foreground_modes, precision=highest)]
    all_to_all x2, waiting for transfers between devices: 18.2 us -> 8.83 us  [global_sum(): lax.all_to_all(jnp.broadcast_to(value, (everyone, 1)), ('tm', 'chan'), 0,...]
    all_to_all x1, waiting for transfers between devices: 50.5 us -> 42.9 us  [per_device(): arrived = lax.all_to_all(local_partial, 'tm', 0, 0, tiled=True)]
    all_to_all x2, starting transfers between devices: 8.99 us -> 15.6 us  [global_sum(): lax.all_to_all(jnp.broadcast_to(value, (everyone, 1)), ('tm', 'chan'), 0,...]
    add x0 -> x3, other arithmetic: none -> 6.15 us  [chan_sum(): total = total + lax.ppermute(value, 'chan', pairs)]
  transfers between devices with their start and end apart: 16 -> 16, of which waited for: 8 -> 7; matrix products, arithmetic and copies ran while one was open for 7% -> 10% of each run, Pallas kernels for 0% -> 6%
where the time goes in v5:
time: 427 us; the launch traced here: 421 us
  Pallas kernels  123 us (29%)
  waiting for transfers between devices  93.7 us (22%)
  blocking collectives  78.6 us (18%)
  starting transfers between devices  46 us (11%)
  other arithmetic  29.4 us (7%)
  matrix products  28.6 us (7%)
  local copies, waits for them, and re-layouts  13.7 us (3%)
  between operations  8.3 us (2%)
    all_to_all x4, blocking collectives, global_sum(): lax.all_to_all(jnp.broadcast_to(value, (everyone, 1)), ('tm', 'chan'), 0,...  78.6 us
    pallas_call x3, Pallas kernels, owner_operator(): pl.pallas_call(bin_kernel, grid_spec=pltpu.PrefetchScalarGridSpec(num_sca...  74.9 us
    pallas_call x3, Pallas kernels, owner_operator(): pl.pallas_call(amp_kernel, grid_spec=pltpu.PrefetchScalarGridSpec(num_sca...  47.9 us
    all_to_all x1, waiting for transfers between devices, per_device(): arrived = lax.all_to_all(local_partial, 'tm', 0, 0, tiled=True)  42.9 us
    ppermute x12, waiting for transfers between devices, chan_sum(): total = total + lax.ppermute(value, 'chan', pairs)  41.4 us
    all_to_all x2, starting transfers between devices, global_sum(): lax.all_to_all(jnp.broadcast_to(value, (everyone, 1)), ('tm', 'chan'), 0,...  15.6 us
    ppermute x12, starting transfers between devices, chan_sum(): total = total + lax.ppermute(value, 'chan', pairs)  14.1 us
    dot_general x1, matrix products, filtered(): jnp.einsum('csk,km->mcs', weighted, foreground_modes, precision=highest)  10.2 us
  transfers between devices with their start and end apart: 16, of which 7 were waited for; matrix products, arithmetic and copies ran while one was open for 10% of the time, Pallas kernels for 6%

profile of v5, /device:TPU:1, one launch (start us, length us, event | category | flops | bytes accessed | tf_op | source)
XLA Modules:
  0.0 421.1 jit_solution(9080010508364128439)
XLA Ops:
  0.6 0.0 copy-start
  0.6 0.8 convert_element_type.36
  1.4 4.5 %pad_maximum_fusion = bf16[32,257,256]{2,1,0:T(8,128)(2,1)} fusion(bf16[32,1,256]{2,1,0:T(2,128)(2,1)S(1)} %convert_element_type.42, bf16[32,256,256]{2,1,0:T(8,128)(2,1)} %bitcast.33), kind=kLoop, calls=%fused_computation.5 | loop fusion | flops 8421376 | bytes 8421376 | tf_op jit(solution)/shard_map/concatenate | solution.py:147
  6.0 8.8 %all-to-all-start.2 = ((bf16[32,257,256]{2,1,0:T(8,128)(2,1)}), bf16[32,257,256]{2,1,0:T(8,128)(2,1)}, u32[]{:S(2)}, u32[]{:S(2)}) async-start(bf16[32,257,256]{2,1,0:T(8,128)(2,1)} %pad_maximum_fusion), calls=%async_computation.2 | async-start | bytes 8650752 | tf_op jit(solution)/shard_map/all_to_all | solution.py:148
  14.7 0.0 copy-start.8
  14.7 10.2 %fusion.6 = f32[16,32,256]{2,0,1:T(8,128)S(1)} fusion(bf16[32,256,256]{2,1,0:T(8,128)(2,1)} %bitcast.34, bf16[32,256,256]{2,1,0:T(8,128)(2,1)} %bitcast.38, f32[256,16]{0,1:T(8,128)S(1)} %copy-done.7), kind=kOutput, calls=%fused_computation.10 | convolution fusion | flops 408944640 | bytes 8929280 | tf_op jit(solution)/shard_map/csk,km->mcs/dot_general | solution.py:166
  24.9 3.8 collective-permute-start.2
  28.7 0.8 collective-permute-start
  29.6 0.0 copy-start.1
  29.6 21.3 %collective-permute-done.2 = f32[16,32,256]{2,0,1:T(8,128)S(1)} collective-permute-done((f32[16,32,256]{2,0,1:T(8,128)S(1)}, f32[16,32,256]{2,0,1:T(8,128)S(1)}, u32[]{:S(2)}, u32[]{:S(2)}) %collective-permute-start.2) | collective-permute-done | bytes 524320 | tf_op jit(solution)/shard_map/ppermute | solution.py:125
  51.0 4.2 collective-permute-done
  55.1 7.1 %fusion.7 = f32[32,256,256]{2,1,0:T(8,128)S(1)} fusion(f32[16,32,256]{2,0,1:T(8,128)S(1)} %collective-permute-done.2, f32[16,32,256]{2,0,1:T(8,128)S(1)} %collective-permute-done.1, f32[16,32,256]{2,0,1:T(8,128)S(1)} %fusion.6, f32[16,32,256]{2,0,1:T(8,128)S(1)} %collective-permute-done, f32[256,16]{0,1:T(8,128)S(1)} %copy-done.7), kind=kOutput, calls=%fused_computation.28 | convolution fusion | flops 403046400 | bytes 10502144 | tf_op jit(solution)/shard_map/mcs,km->csk/dot_general | solution.py:169
  62.2 5.5 %fusion = f32[32,128,256]{2,1,0:T(8,128)} fusion(bf16[32,256,256]{2,1,0:T(8,128)(2,1)S(1)} %bitcast.35, f32[32,256,256]{2,1,0:T(8,128)S(1)} %fusion.7, bf16[32,256,256]{2,1,0:T(8,128)(2,1)S(1)} %bitcast.39, s32[32,256]{1,0:T(8,128)S(1)} %eq.34), kind=kOutput, calls=%fused_computation.2 | convolution fusion | flops 1622147072 | bytes 21004288 | tf_op jit(solution)/shard_map/csp,csk->cpk/dot_general | solution.py:206
  67.7 0.6 all-to-all-done.2
  68.4 7.6 %all-to-all-start = ((f32[32,128,256]{2,1,0:T(8,128)}), f32[32,128,256]{2,1,0:T(8,128)}, u32[]{:S(2)}, u32[]{:S(2)}) async-start(f32[32,128,256]{2,1,0:T(8,128)} %fusion), calls=%async_computation | async-start | bytes 8388608 | tf_op jit(solution)/shard_map/all_to_all | solution.py:207
  76.0 0.2 dynamic-slice_reduce_fusion.blocks_ref
  76.2 1.5 slice_convert_fusion
  77.7 2.7 copy.45.points_ref
  80.4 4.6 %slice.9.weights_ref = bf16[32,256,256]{2,1,0:T(8,128)(2,1)} slice(bf16[32,257,256]{2,1,0:T(8,128)(2,1)} %all-to-all-done.2), slice={[0:32], [0:256], [0:256]} | slice | bytes 8388608 | tf_op jit(solution)/shard_map/slice | solution.py:149
  84.9 42.9 %all-to-all-done = f32[32,128,256]{2,1,0:T(8,128)} async-done(((f32[32,128,256]{2,1,0:T(8,128)}), f32[32,128,256]{2,1,0:T(8,128)}, u32[]{:S(2)}, u32[]{:S(2)}) %all-to-all-start) | async-done | bytes 4194336 | tf_op jit(solution)/shard_map/all_to_all | solution.py:207
  127.9 5.8 %multiply_reduce_fusion.5 = (f32[]{:T(128)}, f32[4,128,256]{2,0,1:T(4,128)S(1)}) fusion(f32[32,128,256]{2,1,0:T(8,128)} %all-to-all-done, s32[32]{0:T(128)S(1)} %dynamic-slice_reduce_fusion.blocks_ref), kind=kOutput, calls=%fused_computation.27 | convolution fusion | flops 25428096 | bytes 4718724 | tf_op jit(solution)/shard_map/cb,cpk->bpk/dot_general | solution.py:208
  133.7 0.9 copy.42
  134.6 16.0 %shard_map.68 = f32[32,16,256]{2,1,0:T(8,128)} custom-call(s32[32]{0:T(128)} %copy-done.9, f32[512,256]{1,0:T(8,128)} %bitcast.36, s32[32,256,1]{2,1,0:T(8,128)} %copy.45.points_ref, bf16[32,256,256]{2,1,0:T(8,128)(2,1)} %slice.9.weights_ref, f32[16,256]{1,0:T(8,128)} %bitcast.40), custom_call_target="tpu_custom_call" | custom-call | flops 2013265920 | bytes 4718592 | tf_op jit(solution)/shard_map/pallas_call | solution.py:84
  150.5 3.8 collective-permute-start.5
  154.3 0.7 collective-permute-start.3
  155.0 1.3 broadcast_in_dim.24
  156.3 9.0 %all-to-all-start.1 = ((f32[128,1,1]{2,1,0:T(1,128)}), f32[128,1,1]{2,1,0:T(1,128)S(1)}, u32[]{:S(2)}, u32[]{:S(2)}) async-start(f32[128,1,1]{2,1,0:T(1,128)} %broadcast_in_dim.24), calls=%async_computation.1 | async-start | bytes 131072 | tf_op jit(solution)/shard_map/all_to_all | solution.py:131
  165.3 11.5 %collective-permute-done.5 = f32[32,16,256]{2,1,0:T(8,128)S(1)} collective-permute-done((f32[32,16,256]{2,1,0:T(8,128)}, f32[32,16,256]{2,1,0:T(8,128)S(1)}, u32[]{:S(2)}, u32[]{:S(2)}) %collective-permute-start.5) | collective-permute-done | bytes 524320 | tf_op jit(solution)/shard_map/ppermute | solution.py:125
  176.9 4.3 %collective-permute-done.3 = f32[32,16,256]{2,1,0:T(8,128)S(1)} collective-permute-done((f32[32,16,256]{2,1,0:T(8,128)}, f32[32,16,256]{2,1,0:T(8,128)S(1)}, u32[]{:S(2)}, u32[]{:S(2)}) %collective-permute-start.3) | collective-permute-done | bytes 524320 | tf_op jit(solution)/shard_map/ppermute | solution.py:125
  181.2 2.0 add_add_fusion.2.amp_ref
  183.2 25.0 %shard_map.69 = f32[512,256]{1,0:T(8,128)} custom-call(s32[32]{0:T(128)} %copy-done.9, f32[512,256]{1,0:T(8,128)} %bitcast.37, s32[32,256,1]{2,1,0:T(8,128)} %copy.45.points_ref, s32[32,1,256]{2,1,0:T(1,128)} %get-tuple-element.8.rows_ref, bf16[32,256,256]{2,1,0:T(8,128)(2,1)} %slice.9.weights_ref, f32[32,16,256]{2,1,0:T(8,128)} %add_add_fusion.2.amp_ref, ...), custom_call_target="tpu_custom_call" | custom-call | flops 3623878656 | bytes 5242880 | tf_op jit(solution)/shard_map/pallas_call | solution.py:101
  208.2 1.8 multiply_reduce_fusion.4
  210.0 1.3 broadcast_in_dim.25
  211.3 6.6 %all-to-all-start.3 = ((f32[128,1,1]{2,1,0:T(1,128)}), f32[128,1,1]{2,1,0:T(1,128)S(1)}, u32[]{:S(2)}, u32[]{:S(2)}) async-start(f32[128,1,1]{2,1,0:T(1,128)} %broadcast_in_dim.25), calls=%async_computation.3 | async-start | bytes 131072 | tf_op jit(solution)/shard_map/all_to_all | solution.py:131
  217.9 0.8 reduce_sum.109
  218.7 8.8 %all-to-all-done.3 = f32[128,1,1]{2,1,0:T(1,128)S(1)} async-done(((f32[128,1,1]{2,1,0:T(1,128)}), f32[128,1,1]{2,1,0:T(1,128)S(1)}, u32[]{:S(2)}, u32[]{:S(2)}) %all-to-all-start.3) | async-done | bytes 544 | tf_op jit(solution)/shard_map/all_to_all | solution.py:131
  227.6 0.7 reduce_sum.111
  229.7 2.5 multiply_reduce_fusion.3
  232.2 16.0 %shard_map.70 = f32[32,16,256]{2,1,0:T(8,128)} custom-call(s32[32]{0:T(128)} %copy-done.9, f32[512,256]{1,0:T(8,128)} %get-tuple-element.7.field_ref, s32[32,256,1]{2,1,0:T(8,128)} %copy.45.points_ref, bf16[32,256,256]{2,1,0:T(8,128)(2,1)} %slice.9.weights_ref, f32[16,256]{1,0:T(8,128)} %bitcast.42), custom_call_target="tpu_custom_call" | custom-call | flops 2013265920 | bytes 4718592 | tf_op jit(solution)/shard_map/pallas_call | solution.py:84
  248.1 0.8 collective-permute-start.8
  248.9 1.8 collective-permute-start.7
  250.8 0.6 broadcast_in_dim.26
  251.4 25.3 %all_to_all.46 = f32[128,1,1]{2,1,0:T(1,128)S(1)} all-to-all(f32[128,1,1]{2,1,0:T(1,128)S(1)} %broadcast_in_dim.26), channel_id=1, replica_groups=mesh['tm'=32,'chan'=4] {'tm','chan'}, dimensions={0} | all-to-all | bytes 1024 | tf_op jit(solution)/shard_map/all_to_all | solution.py:131
  276.7 0.8 reduce_sum.113
  279.0 2.1 add_add_fusion.1.amp_ref
  281.1 25.0 %shard_map.71 = f32[512,256]{1,0:T(8,128)} custom-call(s32[32]{0:T(128)} %copy-done.9, f32[512,256]{1,0:T(8,128)} %get-tuple-element.7.field_ref, s32[32,256,1]{2,1,0:T(8,128)} %copy.45.points_ref, s32[32,1,256]{2,1,0:T(1,128)} %get-tuple-element.8.rows_ref, bf16[32,256,256]{2,1,0:T(8,128)(2,1)} %slice.9.weights_ref, f32[32,16,256]{2,1,0:T(8,128)} %add_add_fusion.1.amp_ref, ...), custom_call_target="tpu_custom_call" | custom-call | flops 3623878656 | bytes 5242880 | tf_op jit(solution)/shard_map/pallas_call | solution.py:101
  306.1 1.8 multiply_reduce_fusion.2
  307.9 0.7 broadcast_in_dim.27
  308.6 14.0 %all_to_all.47 = f32[128,1,1]{2,1,0:T(1,128)S(1)} all-to-all(f32[128,1,1]{2,1,0:T(1,128)S(1)} %broadcast_in_dim.27), channel_id=1, replica_groups=mesh['tm'=32,'chan'=4] {'tm','chan'}, dimensions={0} | all-to-all | bytes 1024 | tf_op jit(solution)/shard_map/all_to_all | solution.py:131
  322.6 0.7 reduce_sum.115
  324.7 1.5 multiply_reduce_fusion.1
  326.3 16.0 %shard_map.72 = f32[32,16,256]{2,1,0:T(8,128)} custom-call(s32[32]{0:T(128)} %copy-done.9, f32[512,256]{1,0:T(8,128)} %get-tuple-element.3.field_ref, s32[32,256,1]{2,1,0:T(8,128)} %copy.45.points_ref, bf16[32,256,256]{2,1,0:T(8,128)(2,1)} %slice.9.weights_ref, f32[16,256]{1,0:T(8,128)} %bitcast.44), custom_call_target="tpu_custom_call" | custom-call | flops 2013265920 | bytes 4718592 | tf_op jit(solution)/shard_map/pallas_call | solution.py:84
  342.2 0.8 collective-permute-start.11
  343.0 1.6 collective-permute-start.10
  344.6 0.7 broadcast_in_dim.28
  345.3 25.3 %all_to_all.48 = f32[128,1,1]{2,1,0:T(1,128)S(1)} all-to-all(f32[128,1,1]{2,1,0:T(1,128)S(1)} %broadcast_in_dim.28), channel_id=1, replica_groups=mesh['tm'=32,'chan'=4] {'tm','chan'}, dimensions={0} | all-to-all | bytes 1024 | tf_op jit(solution)/shard_map/all_to_all | solution.py:131
  370.6 0.8 reduce_sum.117
  372.9 2.1 add_add_fusion.amp_ref
  374.9 25.0 %shard_map.73 = f32[512,256]{1,0:T(8,128)} custom-call(s32[32]{0:T(128)} %copy-done.9, f32[512,256]{1,0:T(8,128)} %get-tuple-element.3.field_ref, s32[32,256,1]{2,1,0:T(8,128)} %copy.45.points_ref, s32[32,1,256]{2,1,0:T(1,128)} %get-tuple-element.8.rows_ref, bf16[32,256,256]{2,1,0:T(8,128)(2,1)} %slice.9.weights_ref, f32[32,16,256]{2,1,0:T(8,128)} %add_add_fusion.amp_ref, ...), custom_call_target="tpu_custom_call" | custom-call | flops 3623878656 | bytes 5242880 | tf_op jit(solution)/shard_map/pallas_call | solution.py:101
  399.9 1.8 multiply_reduce_fusion
  401.7 0.7 broadcast_in_dim.29
  402.4 14.0 %all_to_all.49 = f32[128,1,1]{2,1,0:T(1,128)S(1)} all-to-all(f32[128,1,1]{2,1,0:T(1,128)S(1)} %broadcast_in_dim.29), channel_id=1, replica_groups=mesh['tm'=32,'chan'=4] {'tm','chan'}, dimensions={0} | all-to-all | bytes 1024 | tf_op jit(solution)/shard_map/all_to_all | solution.py:131
  416.3 0.7 reduce_sum.119
  418.5 2.2 multiply_subtract_fusion
  (32 shorter events, 0.1 us)
Async XLA Ops:
  0.6 75.3 %copy-start = (s32[32,32]{1,0:T(8,128)S(1)}, s32[32,32]{1,0:T(8,128)}, u32[]{:S(2)}) copy-start(s32[32,32]{1,0:T(8,128)} %param.8) | copy-start | bytes 12292
  6.0 8.8 %copy-start.7 = (f32[256,16]{0,1:T(8,128)S(1)}, f32[256,16]{0,1:T(8,128)}, u32[]{:S(2)}) copy-start(f32[256,16]{0,1:T(8,128)} %param.9) | copy-start | bytes 49156
  6.0 62.4 %all-to-all-start.2 = ((bf16[32,257,256]{2,1,0:T(8,128)(2,1)}), bf16[32,257,256]{2,1,0:T(8,128)(2,1)}, u32[]{:S(2)}, u32[]{:S(2)}) async-start(bf16[32,257,256]{2,1,0:T(8,128)(2,1)} %pad_maximum_fusion), calls=%async_computation.2 | async-start | bytes 8650752 | tf_op jit(solution)/shard_map/all_to_all | solution.py:148
  14.7 14.8 %copy-start.8 = (s32[8192]{0:T(1024)S(1)}, s32[8192]{0:T(1024)}, u32[]{:S(2)}) copy-start(s32[8192]{0:T(1024)} %param.7) | copy-start | bytes 98308
  24.9 26.0 %collective-permute-start.2 = (f32[16,32,256]{2,0,1:T(8,128)S(1)}, f32[16,32,256]{2,0,1:T(8,128)S(1)}, u32[]{:S(2)}, u32[]{:S(2)}) collective-permute-start(f32[16,32,256]{2,0,1:T(8,128)S(1)} %fusion.6), channel_id=1, source_target_pairs={{0,3},{1,0},{2,1},{3,2},{4,7},{5,4},{6,5},{7,6},{8,11},{9,8},{10,9... | collective-permute-start | bytes 1572872 | tf_op jit(solution)/shard_map/ppermute | solution.py:125
  28.7 22.2 %collective-permute-start.1 = (f32[16,32,256]{2,0,1:T(8,128)S(1)}, f32[16,32,256]{2,0,1:T(8,128)S(1)}, u32[]{:S(2)}, u32[]{:S(2)}) collective-permute-start(f32[16,32,256]{2,0,1:T(8,128)S(1)} %fusion.6), channel_id=1, source_target_pairs={{0,2},{1,3},{2,0},{3,1},{4,6},{5,7},{6,4},{7,5},{8,10},{9,11},{10,... | collective-permute-start | bytes 1572872 | tf_op jit(solution)/shard_map/ppermute | solution.py:125
  28.7 26.4 %collective-permute-start = (f32[16,32,256]{2,0,1:T(8,128)S(1)}, f32[16,32,256]{2,0,1:T(8,128)S(1)}, u32[]{:S(2)}, u32[]{:S(2)}) collective-permute-start(f32[16,32,256]{2,0,1:T(8,128)S(1)} %fusion.6), channel_id=1, source_target_pairs={{0,1},{1,2},{2,3},{3,0},{4,5},{5,6},{6,7},{7,4},{8,9},{9,10},{10,1... | collective-permute-start | bytes 1572872 | tf_op jit(solution)/shard_map/ppermute | solution.py:125
  29.6 32.6 %copy-start.1 = (bf16[8192,256]{1,0:T(8,128)(2,1)S(1)}, bf16[8192,256]{1,0:T(8,128)(2,1)}, u32[]{:S(2)}) copy-start(bf16[8192,256]{1,0:T(8,128)(2,1)} %param.6) | copy-start | bytes 12582916
  29.6 32.6 %copy-start.4 = (bf16[8192,256]{1,0:T(8,128)(2,1)S(1)}, bf16[8192,256]{1,0:T(8,128)(2,1)}, u32[]{:S(2)}) copy-start(bf16[8192,256]{1,0:T(8,128)(2,1)} %param.5) | copy-start | bytes 12582916
  68.4 59.5 %all-to-all-start = ((f32[32,128,256]{2,1,0:T(8,128)}), f32[32,128,256]{2,1,0:T(8,128)}, u32[]{:S(2)}, u32[]{:S(2)}) async-start(f32[32,128,256]{2,1,0:T(8,128)} %fusion), calls=%async_computation | async-start | bytes 8388608 | tf_op jit(solution)/shard_map/all_to_all | solution.py:207
  76.1 51.7 %copy-start.9 = (s32[32]{0:T(128)}, s32[32]{0:T(128)S(1)}, u32[]{:S(2)}) copy-start(s32[32]{0:T(128)S(1)} %dynamic-slice_reduce_fusion.blocks_ref) | copy-start | bytes 388
  150.5 26.4 %collective-permute-start.5 = (f32[32,16,256]{2,1,0:T(8,128)}, f32[32,16,256]{2,1,0:T(8,128)S(1)}, u32[]{:S(2)}, u32[]{:S(2)}) collective-permute-start(f32[32,16,256]{2,1,0:T(8,128)} %shard_map.68), channel_id=1, source_target_pairs={{0,3},{1,0},{2,1},{3,2},{4,7},{5,4},{6,5},{7,6},{8,11},{9,8},{10,9... | collective-permute-start | bytes 1572872 | tf_op jit(solution)/shard_map/ppermute | solution.py:125
  154.3 22.6 %collective-permute-start.4 = (f32[32,16,256]{2,1,0:T(8,128)}, f32[32,16,256]{2,1,0:T(8,128)S(1)}, u32[]{:S(2)}, u32[]{:S(2)}) collective-permute-start(f32[32,16,256]{2,1,0:T(8,128)} %shard_map.68), channel_id=1, source_target_pairs={{0,2},{1,3},{2,0},{3,1},{4,6},{5,7},{6,4},{7,5},{8,10},{9,11},{10,... | collective-permute-start | bytes 1572872 | tf_op jit(solution)/shard_map/ppermute | solution.py:125
  154.3 26.9 %collective-permute-start.3 = (f32[32,16,256]{2,1,0:T(8,128)}, f32[32,16,256]{2,1,0:T(8,128)S(1)}, u32[]{:S(2)}, u32[]{:S(2)}) collective-permute-start(f32[32,16,256]{2,1,0:T(8,128)} %shard_map.68), channel_id=1, source_target_pairs={{0,1},{1,2},{2,3},{3,0},{4,5},{5,6},{6,7},{7,4},{8,9},{9,10},{10,1... | collective-permute-start | bytes 1572872 | tf_op jit(solution)/shard_map/ppermute | solution.py:125
  156.3 53.7 %all-to-all-start.1 = ((f32[128,1,1]{2,1,0:T(1,128)}), f32[128,1,1]{2,1,0:T(1,128)S(1)}, u32[]{:S(2)}, u32[]{:S(2)}) async-start(f32[128,1,1]{2,1,0:T(1,128)} %broadcast_in_dim.24), calls=%async_computation.1 | async-start | bytes 131072 | tf_op jit(solution)/shard_map/all_to_all | solution.py:131
  183.2 25.0 %copy-start.2 = (f32[4,128,256]{2,1,0:T(8,128)S(1)}, f32[4,128,256]{2,1,0:T(8,128)}, u32[]{:S(2)}) copy-start(f32[4,128,256]{2,1,0:T(8,128)} %copy.42) | copy-start | bytes 1572868
  211.3 16.3 %all-to-all-start.3 = ((f32[128,1,1]{2,1,0:T(1,128)}), f32[128,1,1]{2,1,0:T(1,128)S(1)}, u32[]{:S(2)}, u32[]{:S(2)}) async-start(f32[128,1,1]{2,1,0:T(1,128)} %broadcast_in_dim.25), calls=%async_computation.3 | async-start | bytes 131072 | tf_op jit(solution)/shard_map/all_to_all | solution.py:131
  248.1 30.8 %collective-permute-start.8 = (f32[32,16,256]{2,1,0:T(8,128)}, f32[32,16,256]{2,1,0:T(8,128)S(1)}, u32[]{:S(2)}, u32[]{:S(2)}) collective-permute-start(f32[32,16,256]{2,1,0:T(8,128)} %shard_map.70), channel_id=1, source_target_pairs={{0,3},{1,0},{2,1},{3,2},{4,7},{5,4},{6,5},{7,6},{8,11},{9,8},{10,9... | collective-permute-start | bytes 1572872 | tf_op jit(solution)/shard_map/ppermute | solution.py:125
  248.9 30.1 %collective-permute-start.7 = (f32[32,16,256]{2,1,0:T(8,128)}, f32[32,16,256]{2,1,0:T(8,128)S(1)}, u32[]{:S(2)}, u32[]{:S(2)}) collective-permute-start(f32[32,16,256]{2,1,0:T(8,128)} %shard_map.70), channel_id=1, source_target_pairs={{0,2},{1,3},{2,0},{3,1},{4,6},{5,7},{6,4},{7,5},{8,10},{9,11},{10,... | collective-permute-start | bytes 1572872 | tf_op jit(solution)/shard_map/ppermute | solution.py:125
  250.8 28.2 %collective-permute-start.6 = (f32[32,16,256]{2,1,0:T(8,128)}, f32[32,16,256]{2,1,0:T(8,128)S(1)}, u32[]{:S(2)}, u32[]{:S(2)}) collective-permute-start(f32[32,16,256]{2,1,0:T(8,128)} %shard_map.70), channel_id=1, source_target_pairs={{0,1},{1,2},{2,3},{3,0},{4,5},{5,6},{6,7},{7,4},{8,9},{9,10},{10,1... | collective-permute-start | bytes 1572872 | tf_op jit(solution)/shard_map/ppermute | solution.py:125
  281.1 25.0 %copy-start.3 = (f32[512,256]{1,0:T(8,128)S(1)}, f32[512,256]{1,0:T(8,128)}, u32[]{:S(2)}) copy-start(f32[512,256]{1,0:T(8,128)} %get-tuple-element.7.field_ref) | copy-start | bytes 1572868
  281.1 25.0 %copy-start.6 = (f32[512,256]{1,0:T(8,128)S(1)}, f32[512,256]{1,0:T(8,128)}, u32[]{:S(2)}) copy-start(f32[512,256]{1,0:T(8,128)} %shard_map.69) | copy-start | bytes 1572868
  342.2 30.6 %collective-permute-start.11 = (f32[32,16,256]{2,1,0:T(8,128)}, f32[32,16,256]{2,1,0:T(8,128)S(1)}, u32[]{:S(2)}, u32[]{:S(2)}) collective-permute-start(f32[32,16,256]{2,1,0:T(8,128)} %shard_map.72), channel_id=1, source_target_pairs={{0,3},{1,0},{2,1},{3,2},{4,7},{5,4},{6,5},{7,6},{8,11},{9,8},{10,9... | collective-permute-start | bytes 1572872 | tf_op jit(solution)/shard_map/ppermute | solution.py:125
  343.0 29.8 %collective-permute-start.10 = (f32[32,16,256]{2,1,0:T(8,128)}, f32[32,16,256]{2,1,0:T(8,128)S(1)}, u32[]{:S(2)}, u32[]{:S(2)}) collective-permute-start(f32[32,16,256]{2,1,0:T(8,128)} %shard_map.72), channel_id=1, source_target_pairs={{0,2},{1,3},{2,0},{3,1},{4,6},{5,7},{6,4},{7,5},{8,10},{9,11},{10,... | collective-permute-start | bytes 1572872 | tf_op jit(solution)/shard_map/ppermute | solution.py:125
  344.6 28.3 %collective-permute-start.9 = (f32[32,16,256]{2,1,0:T(8,128)}, f32[32,16,256]{2,1,0:T(8,128)S(1)}, u32[]{:S(2)}, u32[]{:S(2)}) collective-permute-start(f32[32,16,256]{2,1,0:T(8,128)} %shard_map.72), channel_id=1, source_target_pairs={{0,1},{1,2},{2,3},{3,0},{4,5},{5,6},{6,7},{7,4},{8,9},{9,10},{10,1... | collective-permute-start | bytes 1572872 | tf_op jit(solution)/shard_map/ppermute | solution.py:125
  374.9 25.0 %copy-start.5 = (f32[512,256]{1,0:T(8,128)S(1)}, f32[512,256]{1,0:T(8,128)}, u32[]{:S(2)}) copy-start(f32[512,256]{1,0:T(8,128)} %get-tuple-element.3.field_ref) | copy-start | bytes 1572868

commit v6 on v5

--- a/solution.py
+++ b/solution.py
@@ -18,25 +18,19 @@
 RUNS = 4
 
 
-def gathered(field_ref, block, points):
+def gathered(parts_ref, block, hits):
     start = pl.multiple_of(block * BLK, BLK)
-    rest = field_ref[pl.ds(start, BLK), :]
-    hits = (points == lax.broadcasted_iota(jnp.int32, (points.shape[0], BLK), 1)).astype(
-        jnp.bfloat16
-    )
     total = None
-    for _ in range(3):
-        part = rest.astype(jnp.bfloat16)
-        rest = rest - part.astype(jnp.float32)
-        term = jnp.dot(hits, part, preferred_element_type=jnp.float32)
+    for k in range(3):
+        term = jnp.dot(hits, parts_ref[k, pl.ds(start, BLK), :], preferred_element_type=jnp.float32)
         total = term if total is None else total + term
     return total
 
 
-def amp_kernel(blocks_ref, field_ref, points_ref, weights_ref, modes_t_ref, amp_ref):
+def amp_kernel(blocks_ref, parts_ref, hits_ref, weights_ref, modes_t_ref, amp_ref):
     step = pl.program_id(0)
     for j in range(RUNS):
-        x = gathered(field_ref, blocks_ref[step * RUNS + j], points_ref[j])
+        x = gathered(parts_ref, blocks_ref[step * RUNS + j], hits_ref[j])
         y = weights_ref[j].astype(jnp.float32) * x
         amp_ref[j] = lax.dot_general(
             modes_t_ref[...], y, (((1,), (1,)), ((), ())),
@@ -44,7 +38,7 @@
         )
 
 
-def bin_kernel(blocks_ref, field_ref, points_ref, rows_ref, weights_ref, amp_ref, modes_t_ref, out_ref):
+def bin_kernel(blocks_ref, parts_ref, hits_ref, rows_ref, weights_ref, amp_ref, modes_t_ref, out_ref):
     step = pl.program_id(0)
 
     @pl.when(step == 0)
@@ -53,32 +47,37 @@
 
     for j in range(RUNS):
         block = blocks_ref[step * RUNS + j]
-        x = gathered(field_ref, block, points_ref[j])
+        x = gathered(parts_ref, block, hits_ref[j])
         w = weights_ref[j].astype(jnp.float32)
-        y = w * x
         correction = lax.dot_general(
             amp_ref[j], modes_t_ref[...], (((0,), (0,)), ((), ())),
             precision=highest, preferred_element_type=jnp.float32,
         )
-        rest = w * (y - correction)
+        rest = w * (w * x - correction)
         hits = (rows_ref[j] == lax.broadcasted_iota(jnp.int32, (BLK, rest.shape[0]), 0)).astype(
             jnp.bfloat16
         )
-        total = None
-        for _ in range(3):
-            part = rest.astype(jnp.bfloat16)
-            rest = rest - part.astype(jnp.float32)
-            term = jnp.dot(hits, part, preferred_element_type=jnp.float32)
-            total = term if total is None else total + term
+        high_part = rest.astype(jnp.bfloat16)
+        low_part = (rest - high_part.astype(jnp.float32)).astype(jnp.bfloat16)
+        total = jnp.dot(hits, high_part, preferred_element_type=jnp.float32) + jnp.dot(
+            hits, low_part, preferred_element_type=jnp.float32
+        )
         start = pl.multiple_of(block * BLK, BLK)
         out_ref[pl.ds(start, BLK), :] += total
 
 
-def owner_operator(blocks, field, points_col, points_row, noise_weights, modes_t):
+def owner_operator(blocks, field, hits, points_row, noise_weights, modes_t):
     groups, run_length, channels = noise_weights.shape
     modes = modes_t.shape[0]
     steps = groups // RUNS
-    full = pl.BlockSpec(field.shape, lambda i, b: (0, 0))
+    parts = []
+    rest = field
+    for _ in range(3):
+        rounded = lax.reduce_precision(rest, exponent_bits=8, mantissa_bits=7)
+        parts.append(rounded.astype(jnp.bfloat16))
+        rest = rest - rounded
+    parts = jnp.stack(parts)
+    full = pl.BlockSpec(parts.shape, lambda i, b: (0, 0, 0))
     per_run = lambda *shape: pl.BlockSpec((RUNS,) + shape, lambda i, b: (i, 0, 0))
     gather_flops = groups * 3 * 2 * run_length * BLK * channels
     amps = pl.pallas_call(
@@ -86,7 +85,7 @@
         grid_spec=pltpu.PrefetchScalarGridSpec(
             num_scalar_prefetch=1,
             grid=(steps,),
-            in_specs=[full, per_run(run_length, 1), per_run(run_length, channels),
+            in_specs=[full, per_run(run_length, BLK), per_run(run_length, channels),
                       pl.BlockSpec(modes_t.shape, lambda i, b: (0, 0))],
             out_specs=per_run(modes, run_length),
         ),
@@ -96,17 +95,17 @@
             bytes_accessed=noise_weights.size * 2 + field.size * 4,
             transcendentals=0,
         ),
-    )(blocks, field, points_col, noise_weights, modes_t)
+    )(blocks, parts, hits, noise_weights, modes_t)
     amps = chan_sum(amps)
     return pl.pallas_call(
         bin_kernel,
         grid_spec=pltpu.PrefetchScalarGridSpec(
             num_scalar_prefetch=1,
             grid=(steps,),
-            in_specs=[full, per_run(run_length, 1), per_run(1, run_length),
+            in_specs=[full, per_run(run_length, BLK), per_run(1, run_length),
                       per_run(run_length, channels), per_run(modes, run_length),
                       pl.BlockSpec(modes_t.shape, lambda i, b: (0, 0))],
-            out_specs=full,
+            out_specs=pl.BlockSpec(field.shape, lambda i, b: (0, 0)),
         ),
         out_shape=jax.ShapeDtypeStruct(field.shape, jnp.float32),
         cost_estimate=pl.CostEstimate(
@@ -114,7 +113,7 @@
             bytes_accessed=noise_weights.size * 2 + field.size * 8,
             transcendentals=0,
         ),
-    )(blocks, field, points_col, points_row, noise_weights, amps, modes_t)
+    )(blocks, parts, hits, points_row, noise_weights, amps, modes_t)
 
 
 def chan_sum(value):
@@ -186,13 +185,15 @@
     def squares(vector):
         return global_sum(jnp.sum(vector * vector))
 
-    points_col = points_in[:, :, None]
+    point_hits = (points_in[:, :, None] == jnp.arange(BLK, dtype=jnp.int32)[None, None, :]).astype(
+        jnp.bfloat16
+    )
     points_row = points_in[:, None, :]
     modes_t = foreground_modes.T
 
     def operate(field):
         return (
-            owner_operator(column, field, points_col, points_row, weights_in, modes_t)
+            owner_operator(column, field, point_hits, points_row, weights_in, modes_t)
             + ridge * field
         )
 

time: 427 us -> 424 us (level)
  starting transfers between devices: 46 us -> 50.7 us
    ppermute x12, waiting for transfers between devices: 41.4 us -> 35.7 us  [chan_sum(): total = total + lax.ppermute(value, 'chan', pairs)]
where the time goes in v6:
time: 424 us; the launch traced here: 419 us
  Pallas kernels  121 us (29%)
  waiting for transfers between devices  90.8 us (21%)
  blocking collectives  76.6 us (18%)
  starting transfers between devices  50.7 us (12%)
  other arithmetic  33.3 us (8%)
  matrix products  28.5 us (7%)
  local copies, waits for them, and re-layouts  10.2 us (2%)
  between operations  7.9 us (2%)
    all_to_all x4, blocking collectives, global_sum(): lax.all_to_all(jnp.broadcast_to(value, (everyone, 1)), ('tm', 'chan'), 0,...  76.6 us
    pallas_call x3, Pallas kernels, owner_operator(): pl.pallas_call(bin_kernel, grid_spec=pltpu.PrefetchScalarGridSpec(num_sca...  74.6 us
    pallas_call x3, Pallas kernels, owner_operator(): pl.pallas_call(amp_kernel, grid_spec=pltpu.PrefetchScalarGridSpec(num_sca...  46.5 us
    all_to_all x1, waiting for transfers between devices, per_device(): arrived = lax.all_to_all(local_partial, 'tm', 0, 0, tiled=True)  43.5 us
    ppermute x12, waiting for transfers between devices, chan_sum(): total = total + lax.ppermute(value, 'chan', pairs)  35.7 us
    ppermute x12, starting transfers between devices, chan_sum(): total = total + lax.ppermute(value, 'chan', pairs)  17.9 us
    all_to_all x2, starting transfers between devices, global_sum(): lax.all_to_all(jnp.broadcast_to(value, (everyone, 1)), ('tm', 'chan'), 0,...  16.5 us
    dot_general x1, matrix products, filtered(): jnp.einsum('csk,km->mcs', weighted, foreground_modes, precision=highest)  10.2 us
  transfers between devices with their start and end apart: 16, of which 7 were waited for; matrix products, arithmetic and copies ran while one was open for 10% of the time, Pallas kernels for 6%

profile of v6, /device:TPU:1, one launch (start us, length us, event | category | flops | bytes accessed | tf_op | source)
XLA Modules:
  0.0 419.1 jit_solution(2432286781869934709)
XLA Ops:
  0.6 0.8 convert_element_type.87
  1.4 4.5 %pad_maximum_fusion = bf16[32,257,256]{2,1,0:T(8,128)(2,1)} fusion(bf16[32,1,256]{2,1,0:T(2,128)(2,1)S(1)} %convert_element_type.100, bf16[32,256,256]{2,1,0:T(8,128)(2,1)} %bitcast.67), kind=kLoop, calls=%fused_computation.5 | loop fusion | flops 8421376 | bytes 8421376 | tf_op jit(solution)/shard_map/concatenate | solution.py:146
  6.0 8.8 %all-to-all-start.2 = ((bf16[32,257,256]{2,1,0:T(8,128)(2,1)}), bf16[32,257,256]{2,1,0:T(8,128)(2,1)}, u32[]{:S(2)}, u32[]{:S(2)}) async-start(bf16[32,257,256]{2,1,0:T(8,128)(2,1)} %pad_maximum_fusion), calls=%async_computation.2 | async-start | bytes 8650752 | tf_op jit(solution)/shard_map/all_to_all | solution.py:147
  14.7 10.2 %fusion.7 = f32[16,32,256]{2,0,1:T(8,128)S(1)} fusion(bf16[32,256,256]{2,1,0:T(8,128)(2,1)} %bitcast.68, bf16[32,256,256]{2,1,0:T(8,128)(2,1)} %bitcast.71, f32[256,16]{0,1:T(8,128)S(1)} %copy-done.4), kind=kOutput, calls=%fused_computation.12 | convolution fusion | flops 408944640 | bytes 8929280 | tf_op jit(solution)/shard_map/csk,km->mcs/dot_general | solution.py:165
  24.9 1.7 collective-permute-start
  26.6 3.3 collective-permute-start.1
  29.9 0.9 collective-permute-start.2
  30.8 10.0 %collective-permute-done = f32[16,32,256]{2,0,1:T(8,128)S(1)} collective-permute-done((f32[16,32,256]{2,0,1:T(8,128)S(1)}, f32[16,32,256]{2,0,1:T(8,128)S(1)}, u32[]{:S(2)}, u32[]{:S(2)}) %collective-permute-start) | collective-permute-done | bytes 524320 | tf_op jit(solution)/shard_map/ppermute | solution.py:124
  40.8 12.1 %collective-permute-done.1 = f32[16,32,256]{2,0,1:T(8,128)S(1)} collective-permute-done((f32[16,32,256]{2,0,1:T(8,128)S(1)}, f32[16,32,256]{2,0,1:T(8,128)S(1)}, u32[]{:S(2)}, u32[]{:S(2)}) %collective-permute-start.1) | collective-permute-done | bytes 524320 | tf_op jit(solution)/shard_map/ppermute | solution.py:124
  53.0 7.1 %fusion.18 = f32[32,256,256]{2,1,0:T(8,128)S(1)} fusion(f32[16,32,256]{2,0,1:T(8,128)S(1)} %collective-permute-done.2, f32[16,32,256]{2,0,1:T(8,128)S(1)} %collective-permute-done.1, f32[16,32,256]{2,0,1:T(8,128)S(1)} %fusion.7, f32[16,32,256]{2,0,1:T(8,128)S(1)} %collective-permute-done, f32[256,16]{0,1:T(8,128)S(1)} %copy-done.4), kind=kOutput, calls=%fused_computation.56 | convolution fusion | flops 403046400 | bytes 10502144 | tf_op jit(solution)/shard_map/mcs,km->csk/dot_general | solution.py:168
  60.1 5.5 %fusion = f32[32,128,256]{2,1,0:T(8,128)} fusion(bf16[32,256,256]{2,1,0:T(8,128)(2,1)S(1)} %bitcast.69, f32[32,256,256]{2,1,0:T(8,128)S(1)} %fusion.18, bf16[32,256,256]{2,1,0:T(8,128)(2,1)S(1)} %bitcast.72, s32[32,256]{1,0:T(8,128)S(1)} %eq.47), kind=kOutput, calls=%fused_computation.2 | convolution fusion | flops 1622147072 | bytes 21004288 | tf_op jit(solution)/shard_map/csp,csk->cpk/dot_general | solution.py:207
  65.6 2.8 all-to-all-done.2
  68.4 7.6 %all-to-all-start = ((f32[32,128,256]{2,1,0:T(8,128)}), f32[32,128,256]{2,1,0:T(8,128)}, u32[]{:S(2)}, u32[]{:S(2)}) async-start(f32[32,128,256]{2,1,0:T(8,128)} %fusion), calls=%async_computation | async-start | bytes 8388608 | tf_op jit(solution)/shard_map/all_to_all | solution.py:208
  76.2 0.9 slice_convert_fusion.rows_ref
  77.1 4.6 %slice.9.weights_ref = bf16[32,256,256]{2,1,0:T(8,128)(2,1)} slice(bf16[32,257,256]{2,1,0:T(8,128)(2,1)} %all-to-all-done.2), slice={[0:32], [0:256], [0:256]} | slice | bytes 8388608 | tf_op jit(solution)/shard_map/slice | solution.py:148
  81.7 2.6 fusion.5.hits_ref
  84.4 43.5 %all-to-all-done = f32[32,128,256]{2,1,0:T(8,128)} async-done(((f32[32,128,256]{2,1,0:T(8,128)}), f32[32,128,256]{2,1,0:T(8,128)}, u32[]{:S(2)}, u32[]{:S(2)}) %all-to-all-start) | async-done | bytes 4194336 | tf_op jit(solution)/shard_map/all_to_all | solution.py:208
  127.9 5.7 %multiply_reduce_fusion.4 = (f32[]{:T(128)}, f32[4,128,256]{2,0,1:T(4,128)S(1)}) fusion(f32[32,128,256]{2,1,0:T(8,128)} %all-to-all-done, s32[32]{0:T(128)S(1)} %dynamic-slice_reduce_fusion.blocks_ref), kind=kOutput, calls=%fused_computation.55 | convolution fusion | flops 25428096 | bytes 4718724 | tf_op jit(solution)/shard_map/cb,cpk->bpk/dot_general | solution.py:209
  133.8 1.0 pad_maximum_fusion.1.parts_ref
  134.8 15.5 %shard_map.68 = f32[32,16,256]{2,1,0:T(8,128)} custom-call(s32[32]{0:T(128)} %copy-done.7, bf16[3,512,256]{2,1,0:T(8,128)(2,1)} %pad_maximum_fusion.1.parts_ref, bf16[32,256,128]{2,1,0:T(8,128)(2,1)} %fusion.5.hits_ref, bf16[32,256,256]{2,1,0:T(8,128)(2,1)} %slice.9.weights_ref, f32[16,256]{1,0:T(8,128)} %bitcast.73), custom_call_target="tpu_custom_call" | custom-call | flops 2013265920 | bytes 4718592 | tf_op jit(solution)/shard_map/pallas_call | solution.py:83
  150.3 1.6 collective-permute-start.3
  152.0 3.3 collective-permute-start.4
  155.3 0.7 collective-permute-start.5
  156.0 1.3 broadcast_in_dim.12
  157.3 7.7 %all-to-all-start.1 = ((f32[128,1,1]{2,1,0:T(1,128)}), f32[128,1,1]{2,1,0:T(1,128)S(1)}, u32[]{:S(2)}, u32[]{:S(2)}) async-start(f32[128,1,1]{2,1,0:T(1,128)} %broadcast_in_dim.12), calls=%async_computation.1 | async-start | bytes 131072 | tf_op jit(solution)/shard_map/all_to_all | solution.py:130
  165.0 0.8 collective-permute-done.3
  165.8 12.8 %collective-permute-done.4 = f32[32,16,256]{2,1,0:T(8,128)S(1)} collective-permute-done((f32[32,16,256]{2,1,0:T(8,128)}, f32[32,16,256]{2,1,0:T(8,128)S(1)}, u32[]{:S(2)}, u32[]{:S(2)}) %collective-permute-start.4) | collective-permute-done | bytes 524320 | tf_op jit(solution)/shard_map/ppermute | solution.py:124
  178.6 2.0 add_add_fusion.2.amp_ref
  180.7 24.8 %shard_map.69 = f32[512,256]{1,0:T(8,128)} custom-call(s32[32]{0:T(128)} %copy-done.7, bf16[3,512,256]{2,1,0:T(8,128)(2,1)} %pad_maximum_fusion.1.parts_ref, bf16[32,256,128]{2,1,0:T(8,128)(2,1)} %fusion.5.hits_ref, s32[32,1,256]{2,1,0:T(1,128)} %copy-done.6, bf16[32,256,256]{2,1,0:T(8,128)(2,1)} %slice.9.weights_ref, f32[32,16,256]{2,1,0:T(8,128)} %add_add_fusion.2.amp_ref, ...), custom_call_target="tpu_custom_call" | custom-call | flops 3623878656 | bytes 5242880 | tf_op jit(solution)/shard_map/pallas_call | solution.py:100
  205.5 1.8 fusion.14
  207.3 1.3 broadcast_in_dim.26
  208.6 8.8 %all-to-all-start.3 = ((f32[128,1,1]{2,1,0:T(1,128)}), f32[128,1,1]{2,1,0:T(1,128)S(1)}, u32[]{:S(2)}, u32[]{:S(2)}) async-start(f32[128,1,1]{2,1,0:T(1,128)} %broadcast_in_dim.26), calls=%async_computation.3 | async-start | bytes 131072 | tf_op jit(solution)/shard_map/all_to_all | solution.py:130
  217.4 0.8 reduce_sum.109
  218.2 8.8 %all-to-all-done.3 = f32[128,1,1]{2,1,0:T(1,128)S(1)} async-done(((f32[128,1,1]{2,1,0:T(1,128)}), f32[128,1,1]{2,1,0:T(1,128)S(1)}, u32[]{:S(2)}, u32[]{:S(2)}) %all-to-all-start.3) | async-done | bytes 544 | tf_op jit(solution)/shard_map/all_to_all | solution.py:130
  227.0 0.7 reduce_sum.111
  229.1 1.8 multiply_reduce_fusion.3
  231.0 1.0 pad_maximum_fusion.2.parts_ref
  232.0 15.5 %shard_map.70 = f32[32,16,256]{2,1,0:T(8,128)} custom-call(s32[32]{0:T(128)} %copy-done.7, bf16[3,512,256]{2,1,0:T(8,128)(2,1)} %pad_maximum_fusion.2.parts_ref, bf16[32,256,128]{2,1,0:T(8,128)(2,1)} %fusion.5.hits_ref, bf16[32,256,256]{2,1,0:T(8,128)(2,1)} %slice.9.weights_ref, f32[16,256]{1,0:T(8,128)} %bitcast.75), custom_call_target="tpu_custom_call" | custom-call | flops 2013265920 | bytes 4718592 | tf_op jit(solution)/shard_map/pallas_call | solution.py:83
  247.5 0.8 collective-permute-start.6
  248.3 1.4 collective-permute-start.7
  249.7 1.2 collective-permute-start.8
  251.5 24.2 %all_to_all.46 = f32[128,1,1]{2,1,0:T(1,128)S(1)} all-to-all(f32[128,1,1]{2,1,0:T(1,128)S(1)} %broadcast_in_dim.27), channel_id=1, replica_groups=mesh['tm'=32,'chan'=4] {'tm','chan'}, dimensions={0} | all-to-all | bytes 1024 | tf_op jit(solution)/shard_map/all_to_all | solution.py:130
  275.7 0.7 reduce_sum.113
  277.7 2.1 add_add_fusion.1.amp_ref
  279.8 25.0 %shard_map.71 = f32[512,256]{1,0:T(8,128)} custom-call(s32[32]{0:T(128)} %copy-done.7, bf16[3,512,256]{2,1,0:T(8,128)(2,1)} %pad_maximum_fusion.2.parts_ref, bf16[32,256,128]{2,1,0:T(8,128)(2,1)} %fusion.5.hits_ref, s32[32,1,256]{2,1,0:T(1,128)} %copy-done.6, bf16[32,256,256]{2,1,0:T(8,128)(2,1)} %slice.9.weights_ref, f32[32,16,256]{2,1,0:T(8,128)} %add_add_fusion.1.amp_ref, ...), custom_call_target="tpu_custom_call" | custom-call | flops 3623878656 | bytes 5242880 | tf_op jit(solution)/shard_map/pallas_call | solution.py:100
  304.7 1.8 multiply_reduce_fusion.2
  306.5 0.7 broadcast_in_dim.28
  307.2 14.8 %all_to_all.47 = f32[128,1,1]{2,1,0:T(1,128)S(1)} all-to-all(f32[128,1,1]{2,1,0:T(1,128)S(1)} %broadcast_in_dim.28), channel_id=1, replica_groups=mesh['tm'=32,'chan'=4] {'tm','chan'}, dimensions={0} | all-to-all | bytes 1024 | tf_op jit(solution)/shard_map/all_to_all | solution.py:130
  322.0 0.7 reduce_sum.115
  324.1 0.7 fusion.27
  324.8 1.0 pad_maximum_fusion.3.parts_ref
  325.8 15.5 %shard_map.72 = f32[32,16,256]{2,1,0:T(8,128)} custom-call(s32[32]{0:T(128)} %copy-done.7, bf16[3,512,256]{2,1,0:T(8,128)(2,1)} %pad_maximum_fusion.3.parts_ref, bf16[32,256,128]{2,1,0:T(8,128)(2,1)} %fusion.5.hits_ref, bf16[32,256,256]{2,1,0:T(8,128)(2,1)} %slice.9.weights_ref, f32[16,256]{1,0:T(8,128)} %bitcast.77), custom_call_target="tpu_custom_call" | custom-call | flops 2013265920 | bytes 4718592 | tf_op jit(solution)/shard_map/pallas_call | solution.py:83
  341.3 1.1 collective-permute-start.10
  342.4 1.9 collective-permute-start.11
  344.3 0.7 broadcast_in_dim.29
  345.0 24.0 %all_to_all.48 = f32[128,1,1]{2,1,0:T(1,128)S(1)} all-to-all(f32[128,1,1]{2,1,0:T(1,128)S(1)} %broadcast_in_dim.29), channel_id=1, replica_groups=mesh['tm'=32,'chan'=4] {'tm','chan'}, dimensions={0} | all-to-all | bytes 1024 | tf_op jit(solution)/shard_map/all_to_all | solution.py:130
  369.0 0.8 reduce_sum.117
  371.1 2.2 add_add_fusion.amp_ref
  373.3 24.8 %shard_map.73 = f32[512,256]{1,0:T(8,128)} custom-call(s32[32]{0:T(128)} %copy-done.7, bf16[3,512,256]{2,1,0:T(8,128)(2,1)} %pad_maximum_fusion.3.parts_ref, bf16[32,256,128]{2,1,0:T(8,128)(2,1)} %fusion.5.hits_ref, s32[32,1,256]{2,1,0:T(1,128)} %copy-done.6, bf16[32,256,256]{2,1,0:T(8,128)(2,1)} %slice.9.weights_ref, f32[32,16,256]{2,1,0:T(8,128)} %add_add_fusion.amp_ref, ...), custom_call_target="tpu_custom_call" | custom-call | flops 3623878656 | bytes 5242880 | tf_op jit(solution)/shard_map/pallas_call | solution.py:100
  398.1 1.8 multiply_reduce_fusion
  400.0 0.7 broadcast_in_dim.30
  400.6 13.6 %all_to_all.49 = f32[128,1,1]{2,1,0:T(1,128)S(1)} all-to-all(f32[128,1,1]{2,1,0:T(1,128)S(1)} %broadcast_in_dim.30), channel_id=1, replica_groups=mesh['tm'=32,'chan'=4] {'tm','chan'}, dimensions={0} | all-to-all | bytes 1024 | tf_op jit(solution)/shard_map/all_to_all | solution.py:130
  414.2 0.7 reduce_sum.119
  416.4 2.3 multiply_subtract_fusion
  (35 shorter events, 1.3 us)
Async XLA Ops:
  0.6 75.3 %copy-start = (s32[32,32]{1,0:T(8,128)S(1)}, s32[32,32]{1,0:T(8,128)}, u32[]{:S(2)}) copy-start(s32[32,32]{1,0:T(8,128)} %param.8) | copy-start | bytes 12292
  6.0 8.8 %copy-start.4 = (f32[256,16]{0,1:T(8,128)S(1)}, f32[256,16]{0,1:T(8,128)}, u32[]{:S(2)}) copy-start(f32[256,16]{0,1:T(8,128)} %param.9) | copy-start | bytes 49156
  6.0 62.4 %all-to-all-start.2 = ((bf16[32,257,256]{2,1,0:T(8,128)(2,1)}), bf16[32,257,256]{2,1,0:T(8,128)(2,1)}, u32[]{:S(2)}, u32[]{:S(2)}) async-start(bf16[32,257,256]{2,1,0:T(8,128)(2,1)} %pad_maximum_fusion), calls=%async_computation.2 | async-start | bytes 8650752 | tf_op jit(solution)/shard_map/all_to_all | solution.py:147
  14.7 16.1 %copy-start.5 = (s32[8192]{0:T(1024)S(1)}, s32[8192]{0:T(1024)}, u32[]{:S(2)}) copy-start(s32[8192]{0:T(1024)} %param.7) | copy-start | bytes 98308
  24.9 15.9 %collective-permute-start = (f32[16,32,256]{2,0,1:T(8,128)S(1)}, f32[16,32,256]{2,0,1:T(8,128)S(1)}, u32[]{:S(2)}, u32[]{:S(2)}) collective-permute-start(f32[16,32,256]{2,0,1:T(8,128)S(1)} %fusion.7), channel_id=1, source_target_pairs={{0,1},{1,2},{2,3},{3,0},{4,5},{5,6},{6,7},{7,4},{8,9},{9,10},{10,1... | collective-permute-start | bytes 1572872 | tf_op jit(solution)/shard_map/ppermute | solution.py:124
  26.6 26.4 %collective-permute-start.1 = (f32[16,32,256]{2,0,1:T(8,128)S(1)}, f32[16,32,256]{2,0,1:T(8,128)S(1)}, u32[]{:S(2)}, u32[]{:S(2)}) collective-permute-start(f32[16,32,256]{2,0,1:T(8,128)S(1)} %fusion.7), channel_id=1, source_target_pairs={{0,2},{1,3},{2,0},{3,1},{4,6},{5,7},{6,4},{7,5},{8,10},{9,11},{10,... | collective-permute-start | bytes 1572872 | tf_op jit(solution)/shard_map/ppermute | solution.py:124
  29.9 23.1 %collective-permute-start.2 = (f32[16,32,256]{2,0,1:T(8,128)S(1)}, f32[16,32,256]{2,0,1:T(8,128)S(1)}, u32[]{:S(2)}, u32[]{:S(2)}) collective-permute-start(f32[16,32,256]{2,0,1:T(8,128)S(1)} %fusion.7), channel_id=1, source_target_pairs={{0,3},{1,0},{2,1},{3,2},{4,7},{5,4},{6,5},{7,6},{8,11},{9,8},{10,9... | collective-permute-start | bytes 1572872 | tf_op jit(solution)/shard_map/ppermute | solution.py:124
  30.8 29.2 %copy-start.1 = (bf16[8192,256]{1,0:T(8,128)(2,1)S(1)}, bf16[8192,256]{1,0:T(8,128)(2,1)}, u32[]{:S(2)}) copy-start(bf16[8192,256]{1,0:T(8,128)(2,1)} %param.6) | copy-start | bytes 12582916
  30.8 29.2 %copy-start.2 = (bf16[8192,256]{1,0:T(8,128)(2,1)S(1)}, bf16[8192,256]{1,0:T(8,128)(2,1)}, u32[]{:S(2)}) copy-start(bf16[8192,256]{1,0:T(8,128)(2,1)} %param.5) | copy-start | bytes 12582916
  68.4 59.5 %all-to-all-start = ((f32[32,128,256]{2,1,0:T(8,128)}), f32[32,128,256]{2,1,0:T(8,128)}, u32[]{:S(2)}, u32[]{:S(2)}) async-start(f32[32,128,256]{2,1,0:T(8,128)} %fusion), calls=%async_computation | async-start | bytes 8388608 | tf_op jit(solution)/shard_map/all_to_all | solution.py:208
  76.1 51.7 %copy-start.7 = (s32[32]{0:T(128)}, s32[32]{0:T(128)S(1)}, u32[]{:S(2)}) copy-start(s32[32]{0:T(128)S(1)} %dynamic-slice_reduce_fusion.blocks_ref) | copy-start | bytes 388
  77.1 4.6 %copy-start.6 = (s32[32,1,256]{2,1,0:T(1,128)}, s32[32,1,256]{2,1,0:T(1,128)S(1)}, u32[]{:S(2)}) copy-start(s32[32,1,256]{2,1,0:T(1,128)S(1)} %slice_convert_fusion.rows_ref) | copy-start | bytes 98308
  150.3 15.5 %collective-permute-start.3 = (f32[32,16,256]{2,1,0:T(8,128)}, f32[32,16,256]{2,1,0:T(8,128)S(1)}, u32[]{:S(2)}, u32[]{:S(2)}) collective-permute-start(f32[32,16,256]{2,1,0:T(8,128)} %shard_map.68), channel_id=1, source_target_pairs={{0,1},{1,2},{2,3},{3,0},{4,5},{5,6},{6,7},{7,4},{8,9},{9,10},{10,1... | collective-permute-start | bytes 1572872 | tf_op jit(solution)/shard_map/ppermute | solution.py:124
  152.0 26.7 %collective-permute-start.4 = (f32[32,16,256]{2,1,0:T(8,128)}, f32[32,16,256]{2,1,0:T(8,128)S(1)}, u32[]{:S(2)}, u32[]{:S(2)}) collective-permute-start(f32[32,16,256]{2,1,0:T(8,128)} %shard_map.68), channel_id=1, source_target_pairs={{0,2},{1,3},{2,0},{3,1},{4,6},{5,7},{6,4},{7,5},{8,10},{9,11},{10,... | collective-permute-start | bytes 1572872 | tf_op jit(solution)/shard_map/ppermute | solution.py:124
  155.3 23.4 %collective-permute-start.5 = (f32[32,16,256]{2,1,0:T(8,128)}, f32[32,16,256]{2,1,0:T(8,128)S(1)}, u32[]{:S(2)}, u32[]{:S(2)}) collective-permute-start(f32[32,16,256]{2,1,0:T(8,128)} %shard_map.68), channel_id=1, source_target_pairs={{0,3},{1,0},{2,1},{3,2},{4,7},{5,4},{6,5},{7,6},{8,11},{9,8},{10,9... | collective-permute-start | bytes 1572872 | tf_op jit(solution)/shard_map/ppermute | solution.py:124
  157.3 50.0 %all-to-all-start.1 = ((f32[128,1,1]{2,1,0:T(1,128)}), f32[128,1,1]{2,1,0:T(1,128)S(1)}, u32[]{:S(2)}, u32[]{:S(2)}) async-start(f32[128,1,1]{2,1,0:T(1,128)} %broadcast_in_dim.12), calls=%async_computation.1 | async-start | bytes 131072 | tf_op jit(solution)/shard_map/all_to_all | solution.py:130
  208.6 18.4 %all-to-all-start.3 = ((f32[128,1,1]{2,1,0:T(1,128)}), f32[128,1,1]{2,1,0:T(1,128)S(1)}, u32[]{:S(2)}, u32[]{:S(2)}) async-start(f32[128,1,1]{2,1,0:T(1,128)} %broadcast_in_dim.26), calls=%async_computation.3 | async-start | bytes 131072 | tf_op jit(solution)/shard_map/all_to_all | solution.py:130
  247.5 30.2 %collective-permute-start.6 = (f32[32,16,256]{2,1,0:T(8,128)}, f32[32,16,256]{2,1,0:T(8,128)S(1)}, u32[]{:S(2)}, u32[]{:S(2)}) collective-permute-start(f32[32,16,256]{2,1,0:T(8,128)} %shard_map.70), channel_id=1, source_target_pairs={{0,1},{1,2},{2,3},{3,0},{4,5},{5,6},{6,7},{7,4},{8,9},{9,10},{10,1... | collective-permute-start | bytes 1572872 | tf_op jit(solution)/shard_map/ppermute | solution.py:124
  248.3 29.4 %collective-permute-start.7 = (f32[32,16,256]{2,1,0:T(8,128)}, f32[32,16,256]{2,1,0:T(8,128)S(1)}, u32[]{:S(2)}, u32[]{:S(2)}) collective-permute-start(f32[32,16,256]{2,1,0:T(8,128)} %shard_map.70), channel_id=1, source_target_pairs={{0,2},{1,3},{2,0},{3,1},{4,6},{5,7},{6,4},{7,5},{8,10},{9,11},{10,... | collective-permute-start | bytes 1572872 | tf_op jit(solution)/shard_map/ppermute | solution.py:124
  249.7 28.0 %collective-permute-start.8 = (f32[32,16,256]{2,1,0:T(8,128)}, f32[32,16,256]{2,1,0:T(8,128)S(1)}, u32[]{:S(2)}, u32[]{:S(2)}) collective-permute-start(f32[32,16,256]{2,1,0:T(8,128)} %shard_map.70), channel_id=1, source_target_pairs={{0,3},{1,0},{2,1},{3,2},{4,7},{5,4},{6,5},{7,6},{8,11},{9,8},{10,9... | collective-permute-start | bytes 1572872 | tf_op jit(solution)/shard_map/ppermute | solution.py:124
  279.8 25.0 %copy-start.3 = (f32[512,256]{1,0:T(8,128)S(1)}, f32[512,256]{1,0:T(8,128)}, u32[]{:S(2)}) copy-start(f32[512,256]{1,0:T(8,128)} %shard_map.69) | copy-start | bytes 1572868
  341.3 29.8 %collective-permute-start.10 = (f32[32,16,256]{2,1,0:T(8,128)}, f32[32,16,256]{2,1,0:T(8,128)S(1)}, u32[]{:S(2)}, u32[]{:S(2)}) collective-permute-start(f32[32,16,256]{2,1,0:T(8,128)} %shard_map.72), channel_id=1, source_target_pairs={{0,2},{1,3},{2,0},{3,1},{4,6},{5,7},{6,4},{7,5},{8,10},{9,11},{10,... | collective-permute-start | bytes 1572872 | tf_op jit(solution)/shard_map/ppermute | solution.py:124
  342.4 28.7 %collective-permute-start.11 = (f32[32,16,256]{2,1,0:T(8,128)}, f32[32,16,256]{2,1,0:T(8,128)S(1)}, u32[]{:S(2)}, u32[]{:S(2)}) collective-permute-start(f32[32,16,256]{2,1,0:T(8,128)} %shard_map.72), channel_id=1, source_target_pairs={{0,3},{1,0},{2,1},{3,2},{4,7},{5,4},{6,5},{7,6},{8,11},{9,8},{10,9... | collective-permute-start | bytes 1572872 | tf_op jit(solution)/shard_map/ppermute | solution.py:124
  344.3 26.9 %collective-permute-start.9 = (f32[32,16,256]{2,1,0:T(8,128)}, f32[32,16,256]{2,1,0:T(8,128)}, u32[]{:S(2)}, u32[]{:S(2)}) collective-permute-start(f32[32,16,256]{2,1,0:T(8,128)} %shard_map.72), channel_id=1, source_target_pairs={{0,1},{1,2},{2,3},{3,0},{4,5},{5,6},{6,7},{7,4},{8,9},{9,10},{10,1... | collective-permute-start | bytes 1572872 | tf_op jit(solution)/shard_map/ppermute | solution.py:124

commit v7 on v6

--- a/solution.py
+++ b/solution.py
@@ -38,7 +38,7 @@
         )
 
 
-def bin_kernel(blocks_ref, parts_ref, hits_ref, rows_ref, weights_ref, amp_ref, modes_t_ref, out_ref):
+def bin_kernel(blocks_ref, parts_ref, hits_ref, rows_ref, weights_ref, amp_ref, stacked_ref, out_ref):
     step = pl.program_id(0)
 
     @pl.when(step == 0)
@@ -49,10 +49,7 @@
         block = blocks_ref[step * RUNS + j]
         x = gathered(parts_ref, block, hits_ref[j])
         w = weights_ref[j].astype(jnp.float32)
-        correction = lax.dot_general(
-            amp_ref[j], modes_t_ref[...], (((0,), (0,)), ((), ())),
-            precision=highest, preferred_element_type=jnp.float32,
-        )
+        correction = jnp.dot(amp_ref[j], stacked_ref[...], preferred_element_type=jnp.float32)
         rest = w * (w * x - correction)
         hits = (rows_ref[j] == lax.broadcasted_iota(jnp.int32, (BLK, rest.shape[0]), 0)).astype(
             jnp.bfloat16
@@ -66,17 +63,21 @@
         out_ref[pl.ds(start, BLK), :] += total
 
 
+def split3(value):
+    parts = []
+    rest = value
+    for _ in range(3):
+        rounded = lax.reduce_precision(rest, exponent_bits=8, mantissa_bits=7)
+        parts.append(rounded.astype(jnp.bfloat16))
+        rest = rest - rounded
+    return parts
+
+
 def owner_operator(blocks, field, hits, points_row, noise_weights, modes_t):
     groups, run_length, channels = noise_weights.shape
     modes = modes_t.shape[0]
     steps = groups // RUNS
-    parts = []
-    rest = field
-    for _ in range(3):
-        rounded = lax.reduce_precision(rest, exponent_bits=8, mantissa_bits=7)
-        parts.append(rounded.astype(jnp.bfloat16))
-        rest = rest - rounded
-    parts = jnp.stack(parts)
+    parts = jnp.stack(split3(field))
     full = pl.BlockSpec(parts.shape, lambda i, b: (0, 0, 0))
     per_run = lambda *shape: pl.BlockSpec((RUNS,) + shape, lambda i, b: (i, 0, 0))
     gather_flops = groups * 3 * 2 * run_length * BLK * channels
@@ -97,14 +98,18 @@
         ),
     )(blocks, parts, hits, noise_weights, modes_t)
     amps = chan_sum(amps)
+    high, middle, low = split3(jnp.swapaxes(amps, 1, 2))
+    amps = jnp.concatenate([high, middle, low, high, middle, high], axis=-1)
+    m_high, m_middle, m_low = split3(modes_t)
+    stacked = jnp.concatenate([m_high, m_high, m_high, m_middle, m_middle, m_low], axis=0)
     return pl.pallas_call(
         bin_kernel,
         grid_spec=pltpu.PrefetchScalarGridSpec(
             num_scalar_prefetch=1,
             grid=(steps,),
             in_specs=[full, per_run(run_length, BLK), per_run(1, run_length),
-                      per_run(run_length, channels), per_run(modes, run_length),
-                      pl.BlockSpec(modes_t.shape, lambda i, b: (0, 0))],
+                      per_run(run_length, channels), per_run(run_length, 6 * modes),
+                      pl.BlockSpec(stacked.shape, lambda i, b: (0, 0))],
             out_specs=pl.BlockSpec(field.shape, lambda i, b: (0, 0)),
         ),
         out_shape=jax.ShapeDtypeStruct(field.shape, jnp.float32),
@@ -113,7 +118,7 @@
             bytes_accessed=noise_weights.size * 2 + field.size * 8,
             transcendentals=0,
         ),
-    )(blocks, parts, hits, points_row, noise_weights, amps, modes_t)
+    )(blocks, parts, hits, points_row, noise_weights, amps, stacked)
 
 
 def chan_sum(value):

time: 424 us -> 489 us (1.15)
  local copies, waits for them, and re-layouts: 10.2 us -> 71.5 us
  other arithmetic: 33.3 us -> 59.9 us
  Pallas kernels: 121 us -> 95 us
    concatenate x0 -> x3, local copies, waits for them, and re-layouts: none -> 37.7 us  [owner_operator(): amps = jnp.concatenate([high, middle, low, high, middle, high], axis=-1)]
    convert_element_type x1 -> x7, other arithmetic: 0.12 us -> 29.6 us  [split3(): parts.append(rounded.astype(jnp.bfloat16))]
    pallas_call x3, Pallas kernels: 74.6 us -> 48.4 us  [owner_operator(): pl.pallas_call(bin_kernel, grid_spec=pltpu.PrefetchScalarGridSpec(num_sca...]
    ppermute x0 -> x6, local copies, waits for them, and re-layouts: none -> 15.6 us  [chan_sum(): total = total + lax.ppermute(value, 'chan', pairs)]
    add x0 -> x3, local copies, waits for them, and re-layouts: none -> 7.89 us  [chan_sum(): total = total + lax.ppermute(value, 'chan', pairs)]
    ppermute x12, waiting for transfers between devices: 35.7 us -> 41.3 us  [chan_sum(): total = total + lax.ppermute(value, 'chan', pairs)]
  transfers between devices with their start and end apart: 16 -> 16, of which waited for: 7 -> 6; matrix products, arithmetic and copies ran while one was open for 10% -> 17% of each run, Pallas kernels for 6% -> 3%
where the time goes in v7:
time: 489 us; the launch traced here: 483 us
  Pallas kernels  95 us (19%)
  waiting for transfers between devices  94 us (19%)
  blocking collectives  77.8 us (16%)
  local copies, waits for them, and re-layouts  71.5 us (15%)
  other arithmetic  59.9 us (12%)
  starting transfers between devices  47.9 us (10%)
  matrix products  28.5 us (6%)
  between operations  7.92 us (2%)
    all_to_all x4, blocking collectives, global_sum(): lax.all_to_all(jnp.broadcast_to(value, (everyone, 1)), ('tm', 'chan'), 0,...  77.8 us
    pallas_call x3, Pallas kernels, owner_operator(): pl.pallas_call(bin_kernel, grid_spec=pltpu.PrefetchScalarGridSpec(num_sca...  48.4 us
    pallas_call x3, Pallas kernels, owner_operator(): pl.pallas_call(amp_kernel, grid_spec=pltpu.PrefetchScalarGridSpec(num_sca...  46.6 us
    all_to_all x1, waiting for transfers between devices, per_device(): arrived = lax.all_to_all(local_partial, 'tm', 0, 0, tiled=True)  43.5 us
    ppermute x12, waiting for transfers between devices, chan_sum(): total = total + lax.ppermute(value, 'chan', pairs)  41.3 us
    concatenate x3, local copies, waits for them, and re-layouts, owner_operator(): amps = jnp.concatenate([high, middle, low, high, middle, high], axis=-1)  37.7 us
    convert_element_type x7, other arithmetic, split3(): parts.append(rounded.astype(jnp.bfloat16))  29.6 us
    ppermute x12, starting transfers between devices, chan_sum(): total = total + lax.ppermute(value, 'chan', pairs)  16 us
  transfers between devices with their start and end apart: 16, of which 6 were waited for; matrix products, arithmetic and copies ran while one was open for 17% of the time, Pallas kernels for 3%

profile of v7, /device:TPU:1, one launch (start us, length us, event | category | flops | bytes accessed | tf_op | source)
XLA Modules:
  0.0 482.6 jit_solution(12972967284103322809)
XLA Ops:
  1.4 4.6 pad_maximum_fusion
  6.0 8.8 %all-to-all-start.2 = ((bf16[32,257,256]{2,1,0:T(8,128)(2,1)}), bf16[32,257,256]{2,1,0:T(8,128)(2,1)}, u32[]{:S(2)}, u32[]{:S(2)}) async-start(bf16[32,257,256]{2,1,0:T(8,128)(2,1)} %pad_maximum_fusion), calls=%async_computation.2 | async-start | bytes 8650752 | tf_op jit(solution)/shard_map/all_to_all | solution.py:152
  14.8 10.2 %fusion.13 = f32[16,32,256]{2,0,1:T(8,128)S(1)} fusion(bf16[32,256,256]{2,1,0:T(8,128)(2,1)} %bitcast.99, bf16[32,256,256]{2,1,0:T(8,128)(2,1)} %bitcast.102, f32[256,16]{0,1:T(8,128)S(1)} %copy-done.9), kind=kOutput, calls=%fused_computation.33 | convolution fusion | flops 408944640 | bytes 8929280 | tf_op jit(solution)/shard_map/csk,km->mcs/dot_general | solution.py:170
  25.0 3.8 collective-permute-start.2
  28.8 1.1 collective-permute-start
  30.0 21.0 %collective-permute-done.2 = f32[16,32,256]{2,0,1:T(8,128)S(1)} collective-permute-done((f32[16,32,256]{2,0,1:T(8,128)S(1)}, f32[16,32,256]{2,0,1:T(8,128)S(1)}, u32[]{:S(2)}, u32[]{:S(2)}) %collective-permute-start.2) | collective-permute-done | bytes 524320 | tf_op jit(solution)/shard_map/ppermute | solution.py:129
  51.0 4.5 collective-permute-done
  55.5 7.0 %fusion.24 = f32[32,256,256]{2,1,0:T(8,128)S(1)} fusion(f32[16,32,256]{2,0,1:T(8,128)S(1)} %collective-permute-done.2, f32[16,32,256]{2,0,1:T(8,128)S(1)} %collective-permute-done.1, f32[16,32,256]{2,0,1:T(8,128)S(1)} %fusion.13, f32[16,32,256]{2,0,1:T(8,128)S(1)} %collective-permute-done, f32[256,16]{0,1:T(8,128)S(1)} %copy-done.9), kind=kOutput, calls=%fused_computation.74 | convolution fusion | flops 403046400 | bytes 10502144 | tf_op jit(solution)/shard_map/mcs,km->csk/dot_general | solution.py:173
  62.6 5.5 %fusion = f32[32,128,256]{2,1,0:T(8,128)} fusion(bf16[32,256,256]{2,1,0:T(8,128)(2,1)S(1)} %bitcast.100, f32[32,256,256]{2,1,0:T(8,128)S(1)} %fusion.24, bf16[32,256,256]{2,1,0:T(8,128)(2,1)S(1)} %bitcast.103, s32[32,256]{1,0:T(8,128)S(1)} %eq.47), kind=kOutput, calls=%fused_computation.2 | convolution fusion | flops 1622147072 | bytes 21004288 | tf_op jit(solution)/shard_map/csp,csk->cpk/dot_general | solution.py:212
  68.4 7.5 %all-to-all-start = ((f32[32,128,256]{2,1,0:T(8,128)}), f32[32,128,256]{2,1,0:T(8,128)}, u32[]{:S(2)}, u32[]{:S(2)}) async-start(f32[32,128,256]{2,1,0:T(8,128)} %fusion), calls=%async_computation | async-start | bytes 8388608 | tf_op jit(solution)/shard_map/all_to_all | solution.py:213
  77.2 4.6 slice.9.weights_ref
  81.8 2.6 fusion.11.hits_ref
  84.4 43.5 %all-to-all-done = f32[32,128,256]{2,1,0:T(8,128)} async-done(((f32[32,128,256]{2,1,0:T(8,128)}), f32[32,128,256]{2,1,0:T(8,128)}, u32[]{:S(2)}, u32[]{:S(2)}) %all-to-all-start) | async-done | bytes 4194336 | tf_op jit(solution)/shard_map/all_to_all | solution.py:213
  127.9 5.8 %multiply_reduce_fusion.4 = (f32[]{:T(128)}, f32[4,128,256]{2,0,1:T(4,128)S(1)}) fusion(f32[32,128,256]{2,1,0:T(8,128)} %all-to-all-done, s32[32]{0:T(128)S(1)} %dynamic-slice_reduce_fusion.blocks_ref), kind=kOutput, calls=%fused_computation.73 | convolution fusion | flops 25428096 | bytes 4718724 | tf_op jit(solution)/shard_map/cb,cpk->bpk/dot_general | solution.py:214
  133.9 1.0 pad_maximum_fusion.1.parts_ref
  134.9 15.6 %shard_map.68 = f32[32,16,256]{2,1,0:T(8,128)} custom-call(s32[32]{0:T(128)} %copy-done.13, bf16[3,512,256]{2,1,0:T(8,128)(2,1)} %pad_maximum_fusion.1.parts_ref, bf16[32,256,128]{2,1,0:T(8,128)(2,1)} %fusion.11.hits_ref, bf16[32,256,256]{2,1,0:T(8,128)(2,1)} %slice.9.weights_ref, f32[16,256]{1,0:T(8,128)} %bitcast.104), custom_call_target="tpu_custom_call" | custom-call | flops 2013265920 | bytes 4718592 | tf_op jit(solution)/shard_map/pallas_call | solution.py:84
  150.5 3.8 collective-permute-start.5
  155.1 1.3 broadcast_in_dim.12
  156.4 9.0 %all-to-all-start.1 = ((f32[128,1,1]{2,1,0:T(1,128)}), f32[128,1,1]{2,1,0:T(1,128)S(1)}, u32[]{:S(2)}, u32[]{:S(2)}) async-start(f32[128,1,1]{2,1,0:T(1,128)} %broadcast_in_dim.12), calls=%async_computation.1 | async-start | bytes 131072 | tf_op jit(solution)/shard_map/all_to_all | solution.py:135
  165.4 15.8 %collective-permute-done.3 = f32[32,16,256]{2,1,0:T(8,128)S(1)} collective-permute-done((f32[32,16,256]{2,1,0:T(8,128)}, f32[32,16,256]{2,1,0:T(8,128)S(1)}, u32[]{:S(2)}, u32[]{:S(2)}) %collective-permute-start.3) | collective-permute-done | bytes 524320 | tf_op jit(solution)/shard_map/ppermute | solution.py:129
  181.2 1.1 add.71
  182.3 2.6 copy.95
  184.9 2.6 copy.96
  187.5 2.6 copy.97
  190.2 7.4 %fusion.4 = (bf16[32,256,16]{2,1,0:T(8,128)(2,1)}, f32[32,16,256]{1,2,0:T(8,128)S(1)}) fusion(f32[32,16,256]{1,2,0:T(8,128)} %copy.97, f32[32,16,256]{1,2,0:T(8,128)} %copy.95, f32[32,16,256]{1,2,0:T(8,128)} %copy.96), kind=kLoop, calls=%fused_computation.19 | loop fusion | flops 1048576 | bytes 2359296 | tf_op jit(solution)/shard_map/convert_element_type | solution.py:71
  197.5 2.5 reduce-precision_convert_fusion.4
  200.0 12.6 %concatenate.18.amp_ref = bf16[32,256,96]{2,1,0:T(8,128)(2,1)} concatenate(bf16[32,256,16]{2,1,0:T(8,128)(2,1)S(1)} %get-tuple-element.19, bf16[32,256,16]{2,1,0:T(8,128)(2,1)} %get-tuple-element.18, bf16[32,256,16]{2,1,0:T(8,128)(2,1)} %get-tuple-element.12, bf16[32,256,16]{2,1,0:T(8,128)(2,1)S(1)} %get-tuple-element.19, bf16[32,256,16]{2,1,0:T(8,128)(2,1)} %get-tuple-element.18, ...), dimensions={2} | concatenate | bytes 3145728 | tf_op jit(solution)/shard_map/concatenate | solution.py:102
  212.5 16.1 %shard_map.69 = f32[512,256]{1,0:T(8,128)} custom-call(s32[32]{0:T(128)} %copy-done.13, bf16[3,512,256]{2,1,0:T(8,128)(2,1)} %pad_maximum_fusion.1.parts_ref, bf16[32,256,128]{2,1,0:T(8,128)(2,1)} %fusion.11.hits_ref, s32[32,1,256]{2,1,0:T(1,128)} %copy-done.12, bf16[32,256,256]{2,1,0:T(8,128)(2,1)} %slice.9.weights_ref, ...), custom_call_target="tpu_custom_call" | custom-call | flops 3623878656 | bytes 5242880 | tf_op jit(solution)/shard_map/pallas_call | solution.py:105
  228.6 1.9 fusion.20
  230.5 1.3 broadcast_in_dim.26
  231.8 6.6 %all-to-all-start.3 = ((f32[128,1,1]{2,1,0:T(1,128)}), f32[128,1,1]{2,1,0:T(1,128)S(1)}, u32[]{:S(2)}, u32[]{:S(2)}) async-start(f32[128,1,1]{2,1,0:T(1,128)} %broadcast_in_dim.26), calls=%async_computation.3 | async-start | bytes 131072 | tf_op jit(solution)/shard_map/all_to_all | solution.py:135
  239.2 8.8 %all-to-all-done.3 = f32[128,1,1]{2,1,0:T(1,128)S(1)} async-done(((f32[128,1,1]{2,1,0:T(1,128)}), f32[128,1,1]{2,1,0:T(1,128)S(1)}, u32[]{:S(2)}, u32[]{:S(2)}) %all-to-all-start.3) | async-done | bytes 544 | tf_op jit(solution)/shard_map/all_to_all | solution.py:135
  250.2 1.8 multiply_reduce_fusion.3
  252.0 1.0 pad_maximum_fusion.2.parts_ref
  253.0 15.5 %shard_map.70 = f32[32,16,256]{2,1,0:T(8,128)} custom-call(s32[32]{0:T(128)} %copy-done.13, bf16[3,512,256]{2,1,0:T(8,128)(2,1)} %pad_maximum_fusion.2.parts_ref, bf16[32,256,128]{2,1,0:T(8,128)(2,1)} %fusion.11.hits_ref, bf16[32,256,256]{2,1,0:T(8,128)(2,1)} %slice.9.weights_ref, f32[16,256]{1,0:T(8,128)} %bitcast.105), custom_call_target="tpu_custom_call" | custom-call | flops 2013265920 | bytes 4718592 | tf_op jit(solution)/shard_map/pallas_call | solution.py:84
  269.1 1.4 collective-permute-start.7
  270.5 1.2 collective-permute-start.8
  272.3 24.2 %all_to_all.46 = f32[128,1,1]{2,1,0:T(1,128)S(1)} all-to-all(f32[128,1,1]{2,1,0:T(1,128)S(1)} %broadcast_in_dim.27), channel_id=1, replica_groups=mesh['tm'=32,'chan'=4] {'tm','chan'}, dimensions={0} | all-to-all | bytes 1024 | tf_op jit(solution)/shard_map/all_to_all | solution.py:135
  298.4 1.1 add.76
  299.6 2.6 copy.100
  302.2 2.6 copy.101
  304.8 2.6 copy.102
  307.4 7.4 %fusion.6 = (bf16[32,256,16]{2,1,0:T(8,128)(2,1)}, f32[32,16,256]{1,2,0:T(8,128)S(1)}) fusion(f32[32,16,256]{1,2,0:T(8,128)} %copy.102, f32[32,16,256]{1,2,0:T(8,128)} %copy.100, f32[32,16,256]{1,2,0:T(8,128)} %copy.101), kind=kLoop, calls=%fused_computation.21 | loop fusion | flops 1048576 | bytes 2359296 | tf_op jit(solution)/shard_map/convert_element_type | solution.py:71
  314.8 2.5 reduce-precision_convert_fusion.2
  317.2 12.6 %concatenate.20.amp_ref = bf16[32,256,96]{2,1,0:T(8,128)(2,1)} concatenate(bf16[32,256,16]{2,1,0:T(8,128)(2,1)S(1)} %get-tuple-element.17, bf16[32,256,16]{2,1,0:T(8,128)(2,1)} %get-tuple-element.16, bf16[32,256,16]{2,1,0:T(8,128)(2,1)} %get-tuple-element.10, bf16[32,256,16]{2,1,0:T(8,128)(2,1)S(1)} %get-tuple-element.17, bf16[32,256,16]{2,1,0:T(8,128)(2,1)} %get-tuple-element.16, ...), dimensions={2} | concatenate | bytes 3145728 | tf_op jit(solution)/shard_map/concatenate | solution.py:102
  329.8 16.2 %shard_map.71 = f32[512,256]{1,0:T(8,128)} custom-call(s32[32]{0:T(128)} %copy-done.13, bf16[3,512,256]{2,1,0:T(8,128)(2,1)} %pad_maximum_fusion.2.parts_ref, bf16[32,256,128]{2,1,0:T(8,128)(2,1)} %fusion.11.hits_ref, s32[32,1,256]{2,1,0:T(1,128)} %copy-done.12, bf16[32,256,256]{2,1,0:T(8,128)(2,1)} %slice.9.weights_ref, ...), custom_call_target="tpu_custom_call" | custom-call | flops 3623878656 | bytes 5242880 | tf_op jit(solution)/shard_map/pallas_call | solution.py:105
  346.0 1.8 multiply_reduce_fusion.2
  348.5 14.8 %all_to_all.47 = f32[128,1,1]{2,1,0:T(1,128)S(1)} all-to-all(f32[128,1,1]{2,1,0:T(1,128)S(1)} %broadcast_in_dim.28), channel_id=1, replica_groups=mesh['tm'=32,'chan'=4] {'tm','chan'}, dimensions={0} | all-to-all | bytes 1024 | tf_op jit(solution)/shard_map/all_to_all | solution.py:135
  366.2 1.0 pad_maximum_fusion.3.parts_ref
  367.2 15.5 %shard_map.72 = f32[32,16,256]{2,1,0:T(8,128)} custom-call(s32[32]{0:T(128)} %copy-done.13, bf16[3,512,256]{2,1,0:T(8,128)(2,1)} %pad_maximum_fusion.3.parts_ref, bf16[32,256,128]{2,1,0:T(8,128)(2,1)} %fusion.11.hits_ref, bf16[32,256,256]{2,1,0:T(8,128)(2,1)} %slice.9.weights_ref, f32[16,256]{1,0:T(8,128)} %bitcast.106), custom_call_target="tpu_custom_call" | custom-call | flops 2013265920 | bytes 4718592 | tf_op jit(solution)/shard_map/pallas_call | solution.py:84
  383.3 1.6 collective-permute-start.10
  384.9 1.2 collective-permute-start.11
  386.8 24.0 %all_to_all.48 = f32[128,1,1]{2,1,0:T(1,128)S(1)} all-to-all(f32[128,1,1]{2,1,0:T(1,128)S(1)} %broadcast_in_dim.29), channel_id=1, replica_groups=mesh['tm'=32,'chan'=4] {'tm','chan'}, dimensions={0} | all-to-all | bytes 1024 | tf_op jit(solution)/shard_map/all_to_all | solution.py:135
  412.9 1.1 add.83
  414.1 2.6 copy.105
  416.7 2.6 copy.106
  419.3 2.6 copy.107
  421.9 7.4 %fusion.8 = (bf16[32,256,16]{2,1,0:T(8,128)(2,1)}, f32[32,16,256]{1,2,0:T(8,128)S(1)}) fusion(f32[32,16,256]{1,2,0:T(8,128)} %copy.107, f32[32,16,256]{1,2,0:T(8,128)} %copy.105, f32[32,16,256]{1,2,0:T(8,128)} %copy.106), kind=kLoop, calls=%fused_computation.23 | loop fusion | flops 1048576 | bytes 2359296 | tf_op jit(solution)/shard_map/convert_element_type | solution.py:71
  429.3 2.5 reduce-precision_convert_fusion
  431.7 12.6 %concatenate.21.amp_ref = bf16[32,256,96]{2,1,0:T(8,128)(2,1)} concatenate(bf16[32,256,16]{2,1,0:T(8,128)(2,1)S(1)} %get-tuple-element.15, bf16[32,256,16]{2,1,0:T(8,128)(2,1)} %get-tuple-element.14, bf16[32,256,16]{2,1,0:T(8,128)(2,1)} %get-tuple-element.2, bf16[32,256,16]{2,1,0:T(8,128)(2,1)S(1)} %get-tuple-element.15, bf16[32,256,16]{2,1,0:T(8,128)(2,1)} %get-tuple-element.14, ...), dimensions={2} | concatenate | bytes 3145728 | tf_op jit(solution)/shard_map/concatenate | solution.py:102
  444.3 16.2 %shard_map.73 = f32[512,256]{1,0:T(8,128)} custom-call(s32[32]{0:T(128)} %copy-done.13, bf16[3,512,256]{2,1,0:T(8,128)(2,1)} %pad_maximum_fusion.3.parts_ref, bf16[32,256,128]{2,1,0:T(8,128)(2,1)} %fusion.11.hits_ref, s32[32,1,256]{2,1,0:T(1,128)} %copy-done.12, bf16[32,256,256]{2,1,0:T(8,128)(2,1)} %slice.9.weights_ref, ...), custom_call_target="tpu_custom_call" | custom-call | flops 3623878656 | bytes 5242880 | tf_op jit(solution)/shard_map/pallas_call | solution.py:105
  460.5 1.8 multiply_reduce_fusion
  463.0 14.8 %all_to_all.49 = f32[128,1,1]{2,1,0:T(1,128)S(1)} all-to-all(f32[128,1,1]{2,1,0:T(1,128)S(1)} %broadcast_in_dim.30), channel_id=1, replica_groups=mesh['tm'=32,'chan'=4] {'tm','chan'}, dimensions={0} | all-to-all | bytes 1024 | tf_op jit(solution)/shard_map/all_to_all | solution.py:135
  479.9 2.2 multiply_subtract_fusion
  (73 shorter events, 12.7 us)
Async XLA Ops:
  0.6 75.3 %copy-start = (s32[32,32]{1,0:T(8,128)S(1)}, s32[32,32]{1,0:T(8,128)}, u32[]{:S(2)}) copy-start(s32[32,32]{1,0:T(8,128)} %param.8) | copy-start | bytes 12292
  6.0 8.8 %copy-start.9 = (f32[256,16]{0,1:T(8,128)S(1)}, f32[256,16]{0,1:T(8,128)}, u32[]{:S(2)}) copy-start(f32[256,16]{0,1:T(8,128)} %param.9) | copy-start | bytes 49156
  6.0 62.4 %all-to-all-start.2 = ((bf16[32,257,256]{2,1,0:T(8,128)(2,1)}), bf16[32,257,256]{2,1,0:T(8,128)(2,1)}, u32[]{:S(2)}, u32[]{:S(2)}) async-start(bf16[32,257,256]{2,1,0:T(8,128)(2,1)} %pad_maximum_fusion), calls=%async_computation.2 | async-start | bytes 8650752 | tf_op jit(solution)/shard_map/all_to_all | solution.py:152
  14.8 15.1 %copy-start.11 = (s32[8192]{0:T(1024)S(1)}, s32[8192]{0:T(1024)}, u32[]{:S(2)}) copy-start(s32[8192]{0:T(1024)} %param.7) | copy-start | bytes 98308
  25.0 26.0 %collective-permute-start.2 = (f32[16,32,256]{2,0,1:T(8,128)S(1)}, f32[16,32,256]{2,0,1:T(8,128)S(1)}, u32[]{:S(2)}, u32[]{:S(2)}) collective-permute-start(f32[16,32,256]{2,0,1:T(8,128)S(1)} %fusion.13), channel_id=1, source_target_pairs={{0,3},{1,0},{2,1},{3,2},{4,7},{5,4},{6,5},{7,6},{8,11},{9,8},{10,9... | collective-permute-start | bytes 1572872 | tf_op jit(solution)/shard_map/ppermute | solution.py:129
  28.8 22.2 %collective-permute-start.1 = (f32[16,32,256]{2,0,1:T(8,128)S(1)}, f32[16,32,256]{2,0,1:T(8,128)S(1)}, u32[]{:S(2)}, u32[]{:S(2)}) collective-permute-start(f32[16,32,256]{2,0,1:T(8,128)S(1)} %fusion.13), channel_id=1, source_target_pairs={{0,2},{1,3},{2,0},{3,1},{4,6},{5,7},{6,4},{7,5},{8,10},{9,11},{10,... | collective-permute-start | bytes 1572872 | tf_op jit(solution)/shard_map/ppermute | solution.py:129
  28.8 26.7 %collective-permute-start = (f32[16,32,256]{2,0,1:T(8,128)S(1)}, f32[16,32,256]{2,0,1:T(8,128)S(1)}, u32[]{:S(2)}, u32[]{:S(2)}) collective-permute-start(f32[16,32,256]{2,0,1:T(8,128)S(1)} %fusion.13), channel_id=1, source_target_pairs={{0,1},{1,2},{2,3},{3,0},{4,5},{5,6},{6,7},{7,4},{8,9},{9,10},{10,1... | collective-permute-start | bytes 1572872 | tf_op jit(solution)/shard_map/ppermute | solution.py:129
  30.0 32.6 %copy-start.2 = (bf16[8192,256]{1,0:T(8,128)(2,1)S(1)}, bf16[8192,256]{1,0:T(8,128)(2,1)}, u32[]{:S(2)}) copy-start(bf16[8192,256]{1,0:T(8,128)(2,1)} %param.6) | copy-start | bytes 12582916
  30.0 32.6 %copy-start.3 = (bf16[8192,256]{1,0:T(8,128)(2,1)S(1)}, bf16[8192,256]{1,0:T(8,128)(2,1)}, u32[]{:S(2)}) copy-start(bf16[8192,256]{1,0:T(8,128)(2,1)} %param.5) | copy-start | bytes 12582916
  68.4 59.5 %all-to-all-start = ((f32[32,128,256]{2,1,0:T(8,128)}), f32[32,128,256]{2,1,0:T(8,128)}, u32[]{:S(2)}, u32[]{:S(2)}) async-start(f32[32,128,256]{2,1,0:T(8,128)} %fusion), calls=%async_computation | async-start | bytes 8388608 | tf_op jit(solution)/shard_map/all_to_all | solution.py:213
  76.2 51.7 %copy-start.13 = (s32[32]{0:T(128)}, s32[32]{0:T(128)S(1)}, u32[]{:S(2)}) copy-start(s32[32]{0:T(128)S(1)} %dynamic-slice_reduce_fusion.blocks_ref) | copy-start | bytes 388
  77.1 4.6 copy-start.12
  134.9 20.1 %copy-start.10 = (f32[256,16]{0,1:T(8,128)S(1)}, f32[256,16]{0,1:T(8,128)}, u32[]{:S(2)}) copy-start(f32[256,16]{0,1:T(8,128)} %param.9) | copy-start | bytes 49156
  150.5 37.0 %collective-permute-start.5 = (f32[32,16,256]{2,1,0:T(8,128)}, f32[32,16,256]{2,1,0:T(8,128)S(1)}, u32[]{:S(2)}, u32[]{:S(2)}) collective-permute-start(f32[32,16,256]{2,1,0:T(8,128)} %shard_map.68), channel_id=1, source_target_pairs={{0,3},{1,0},{2,1},{3,2},{4,7},{5,4},{6,5},{7,6},{8,11},{9,8},{10,9... | collective-permute-start | bytes 1572872 | tf_op jit(solution)/shard_map/ppermute | solution.py:129
  154.3 30.6 %collective-permute-start.4 = (f32[32,16,256]{2,1,0:T(8,128)}, f32[32,16,256]{2,1,0:T(8,128)S(1)}, u32[]{:S(2)}, u32[]{:S(2)}) collective-permute-start(f32[32,16,256]{2,1,0:T(8,128)} %shard_map.68), channel_id=1, source_target_pairs={{0,2},{1,3},{2,0},{3,1},{4,6},{5,7},{6,4},{7,5},{8,10},{9,11},{10,... | collective-permute-start | bytes 1572872 | tf_op jit(solution)/shard_map/ppermute | solution.py:129
  154.3 26.9 %collective-permute-start.3 = (f32[32,16,256]{2,1,0:T(8,128)}, f32[32,16,256]{2,1,0:T(8,128)S(1)}, u32[]{:S(2)}, u32[]{:S(2)}) collective-permute-start(f32[32,16,256]{2,1,0:T(8,128)} %shard_map.68), channel_id=1, source_target_pairs={{0,1},{1,2},{2,3},{3,0},{4,5},{5,6},{6,7},{7,4},{8,9},{9,10},{10,1... | collective-permute-start | bytes 1572872 | tf_op jit(solution)/shard_map/ppermute | solution.py:129
  155.0 32.5 %copy-start.14 = (bf16[96,256]{1,0:T(8,128)(2,1)}, bf16[96,256]{1,0:T(8,128)(2,1)S(1)}, u32[]{:S(2)}) copy-start(bf16[96,256]{1,0:T(8,128)(2,1)S(1)} %constant_dynamic-update-slice_fusion.stacked_ref) | copy-start | bytes 147460
  156.4 74.1 %all-to-all-start.1 = ((f32[128,1,1]{2,1,0:T(1,128)}), f32[128,1,1]{2,1,0:T(1,128)S(1)}, u32[]{:S(2)}, u32[]{:S(2)}) async-start(f32[128,1,1]{2,1,0:T(1,128)} %broadcast_in_dim.12), calls=%async_computation.1 | async-start | bytes 131072 | tf_op jit(solution)/shard_map/all_to_all | solution.py:135
  231.8 16.2 %all-to-all-start.3 = ((f32[128,1,1]{2,1,0:T(1,128)}), f32[128,1,1]{2,1,0:T(1,128)S(1)}, u32[]{:S(2)}, u32[]{:S(2)}) async-start(f32[128,1,1]{2,1,0:T(1,128)} %broadcast_in_dim.26), calls=%async_computation.3 | async-start | bytes 131072 | tf_op jit(solution)/shard_map/all_to_all | solution.py:135
  268.5 29.9 %collective-permute-start.6 = (f32[32,16,256]{2,1,0:T(8,128)}, f32[32,16,256]{2,1,0:T(8,128)S(1)}, u32[]{:S(2)}, u32[]{:S(2)}) collective-permute-start(f32[32,16,256]{2,1,0:T(8,128)} %shard_map.70), channel_id=1, source_target_pairs={{0,1},{1,2},{2,3},{3,0},{4,5},{5,6},{6,7},{7,4},{8,9},{9,10},{10,1... | collective-permute-start | bytes 1572872 | tf_op jit(solution)/shard_map/ppermute | solution.py:129
  269.1 33.1 %collective-permute-start.7 = (f32[32,16,256]{2,1,0:T(8,128)}, f32[32,16,256]{2,1,0:T(8,128)S(1)}, u32[]{:S(2)}, u32[]{:S(2)}) collective-permute-start(f32[32,16,256]{2,1,0:T(8,128)} %shard_map.70), channel_id=1, source_target_pairs={{0,2},{1,3},{2,0},{3,1},{4,6},{5,7},{6,4},{7,5},{8,10},{9,11},{10,... | collective-permute-start | bytes 1572872 | tf_op jit(solution)/shard_map/ppermute | solution.py:129
  270.5 34.3 %collective-permute-start.8 = (f32[32,16,256]{2,1,0:T(8,128)}, f32[32,16,256]{2,1,0:T(8,128)S(1)}, u32[]{:S(2)}, u32[]{:S(2)}) collective-permute-start(f32[32,16,256]{2,1,0:T(8,128)} %shard_map.70), channel_id=1, source_target_pairs={{0,3},{1,0},{2,1},{3,2},{4,7},{5,4},{6,5},{7,6},{8,11},{9,8},{10,9... | collective-permute-start | bytes 1572872 | tf_op jit(solution)/shard_map/ppermute | solution.py:129
  329.8 16.2 %copy-start.8 = (f32[512,256]{1,0:T(8,128)S(1)}, f32[512,256]{1,0:T(8,128)}, u32[]{:S(2)}) copy-start(f32[512,256]{1,0:T(8,128)} %shard_map.69) | copy-start | bytes 1572868
  347.8 34.8 %copy-start.4 = (f32[512,256]{1,0:T(8,128)}, f32[512,256]{1,0:T(8,128)S(1)}, u32[]{:S(2)}) copy-start(f32[512,256]{1,0:T(8,128)S(1)} %get-tuple-element.7) | copy-start | bytes 1572868
  365.3 17.3 %copy-start.6 = (f32[512,256]{1,0:T(8,128)}, f32[512,256]{1,0:T(8,128)S(1)}, u32[]{:S(2)}) copy-start(f32[512,256]{1,0:T(8,128)S(1)} %get-tuple-element.5) | copy-start | bytes 1572868
  382.6 30.3 %collective-permute-start.9 = (f32[32,16,256]{2,1,0:T(8,128)}, f32[32,16,256]{2,1,0:T(8,128)S(1)}, u32[]{:S(2)}, u32[]{:S(2)}) collective-permute-start(f32[32,16,256]{2,1,0:T(8,128)} %shard_map.72), channel_id=1, source_target_pairs={{0,1},{1,2},{2,3},{3,0},{4,5},{5,6},{6,7},{7,4},{8,9},{9,10},{10,1... | collective-permute-start | bytes 1572872 | tf_op jit(solution)/shard_map/ppermute | solution.py:129
  383.3 33.4 %collective-permute-start.10 = (f32[32,16,256]{2,1,0:T(8,128)}, f32[32,16,256]{2,1,0:T(8,128)S(1)}, u32[]{:S(2)}, u32[]{:S(2)}) collective-permute-start(f32[32,16,256]{2,1,0:T(8,128)} %shard_map.72), channel_id=1, source_target_pairs={{0,2},{1,3},{2,0},{3,1},{4,6},{5,7},{6,4},{7,5},{8,10},{9,11},{10,... | collective-permute-start | bytes 1572872 | tf_op jit(solution)/shard_map/ppermute | solution.py:129
  384.9 34.4 %collective-permute-start.11 = (f32[32,16,256]{2,1,0:T(8,128)}, f32[32,16,256]{2,1,0:T(8,128)S(1)}, u32[]{:S(2)}, u32[]{:S(2)}) collective-permute-start(f32[32,16,256]{2,1,0:T(8,128)} %shard_map.72), channel_id=1, source_target_pairs={{0,3},{1,0},{2,1},{3,2},{4,7},{5,4},{6,5},{7,6},{8,11},{9,8},{10,9... | collective-permute-start | bytes 1572872 | tf_op jit(solution)/shard_map/ppermute | solution.py:129
  444.3 16.2 %copy-start.5 = (f32[512,256]{1,0:T(8,128)S(1)}, f32[512,256]{1,0:T(8,128)}, u32[]{:S(2)}) copy-start(f32[512,256]{1,0:T(8,128)} %copy-done.4) | copy-start | bytes 1572868
  444.3 16.2 %copy-start.7 = (f32[512,256]{1,0:T(8,128)S(1)}, f32[512,256]{1,0:T(8,128)}, u32[]{:S(2)}) copy-start(f32[512,256]{1,0:T(8,128)} %copy-done.6) | copy-start | bytes 1572868
  444.3 37.9 %copy-start.1 = (s32[32,32]{1,0:T(8,128)S(1)}, s32[32,32]{1,0:T(8,128)}, u32[]{:S(2)}) copy-start(s32[32,32]{1,0:T(8,128)} %param.8) | copy-start | bytes 12292

commit v8 on v7

--- a/solution.py
+++ b/solution.py
@@ -49,7 +49,18 @@
         block = blocks_ref[step * RUNS + j]
         x = gathered(parts_ref, block, hits_ref[j])
         w = weights_ref[j].astype(jnp.float32)
-        correction = jnp.dot(amp_ref[j], stacked_ref[...], preferred_element_type=jnp.float32)
+        rest = amp_ref[j]
+        pieces = []
+        for _ in range(3):
+            piece = rest.astype(jnp.bfloat16)
+            rest = rest - piece.astype(jnp.float32)
+            pieces.append(piece)
+        high, middle, low = pieces
+        amp_stack = jnp.concatenate([high, middle, low, high, middle, high], axis=0)
+        correction = lax.dot_general(
+            amp_stack, stacked_ref[...], (((0,), (0,)), ((), ())),
+            preferred_element_type=jnp.float32,
+        )
         rest = w * (w * x - correction)
         hits = (rows_ref[j] == lax.broadcasted_iota(jnp.int32, (BLK, rest.shape[0]), 0)).astype(
             jnp.bfloat16
@@ -98,8 +109,6 @@
         ),
     )(blocks, parts, hits, noise_weights, modes_t)
     amps = chan_sum(amps)
-    high, middle, low = split3(jnp.swapaxes(amps, 1, 2))
-    amps = jnp.concatenate([high, middle, low, high, middle, high], axis=-1)
     m_high, m_middle, m_low = split3(modes_t)
     stacked = jnp.concatenate([m_high, m_high, m_high, m_middle, m_middle, m_low], axis=0)
     return pl.pallas_call(
@@ -108,7 +117,7 @@
             num_scalar_prefetch=1,
             grid=(steps,),
             in_specs=[full, per_run(run_length, BLK), per_run(1, run_length),
-                      per_run(run_length, channels), per_run(run_length, 6 * modes),
+                      per_run(run_length, channels), per_run(modes, run_length),
                       pl.BlockSpec(stacked.shape, lambda i, b: (0, 0))],
             out_specs=pl.BlockSpec(field.shape, lambda i, b: (0, 0)),
         ),

time: 489 us -> 398 us (0.81)
  local copies, waits for them, and re-layouts: 71.5 us -> 10.3 us
  other arithmetic: 59.9 us -> 33.3 us
    concatenate x3 -> x0, local copies, waits for them, and re-layouts: 37.7 us -> none  [owner_operator(): amps = jnp.concatenate([high, middle, low, high, middle, high], axis=-1)]
    convert_element_type x7 -> x1, other arithmetic: 29.6 us -> 0.12 us  [split3(): parts.append(rounded.astype(jnp.bfloat16))]
    ppermute x6 -> x0, local copies, waits for them, and re-layouts: 15.6 us -> none  [chan_sum(): total = total + lax.ppermute(value, 'chan', pairs)]
    add x3 -> x0, local copies, waits for them, and re-layouts: 7.89 us -> none  [chan_sum(): total = total + lax.ppermute(value, 'chan', pairs)]
    ppermute x12, waiting for transfers between devices: 41.3 us -> 35.7 us  [chan_sum(): total = total + lax.ppermute(value, 'chan', pairs)]
  transfers between devices with their start and end apart: 16 -> 16, of which waited for: 6 -> 7; matrix products, arithmetic and copies ran while one was open for 17% -> 10% of each run, Pallas kernels for 3% -> 4%
where the time goes in v8:
time: 398 us; the launch traced here: 392 us
  Pallas kernels  94.4 us (24%)
  waiting for transfers between devices  90.7 us (23%)
  blocking collectives  76.2 us (19%)
  starting transfers between devices  50.7 us (13%)
  other arithmetic  33.3 us (8%)
  matrix products  28.5 us (7%)
  local copies, waits for them, and re-layouts  10.3 us (3%)
  between operations  7.77 us (2%)
    all_to_all x4, blocking collectives, global_sum(): lax.all_to_all(jnp.broadcast_to(value, (everyone, 1)), ('tm', 'chan'), 0,...  76.2 us
    pallas_call x3, Pallas kernels, owner_operator(): pl.pallas_call(bin_kernel, grid_spec=pltpu.PrefetchScalarGridSpec(num_sca...  47.8 us
    pallas_call x3, Pallas kernels, owner_operator(): pl.pallas_call(amp_kernel, grid_spec=pltpu.PrefetchScalarGridSpec(num_sca...  46.6 us
    all_to_all x1, waiting for transfers between devices, per_device(): arrived = lax.all_to_all(local_partial, 'tm', 0, 0, tiled=True)  43.5 us
    ppermute x12, waiting for transfers between devices, chan_sum(): total = total + lax.ppermute(value, 'chan', pairs)  35.7 us
    ppermute x12, starting transfers between devices, chan_sum(): total = total + lax.ppermute(value, 'chan', pairs)  17.9 us
    all_to_all x2, starting transfers between devices, global_sum(): lax.all_to_all(jnp.broadcast_to(value, (everyone, 1)), ('tm', 'chan'), 0,...  16.5 us
    dot_general x1, matrix products, filtered(): jnp.einsum('csk,km->mcs', weighted, foreground_modes, precision=highest)  10.2 us
  transfers between devices with their start and end apart: 16, of which 7 were waited for; matrix products, arithmetic and copies ran while one was open for 10% of the time, Pallas kernels for 4%

profile of v8, /device:TPU:1, one launch (start us, length us, event | category | flops | bytes accessed | tf_op | source)
XLA Modules:
  0.0 392.0 jit_solution(10202537051022739415)
XLA Ops:
  0.6 0.8 convert_element_type.102
  1.4 4.5 %pad_maximum_fusion = bf16[32,257,256]{2,1,0:T(8,128)(2,1)} fusion(bf16[32,1,256]{2,1,0:T(2,128)(2,1)S(1)} %convert_element_type.118, bf16[32,256,256]{2,1,0:T(8,128)(2,1)} %bitcast.77), kind=kLoop, calls=%fused_computation.5 | loop fusion | flops 8421376 | bytes 8421376 | tf_op jit(solution)/shard_map/concatenate | solution.py:160
  6.0 8.8 %all-to-all-start.2 = ((bf16[32,257,256]{2,1,0:T(8,128)(2,1)}), bf16[32,257,256]{2,1,0:T(8,128)(2,1)}, u32[]{:S(2)}, u32[]{:S(2)}) async-start(bf16[32,257,256]{2,1,0:T(8,128)(2,1)} %pad_maximum_fusion), calls=%async_computation.2 | async-start | bytes 8650752 | tf_op jit(solution)/shard_map/all_to_all | solution.py:161
  14.7 10.2 %fusion.7 = f32[16,32,256]{2,0,1:T(8,128)S(1)} fusion(bf16[32,256,256]{2,1,0:T(8,128)(2,1)} %bitcast.78, bf16[32,256,256]{2,1,0:T(8,128)(2,1)} %bitcast.81, f32[256,16]{0,1:T(8,128)S(1)} %copy-done.4), kind=kOutput, calls=%fused_computation.12 | convolution fusion | flops 408944640 | bytes 8929280 | tf_op jit(solution)/shard_map/csk,km->mcs/dot_general | solution.py:179
  24.9 1.7 collective-permute-start
  26.6 3.3 collective-permute-start.1
  29.9 0.9 collective-permute-start.2
  30.8 10.0 %collective-permute-done = f32[16,32,256]{2,0,1:T(8,128)S(1)} collective-permute-done((f32[16,32,256]{2,0,1:T(8,128)S(1)}, f32[16,32,256]{2,0,1:T(8,128)S(1)}, u32[]{:S(2)}, u32[]{:S(2)}) %collective-permute-start) | collective-permute-done | bytes 524320 | tf_op jit(solution)/shard_map/ppermute | solution.py:138
  40.8 12.1 %collective-permute-done.1 = f32[16,32,256]{2,0,1:T(8,128)S(1)} collective-permute-done((f32[16,32,256]{2,0,1:T(8,128)S(1)}, f32[16,32,256]{2,0,1:T(8,128)S(1)}, u32[]{:S(2)}, u32[]{:S(2)}) %collective-permute-start.1) | collective-permute-done | bytes 524320 | tf_op jit(solution)/shard_map/ppermute | solution.py:138
  53.0 7.1 %fusion.18 = f32[32,256,256]{2,1,0:T(8,128)S(1)} fusion(f32[16,32,256]{2,0,1:T(8,128)S(1)} %collective-permute-done.2, f32[16,32,256]{2,0,1:T(8,128)S(1)} %collective-permute-done.1, f32[16,32,256]{2,0,1:T(8,128)S(1)} %fusion.7, f32[16,32,256]{2,0,1:T(8,128)S(1)} %collective-permute-done, f32[256,16]{0,1:T(8,128)S(1)} %copy-done.4), kind=kOutput, calls=%fused_computation.56 | convolution fusion | flops 403046400 | bytes 10502144 | tf_op jit(solution)/shard_map/mcs,km->csk/dot_general | solution.py:182
  60.1 5.5 %fusion = f32[32,128,256]{2,1,0:T(8,128)} fusion(bf16[32,256,256]{2,1,0:T(8,128)(2,1)S(1)} %bitcast.79, f32[32,256,256]{2,1,0:T(8,128)S(1)} %fusion.18, bf16[32,256,256]{2,1,0:T(8,128)(2,1)S(1)} %bitcast.82, s32[32,256]{1,0:T(8,128)S(1)} %eq.47), kind=kOutput, calls=%fused_computation.2 | convolution fusion | flops 1622147072 | bytes 21004288 | tf_op jit(solution)/shard_map/csp,csk->cpk/dot_general | solution.py:221
  65.6 2.8 all-to-all-done.2
  68.4 7.6 %all-to-all-start = ((f32[32,128,256]{2,1,0:T(8,128)}), f32[32,128,256]{2,1,0:T(8,128)}, u32[]{:S(2)}, u32[]{:S(2)}) async-start(f32[32,128,256]{2,1,0:T(8,128)} %fusion), calls=%async_computation | async-start | bytes 8388608 | tf_op jit(solution)/shard_map/all_to_all | solution.py:222
  76.2 0.9 slice_convert_fusion.rows_ref
  77.1 4.6 %slice.9.weights_ref = bf16[32,256,256]{2,1,0:T(8,128)(2,1)} slice(bf16[32,257,256]{2,1,0:T(8,128)(2,1)} %all-to-all-done.2), slice={[0:32], [0:256], [0:256]} | slice | bytes 8388608 | tf_op jit(solution)/shard_map/slice | solution.py:162
  81.8 2.6 fusion.5.hits_ref
  84.4 43.5 %all-to-all-done = f32[32,128,256]{2,1,0:T(8,128)} async-done(((f32[32,128,256]{2,1,0:T(8,128)}), f32[32,128,256]{2,1,0:T(8,128)}, u32[]{:S(2)}, u32[]{:S(2)}) %all-to-all-start) | async-done | bytes 4194336 | tf_op jit(solution)/shard_map/all_to_all | solution.py:222
  127.9 5.7 %multiply_reduce_fusion.4 = (f32[]{:T(128)}, f32[4,128,256]{2,0,1:T(4,128)S(1)}) fusion(f32[32,128,256]{2,1,0:T(8,128)} %all-to-all-done, s32[32]{0:T(128)S(1)} %dynamic-slice_reduce_fusion.blocks_ref), kind=kOutput, calls=%fused_computation.55 | convolution fusion | flops 25428096 | bytes 4718724 | tf_op jit(solution)/shard_map/cb,cpk->bpk/dot_general | solution.py:223
  133.8 1.0 pad_maximum_fusion.1.parts_ref
  134.8 15.6 %shard_map.68 = f32[32,16,256]{2,1,0:T(8,128)} custom-call(s32[32]{0:T(128)} %copy-done.8, bf16[3,512,256]{2,1,0:T(8,128)(2,1)} %pad_maximum_fusion.1.parts_ref, bf16[32,256,128]{2,1,0:T(8,128)(2,1)} %fusion.5.hits_ref, bf16[32,256,256]{2,1,0:T(8,128)(2,1)} %slice.9.weights_ref, f32[16,256]{1,0:T(8,128)} %bitcast.83), custom_call_target="tpu_custom_call" | custom-call | flops 2013265920 | bytes 4718592 | tf_op jit(solution)/shard_map/pallas_call | solution.py:95
  150.5 1.6 collective-permute-start.3
  152.1 3.3 collective-permute-start.4
  155.4 0.7 collective-permute-start.5
  156.2 1.3 broadcast_in_dim.12
  157.5 7.7 %all-to-all-start.1 = ((f32[128,1,1]{2,1,0:T(1,128)}), f32[128,1,1]{2,1,0:T(1,128)S(1)}, u32[]{:S(2)}, u32[]{:S(2)}) async-start(f32[128,1,1]{2,1,0:T(1,128)} %broadcast_in_dim.12), calls=%async_computation.1 | async-start | bytes 131072 | tf_op jit(solution)/shard_map/all_to_all | solution.py:144
  165.3 0.7 collective-permute-done.3
  166.0 12.8 %collective-permute-done.4 = f32[32,16,256]{2,1,0:T(8,128)S(1)} collective-permute-done((f32[32,16,256]{2,1,0:T(8,128)}, f32[32,16,256]{2,1,0:T(8,128)S(1)}, u32[]{:S(2)}, u32[]{:S(2)}) %collective-permute-start.4) | collective-permute-done | bytes 524320 | tf_op jit(solution)/shard_map/ppermute | solution.py:138
  178.8 2.0 add_add_fusion.2.amp_ref
  180.8 15.9 %shard_map.69 = f32[512,256]{1,0:T(8,128)} custom-call(s32[32]{0:T(128)} %copy-done.8, bf16[3,512,256]{2,1,0:T(8,128)(2,1)} %pad_maximum_fusion.1.parts_ref, bf16[32,256,128]{2,1,0:T(8,128)(2,1)} %fusion.5.hits_ref, s32[32,1,256]{2,1,0:T(1,128)} %copy-done.7, bf16[32,256,256]{2,1,0:T(8,128)(2,1)} %slice.9.weights_ref, f32[32,16,256]{2,1,0:T(8,128)} %add_add_fusion.2.amp_ref, ...), custom_call_target="tpu_custom_call" | custom-call | flops 3623878656 | bytes 5242880 | tf_op jit(solution)/shard_map/pallas_call | solution.py:114
  196.7 1.8 fusion.14
  198.5 1.2 broadcast_in_dim.26
  199.7 8.8 %all-to-all-start.3 = ((f32[128,1,1]{2,1,0:T(1,128)}), f32[128,1,1]{2,1,0:T(1,128)S(1)}, u32[]{:S(2)}, u32[]{:S(2)}) async-start(f32[128,1,1]{2,1,0:T(1,128)} %broadcast_in_dim.26), calls=%async_computation.3 | async-start | bytes 131072 | tf_op jit(solution)/shard_map/all_to_all | solution.py:144
  208.5 0.8 reduce_sum.109
  209.3 8.8 %all-to-all-done.3 = f32[128,1,1]{2,1,0:T(1,128)S(1)} async-done(((f32[128,1,1]{2,1,0:T(1,128)}), f32[128,1,1]{2,1,0:T(1,128)S(1)}, u32[]{:S(2)}, u32[]{:S(2)}) %all-to-all-start.3) | async-done | bytes 544 | tf_op jit(solution)/shard_map/all_to_all | solution.py:144
  218.2 0.7 reduce_sum.111
  220.2 1.8 multiply_reduce_fusion.3
  222.2 1.0 pad_maximum_fusion.2.parts_ref
  223.2 15.5 %shard_map.70 = f32[32,16,256]{2,1,0:T(8,128)} custom-call(s32[32]{0:T(128)} %copy-done.8, bf16[3,512,256]{2,1,0:T(8,128)(2,1)} %pad_maximum_fusion.2.parts_ref, bf16[32,256,128]{2,1,0:T(8,128)(2,1)} %fusion.5.hits_ref, bf16[32,256,256]{2,1,0:T(8,128)(2,1)} %slice.9.weights_ref, f32[16,256]{1,0:T(8,128)} %bitcast.84), custom_call_target="tpu_custom_call" | custom-call | flops 2013265920 | bytes 4718592 | tf_op jit(solution)/shard_map/pallas_call | solution.py:95
  239.3 1.4 collective-permute-start.7
  240.7 1.4 collective-permute-start.8
  242.1 0.7 broadcast_in_dim.27
  242.8 23.8 %all_to_all.46 = f32[128,1,1]{2,1,0:T(1,128)S(1)} all-to-all(f32[128,1,1]{2,1,0:T(1,128)S(1)} %broadcast_in_dim.27), channel_id=1, replica_groups=mesh['tm'=32,'chan'=4] {'tm','chan'}, dimensions={0} | all-to-all | bytes 1024 | tf_op jit(solution)/shard_map/all_to_all | solution.py:144
  266.6 0.7 reduce_sum.113
  268.6 2.1 add_add_fusion.1.amp_ref
  270.7 16.0 %shard_map.71 = f32[512,256]{1,0:T(8,128)} custom-call(s32[32]{0:T(128)} %copy-done.8, bf16[3,512,256]{2,1,0:T(8,128)(2,1)} %pad_maximum_fusion.2.parts_ref, bf16[32,256,128]{2,1,0:T(8,128)(2,1)} %fusion.5.hits_ref, s32[32,1,256]{2,1,0:T(1,128)} %copy-done.7, bf16[32,256,256]{2,1,0:T(8,128)(2,1)} %slice.9.weights_ref, f32[32,16,256]{2,1,0:T(8,128)} %add_add_fusion.1.amp_ref, ...), custom_call_target="tpu_custom_call" | custom-call | flops 3623878656 | bytes 5242880 | tf_op jit(solution)/shard_map/pallas_call | solution.py:114
  286.7 1.8 multiply_reduce_fusion.2
  288.6 0.7 broadcast_in_dim.28
  289.2 14.8 %all_to_all.47 = f32[128,1,1]{2,1,0:T(1,128)S(1)} all-to-all(f32[128,1,1]{2,1,0:T(1,128)S(1)} %broadcast_in_dim.28), channel_id=1, replica_groups=mesh['tm'=32,'chan'=4] {'tm','chan'}, dimensions={0} | all-to-all | bytes 1024 | tf_op jit(solution)/shard_map/all_to_all | solution.py:144
  304.0 0.7 reduce_sum.115
  306.1 0.7 fusion.27
  306.8 1.0 pad_maximum_fusion.3.parts_ref
  307.8 15.5 %shard_map.72 = f32[32,16,256]{2,1,0:T(8,128)} custom-call(s32[32]{0:T(128)} %copy-done.8, bf16[3,512,256]{2,1,0:T(8,128)(2,1)} %pad_maximum_fusion.3.parts_ref, bf16[32,256,128]{2,1,0:T(8,128)(2,1)} %fusion.5.hits_ref, bf16[32,256,256]{2,1,0:T(8,128)(2,1)} %slice.9.weights_ref, f32[16,256]{1,0:T(8,128)} %bitcast.85), custom_call_target="tpu_custom_call" | custom-call | flops 2013265920 | bytes 4718592 | tf_op jit(solution)/shard_map/pallas_call | solution.py:95
  323.3 1.1 collective-permute-start.10
  324.4 1.9 collective-permute-start.11
  326.3 0.7 broadcast_in_dim.29
  327.0 24.0 %all_to_all.48 = f32[128,1,1]{2,1,0:T(1,128)S(1)} all-to-all(f32[128,1,1]{2,1,0:T(1,128)S(1)} %broadcast_in_dim.29), channel_id=1, replica_groups=mesh['tm'=32,'chan'=4] {'tm','chan'}, dimensions={0} | all-to-all | bytes 1024 | tf_op jit(solution)/shard_map/all_to_all | solution.py:144
  351.0 0.8 reduce_sum.117
  353.1 2.2 add_add_fusion.amp_ref
  355.3 15.9 %shard_map.73 = f32[512,256]{1,0:T(8,128)} custom-call(s32[32]{0:T(128)} %copy-done.8, bf16[3,512,256]{2,1,0:T(8,128)(2,1)} %pad_maximum_fusion.3.parts_ref, bf16[32,256,128]{2,1,0:T(8,128)(2,1)} %fusion.5.hits_ref, s32[32,1,256]{2,1,0:T(1,128)} %copy-done.7, bf16[32,256,256]{2,1,0:T(8,128)(2,1)} %slice.9.weights_ref, f32[32,16,256]{2,1,0:T(8,128)} %add_add_fusion.amp_ref, ...), custom_call_target="tpu_custom_call" | custom-call | flops 3623878656 | bytes 5242880 | tf_op jit(solution)/shard_map/pallas_call | solution.py:114
  371.2 1.8 multiply_reduce_fusion
  373.0 0.7 broadcast_in_dim.30
  373.7 13.6 %all_to_all.49 = f32[128,1,1]{2,1,0:T(1,128)S(1)} all-to-all(f32[128,1,1]{2,1,0:T(1,128)S(1)} %broadcast_in_dim.30), channel_id=1, replica_groups=mesh['tm'=32,'chan'=4] {'tm','chan'}, dimensions={0} | all-to-all | bytes 1024 | tf_op jit(solution)/shard_map/all_to_all | solution.py:144
  387.3 0.7 reduce_sum.119
  389.3 2.3 multiply_subtract_fusion
  (45 shorter events, 1.3 us)
Async XLA Ops:
  0.6 75.3 %copy-start = (s32[32,32]{1,0:T(8,128)S(1)}, s32[32,32]{1,0:T(8,128)}, u32[]{:S(2)}) copy-start(s32[32,32]{1,0:T(8,128)} %param.8) | copy-start | bytes 12292
  6.0 8.8 %copy-start.4 = (f32[256,16]{0,1:T(8,128)S(1)}, f32[256,16]{0,1:T(8,128)}, u32[]{:S(2)}) copy-start(f32[256,16]{0,1:T(8,128)} %param.9) | copy-start | bytes 49156
  6.0 62.4 %all-to-all-start.2 = ((bf16[32,257,256]{2,1,0:T(8,128)(2,1)}), bf16[32,257,256]{2,1,0:T(8,128)(2,1)}, u32[]{:S(2)}, u32[]{:S(2)}) async-start(bf16[32,257,256]{2,1,0:T(8,128)(2,1)} %pad_maximum_fusion), calls=%async_computation.2 | async-start | bytes 8650752 | tf_op jit(solution)/shard_map/all_to_all | solution.py:161
  14.7 16.1 %copy-start.6 = (s32[8192]{0:T(1024)S(1)}, s32[8192]{0:T(1024)}, u32[]{:S(2)}) copy-start(s32[8192]{0:T(1024)} %param.7) | copy-start | bytes 98308
  24.9 15.9 %collective-permute-start = (f32[16,32,256]{2,0,1:T(8,128)S(1)}, f32[16,32,256]{2,0,1:T(8,128)S(1)}, u32[]{:S(2)}, u32[]{:S(2)}) collective-permute-start(f32[16,32,256]{2,0,1:T(8,128)S(1)} %fusion.7), channel_id=1, source_target_pairs={{0,1},{1,2},{2,3},{3,0},{4,5},{5,6},{6,7},{7,4},{8,9},{9,10},{10,1... | collective-permute-start | bytes 1572872 | tf_op jit(solution)/shard_map/ppermute | solution.py:138
  26.6 26.4 %collective-permute-start.1 = (f32[16,32,256]{2,0,1:T(8,128)S(1)}, f32[16,32,256]{2,0,1:T(8,128)S(1)}, u32[]{:S(2)}, u32[]{:S(2)}) collective-permute-start(f32[16,32,256]{2,0,1:T(8,128)S(1)} %fusion.7), channel_id=1, source_target_pairs={{0,2},{1,3},{2,0},{3,1},{4,6},{5,7},{6,4},{7,5},{8,10},{9,11},{10,... | collective-permute-start | bytes 1572872 | tf_op jit(solution)/shard_map/ppermute | solution.py:138
  29.9 23.1 %collective-permute-start.2 = (f32[16,32,256]{2,0,1:T(8,128)S(1)}, f32[16,32,256]{2,0,1:T(8,128)S(1)}, u32[]{:S(2)}, u32[]{:S(2)}) collective-permute-start(f32[16,32,256]{2,0,1:T(8,128)S(1)} %fusion.7), channel_id=1, source_target_pairs={{0,3},{1,0},{2,1},{3,2},{4,7},{5,4},{6,5},{7,6},{8,11},{9,8},{10,9... | collective-permute-start | bytes 1572872 | tf_op jit(solution)/shard_map/ppermute | solution.py:138
  30.8 29.2 %copy-start.1 = (bf16[8192,256]{1,0:T(8,128)(2,1)S(1)}, bf16[8192,256]{1,0:T(8,128)(2,1)}, u32[]{:S(2)}) copy-start(bf16[8192,256]{1,0:T(8,128)(2,1)} %param.6) | copy-start | bytes 12582916
  30.8 29.2 %copy-start.2 = (bf16[8192,256]{1,0:T(8,128)(2,1)S(1)}, bf16[8192,256]{1,0:T(8,128)(2,1)}, u32[]{:S(2)}) copy-start(bf16[8192,256]{1,0:T(8,128)(2,1)} %param.5) | copy-start | bytes 12582916
  68.4 59.5 %all-to-all-start = ((f32[32,128,256]{2,1,0:T(8,128)}), f32[32,128,256]{2,1,0:T(8,128)}, u32[]{:S(2)}, u32[]{:S(2)}) async-start(f32[32,128,256]{2,1,0:T(8,128)} %fusion), calls=%async_computation | async-start | bytes 8388608 | tf_op jit(solution)/shard_map/all_to_all | solution.py:222
  76.1 51.7 %copy-start.8 = (s32[32]{0:T(128)}, s32[32]{0:T(128)S(1)}, u32[]{:S(2)}) copy-start(s32[32]{0:T(128)S(1)} %dynamic-slice_reduce_fusion.blocks_ref) | copy-start | bytes 388
  77.1 4.6 %copy-start.7 = (s32[32,1,256]{2,1,0:T(1,128)}, s32[32,1,256]{2,1,0:T(1,128)S(1)}, u32[]{:S(2)}) copy-start(s32[32,1,256]{2,1,0:T(1,128)S(1)} %slice_convert_fusion.rows_ref) | copy-start | bytes 98308
  134.8 21.3 %copy-start.5 = (f32[256,16]{0,1:T(8,128)S(1)}, f32[256,16]{0,1:T(8,128)}, u32[]{:S(2)}) copy-start(f32[256,16]{0,1:T(8,128)} %param.9) | copy-start | bytes 49156
  150.5 15.5 %collective-permute-start.3 = (f32[32,16,256]{2,1,0:T(8,128)}, f32[32,16,256]{2,1,0:T(8,128)S(1)}, u32[]{:S(2)}, u32[]{:S(2)}) collective-permute-start(f32[32,16,256]{2,1,0:T(8,128)} %shard_map.68), channel_id=1, source_target_pairs={{0,1},{1,2},{2,3},{3,0},{4,5},{5,6},{6,7},{7,4},{8,9},{9,10},{10,1... | collective-permute-start | bytes 1572872 | tf_op jit(solution)/shard_map/ppermute | solution.py:138
  152.1 26.7 %collective-permute-start.4 = (f32[32,16,256]{2,1,0:T(8,128)}, f32[32,16,256]{2,1,0:T(8,128)S(1)}, u32[]{:S(2)}, u32[]{:S(2)}) collective-permute-start(f32[32,16,256]{2,1,0:T(8,128)} %shard_map.68), channel_id=1, source_target_pairs={{0,2},{1,3},{2,0},{3,1},{4,6},{5,7},{6,4},{7,5},{8,10},{9,11},{10,... | collective-permute-start | bytes 1572872 | tf_op jit(solution)/shard_map/ppermute | solution.py:138
  155.4 23.4 %collective-permute-start.5 = (f32[32,16,256]{2,1,0:T(8,128)}, f32[32,16,256]{2,1,0:T(8,128)S(1)}, u32[]{:S(2)}, u32[]{:S(2)}) collective-permute-start(f32[32,16,256]{2,1,0:T(8,128)} %shard_map.68), channel_id=1, source_target_pairs={{0,3},{1,0},{2,1},{3,2},{4,7},{5,4},{6,5},{7,6},{8,11},{9,8},{10,9... | collective-permute-start | bytes 1572872 | tf_op jit(solution)/shard_map/ppermute | solution.py:138
  156.2 24.6 %copy-start.9 = (bf16[96,256]{1,0:T(8,128)(2,1)}, bf16[96,256]{1,0:T(8,128)(2,1)S(1)}, u32[]{:S(2)}) copy-start(bf16[96,256]{1,0:T(8,128)(2,1)S(1)} %constant_dynamic-update-slice_fusion.stacked_ref) | copy-start | bytes 147460
  157.5 41.0 %all-to-all-start.1 = ((f32[128,1,1]{2,1,0:T(1,128)}), f32[128,1,1]{2,1,0:T(1,128)S(1)}, u32[]{:S(2)}, u32[]{:S(2)}) async-start(f32[128,1,1]{2,1,0:T(1,128)} %broadcast_in_dim.12), calls=%async_computation.1 | async-start | bytes 131072 | tf_op jit(solution)/shard_map/all_to_all | solution.py:144
  199.7 18.4 %all-to-all-start.3 = ((f32[128,1,1]{2,1,0:T(1,128)}), f32[128,1,1]{2,1,0:T(1,128)S(1)}, u32[]{:S(2)}, u32[]{:S(2)}) async-start(f32[128,1,1]{2,1,0:T(1,128)} %broadcast_in_dim.26), calls=%async_computation.3 | async-start | bytes 131072 | tf_op jit(solution)/shard_map/all_to_all | solution.py:144
  238.7 29.9 %collective-permute-start.6 = (f32[32,16,256]{2,1,0:T(8,128)}, f32[32,16,256]{2,1,0:T(8,128)S(1)}, u32[]{:S(2)}, u32[]{:S(2)}) collective-permute-start(f32[32,16,256]{2,1,0:T(8,128)} %shard_map.70), channel_id=1, source_target_pairs={{0,1},{1,2},{2,3},{3,0},{4,5},{5,6},{6,7},{7,4},{8,9},{9,10},{10,1... | collective-permute-start | bytes 1572872 | tf_op jit(solution)/shard_map/ppermute | solution.py:138
  239.3 29.4 %collective-permute-start.7 = (f32[32,16,256]{2,1,0:T(8,128)}, f32[32,16,256]{2,1,0:T(8,128)S(1)}, u32[]{:S(2)}, u32[]{:S(2)}) collective-permute-start(f32[32,16,256]{2,1,0:T(8,128)} %shard_map.70), channel_id=1, source_target_pairs={{0,2},{1,3},{2,0},{3,1},{4,6},{5,7},{6,4},{7,5},{8,10},{9,11},{10,... | collective-permute-start | bytes 1572872 | tf_op jit(solution)/shard_map/ppermute | solution.py:138
  240.7 27.9 %collective-permute-start.8 = (f32[32,16,256]{2,1,0:T(8,128)}, f32[32,16,256]{2,1,0:T(8,128)S(1)}, u32[]{:S(2)}, u32[]{:S(2)}) collective-permute-start(f32[32,16,256]{2,1,0:T(8,128)} %shard_map.70), channel_id=1, source_target_pairs={{0,3},{1,0},{2,1},{3,2},{4,7},{5,4},{6,5},{7,6},{8,11},{9,8},{10,9... | collective-permute-start | bytes 1572872 | tf_op jit(solution)/shard_map/ppermute | solution.py:138
  270.7 16.1 %copy-start.3 = (f32[512,256]{1,0:T(8,128)S(1)}, f32[512,256]{1,0:T(8,128)}, u32[]{:S(2)}) copy-start(f32[512,256]{1,0:T(8,128)} %shard_map.69) | copy-start | bytes 1572868
  323.3 29.7 %collective-permute-start.10 = (f32[32,16,256]{2,1,0:T(8,128)}, f32[32,16,256]{2,1,0:T(8,128)S(1)}, u32[]{:S(2)}, u32[]{:S(2)}) collective-permute-start(f32[32,16,256]{2,1,0:T(8,128)} %shard_map.72), channel_id=1, source_target_pairs={{0,2},{1,3},{2,0},{3,1},{4,6},{5,7},{6,4},{7,5},{8,10},{9,11},{10,... | collective-permute-start | bytes 1572872 | tf_op jit(solution)/shard_map/ppermute | solution.py:138
  324.4 28.6 %collective-permute-start.11 = (f32[32,16,256]{2,1,0:T(8,128)}, f32[32,16,256]{2,1,0:T(8,128)S(1)}, u32[]{:S(2)}, u32[]{:S(2)}) collective-permute-start(f32[32,16,256]{2,1,0:T(8,128)} %shard_map.72), channel_id=1, source_target_pairs={{0,3},{1,0},{2,1},{3,2},{4,7},{5,4},{6,5},{7,6},{8,11},{9,8},{10,9... | collective-permute-start | bytes 1572872 | tf_op jit(solution)/shard_map/ppermute | solution.py:138
  326.3 26.8 %collective-permute-start.9 = (f32[32,16,256]{2,1,0:T(8,128)}, f32[32,16,256]{2,1,0:T(8,128)}, u32[]{:S(2)}, u32[]{:S(2)}) collective-permute-start(f32[32,16,256]{2,1,0:T(8,128)} %shard_map.72), channel_id=1, source_target_pairs={{0,1},{1,2},{2,3},{3,0},{4,5},{5,6},{6,7},{7,4},{8,9},{9,10},{10,1... | collective-permute-start | bytes 1572872 | tf_op jit(solution)/shard_map/ppermute | solution.py:138

commit v9 on v8

--- a/solution.py
+++ b/solution.py
@@ -21,7 +21,7 @@
 def gathered(parts_ref, block, hits):
     start = pl.multiple_of(block * BLK, BLK)
     total = None
-    for k in range(3):
+    for k in range(parts_ref.shape[0]):
         term = jnp.dot(hits, parts_ref[k, pl.ds(start, BLK), :], preferred_element_type=jnp.float32)
         total = term if total is None else total + term
     return total
@@ -88,10 +88,10 @@
     groups, run_length, channels = noise_weights.shape
     modes = modes_t.shape[0]
     steps = groups // RUNS
-    parts = jnp.stack(split3(field))
+    parts = jnp.stack(split3(field)[:2])
     full = pl.BlockSpec(parts.shape, lambda i, b: (0, 0, 0))
     per_run = lambda *shape: pl.BlockSpec((RUNS,) + shape, lambda i, b: (i, 0, 0))
-    gather_flops = groups * 3 * 2 * run_length * BLK * channels
+    gather_flops = groups * 2 * 2 * run_length * BLK * channels
     amps = pl.pallas_call(
         amp_kernel,
         grid_spec=pltpu.PrefetchScalarGridSpec(

time: 398 us -> 386 us (0.970)
  Pallas kernels: 94.4 us -> 83.7 us
    pallas_call x3, Pallas kernels: 47.8 us -> 40.8 us  [owner_operator(): pl.pallas_call(bin_kernel, grid_spec=pltpu.PrefetchScalarGridSpec(num_sca...]
where the time goes in v9:
time: 386 us; the launch traced here: 381 us
  waiting for transfers between devices  90.8 us (24%)
  Pallas kernels  83.7 us (22%)
  blocking collectives  76.5 us (20%)
  starting transfers between devices  50.5 us (13%)
  other arithmetic  32.7 us (8%)
  matrix products  28.6 us (7%)
  local copies, waits for them, and re-layouts  10.3 us (3%)
  between operations  7.75 us (2%)
    all_to_all x4, blocking collectives, global_sum(): lax.all_to_all(jnp.broadcast_to(value, (everyone, 1)), ('tm', 'chan'), 0,...  76.5 us
    all_to_all x1, waiting for transfers between devices, per_device(): arrived = lax.all_to_all(local_partial, 'tm', 0, 0, tiled=True)  43.5 us
    pallas_call x3, Pallas kernels, owner_operator(): pl.pallas_call(amp_kernel, grid_spec=pltpu.PrefetchScalarGridSpec(num_sca...  43 us
    pallas_call x3, Pallas kernels, owner_operator(): pl.pallas_call(bin_kernel, grid_spec=pltpu.PrefetchScalarGridSpec(num_sca...  40.8 us
    ppermute x12, waiting for transfers between devices, chan_sum(): total = total + lax.ppermute(value, 'chan', pairs)  35.6 us
    ppermute x12, starting transfers between devices, chan_sum(): total = total + lax.ppermute(value, 'chan', pairs)  17.7 us
    all_to_all x2, starting transfers between devices, global_sum(): lax.all_to_all(jnp.broadcast_to(value, (everyone, 1)), ('tm', 'chan'), 0,...  16.5 us
    dot_general x1, matrix products, filtered(): jnp.einsum('csk,km->mcs', weighted, foreground_modes, precision=highest)  10.2 us
  transfers between devices with their start and end apart: 16, of which 7 were waited for; matrix products, arithmetic and copies ran while one was open for 10% of the time, Pallas kernels for 4%

profile of v9, /device:TPU:1, one launch (start us, length us, event | category | flops | bytes accessed | tf_op | source)
XLA Modules:
  0.0 380.9 jit_solution(18092060738758313837)
XLA Ops:
  0.6 0.8 convert_element_type.85
  1.4 4.5 %pad_maximum_fusion = bf16[32,257,256]{2,1,0:T(8,128)(2,1)} fusion(bf16[32,1,256]{2,1,0:T(2,128)(2,1)S(1)} %convert_element_type.99, bf16[32,256,256]{2,1,0:T(8,128)(2,1)} %bitcast.69), kind=kLoop, calls=%fused_computation.5 | loop fusion | flops 8421376 | bytes 8421376 | tf_op jit(solution)/shard_map/concatenate | solution.py:160
  6.0 8.8 %all-to-all-start.2 = ((bf16[32,257,256]{2,1,0:T(8,128)(2,1)}), bf16[32,257,256]{2,1,0:T(8,128)(2,1)}, u32[]{:S(2)}, u32[]{:S(2)}) async-start(bf16[32,257,256]{2,1,0:T(8,128)(2,1)} %pad_maximum_fusion), calls=%async_computation.2 | async-start | bytes 8650752 | tf_op jit(solution)/shard_map/all_to_all | solution.py:161
  14.7 10.2 %fusion.7 = f32[16,32,256]{2,0,1:T(8,128)S(1)} fusion(bf16[32,256,256]{2,1,0:T(8,128)(2,1)} %bitcast.70, bf16[32,256,256]{2,1,0:T(8,128)(2,1)} %bitcast.73, f32[256,16]{0,1:T(8,128)S(1)} %copy-done.4), kind=kOutput, calls=%fused_computation.12 | convolution fusion | flops 408944640 | bytes 8929280 | tf_op jit(solution)/shard_map/csk,km->mcs/dot_general | solution.py:179
  24.9 1.7 collective-permute-start
  26.6 3.3 collective-permute-start.1
  29.9 0.9 collective-permute-start.2
  30.8 10.0 %collective-permute-done = f32[16,32,256]{2,0,1:T(8,128)S(1)} collective-permute-done((f32[16,32,256]{2,0,1:T(8,128)S(1)}, f32[16,32,256]{2,0,1:T(8,128)S(1)}, u32[]{:S(2)}, u32[]{:S(2)}) %collective-permute-start) | collective-permute-done | bytes 524320 | tf_op jit(solution)/shard_map/ppermute | solution.py:138
  40.8 12.1 %collective-permute-done.1 = f32[16,32,256]{2,0,1:T(8,128)S(1)} collective-permute-done((f32[16,32,256]{2,0,1:T(8,128)S(1)}, f32[16,32,256]{2,0,1:T(8,128)S(1)}, u32[]{:S(2)}, u32[]{:S(2)}) %collective-permute-start.1) | collective-permute-done | bytes 524320 | tf_op jit(solution)/shard_map/ppermute | solution.py:138
  53.0 7.1 %fusion.18 = f32[32,256,256]{2,1,0:T(8,128)S(1)} fusion(f32[16,32,256]{2,0,1:T(8,128)S(1)} %collective-permute-done.2, f32[16,32,256]{2,0,1:T(8,128)S(1)} %collective-permute-done.1, f32[16,32,256]{2,0,1:T(8,128)S(1)} %fusion.7, f32[16,32,256]{2,0,1:T(8,128)S(1)} %collective-permute-done, f32[256,16]{0,1:T(8,128)S(1)} %copy-done.4), kind=kOutput, calls=%fused_computation.50 | convolution fusion | flops 403046400 | bytes 10502144 | tf_op jit(solution)/shard_map/mcs,km->csk/dot_general | solution.py:182
  60.1 5.5 %fusion = f32[32,128,256]{2,1,0:T(8,128)} fusion(bf16[32,256,256]{2,1,0:T(8,128)(2,1)S(1)} %bitcast.71, f32[32,256,256]{2,1,0:T(8,128)S(1)} %fusion.18, bf16[32,256,256]{2,1,0:T(8,128)(2,1)S(1)} %bitcast.74, s32[32,256]{1,0:T(8,128)S(1)} %eq.47), kind=kOutput, calls=%fused_computation.2 | convolution fusion | flops 1622147072 | bytes 21004288 | tf_op jit(solution)/shard_map/csp,csk->cpk/dot_general | solution.py:221
  65.6 2.8 all-to-all-done.2
  68.4 7.6 %all-to-all-start = ((f32[32,128,256]{2,1,0:T(8,128)}), f32[32,128,256]{2,1,0:T(8,128)}, u32[]{:S(2)}, u32[]{:S(2)}) async-start(f32[32,128,256]{2,1,0:T(8,128)} %fusion), calls=%async_computation | async-start | bytes 8388608 | tf_op jit(solution)/shard_map/all_to_all | solution.py:222
  76.2 0.9 slice_convert_fusion.rows_ref
  77.1 4.6 %slice.9.weights_ref = bf16[32,256,256]{2,1,0:T(8,128)(2,1)} slice(bf16[32,257,256]{2,1,0:T(8,128)(2,1)} %all-to-all-done.2), slice={[0:32], [0:256], [0:256]} | slice | bytes 8388608 | tf_op jit(solution)/shard_map/slice | solution.py:162
  81.8 2.6 fusion.5.hits_ref
  84.4 43.5 %all-to-all-done = f32[32,128,256]{2,1,0:T(8,128)} async-done(((f32[32,128,256]{2,1,0:T(8,128)}), f32[32,128,256]{2,1,0:T(8,128)}, u32[]{:S(2)}, u32[]{:S(2)}) %all-to-all-start) | async-done | bytes 4194336 | tf_op jit(solution)/shard_map/all_to_all | solution.py:222
  127.9 5.8 %multiply_reduce_fusion.4 = (f32[]{:T(128)}, f32[4,128,256]{2,0,1:T(4,128)S(1)}) fusion(f32[32,128,256]{2,1,0:T(8,128)} %all-to-all-done, s32[32]{0:T(128)S(1)} %dynamic-slice_reduce_fusion.blocks_ref), kind=kOutput, calls=%fused_computation.49 | convolution fusion | flops 25428096 | bytes 4718724 | tf_op jit(solution)/shard_map/cb,cpk->bpk/dot_general | solution.py:223
  133.9 0.8 pad_maximum_fusion.1.parts_ref
  134.7 14.3 %shard_map.68 = f32[32,16,256]{2,1,0:T(8,128)} custom-call(s32[32]{0:T(128)} %copy-done.8, bf16[2,512,256]{2,1,0:T(8,128)(2,1)} %pad_maximum_fusion.1.parts_ref, bf16[32,256,128]{2,1,0:T(8,128)(2,1)} %fusion.5.hits_ref, bf16[32,256,256]{2,1,0:T(8,128)(2,1)} %slice.9.weights_ref, f32[16,256]{1,0:T(8,128)} %bitcast.75), custom_call_target="tpu_custom_call" | custom-call | flops 1476395008 | bytes 4718592 | tf_op jit(solution)/shard_map/pallas_call | solution.py:95
  149.0 1.6 collective-permute-start.3
  150.7 3.3 collective-permute-start.4
  154.0 0.7 collective-permute-start.5
  154.8 1.3 broadcast_in_dim.12
  156.1 7.8 %all-to-all-start.1 = ((f32[128,1,1]{2,1,0:T(1,128)}), f32[128,1,1]{2,1,0:T(1,128)S(1)}, u32[]{:S(2)}, u32[]{:S(2)}) async-start(f32[128,1,1]{2,1,0:T(1,128)} %broadcast_in_dim.12), calls=%async_computation.1 | async-start | bytes 131072 | tf_op jit(solution)/shard_map/all_to_all | solution.py:144
  163.9 0.7 collective-permute-done.3
  164.6 12.8 %collective-permute-done.4 = f32[32,16,256]{2,1,0:T(8,128)S(1)} collective-permute-done((f32[32,16,256]{2,1,0:T(8,128)}, f32[32,16,256]{2,1,0:T(8,128)S(1)}, u32[]{:S(2)}, u32[]{:S(2)}) %collective-permute-start.4) | collective-permute-done | bytes 524320 | tf_op jit(solution)/shard_map/ppermute | solution.py:138
  177.4 2.0 add_add_fusion.2.amp_ref
  179.4 13.5 %shard_map.69 = f32[512,256]{1,0:T(8,128)} custom-call(s32[32]{0:T(128)} %copy-done.8, bf16[2,512,256]{2,1,0:T(8,128)(2,1)} %pad_maximum_fusion.1.parts_ref, bf16[32,256,128]{2,1,0:T(8,128)(2,1)} %fusion.5.hits_ref, s32[32,1,256]{2,1,0:T(1,128)} %copy-done.7, bf16[32,256,256]{2,1,0:T(8,128)(2,1)} %slice.9.weights_ref, f32[32,16,256]{2,1,0:T(8,128)} %add_add_fusion.2.amp_ref, ...), custom_call_target="tpu_custom_call" | custom-call | flops 2550136832 | bytes 5242880 | tf_op jit(solution)/shard_map/pallas_call | solution.py:114
  192.9 1.8 fusion.14
  194.8 1.3 broadcast_in_dim.26
  196.1 8.8 %all-to-all-start.3 = ((f32[128,1,1]{2,1,0:T(1,128)}), f32[128,1,1]{2,1,0:T(1,128)S(1)}, u32[]{:S(2)}, u32[]{:S(2)}) async-start(f32[128,1,1]{2,1,0:T(1,128)} %broadcast_in_dim.26), calls=%async_computation.3 | async-start | bytes 131072 | tf_op jit(solution)/shard_map/all_to_all | solution.py:144
  204.8 0.7 reduce_sum.109
  205.6 8.9 %all-to-all-done.3 = f32[128,1,1]{2,1,0:T(1,128)S(1)} async-done(((f32[128,1,1]{2,1,0:T(1,128)}), f32[128,1,1]{2,1,0:T(1,128)S(1)}, u32[]{:S(2)}, u32[]{:S(2)}) %all-to-all-start.3) | async-done | bytes 544 | tf_op jit(solution)/shard_map/all_to_all | solution.py:144
  214.5 0.7 reduce_sum.111
  216.5 1.9 multiply_reduce_fusion.3
  218.5 0.8 pad_maximum_fusion.2.parts_ref
  219.3 14.3 %shard_map.70 = f32[32,16,256]{2,1,0:T(8,128)} custom-call(s32[32]{0:T(128)} %copy-done.8, bf16[2,512,256]{2,1,0:T(8,128)(2,1)} %pad_maximum_fusion.2.parts_ref, bf16[32,256,128]{2,1,0:T(8,128)(2,1)} %fusion.5.hits_ref, bf16[32,256,256]{2,1,0:T(8,128)(2,1)} %slice.9.weights_ref, f32[16,256]{1,0:T(8,128)} %bitcast.76), custom_call_target="tpu_custom_call" | custom-call | flops 1476395008 | bytes 4718592 | tf_op jit(solution)/shard_map/pallas_call | solution.py:95
  234.2 1.4 collective-permute-start.7
  235.6 1.2 collective-permute-start.8
  236.8 0.7 broadcast_in_dim.27
  237.5 24.1 %all_to_all.46 = f32[128,1,1]{2,1,0:T(1,128)S(1)} all-to-all(f32[128,1,1]{2,1,0:T(1,128)S(1)} %broadcast_in_dim.27), channel_id=1, replica_groups=mesh['tm'=32,'chan'=4] {'tm','chan'}, dimensions={0} | all-to-all | bytes 1024 | tf_op jit(solution)/shard_map/all_to_all | solution.py:144
  261.5 0.7 reduce_sum.113
  263.6 2.1 add_add_fusion.1.amp_ref
  265.6 13.7 %shard_map.71 = f32[512,256]{1,0:T(8,128)} custom-call(s32[32]{0:T(128)} %copy-done.8, bf16[2,512,256]{2,1,0:T(8,128)(2,1)} %pad_maximum_fusion.2.parts_ref, bf16[32,256,128]{2,1,0:T(8,128)(2,1)} %fusion.5.hits_ref, s32[32,1,256]{2,1,0:T(1,128)} %copy-done.7, bf16[32,256,256]{2,1,0:T(8,128)(2,1)} %slice.9.weights_ref, f32[32,16,256]{2,1,0:T(8,128)} %add_add_fusion.1.amp_ref, ...), custom_call_target="tpu_custom_call" | custom-call | flops 2550136832 | bytes 5242880 | tf_op jit(solution)/shard_map/pallas_call | solution.py:114
  279.3 1.8 multiply_reduce_fusion.2
  281.1 0.7 broadcast_in_dim.28
  281.8 14.8 %all_to_all.47 = f32[128,1,1]{2,1,0:T(1,128)S(1)} all-to-all(f32[128,1,1]{2,1,0:T(1,128)S(1)} %broadcast_in_dim.28), channel_id=1, replica_groups=mesh['tm'=32,'chan'=4] {'tm','chan'}, dimensions={0} | all-to-all | bytes 1024 | tf_op jit(solution)/shard_map/all_to_all | solution.py:144
  296.6 0.7 reduce_sum.115
  298.7 0.8 fusion.22
  299.4 0.8 pad_maximum_fusion.3.parts_ref
  300.3 14.3 %shard_map.72 = f32[32,16,256]{2,1,0:T(8,128)} custom-call(s32[32]{0:T(128)} %copy-done.8, bf16[2,512,256]{2,1,0:T(8,128)(2,1)} %pad_maximum_fusion.3.parts_ref, bf16[32,256,128]{2,1,0:T(8,128)(2,1)} %fusion.5.hits_ref, bf16[32,256,256]{2,1,0:T(8,128)(2,1)} %slice.9.weights_ref, f32[16,256]{1,0:T(8,128)} %bitcast.77), custom_call_target="tpu_custom_call" | custom-call | flops 1476395008 | bytes 4718592 | tf_op jit(solution)/shard_map/pallas_call | solution.py:95
  314.6 1.1 collective-permute-start.10
  315.7 1.9 collective-permute-start.11
  317.5 0.7 broadcast_in_dim.29
  318.2 24.1 %all_to_all.48 = f32[128,1,1]{2,1,0:T(1,128)S(1)} all-to-all(f32[128,1,1]{2,1,0:T(1,128)S(1)} %broadcast_in_dim.29), channel_id=1, replica_groups=mesh['tm'=32,'chan'=4] {'tm','chan'}, dimensions={0} | all-to-all | bytes 1024 | tf_op jit(solution)/shard_map/all_to_all | solution.py:144
  342.3 0.7 reduce_sum.117
  344.3 2.2 add_add_fusion.amp_ref
  346.5 13.5 %shard_map.73 = f32[512,256]{1,0:T(8,128)} custom-call(s32[32]{0:T(128)} %copy-done.8, bf16[2,512,256]{2,1,0:T(8,128)(2,1)} %pad_maximum_fusion.3.parts_ref, bf16[32,256,128]{2,1,0:T(8,128)(2,1)} %fusion.5.hits_ref, s32[32,1,256]{2,1,0:T(1,128)} %copy-done.7, bf16[32,256,256]{2,1,0:T(8,128)(2,1)} %slice.9.weights_ref, f32[32,16,256]{2,1,0:T(8,128)} %add_add_fusion.amp_ref, ...), custom_call_target="tpu_custom_call" | custom-call | flops 2550136832 | bytes 5242880 | tf_op jit(solution)/shard_map/pallas_call | solution.py:114
  360.0 1.8 multiply_reduce_fusion
  361.8 0.7 broadcast_in_dim.30
  362.5 13.6 %all_to_all.49 = f32[128,1,1]{2,1,0:T(1,128)S(1)} all-to-all(f32[128,1,1]{2,1,0:T(1,128)S(1)} %broadcast_in_dim.30), channel_id=1, replica_groups=mesh['tm'=32,'chan'=4] {'tm','chan'}, dimensions={0} | all-to-all | bytes 1024 | tf_op jit(solution)/shard_map/all_to_all | solution.py:144
  376.1 0.7 reduce_sum.119
  378.2 2.2 multiply_subtract_fusion
  (45 shorter events, 1.2 us)
Async XLA Ops:
  0.6 75.3 %copy-start = (s32[32,32]{1,0:T(8,128)S(1)}, s32[32,32]{1,0:T(8,128)}, u32[]{:S(2)}) copy-start(s32[32,32]{1,0:T(8,128)} %param.8) | copy-start | bytes 12292
  6.0 8.8 %copy-start.4 = (f32[256,16]{0,1:T(8,128)S(1)}, f32[256,16]{0,1:T(8,128)}, u32[]{:S(2)}) copy-start(f32[256,16]{0,1:T(8,128)} %param.9) | copy-start | bytes 49156
  6.0 62.4 %all-to-all-start.2 = ((bf16[32,257,256]{2,1,0:T(8,128)(2,1)}), bf16[32,257,256]{2,1,0:T(8,128)(2,1)}, u32[]{:S(2)}, u32[]{:S(2)}) async-start(bf16[32,257,256]{2,1,0:T(8,128)(2,1)} %pad_maximum_fusion), calls=%async_computation.2 | async-start | bytes 8650752 | tf_op jit(solution)/shard_map/all_to_all | solution.py:161
  14.7 16.1 %copy-start.6 = (s32[8192]{0:T(1024)S(1)}, s32[8192]{0:T(1024)}, u32[]{:S(2)}) copy-start(s32[8192]{0:T(1024)} %param.7) | copy-start | bytes 98308
  24.9 15.9 %collective-permute-start = (f32[16,32,256]{2,0,1:T(8,128)S(1)}, f32[16,32,256]{2,0,1:T(8,128)S(1)}, u32[]{:S(2)}, u32[]{:S(2)}) collective-permute-start(f32[16,32,256]{2,0,1:T(8,128)S(1)} %fusion.7), channel_id=1, source_target_pairs={{0,1},{1,2},{2,3},{3,0},{4,5},{5,6},{6,7},{7,4},{8,9},{9,10},{10,1... | collective-permute-start | bytes 1572872 | tf_op jit(solution)/shard_map/ppermute | solution.py:138
  26.6 26.4 %collective-permute-start.1 = (f32[16,32,256]{2,0,1:T(8,128)S(1)}, f32[16,32,256]{2,0,1:T(8,128)S(1)}, u32[]{:S(2)}, u32[]{:S(2)}) collective-permute-start(f32[16,32,256]{2,0,1:T(8,128)S(1)} %fusion.7), channel_id=1, source_target_pairs={{0,2},{1,3},{2,0},{3,1},{4,6},{5,7},{6,4},{7,5},{8,10},{9,11},{10,... | collective-permute-start | bytes 1572872 | tf_op jit(solution)/shard_map/ppermute | solution.py:138
  29.9 23.1 %collective-permute-start.2 = (f32[16,32,256]{2,0,1:T(8,128)S(1)}, f32[16,32,256]{2,0,1:T(8,128)S(1)}, u32[]{:S(2)}, u32[]{:S(2)}) collective-permute-start(f32[16,32,256]{2,0,1:T(8,128)S(1)} %fusion.7), channel_id=1, source_target_pairs={{0,3},{1,0},{2,1},{3,2},{4,7},{5,4},{6,5},{7,6},{8,11},{9,8},{10,9... | collective-permute-start | bytes 1572872 | tf_op jit(solution)/shard_map/ppermute | solution.py:138
  30.8 29.2 %copy-start.1 = (bf16[8192,256]{1,0:T(8,128)(2,1)S(1)}, bf16[8192,256]{1,0:T(8,128)(2,1)}, u32[]{:S(2)}) copy-start(bf16[8192,256]{1,0:T(8,128)(2,1)} %param.6) | copy-start | bytes 12582916
  30.8 29.2 %copy-start.2 = (bf16[8192,256]{1,0:T(8,128)(2,1)S(1)}, bf16[8192,256]{1,0:T(8,128)(2,1)}, u32[]{:S(2)}) copy-start(bf16[8192,256]{1,0:T(8,128)(2,1)} %param.5) | copy-start | bytes 12582916
  68.4 59.5 %all-to-all-start = ((f32[32,128,256]{2,1,0:T(8,128)}), f32[32,128,256]{2,1,0:T(8,128)}, u32[]{:S(2)}, u32[]{:S(2)}) async-start(f32[32,128,256]{2,1,0:T(8,128)} %fusion), calls=%async_computation | async-start | bytes 8388608 | tf_op jit(solution)/shard_map/all_to_all | solution.py:222
  76.1 51.7 %copy-start.8 = (s32[32]{0:T(128)}, s32[32]{0:T(128)S(1)}, u32[]{:S(2)}) copy-start(s32[32]{0:T(128)S(1)} %dynamic-slice_reduce_fusion.blocks_ref) | copy-start | bytes 388
  77.1 4.6 %copy-start.7 = (s32[32,1,256]{2,1,0:T(1,128)}, s32[32,1,256]{2,1,0:T(1,128)S(1)}, u32[]{:S(2)}) copy-start(s32[32,1,256]{2,1,0:T(1,128)S(1)} %slice_convert_fusion.rows_ref) | copy-start | bytes 98308
  133.9 20.8 %copy-start.5 = (f32[256,16]{0,1:T(8,128)S(1)}, f32[256,16]{0,1:T(8,128)}, u32[]{:S(2)}) copy-start(f32[256,16]{0,1:T(8,128)} %param.9) | copy-start | bytes 49156
  149.0 15.5 %collective-permute-start.3 = (f32[32,16,256]{2,1,0:T(8,128)}, f32[32,16,256]{2,1,0:T(8,128)S(1)}, u32[]{:S(2)}, u32[]{:S(2)}) collective-permute-start(f32[32,16,256]{2,1,0:T(8,128)} %shard_map.68), channel_id=1, source_target_pairs={{0,1},{1,2},{2,3},{3,0},{4,5},{5,6},{6,7},{7,4},{8,9},{9,10},{10,1... | collective-permute-start | bytes 1572872 | tf_op jit(solution)/shard_map/ppermute | solution.py:138
  150.7 26.7 %collective-permute-start.4 = (f32[32,16,256]{2,1,0:T(8,128)}, f32[32,16,256]{2,1,0:T(8,128)S(1)}, u32[]{:S(2)}, u32[]{:S(2)}) collective-permute-start(f32[32,16,256]{2,1,0:T(8,128)} %shard_map.68), channel_id=1, source_target_pairs={{0,2},{1,3},{2,0},{3,1},{4,6},{5,7},{6,4},{7,5},{8,10},{9,11},{10,... | collective-permute-start | bytes 1572872 | tf_op jit(solution)/shard_map/ppermute | solution.py:138
  154.0 23.4 %collective-permute-start.5 = (f32[32,16,256]{2,1,0:T(8,128)}, f32[32,16,256]{2,1,0:T(8,128)S(1)}, u32[]{:S(2)}, u32[]{:S(2)}) collective-permute-start(f32[32,16,256]{2,1,0:T(8,128)} %shard_map.68), channel_id=1, source_target_pairs={{0,3},{1,0},{2,1},{3,2},{4,7},{5,4},{6,5},{7,6},{8,11},{9,8},{10,9... | collective-permute-start | bytes 1572872 | tf_op jit(solution)/shard_map/ppermute | solution.py:138
  154.8 24.6 %copy-start.9 = (bf16[96,256]{1,0:T(8,128)(2,1)}, bf16[96,256]{1,0:T(8,128)(2,1)S(1)}, u32[]{:S(2)}) copy-start(bf16[96,256]{1,0:T(8,128)(2,1)S(1)} %constant_dynamic-update-slice_fusion.stacked_ref) | copy-start | bytes 147460
  156.1 38.7 %all-to-all-start.1 = ((f32[128,1,1]{2,1,0:T(1,128)}), f32[128,1,1]{2,1,0:T(1,128)S(1)}, u32[]{:S(2)}, u32[]{:S(2)}) async-start(f32[128,1,1]{2,1,0:T(1,128)} %broadcast_in_dim.12), calls=%async_computation.1 | async-start | bytes 131072 | tf_op jit(solution)/shard_map/all_to_all | solution.py:144
  196.1 18.4 %all-to-all-start.3 = ((f32[128,1,1]{2,1,0:T(1,128)}), f32[128,1,1]{2,1,0:T(1,128)S(1)}, u32[]{:S(2)}, u32[]{:S(2)}) async-start(f32[128,1,1]{2,1,0:T(1,128)} %broadcast_in_dim.26), calls=%async_computation.3 | async-start | bytes 131072 | tf_op jit(solution)/shard_map/all_to_all | solution.py:144
  233.6 29.9 %collective-permute-start.6 = (f32[32,16,256]{2,1,0:T(8,128)}, f32[32,16,256]{2,1,0:T(8,128)S(1)}, u32[]{:S(2)}, u32[]{:S(2)}) collective-permute-start(f32[32,16,256]{2,1,0:T(8,128)} %shard_map.70), channel_id=1, source_target_pairs={{0,1},{1,2},{2,3},{3,0},{4,5},{5,6},{6,7},{7,4},{8,9},{9,10},{10,1... | collective-permute-start | bytes 1572872 | tf_op jit(solution)/shard_map/ppermute | solution.py:138
  234.2 29.4 %collective-permute-start.7 = (f32[32,16,256]{2,1,0:T(8,128)}, f32[32,16,256]{2,1,0:T(8,128)S(1)}, u32[]{:S(2)}, u32[]{:S(2)}) collective-permute-start(f32[32,16,256]{2,1,0:T(8,128)} %shard_map.70), channel_id=1, source_target_pairs={{0,2},{1,3},{2,0},{3,1},{4,6},{5,7},{6,4},{7,5},{8,10},{9,11},{10,... | collective-permute-start | bytes 1572872 | tf_op jit(solution)/shard_map/ppermute | solution.py:138
  235.6 27.9 %collective-permute-start.8 = (f32[32,16,256]{2,1,0:T(8,128)}, f32[32,16,256]{2,1,0:T(8,128)S(1)}, u32[]{:S(2)}, u32[]{:S(2)}) collective-permute-start(f32[32,16,256]{2,1,0:T(8,128)} %shard_map.70), channel_id=1, source_target_pairs={{0,3},{1,0},{2,1},{3,2},{4,7},{5,4},{6,5},{7,6},{8,11},{9,8},{10,9... | collective-permute-start | bytes 1572872 | tf_op jit(solution)/shard_map/ppermute | solution.py:138
  265.6 13.7 %copy-start.3 = (f32[512,256]{1,0:T(8,128)S(1)}, f32[512,256]{1,0:T(8,128)}, u32[]{:S(2)}) copy-start(f32[512,256]{1,0:T(8,128)} %shard_map.69) | copy-start | bytes 1572868
  314.6 29.7 %collective-permute-start.10 = (f32[32,16,256]{2,1,0:T(8,128)}, f32[32,16,256]{2,1,0:T(8,128)S(1)}, u32[]{:S(2)}, u32[]{:S(2)}) collective-permute-start(f32[32,16,256]{2,1,0:T(8,128)} %shard_map.72), channel_id=1, source_target_pairs={{0,2},{1,3},{2,0},{3,1},{4,6},{5,7},{6,4},{7,5},{8,10},{9,11},{10,... | collective-permute-start | bytes 1572872 | tf_op jit(solution)/shard_map/ppermute | solution.py:138
  315.7 28.6 %collective-permute-start.11 = (f32[32,16,256]{2,1,0:T(8,128)}, f32[32,16,256]{2,1,0:T(8,128)S(1)}, u32[]{:S(2)}, u32[]{:S(2)}) collective-permute-start(f32[32,16,256]{2,1,0:T(8,128)} %shard_map.72), channel_id=1, source_target_pairs={{0,3},{1,0},{2,1},{3,2},{4,7},{5,4},{6,5},{7,6},{8,11},{9,8},{10,9... | collective-permute-start | bytes 1572872 | tf_op jit(solution)/shard_map/ppermute | solution.py:138
  317.5 26.7 %collective-permute-start.9 = (f32[32,16,256]{2,1,0:T(8,128)}, f32[32,16,256]{2,1,0:T(8,128)}, u32[]{:S(2)}, u32[]{:S(2)}) collective-permute-start(f32[32,16,256]{2,1,0:T(8,128)} %shard_map.72), channel_id=1, source_target_pairs={{0,1},{1,2},{2,3},{3,0},{4,5},{5,6},{6,7},{7,4},{8,9},{9,10},{10,1... | collective-permute-start | bytes 1572872 | tf_op jit(solution)/shard_map/ppermute | solution.py:138

commit v10 on v9

--- a/solution.py
+++ b/solution.py
@@ -27,8 +27,8 @@
     return total
 
 
-def amp_kernel(blocks_ref, parts_ref, hits_ref, weights_ref, modes_t_ref, amp_ref):
-    step = pl.program_id(0)
+def amp_kernel(offset, blocks_ref, parts_ref, hits_ref, weights_ref, modes_t_ref, amp_ref):
+    step = pl.program_id(0) + offset
     for j in range(RUNS):
         x = gathered(parts_ref, blocks_ref[step * RUNS + j], hits_ref[j])
         y = weights_ref[j].astype(jnp.float32) * x
@@ -38,10 +38,10 @@
         )
 
 
-def bin_kernel(blocks_ref, parts_ref, hits_ref, rows_ref, weights_ref, amp_ref, stacked_ref, out_ref):
-    step = pl.program_id(0)
-
-    @pl.when(step == 0)
+def bin_kernel(offset, blocks_ref, parts_ref, hits_ref, rows_ref, weights_ref, amp_ref, stacked_ref, out_ref):
+    step = pl.program_id(0) + offset
+
+    @pl.when(step == offset)
     def _():
         out_ref[...] = jnp.zeros_like(out_ref)
 
@@ -90,44 +90,52 @@
     steps = groups // RUNS
     parts = jnp.stack(split3(field)[:2])
     full = pl.BlockSpec(parts.shape, lambda i, b: (0, 0, 0))
-    per_run = lambda *shape: pl.BlockSpec((RUNS,) + shape, lambda i, b: (i, 0, 0))
     gather_flops = groups * 2 * 2 * run_length * BLK * channels
-    amps = pl.pallas_call(
-        amp_kernel,
-        grid_spec=pltpu.PrefetchScalarGridSpec(
-            num_scalar_prefetch=1,
-            grid=(steps,),
-            in_specs=[full, per_run(run_length, BLK), per_run(run_length, channels),
-                      pl.BlockSpec(modes_t.shape, lambda i, b: (0, 0))],
-            out_specs=per_run(modes, run_length),
-        ),
-        out_shape=jax.ShapeDtypeStruct((groups, modes, run_length), jnp.float32),
-        cost_estimate=pl.CostEstimate(
-            flops=gather_flops + groups * 12 * run_length * channels * modes,
-            bytes_accessed=noise_weights.size * 2 + field.size * 4,
-            transcendentals=0,
-        ),
-    )(blocks, parts, hits, noise_weights, modes_t)
-    amps = chan_sum(amps)
     m_high, m_middle, m_low = split3(modes_t)
     stacked = jnp.concatenate([m_high, m_high, m_high, m_middle, m_middle, m_low], axis=0)
-    return pl.pallas_call(
-        bin_kernel,
-        grid_spec=pltpu.PrefetchScalarGridSpec(
-            num_scalar_prefetch=1,
-            grid=(steps,),
-            in_specs=[full, per_run(run_length, BLK), per_run(1, run_length),
-                      per_run(run_length, channels), per_run(modes, run_length),
-                      pl.BlockSpec(stacked.shape, lambda i, b: (0, 0))],
-            out_specs=pl.BlockSpec(field.shape, lambda i, b: (0, 0)),
-        ),
-        out_shape=jax.ShapeDtypeStruct(field.shape, jnp.float32),
-        cost_estimate=pl.CostEstimate(
-            flops=2 * gather_flops + groups * 12 * run_length * channels * modes,
-            bytes_accessed=noise_weights.size * 2 + field.size * 8,
-            transcendentals=0,
-        ),
-    )(blocks, parts, hits, points_row, noise_weights, amps, stacked)
+    halves = 2 if steps % 2 == 0 else 1
+    span = steps // halves
+    binned = None
+    for half in range(halves):
+        offset = half * span
+        per_run = lambda *shape: pl.BlockSpec((RUNS,) + shape, lambda i, b: (i + offset, 0, 0))
+        own_run = lambda *shape: pl.BlockSpec((RUNS,) + shape, lambda i, b: (i, 0, 0))
+        amps = pl.pallas_call(
+            functools.partial(amp_kernel, offset),
+            grid_spec=pltpu.PrefetchScalarGridSpec(
+                num_scalar_prefetch=1,
+                grid=(span,),
+                in_specs=[full, per_run(run_length, BLK), per_run(run_length, channels),
+                          pl.BlockSpec(modes_t.shape, lambda i, b: (0, 0))],
+                out_specs=own_run(modes, run_length),
+            ),
+            out_shape=jax.ShapeDtypeStruct((span * RUNS, modes, run_length), jnp.float32),
+            cost_estimate=pl.CostEstimate(
+                flops=(gather_flops + groups * 12 * run_length * channels * modes) // halves,
+                bytes_accessed=noise_weights.size * 2 // halves + field.size * 4,
+                transcendentals=0,
+            ),
+        )(blocks, parts, hits, noise_weights, modes_t)
+        amps = chan_sum(amps)
+        part = pl.pallas_call(
+            functools.partial(bin_kernel, offset),
+            grid_spec=pltpu.PrefetchScalarGridSpec(
+                num_scalar_prefetch=1,
+                grid=(span,),
+                in_specs=[full, per_run(run_length, BLK), per_run(1, run_length),
+                          per_run(run_length, channels), own_run(modes, run_length),
+                          pl.BlockSpec(stacked.shape, lambda i, b: (0, 0))],
+                out_specs=pl.BlockSpec(field.shape, lambda i, b: (0, 0)),
+            ),
+            out_shape=jax.ShapeDtypeStruct(field.shape, jnp.float32),
+            cost_estimate=pl.CostEstimate(
+                flops=(2 * gather_flops + groups * 12 * run_length * channels * modes) // halves,
+                bytes_accessed=noise_weights.size * 2 // halves + field.size * 8,
+                transcendentals=0,
+            ),
+        )(blocks, parts, hits, points_row, noise_weights, amps, stacked)
+        binned = part if binned is None else binned + part
+    return binned
 
 
 def chan_sum(value):

time: 386 us -> 379 us (0.982)
  blocking collectives: 76.5 us -> 37.2 us
  starting transfers between devices: 50.5 us -> 78.1 us
  Pallas kernels: 83.7 us -> 99.8 us
  waiting for transfers between devices: 90.8 us -> 77.4 us
    all_to_all x4 -> x2, blocking collectives: 76.5 us -> 37.2 us  [global_sum(): lax.all_to_all(jnp.broadcast_to(value, (everyone, 1)), ('tm', 'chan'), 0,...]
    pallas_call x6 -> x12, Pallas kernels: 83.7 us -> 99.8 us  [the longest x6 50.8 us: owner_operator(): pl.pallas_call(functools.partial(amp_kernel, offset), grid_spec=pltpu.Pre...]
    ppermute x12 -> x21, starting transfers between devices: 17.7 us -> 32.5 us  [chan_sum(): total = total + lax.ppermute(value, 'chan', pairs)]
    ppermute x12 -> x21, waiting for transfers between devices: 35.6 us -> 22.3 us  [chan_sum(): total = total + lax.ppermute(value, 'chan', pairs)]
    all_to_all x2 -> x4, starting transfers between devices: 16.5 us -> 29.3 us  [global_sum(): lax.all_to_all(jnp.broadcast_to(value, (everyone, 1)), ('tm', 'chan'), 0,...]
    add x3 -> x6, other arithmetic: 6.31 us -> 7.86 us  [chan_sum(): total = total + lax.ppermute(value, 'chan', pairs)]
    all_to_all x2 -> x4, waiting for transfers between devices: 8.9 us -> 8.91 us  [global_sum(): lax.all_to_all(jnp.broadcast_to(value, (everyone, 1)), ('tm', 'chan'), 0,...]
  transfers between devices with their start and end apart: 16 -> 27, of which waited for: 7 -> 6; matrix products, arithmetic and copies ran while one was open for 10% -> 12% of each run, Pallas kernels for 4% -> 16%
where the time goes in v10:
time: 379 us; the launch traced here: 373 us
  Pallas kernels  99.8 us (26%)
  starting transfers between devices  78.1 us (21%)
  waiting for transfers between devices  77.4 us (20%)
  blocking collectives  37.2 us (10%)
  other arithmetic  33.1 us (9%)
  matrix products  28.6 us (8%)
  local copies, waits for them, and re-layouts  11.5 us (3%)
  between operations  7.34 us (2%)
    pallas_call x6, Pallas kernels, owner_operator(): pl.pallas_call(functools.partial(amp_kernel, offset), grid_spec=pltpu.Pre...  50.8 us
    pallas_call x6, Pallas kernels, owner_operator(): pl.pallas_call(functools.partial(bin_kernel, offset), grid_spec=pltpu.Pre...  49.1 us
    all_to_all x1, waiting for transfers between devices, per_device(): arrived = lax.all_to_all(local_partial, 'tm', 0, 0, tiled=True)  43.4 us
    all_to_all x2, blocking collectives, global_sum(): lax.all_to_all(jnp.broadcast_to(value, (everyone, 1)), ('tm', 'chan'), 0,...  37.2 us
    ppermute x21, starting transfers between devices, chan_sum(): total = total + lax.ppermute(value, 'chan', pairs)  32.5 us
    all_to_all x4, starting transfers between devices, global_sum(): lax.all_to_all(jnp.broadcast_to(value, (everyone, 1)), ('tm', 'chan'), 0,...  29.3 us
    ppermute x21, waiting for transfers between devices, chan_sum(): total = total + lax.ppermute(value, 'chan', pairs)  22.3 us
    dot_general x1, matrix products, filtered(): jnp.einsum('csk,km->mcs', weighted, foreground_modes, precision=highest)  10.2 us
  transfers between devices with their start and end apart: 27, of which 6 were waited for; matrix products, arithmetic and copies ran while one was open for 12% of the time, Pallas kernels for 16%

profile of v10, /device:TPU:1, one launch (start us, length us, event | category | flops | bytes accessed | tf_op | source)
XLA Modules:
  0.0 373.1 jit_solution(12271965155976605865)
XLA Ops:
  1.4 4.6 %pad_maximum_fusion = bf16[32,257,256]{2,1,0:T(8,128)(2,1)} fusion(bf16[32,1,256]{2,1,0:T(2,128)(2,1)S(1)} %convert_element_type.99, bf16[32,256,256]{2,1,0:T(8,128)(2,1)} %bitcast.69), kind=kLoop, calls=%fused_computation.5 | loop fusion | flops 8421376 | bytes 8421376 | tf_op jit(solution)/shard_map/concatenate | solution.py:168
  6.0 8.8 %all-to-all-start.2 = ((bf16[32,257,256]{2,1,0:T(8,128)(2,1)}), bf16[32,257,256]{2,1,0:T(8,128)(2,1)}, u32[]{:S(2)}, u32[]{:S(2)}) async-start(bf16[32,257,256]{2,1,0:T(8,128)(2,1)} %pad_maximum_fusion), calls=%async_computation.2 | async-start | bytes 8650752 | tf_op jit(solution)/shard_map/all_to_all | solution.py:169
  14.8 10.2 %fusion.7 = f32[16,32,256]{2,0,1:T(8,128)S(1)} fusion(bf16[32,256,256]{2,1,0:T(8,128)(2,1)} %bitcast.70, bf16[32,256,256]{2,1,0:T(8,128)(2,1)} %bitcast.73, f32[256,16]{0,1:T(8,128)S(1)} %copy-done.5), kind=kOutput, calls=%fused_computation.12 | convolution fusion | flops 408944640 | bytes 8929280 | tf_op jit(solution)/shard_map/csk,km->mcs/dot_general | solution.py:187
  25.0 1.7 collective-permute-start
  26.7 3.3 collective-permute-start.1
  30.0 0.9 collective-permute-start.2
  30.9 10.0 %collective-permute-done = f32[16,32,256]{2,0,1:T(8,128)S(1)} collective-permute-done((f32[16,32,256]{2,0,1:T(8,128)S(1)}, f32[16,32,256]{2,0,1:T(8,128)S(1)}, u32[]{:S(2)}, u32[]{:S(2)}) %collective-permute-start) | collective-permute-done | bytes 524320 | tf_op jit(solution)/shard_map/ppermute | solution.py:146
  40.9 12.1 %collective-permute-done.1 = f32[16,32,256]{2,0,1:T(8,128)S(1)} collective-permute-done((f32[16,32,256]{2,0,1:T(8,128)S(1)}, f32[16,32,256]{2,0,1:T(8,128)S(1)}, u32[]{:S(2)}, u32[]{:S(2)}) %collective-permute-start.1) | collective-permute-done | bytes 524320 | tf_op jit(solution)/shard_map/ppermute | solution.py:146
  53.0 7.0 %fusion.18 = f32[32,256,256]{2,1,0:T(8,128)S(1)} fusion(f32[16,32,256]{2,0,1:T(8,128)S(1)} %collective-permute-done.2, f32[16,32,256]{2,0,1:T(8,128)S(1)} %collective-permute-done.1, f32[16,32,256]{2,0,1:T(8,128)S(1)} %fusion.7, f32[16,32,256]{2,0,1:T(8,128)S(1)} %collective-permute-done, f32[256,16]{0,1:T(8,128)S(1)} %copy-done.5), kind=kOutput, calls=%fused_computation.47 | convolution fusion | flops 403046400 | bytes 10502144 | tf_op jit(solution)/shard_map/mcs,km->csk/dot_general | solution.py:190
  60.1 5.5 %fusion = f32[32,128,256]{2,1,0:T(8,128)} fusion(bf16[32,256,256]{2,1,0:T(8,128)(2,1)S(1)} %bitcast.71, f32[32,256,256]{2,1,0:T(8,128)S(1)} %fusion.18, bf16[32,256,256]{2,1,0:T(8,128)(2,1)S(1)} %bitcast.74, s32[32,256]{1,0:T(8,128)S(1)} %eq.47), kind=kOutput, calls=%fused_computation.2 | convolution fusion | flops 1622147072 | bytes 21004288 | tf_op jit(solution)/shard_map/csp,csk->cpk/dot_general | solution.py:229
  65.6 2.8 all-to-all-done.2
  68.4 7.6 %all-to-all-start = ((f32[32,128,256]{2,1,0:T(8,128)}), f32[32,128,256]{2,1,0:T(8,128)}, u32[]{:S(2)}, u32[]{:S(2)}) async-start(f32[32,128,256]{2,1,0:T(8,128)} %fusion), calls=%async_computation | async-start | bytes 8388608 | tf_op jit(solution)/shard_map/all_to_all | solution.py:230
  76.3 0.9 slice_convert_fusion.rows_ref
  77.2 4.7 %slice.9.weights_ref = bf16[32,256,256]{2,1,0:T(8,128)(2,1)} slice(bf16[32,257,256]{2,1,0:T(8,128)(2,1)} %all-to-all-done.2), slice={[0:32], [0:256], [0:256]} | slice | bytes 8388608 | tf_op jit(solution)/shard_map/slice | solution.py:170
  81.9 2.6 fusion.5.hits_ref
  84.5 43.4 %all-to-all-done = f32[32,128,256]{2,1,0:T(8,128)} async-done(((f32[32,128,256]{2,1,0:T(8,128)}), f32[32,128,256]{2,1,0:T(8,128)}, u32[]{:S(2)}, u32[]{:S(2)}) %all-to-all-start) | async-done | bytes 4194336 | tf_op jit(solution)/shard_map/all_to_all | solution.py:230
  127.9 5.8 %multiply_reduce_fusion.4 = (f32[]{:T(128)}, f32[4,128,256]{2,0,1:T(4,128)S(1)}) fusion(f32[32,128,256]{2,1,0:T(8,128)} %all-to-all-done, s32[32]{0:T(128)S(1)} %dynamic-slice_reduce_fusion.blocks_ref), kind=kOutput, calls=%fused_computation.46 | convolution fusion | flops 25428096 | bytes 4718724 | tf_op jit(solution)/shard_map/cb,cpk->bpk/dot_general | solution.py:231
  133.9 0.8 pad_maximum_fusion.1.parts_ref
  134.8 8.5 %shard_map.70 = f32[16,16,256]{2,1,0:T(8,128)} custom-call(s32[32]{0:T(128)} %copy-done.18, bf16[2,512,256]{2,1,0:T(8,128)(2,1)} %pad_maximum_fusion.1.parts_ref, bf16[32,256,128]{2,1,0:T(8,128)(2,1)} %fusion.5.hits_ref, bf16[32,256,256]{2,1,0:T(8,128)(2,1)} %slice.9.weights_ref, f32[16,256]{1,0:T(8,128)} %bitcast.75), custom_call_target="tpu_custom_call" | custom-call | flops 738197504 | bytes 2621440 | tf_op jit(solution)/shard_map/pallas_call | solution.py:103
  143.2 1.6 collective-permute-start.6
  144.9 3.3 collective-permute-start.7
  148.9 8.5 %shard_map.68 = f32[16,16,256]{2,1,0:T(8,128)} custom-call(s32[32]{0:T(128)} %copy-done.18, bf16[2,512,256]{2,1,0:T(8,128)(2,1)} %pad_maximum_fusion.1.parts_ref, bf16[32,256,128]{2,1,0:T(8,128)(2,1)} %fusion.5.hits_ref, bf16[32,256,256]{2,1,0:T(8,128)(2,1)} %slice.9.weights_ref, f32[16,256]{1,0:T(8,128)} %bitcast.76), custom_call_target="tpu_custom_call" | custom-call | flops 738197504 | bytes 2621440 | tf_op jit(solution)/shard_map/pallas_call | solution.py:103
  158.6 1.3 broadcast_in_dim.12
  159.9 10.1 %all-to-all-start.1 = ((f32[128,1,1]{2,1,0:T(1,128)}), f32[128,1,1]{2,1,0:T(1,128)S(1)}, u32[]{:S(2)}, u32[]{:S(2)}) async-start(f32[128,1,1]{2,1,0:T(1,128)} %broadcast_in_dim.12), calls=%async_computation.1 | async-start | bytes 131072 | tf_op jit(solution)/shard_map/all_to_all | solution.py:152
  170.1 3.3 collective-permute-start.5
  173.4 0.8 add_add_fusion.4.amp_ref
  174.2 8.2 %shard_map.71 = f32[512,256]{1,0:T(8,128)} custom-call(s32[32]{0:T(128)} %copy-done.18, bf16[2,512,256]{2,1,0:T(8,128)(2,1)} %pad_maximum_fusion.1.parts_ref, bf16[32,256,128]{2,1,0:T(8,128)(2,1)} %fusion.5.hits_ref, s32[32,1,256]{2,1,0:T(1,128)} %copy-done.7, bf16[32,256,256]{2,1,0:T(8,128)(2,1)} %slice.9.weights_ref, ...), custom_call_target="tpu_custom_call" | custom-call | flops 1275068416 | bytes 3145728 | tf_op jit(solution)/shard_map/pallas_call | solution.py:120
  183.2 8.2 %shard_map.69 = f32[512,256]{1,0:T(8,128)} custom-call(s32[32]{0:T(128)} %copy-done.18, bf16[2,512,256]{2,1,0:T(8,128)(2,1)} %pad_maximum_fusion.1.parts_ref, bf16[32,256,128]{2,1,0:T(8,128)(2,1)} %fusion.5.hits_ref, s32[32,1,256]{2,1,0:T(1,128)} %copy-done.7, bf16[32,256,256]{2,1,0:T(8,128)(2,1)} %slice.9.weights_ref, ...), custom_call_target="tpu_custom_call" | custom-call | flops 1275068416 | bytes 3145728 | tf_op jit(solution)/shard_map/pallas_call | solution.py:120
  191.4 1.8 fusion.14
  193.2 1.2 broadcast_in_dim.26
  194.4 7.2 %all-to-all-start.3 = ((f32[128,1,1]{2,1,0:T(1,128)}), f32[128,1,1]{2,1,0:T(1,128)S(1)}, u32[]{:S(2)}, u32[]{:S(2)}) async-start(f32[128,1,1]{2,1,0:T(1,128)} %broadcast_in_dim.26), calls=%async_computation.3 | async-start | bytes 131072 | tf_op jit(solution)/shard_map/all_to_all | solution.py:152
  202.3 8.9 %all-to-all-done.3 = f32[128,1,1]{2,1,0:T(1,128)S(1)} async-done(((f32[128,1,1]{2,1,0:T(1,128)}), f32[128,1,1]{2,1,0:T(1,128)S(1)}, u32[]{:S(2)}, u32[]{:S(2)}) %all-to-all-start.3) | async-done | bytes 544 | tf_op jit(solution)/shard_map/all_to_all | solution.py:152
  213.2 1.8 multiply_reduce_fusion.3
  215.1 0.8 pad_maximum_fusion.2.parts_ref
  215.9 8.5 %shard_map.74 = f32[16,16,256]{2,1,0:T(8,128)} custom-call(s32[32]{0:T(128)} %copy-done.18, bf16[2,512,256]{2,1,0:T(8,128)(2,1)} %pad_maximum_fusion.2.parts_ref, bf16[32,256,128]{2,1,0:T(8,128)(2,1)} %fusion.5.hits_ref, bf16[32,256,256]{2,1,0:T(8,128)(2,1)} %slice.9.weights_ref, f32[16,256]{1,0:T(8,128)} %bitcast.77), custom_call_target="tpu_custom_call" | custom-call | flops 738197504 | bytes 2621440 | tf_op jit(solution)/shard_map/pallas_call | solution.py:103
  224.9 1.4 collective-permute-start.13
  226.4 1.2 collective-permute-start.14
  227.5 1.2 broadcast_in_dim.27
  228.7 6.0 %all-to-all-start.4 = ((f32[128,1,1]{2,1,0:T(1,128)}), f32[128,1,1]{2,1,0:T(1,128)S(1)}, u32[]{:S(2)}, u32[]{:S(2)}) async-start(f32[128,1,1]{2,1,0:T(1,128)} %broadcast_in_dim.27), calls=%async_computation.4 | async-start | bytes 131072 | tf_op jit(solution)/shard_map/all_to_all | solution.py:152
  234.7 8.5 %shard_map.72 = f32[16,16,256]{2,1,0:T(8,128)} custom-call(s32[32]{0:T(128)} %copy-done.18, bf16[2,512,256]{2,1,0:T(8,128)(2,1)} %pad_maximum_fusion.2.parts_ref, bf16[32,256,128]{2,1,0:T(8,128)(2,1)} %fusion.5.hits_ref, bf16[32,256,256]{2,1,0:T(8,128)(2,1)} %slice.9.weights_ref, f32[16,256]{1,0:T(8,128)} %bitcast.78), custom_call_target="tpu_custom_call" | custom-call | flops 738197504 | bytes 2621440 | tf_op jit(solution)/shard_map/pallas_call | solution.py:103
  243.2 3.3 collective-permute-start.10
  249.0 0.9 collective-permute-start.9
  250.7 8.2 %shard_map.75 = f32[512,256]{1,0:T(8,128)} custom-call(s32[32]{0:T(128)} %copy-done.18, bf16[2,512,256]{2,1,0:T(8,128)(2,1)} %pad_maximum_fusion.2.parts_ref, bf16[32,256,128]{2,1,0:T(8,128)(2,1)} %fusion.5.hits_ref, s32[32,1,256]{2,1,0:T(1,128)} %copy-done.7, bf16[32,256,256]{2,1,0:T(8,128)(2,1)} %slice.9.weights_ref, ...), custom_call_target="tpu_custom_call" | custom-call | flops 1275068416 | bytes 3145728 | tf_op jit(solution)/shard_map/pallas_call | solution.py:120
  259.0 1.9 add_add_fusion.3.amp_ref
  260.9 8.2 %shard_map.73 = f32[512,256]{1,0:T(8,128)} custom-call(s32[32]{0:T(128)} %copy-done.18, bf16[2,512,256]{2,1,0:T(8,128)(2,1)} %pad_maximum_fusion.2.parts_ref, bf16[32,256,128]{2,1,0:T(8,128)(2,1)} %fusion.5.hits_ref, s32[32,1,256]{2,1,0:T(1,128)} %copy-done.7, bf16[32,256,256]{2,1,0:T(8,128)(2,1)} %slice.9.weights_ref, ...), custom_call_target="tpu_custom_call" | custom-call | flops 1275068416 | bytes 3145728 | tf_op jit(solution)/shard_map/pallas_call | solution.py:120
  269.1 1.9 multiply_reduce_fusion.2
  271.6 19.2 %all_to_all.46 = f32[128,1,1]{2,1,0:T(1,128)S(1)} all-to-all(f32[128,1,1]{2,1,0:T(1,128)S(1)} %broadcast_in_dim.28), channel_id=1, replica_groups=mesh['tm'=32,'chan'=4] {'tm','chan'}, dimensions={0} | all-to-all | bytes 1024 | tf_op jit(solution)/shard_map/all_to_all | solution.py:152
  293.6 0.8 pad_maximum_fusion.3.parts_ref
  294.5 8.5 %shard_map.78 = f32[16,16,256]{2,1,0:T(8,128)} custom-call(s32[32]{0:T(128)} %copy-done.18, bf16[2,512,256]{2,1,0:T(8,128)(2,1)} %pad_maximum_fusion.3.parts_ref, bf16[32,256,128]{2,1,0:T(8,128)(2,1)} %fusion.5.hits_ref, bf16[32,256,256]{2,1,0:T(8,128)(2,1)} %slice.9.weights_ref, f32[16,256]{1,0:T(8,128)} %bitcast.79), custom_call_target="tpu_custom_call" | custom-call | flops 738197504 | bytes 2621440 | tf_op jit(solution)/shard_map/pallas_call | solution.py:103
  303.5 1.4 collective-permute-start.19
  304.9 1.2 collective-permute-start.20
  306.1 1.3 broadcast_in_dim.29
  307.4 6.0 %all-to-all-start.6 = ((f32[128,1,1]{2,1,0:T(1,128)}), f32[128,1,1]{2,1,0:T(1,128)S(1)}, u32[]{:S(2)}, u32[]{:S(2)}) async-start(f32[128,1,1]{2,1,0:T(1,128)} %broadcast_in_dim.29), calls=%async_computation.6 | async-start | bytes 131072 | tf_op jit(solution)/shard_map/all_to_all | solution.py:152
  313.4 8.5 %shard_map.76 = f32[16,16,256]{2,1,0:T(8,128)} custom-call(s32[32]{0:T(128)} %copy-done.18, bf16[2,512,256]{2,1,0:T(8,128)(2,1)} %pad_maximum_fusion.3.parts_ref, bf16[32,256,128]{2,1,0:T(8,128)(2,1)} %fusion.5.hits_ref, bf16[32,256,256]{2,1,0:T(8,128)(2,1)} %slice.9.weights_ref, f32[16,256]{1,0:T(8,128)} %bitcast.80), custom_call_target="tpu_custom_call" | custom-call | flops 738197504 | bytes 2621440 | tf_op jit(solution)/shard_map/pallas_call | solution.py:103
  321.8 1.5 collective-permute-start.15
  323.3 2.9 collective-permute-start.16
  328.2 1.0 collective-permute-start.17
  329.2 1.7 add_add_fusion.amp_ref
  330.9 8.2 %shard_map.79 = f32[512,256]{1,0:T(8,128)} custom-call(s32[32]{0:T(128)} %copy-done.18, bf16[2,512,256]{2,1,0:T(8,128)(2,1)} %pad_maximum_fusion.3.parts_ref, bf16[32,256,128]{2,1,0:T(8,128)(2,1)} %fusion.5.hits_ref, s32[32,1,256]{2,1,0:T(1,128)} %copy-done.7, bf16[32,256,256]{2,1,0:T(8,128)(2,1)} %slice.9.weights_ref, f32[16,16,256]{2,1,0:T(8,128)} %add_add_fusion.amp_ref, ...), custom_call_target="tpu_custom_call" | custom-call | flops 1275068416 | bytes 3145728 | tf_op jit(solution)/shard_map/pallas_call | solution.py:120
  339.1 1.9 add_add_fusion.1.amp_ref
  341.0 8.2 %shard_map.77 = f32[512,256]{1,0:T(8,128)} custom-call(s32[32]{0:T(128)} %copy-done.18, bf16[2,512,256]{2,1,0:T(8,128)(2,1)} %pad_maximum_fusion.3.parts_ref, bf16[32,256,128]{2,1,0:T(8,128)(2,1)} %fusion.5.hits_ref, s32[32,1,256]{2,1,0:T(1,128)} %copy-done.7, bf16[32,256,256]{2,1,0:T(8,128)(2,1)} %slice.9.weights_ref, ...), custom_call_target="tpu_custom_call" | custom-call | flops 1275068416 | bytes 3145728 | tf_op jit(solution)/shard_map/pallas_call | solution.py:120
  349.2 1.8 multiply_reduce_fusion
  351.7 18.0 %all_to_all.47 = f32[128,1,1]{2,1,0:T(1,128)S(1)} all-to-all(f32[128,1,1]{2,1,0:T(1,128)S(1)} %broadcast_in_dim.30), channel_id=1, replica_groups=mesh['tm'=32,'chan'=4] {'tm','chan'}, dimensions={0} | all-to-all | bytes 1024 | tf_op jit(solution)/shard_map/all_to_all | solution.py:152
  371.7 1.2 multiply_subtract_fusion
  (92 shorter events, 13.3 us)
Async XLA Ops:
  0.6 75.4 %copy-start = (s32[32,32]{1,0:T(8,128)S(1)}, s32[32,32]{1,0:T(8,128)}, u32[]{:S(2)}) copy-start(s32[32,32]{1,0:T(8,128)} %param.8) | copy-start | bytes 12292
  6.0 8.8 %copy-start.5 = (f32[256,16]{0,1:T(8,128)S(1)}, f32[256,16]{0,1:T(8,128)}, u32[]{:S(2)}) copy-start(f32[256,16]{0,1:T(8,128)} %param.9) | copy-start | bytes 49156
  6.0 62.4 %all-to-all-start.2 = ((bf16[32,257,256]{2,1,0:T(8,128)(2,1)}), bf16[32,257,256]{2,1,0:T(8,128)(2,1)}, u32[]{:S(2)}, u32[]{:S(2)}) async-start(bf16[32,257,256]{2,1,0:T(8,128)(2,1)} %pad_maximum_fusion), calls=%async_computation.2 | async-start | bytes 8650752 | tf_op jit(solution)/shard_map/all_to_all | solution.py:169
  14.8 16.1 %copy-start.17 = (s32[8192]{0:T(1024)S(1)}, s32[8192]{0:T(1024)}, u32[]{:S(2)}) copy-start(s32[8192]{0:T(1024)} %param.7) | copy-start | bytes 98308
  25.0 15.9 %collective-permute-start = (f32[16,32,256]{2,0,1:T(8,128)S(1)}, f32[16,32,256]{2,0,1:T(8,128)S(1)}, u32[]{:S(2)}, u32[]{:S(2)}) collective-permute-start(f32[16,32,256]{2,0,1:T(8,128)S(1)} %fusion.7), channel_id=1, source_target_pairs={{0,1},{1,2},{2,3},{3,0},{4,5},{5,6},{6,7},{7,4},{8,9},{9,10},{10,1... | collective-permute-start | bytes 1572872 | tf_op jit(solution)/shard_map/ppermute | solution.py:146
  26.7 26.4 %collective-permute-start.1 = (f32[16,32,256]{2,0,1:T(8,128)S(1)}, f32[16,32,256]{2,0,1:T(8,128)S(1)}, u32[]{:S(2)}, u32[]{:S(2)}) collective-permute-start(f32[16,32,256]{2,0,1:T(8,128)S(1)} %fusion.7), channel_id=1, source_target_pairs={{0,2},{1,3},{2,0},{3,1},{4,6},{5,7},{6,4},{7,5},{8,10},{9,11},{10,... | collective-permute-start | bytes 1572872 | tf_op jit(solution)/shard_map/ppermute | solution.py:146
  30.0 23.1 %collective-permute-start.2 = (f32[16,32,256]{2,0,1:T(8,128)S(1)}, f32[16,32,256]{2,0,1:T(8,128)S(1)}, u32[]{:S(2)}, u32[]{:S(2)}) collective-permute-start(f32[16,32,256]{2,0,1:T(8,128)S(1)} %fusion.7), channel_id=1, source_target_pairs={{0,3},{1,0},{2,1},{3,2},{4,7},{5,4},{6,5},{7,6},{8,11},{9,8},{10,9... | collective-permute-start | bytes 1572872 | tf_op jit(solution)/shard_map/ppermute | solution.py:146
  30.9 29.2 %copy-start.1 = (bf16[8192,256]{1,0:T(8,128)(2,1)S(1)}, bf16[8192,256]{1,0:T(8,128)(2,1)}, u32[]{:S(2)}) copy-start(bf16[8192,256]{1,0:T(8,128)(2,1)} %param.6) | copy-start | bytes 12582916
  30.9 29.2 %copy-start.2 = (bf16[8192,256]{1,0:T(8,128)(2,1)S(1)}, bf16[8192,256]{1,0:T(8,128)(2,1)}, u32[]{:S(2)}) copy-start(bf16[8192,256]{1,0:T(8,128)(2,1)} %param.5) | copy-start | bytes 12582916
  68.4 59.5 %all-to-all-start = ((f32[32,128,256]{2,1,0:T(8,128)}), f32[32,128,256]{2,1,0:T(8,128)}, u32[]{:S(2)}, u32[]{:S(2)}) async-start(f32[32,128,256]{2,1,0:T(8,128)} %fusion), calls=%async_computation | async-start | bytes 8388608 | tf_op jit(solution)/shard_map/all_to_all | solution.py:230
  76.2 51.7 %copy-start.18 = (s32[32]{0:T(128)}, s32[32]{0:T(128)S(1)}, u32[]{:S(2)}) copy-start(s32[32]{0:T(128)S(1)} %dynamic-slice_reduce_fusion.blocks_ref) | copy-start | bytes 388
  77.2 4.7 %copy-start.7 = (s32[32,1,256]{2,1,0:T(1,128)}, s32[32,1,256]{2,1,0:T(1,128)S(1)}, u32[]{:S(2)}) copy-start(s32[32,1,256]{2,1,0:T(1,128)S(1)} %slice_convert_fusion.rows_ref) | copy-start | bytes 98308
  133.9 15.0 %copy-start.6 = (f32[256,16]{0,1:T(8,128)S(1)}, f32[256,16]{0,1:T(8,128)}, u32[]{:S(2)}) copy-start(f32[256,16]{0,1:T(8,128)} %param.9) | copy-start | bytes 49156
  143.2 30.1 %copy-start.16 = (f32[16,16,256]{2,1,0:T(8,128)S(1)}, f32[16,16,256]{2,1,0:T(8,128)}, u32[]{:S(2)}) copy-start(f32[16,16,256]{2,1,0:T(8,128)} %shard_map.70) | copy-start | bytes 786436
  143.2 26.8 %collective-permute-start.6 = (f32[16,16,256]{2,1,0:T(8,128)}, f32[16,16,256]{2,1,0:T(8,128)S(1)}, u32[]{:S(2)}, u32[]{:S(2)}) collective-permute-start(f32[16,16,256]{2,1,0:T(8,128)} %shard_map.70), channel_id=1, source_target_pairs={{0,1},{1,2},{2,3},{3,0},{4,5},{5,6},{6,7},{7,4},{8,9},{9,10},{10,1... | collective-permute-start | bytes 786440 | tf_op jit(solution)/shard_map/ppermute | solution.py:146
  144.9 28.5 %collective-permute-start.7 = (f32[16,16,256]{2,1,0:T(8,128)}, f32[16,16,256]{2,1,0:T(8,128)S(1)}, u32[]{:S(2)}, u32[]{:S(2)}) collective-permute-start(f32[16,16,256]{2,1,0:T(8,128)} %shard_map.70), channel_id=1, source_target_pairs={{0,2},{1,3},{2,0},{3,1},{4,6},{5,7},{6,4},{7,5},{8,10},{9,11},{10,... | collective-permute-start | bytes 786440 | tf_op jit(solution)/shard_map/ppermute | solution.py:146
  148.2 25.2 %collective-permute-start.8 = (f32[16,16,256]{2,1,0:T(8,128)}, f32[16,16,256]{2,1,0:T(8,128)S(1)}, u32[]{:S(2)}, u32[]{:S(2)}) collective-permute-start(f32[16,16,256]{2,1,0:T(8,128)} %shard_map.70), channel_id=1, source_target_pairs={{0,3},{1,0},{2,1},{3,2},{4,7},{5,4},{6,5},{7,6},{8,11},{9,8},{10,9... | collective-permute-start | bytes 786440 | tf_op jit(solution)/shard_map/ppermute | solution.py:146
  148.9 25.3 %copy-start.10 = (bf16[96,256]{1,0:T(8,128)(2,1)}, bf16[96,256]{1,0:T(8,128)(2,1)S(1)}, u32[]{:S(2)}) copy-start(bf16[96,256]{1,0:T(8,128)(2,1)S(1)} %constant_dynamic-update-slice_fusion.stacked_ref) | copy-start | bytes 147460
  157.4 25.0 %collective-permute-start.3 = (f32[16,16,256]{2,1,0:T(8,128)}, f32[16,16,256]{2,1,0:T(8,128)S(1)}, u32[]{:S(2)}, u32[]{:S(2)}) collective-permute-start(f32[16,16,256]{2,1,0:T(8,128)} %shard_map.68), channel_id=1, source_target_pairs={{0,1},{1,2},{2,3},{3,0},{4,5},{5,6},{6,7},{7,4},{8,9},{9,10},{10,1... | collective-permute-start | bytes 786440 | tf_op jit(solution)/shard_map/ppermute | solution.py:146
  158.1 24.2 %collective-permute-start.4 = (f32[16,16,256]{2,1,0:T(8,128)}, f32[16,16,256]{2,1,0:T(8,128)S(1)}, u32[]{:S(2)}, u32[]{:S(2)}) collective-permute-start(f32[16,16,256]{2,1,0:T(8,128)} %shard_map.68), channel_id=1, source_target_pairs={{0,2},{1,3},{2,0},{3,1},{4,6},{5,7},{6,4},{7,5},{8,10},{9,11},{10,... | collective-permute-start | bytes 786440 | tf_op jit(solution)/shard_map/ppermute | solution.py:146
  159.9 33.2 %all-to-all-start.1 = ((f32[128,1,1]{2,1,0:T(1,128)}), f32[128,1,1]{2,1,0:T(1,128)S(1)}, u32[]{:S(2)}, u32[]{:S(2)}) async-start(f32[128,1,1]{2,1,0:T(1,128)} %broadcast_in_dim.12), calls=%async_computation.1 | async-start | bytes 131072 | tf_op jit(solution)/shard_map/all_to_all | solution.py:152
  170.0 12.4 %copy-start.15 = (f32[16,16,256]{2,1,0:T(8,128)S(1)}, f32[16,16,256]{2,1,0:T(8,128)}, u32[]{:S(2)}) copy-start(f32[16,16,256]{2,1,0:T(8,128)} %shard_map.68) | copy-start | bytes 786436
  170.1 12.3 %collective-permute-start.5 = (f32[16,16,256]{2,1,0:T(8,128)}, f32[16,16,256]{2,1,0:T(8,128)S(1)}, u32[]{:S(2)}, u32[]{:S(2)}) collective-permute-start(f32[16,16,256]{2,1,0:T(8,128)} %shard_map.68), channel_id=1, source_target_pairs={{0,3},{1,0},{2,1},{3,2},{4,7},{5,4},{6,5},{7,6},{8,11},{9,8},{10,9... | collective-permute-start | bytes 786440 | tf_op jit(solution)/shard_map/ppermute | solution.py:146
  182.4 9.0 %copy-start.3 = (f32[512,256]{1,0:T(8,128)S(1)}, f32[512,256]{1,0:T(8,128)}, u32[]{:S(2)}) copy-start(f32[512,256]{1,0:T(8,128)} %shard_map.71) | copy-start | bytes 1572868
  194.4 16.9 %all-to-all-start.3 = ((f32[128,1,1]{2,1,0:T(1,128)}), f32[128,1,1]{2,1,0:T(1,128)S(1)}, u32[]{:S(2)}, u32[]{:S(2)}) async-start(f32[128,1,1]{2,1,0:T(1,128)} %broadcast_in_dim.26), calls=%async_computation.3 | async-start | bytes 131072 | tf_op jit(solution)/shard_map/all_to_all | solution.py:152
  224.4 25.5 %copy-start.11 = (f32[16,16,256]{2,1,0:T(8,128)S(1)}, f32[16,16,256]{2,1,0:T(8,128)}, u32[]{:S(2)}) copy-start(f32[16,16,256]{2,1,0:T(8,128)} %shard_map.74) | copy-start | bytes 786436
  224.4 24.6 %collective-permute-start.12 = (f32[16,16,256]{2,1,0:T(8,128)}, f32[16,16,256]{2,1,0:T(8,128)S(1)}, u32[]{:S(2)}, u32[]{:S(2)}) collective-permute-start(f32[16,16,256]{2,1,0:T(8,128)} %shard_map.74), channel_id=1, source_target_pairs={{0,1},{1,2},{2,3},{3,0},{4,5},{5,6},{6,7},{7,4},{8,9},{9,10},{10,1... | collective-permute-start | bytes 786440 | tf_op jit(solution)/shard_map/ppermute | solution.py:146
  224.9 25.0 %collective-permute-start.13 = (f32[16,16,256]{2,1,0:T(8,128)}, f32[16,16,256]{2,1,0:T(8,128)S(1)}, u32[]{:S(2)}, u32[]{:S(2)}) collective-permute-start(f32[16,16,256]{2,1,0:T(8,128)} %shard_map.74), channel_id=1, source_target_pairs={{0,2},{1,3},{2,0},{3,1},{4,6},{5,7},{6,4},{7,5},{8,10},{9,11},{10,... | collective-permute-start | bytes 786440 | tf_op jit(solution)/shard_map/ppermute | solution.py:146
  226.4 23.6 %collective-permute-start.14 = (f32[16,16,256]{2,1,0:T(8,128)}, f32[16,16,256]{2,1,0:T(8,128)S(1)}, u32[]{:S(2)}, u32[]{:S(2)}) collective-permute-start(f32[16,16,256]{2,1,0:T(8,128)} %shard_map.74), channel_id=1, source_target_pairs={{0,3},{1,0},{2,1},{3,2},{4,7},{5,4},{6,5},{7,6},{8,11},{9,8},{10,9... | collective-permute-start | bytes 786440 | tf_op jit(solution)/shard_map/ppermute | solution.py:146
  228.7 18.3 %all-to-all-start.4 = ((f32[128,1,1]{2,1,0:T(1,128)}), f32[128,1,1]{2,1,0:T(1,128)S(1)}, u32[]{:S(2)}, u32[]{:S(2)}) async-start(f32[128,1,1]{2,1,0:T(1,128)} %broadcast_in_dim.27), calls=%async_computation.4 | async-start | bytes 131072 | tf_op jit(solution)/shard_map/all_to_all | solution.py:152
  243.2 15.7 %collective-permute-start.10 = (f32[16,16,256]{2,1,0:T(8,128)}, f32[16,16,256]{2,1,0:T(8,128)S(1)}, u32[]{:S(2)}, u32[]{:S(2)}) collective-permute-start(f32[16,16,256]{2,1,0:T(8,128)} %shard_map.72), channel_id=1, source_target_pairs={{0,2},{1,3},{2,0},{3,1},{4,6},{5,7},{6,4},{7,5},{8,10},{9,11},{10,... | collective-permute-start | bytes 786440 | tf_op jit(solution)/shard_map/ppermute | solution.py:146
  246.5 12.5 %collective-permute-start.11 = (f32[16,16,256]{2,1,0:T(8,128)}, f32[16,16,256]{2,1,0:T(8,128)}, u32[]{:S(2)}, u32[]{:S(2)}) collective-permute-start(f32[16,16,256]{2,1,0:T(8,128)} %shard_map.72), channel_id=1, source_target_pairs={{0,3},{1,0},{2,1},{3,2},{4,7},{5,4},{6,5},{7,6},{8,11},{9,8},{10,9... | collective-permute-start | bytes 786440 | tf_op jit(solution)/shard_map/ppermute | solution.py:146
  249.0 10.1 %copy-start.13 = (f32[16,16,256]{2,1,0:T(8,128)S(1)}, f32[16,16,256]{2,1,0:T(8,128)}, u32[]{:S(2)}) copy-start(f32[16,16,256]{2,1,0:T(8,128)} %shard_map.72) | copy-start | bytes 786436
  249.0 10.0 %collective-permute-start.9 = (f32[16,16,256]{2,1,0:T(8,128)}, f32[16,16,256]{2,1,0:T(8,128)}, u32[]{:S(2)}, u32[]{:S(2)}) collective-permute-start(f32[16,16,256]{2,1,0:T(8,128)} %shard_map.72), channel_id=1, source_target_pairs={{0,1},{1,2},{2,3},{3,0},{4,5},{5,6},{6,7},{7,4},{8,9},{9,10},{10,1... | collective-permute-start | bytes 786440 | tf_op jit(solution)/shard_map/ppermute | solution.py:146
  258.9 10.2 %copy-start.4 = (f32[512,256]{1,0:T(8,128)S(1)}, f32[512,256]{1,0:T(8,128)}, u32[]{:S(2)}) copy-start(f32[512,256]{1,0:T(8,128)} %shard_map.69) | copy-start | bytes 1572868
  258.9 10.2 %copy-start.9 = (f32[512,256]{1,0:T(8,128)S(1)}, f32[512,256]{1,0:T(8,128)}, u32[]{:S(2)}) copy-start(f32[512,256]{1,0:T(8,128)} %shard_map.75) | copy-start | bytes 1572868
  302.9 26.3 %copy-start.12 = (f32[16,16,256]{2,1,0:T(8,128)S(1)}, f32[16,16,256]{2,1,0:T(8,128)}, u32[]{:S(2)}) copy-start(f32[16,16,256]{2,1,0:T(8,128)} %shard_map.78) | copy-start | bytes 786436
  302.9 25.3 %collective-permute-start.18 = (f32[16,16,256]{2,1,0:T(8,128)}, f32[16,16,256]{2,1,0:T(8,128)S(1)}, u32[]{:S(2)}, u32[]{:S(2)}) collective-permute-start(f32[16,16,256]{2,1,0:T(8,128)} %shard_map.78), channel_id=1, source_target_pairs={{0,1},{1,2},{2,3},{3,0},{4,5},{5,6},{6,7},{7,4},{8,9},{9,10},{10,1... | collective-permute-start | bytes 786440 | tf_op jit(solution)/shard_map/ppermute | solution.py:146
  303.5 25.7 %collective-permute-start.19 = (f32[16,16,256]{2,1,0:T(8,128)}, f32[16,16,256]{2,1,0:T(8,128)S(1)}, u32[]{:S(2)}, u32[]{:S(2)}) collective-permute-start(f32[16,16,256]{2,1,0:T(8,128)} %shard_map.78), channel_id=1, source_target_pairs={{0,2},{1,3},{2,0},{3,1},{4,6},{5,7},{6,4},{7,5},{8,10},{9,11},{10,... | collective-permute-start | bytes 786440 | tf_op jit(solution)/shard_map/ppermute | solution.py:146
  304.9 24.3 %collective-permute-start.20 = (f32[16,16,256]{2,1,0:T(8,128)}, f32[16,16,256]{2,1,0:T(8,128)}, u32[]{:S(2)}, u32[]{:S(2)}) collective-permute-start(f32[16,16,256]{2,1,0:T(8,128)} %shard_map.78), channel_id=1, source_target_pairs={{0,3},{1,0},{2,1},{3,2},{4,7},{5,4},{6,5},{7,6},{8,11},{9,8},{10,9... | collective-permute-start | bytes 786440 | tf_op jit(solution)/shard_map/ppermute | solution.py:146
  307.4 18.9 %all-to-all-start.6 = ((f32[128,1,1]{2,1,0:T(1,128)}), f32[128,1,1]{2,1,0:T(1,128)S(1)}, u32[]{:S(2)}, u32[]{:S(2)}) async-start(f32[128,1,1]{2,1,0:T(1,128)} %broadcast_in_dim.29), calls=%async_computation.6 | async-start | bytes 131072 | tf_op jit(solution)/shard_map/all_to_all | solution.py:152
  321.8 17.3 %collective-permute-start.15 = (f32[16,16,256]{2,1,0:T(8,128)}, f32[16,16,256]{2,1,0:T(8,128)S(1)}, u32[]{:S(2)}, u32[]{:S(2)}) collective-permute-start(f32[16,16,256]{2,1,0:T(8,128)} %shard_map.76), channel_id=1, source_target_pairs={{0,1},{1,2},{2,3},{3,0},{4,5},{5,6},{6,7},{7,4},{8,9},{9,10},{10,1... | collective-permute-start | bytes 786440 | tf_op jit(solution)/shard_map/ppermute | solution.py:146
  323.3 15.8 %collective-permute-start.16 = (f32[16,16,256]{2,1,0:T(8,128)}, f32[16,16,256]{2,1,0:T(8,128)}, u32[]{:S(2)}, u32[]{:S(2)}) collective-permute-start(f32[16,16,256]{2,1,0:T(8,128)} %shard_map.76), channel_id=1, source_target_pairs={{0,2},{1,3},{2,0},{3,1},{4,6},{5,7},{6,4},{7,5},{8,10},{9,11},{10,... | collective-permute-start | bytes 786440 | tf_op jit(solution)/shard_map/ppermute | solution.py:146
  328.2 11.0 %copy-start.14 = (f32[16,16,256]{2,1,0:T(8,128)S(1)}, f32[16,16,256]{2,1,0:T(8,128)}, u32[]{:S(2)}) copy-start(f32[16,16,256]{2,1,0:T(8,128)} %shard_map.76) | copy-start | bytes 786436
  328.2 10.9 %collective-permute-start.17 = (f32[16,16,256]{2,1,0:T(8,128)}, f32[16,16,256]{2,1,0:T(8,128)}, u32[]{:S(2)}, u32[]{:S(2)}) collective-permute-start(f32[16,16,256]{2,1,0:T(8,128)} %shard_map.76), channel_id=1, source_target_pairs={{0,3},{1,0},{2,1},{3,2},{4,7},{5,4},{6,5},{7,6},{8,11},{9,8},{10,9... | collective-permute-start | bytes 786440 | tf_op jit(solution)/shard_map/ppermute | solution.py:146
  339.1 10.1 %copy-start.8 = (f32[512,256]{1,0:T(8,128)S(1)}, f32[512,256]{1,0:T(8,128)}, u32[]{:S(2)}) copy-start(f32[512,256]{1,0:T(8,128)} %shard_map.79) | copy-start | bytes 1572868

commit v11 on v10

--- a/solution.py
+++ b/solution.py
@@ -15,7 +15,7 @@
 highest = lax.Precision.HIGHEST
 high = lax.Precision.HIGH
 ridge = 1.0
-RUNS = 4
+RUNS = 8
 
 
 def gathered(parts_ref, block, hits):

time: 379 us -> 378 us (level)
  transfers between devices with their start and end apart: 27 -> 27, of which waited for: 6 -> 6; matrix products, arithmetic and copies ran while one was open for 12% -> 12% of each run, Pallas kernels for 16% -> 15%
where the time goes in v11:
time: 378 us; the launch traced here: 372 us
  Pallas kernels  97.4 us (26%)
  starting transfers between devices  79.6 us (21%)
  waiting for transfers between devices  77 us (20%)
  blocking collectives  37.4 us (10%)
  other arithmetic  33.1 us (9%)
  matrix products  28.6 us (8%)
  local copies, waits for them, and re-layouts  11.5 us (3%)
  between operations  7.34 us (2%)
    pallas_call x6, Pallas kernels, owner_operator(): pl.pallas_call(functools.partial(amp_kernel, offset), grid_spec=pltpu.Pre...  50.6 us
    pallas_call x6, Pallas kernels, owner_operator(): pl.pallas_call(functools.partial(bin_kernel, offset), grid_spec=pltpu.Pre...  46.8 us
    all_to_all x1, waiting for transfers between devices, per_device(): arrived = lax.all_to_all(local_partial, 'tm', 0, 0, tiled=True)  43.4 us
    all_to_all x2, blocking collectives, global_sum(): lax.all_to_all(jnp.broadcast_to(value, (everyone, 1)), ('tm', 'chan'), 0,...  37.4 us
    ppermute x21, starting transfers between devices, chan_sum(): total = total + lax.ppermute(value, 'chan', pairs)  33.7 us
    all_to_all x4, starting transfers between devices, global_sum(): lax.all_to_all(jnp.broadcast_to(value, (everyone, 1)), ('tm', 'chan'), 0,...  29.6 us
    ppermute x21, waiting for transfers between devices, chan_sum(): total = total + lax.ppermute(value, 'chan', pairs)  21.9 us
    dot_general x1, matrix products, filtered(): jnp.einsum('csk,km->mcs', weighted, foreground_modes, precision=highest)  10.2 us
  transfers between devices with their start and end apart: 27, of which 6 were waited for; matrix products, arithmetic and copies ran while one was open for 12% of the time, Pallas kernels for 15%

profile of v11, /device:TPU:1, one launch (start us, length us, event | category | flops | bytes accessed | tf_op | source)
XLA Modules:
  0.0 372.0 jit_solution(10281558353035066691)
XLA Ops:
  1.4 4.6 %pad_maximum_fusion = bf16[32,257,256]{2,1,0:T(8,128)(2,1)} fusion(bf16[32,1,256]{2,1,0:T(2,128)(2,1)S(1)} %convert_element_type.99, bf16[32,256,256]{2,1,0:T(8,128)(2,1)} %bitcast.69), kind=kLoop, calls=%fused_computation.5 | loop fusion | flops 8421376 | bytes 8421376 | tf_op jit(solution)/shard_map/concatenate | solution.py:168
  6.0 8.8 %all-to-all-start.2 = ((bf16[32,257,256]{2,1,0:T(8,128)(2,1)}), bf16[32,257,256]{2,1,0:T(8,128)(2,1)}, u32[]{:S(2)}, u32[]{:S(2)}) async-start(bf16[32,257,256]{2,1,0:T(8,128)(2,1)} %pad_maximum_fusion), calls=%async_computation.2 | async-start | bytes 8650752 | tf_op jit(solution)/shard_map/all_to_all | solution.py:169
  14.8 10.2 %fusion.7 = f32[16,32,256]{2,0,1:T(8,128)S(1)} fusion(bf16[32,256,256]{2,1,0:T(8,128)(2,1)} %bitcast.70, bf16[32,256,256]{2,1,0:T(8,128)(2,1)} %bitcast.73, f32[256,16]{0,1:T(8,128)S(1)} %copy-done.5), kind=kOutput, calls=%fused_computation.12 | convolution fusion | flops 408944640 | bytes 8929280 | tf_op jit(solution)/shard_map/csk,km->mcs/dot_general | solution.py:187
  25.0 1.7 collective-permute-start
  26.7 3.3 collective-permute-start.1
  30.0 1.2 collective-permute-start.2
  31.2 9.7 %collective-permute-done = f32[16,32,256]{2,0,1:T(8,128)S(1)} collective-permute-done((f32[16,32,256]{2,0,1:T(8,128)S(1)}, f32[16,32,256]{2,0,1:T(8,128)S(1)}, u32[]{:S(2)}, u32[]{:S(2)}) %collective-permute-start) | collective-permute-done | bytes 524320 | tf_op jit(solution)/shard_map/ppermute | solution.py:146
  40.9 12.1 %collective-permute-done.1 = f32[16,32,256]{2,0,1:T(8,128)S(1)} collective-permute-done((f32[16,32,256]{2,0,1:T(8,128)S(1)}, f32[16,32,256]{2,0,1:T(8,128)S(1)}, u32[]{:S(2)}, u32[]{:S(2)}) %collective-permute-start.1) | collective-permute-done | bytes 524320 | tf_op jit(solution)/shard_map/ppermute | solution.py:146
  53.0 7.1 %fusion.18 = f32[32,256,256]{2,1,0:T(8,128)S(1)} fusion(f32[16,32,256]{2,0,1:T(8,128)S(1)} %collective-permute-done.2, f32[16,32,256]{2,0,1:T(8,128)S(1)} %collective-permute-done.1, f32[16,32,256]{2,0,1:T(8,128)S(1)} %fusion.7, f32[16,32,256]{2,0,1:T(8,128)S(1)} %collective-permute-done, f32[256,16]{0,1:T(8,128)S(1)} %copy-done.5), kind=kOutput, calls=%fused_computation.47 | convolution fusion | flops 403046400 | bytes 10502144 | tf_op jit(solution)/shard_map/mcs,km->csk/dot_general | solution.py:190
  60.1 5.5 %fusion = f32[32,128,256]{2,1,0:T(8,128)} fusion(bf16[32,256,256]{2,1,0:T(8,128)(2,1)S(1)} %bitcast.71, f32[32,256,256]{2,1,0:T(8,128)S(1)} %fusion.18, bf16[32,256,256]{2,1,0:T(8,128)(2,1)S(1)} %bitcast.74, s32[32,256]{1,0:T(8,128)S(1)} %eq.47), kind=kOutput, calls=%fused_computation.2 | convolution fusion | flops 1622147072 | bytes 21004288 | tf_op jit(solution)/shard_map/csp,csk->cpk/dot_general | solution.py:229
  65.6 2.8 all-to-all-done.2
  68.4 7.5 %all-to-all-start = ((f32[32,128,256]{2,1,0:T(8,128)}), f32[32,128,256]{2,1,0:T(8,128)}, u32[]{:S(2)}, u32[]{:S(2)}) async-start(f32[32,128,256]{2,1,0:T(8,128)} %fusion), calls=%async_computation | async-start | bytes 8388608 | tf_op jit(solution)/shard_map/all_to_all | solution.py:230
  76.2 0.9 slice_convert_fusion.rows_ref
  77.2 4.7 %slice.9.weights_ref = bf16[32,256,256]{2,1,0:T(8,128)(2,1)} slice(bf16[32,257,256]{2,1,0:T(8,128)(2,1)} %all-to-all-done.2), slice={[0:32], [0:256], [0:256]} | slice | bytes 8388608 | tf_op jit(solution)/shard_map/slice | solution.py:170
  81.9 2.6 fusion.5.hits_ref
  84.5 43.4 %all-to-all-done = f32[32,128,256]{2,1,0:T(8,128)} async-done(((f32[32,128,256]{2,1,0:T(8,128)}), f32[32,128,256]{2,1,0:T(8,128)}, u32[]{:S(2)}, u32[]{:S(2)}) %all-to-all-start) | async-done | bytes 4194336 | tf_op jit(solution)/shard_map/all_to_all | solution.py:230
  127.9 5.8 %multiply_reduce_fusion.4 = (f32[]{:T(128)}, f32[4,128,256]{2,0,1:T(4,128)S(1)}) fusion(f32[32,128,256]{2,1,0:T(8,128)} %all-to-all-done, s32[32]{0:T(128)S(1)} %dynamic-slice_reduce_fusion.blocks_ref), kind=kOutput, calls=%fused_computation.46 | convolution fusion | flops 25428096 | bytes 4718724 | tf_op jit(solution)/shard_map/cb,cpk->bpk/dot_general | solution.py:231
  133.9 0.8 pad_maximum_fusion.1.parts_ref
  134.7 8.4 %shard_map.70 = f32[16,16,256]{2,1,0:T(8,128)} custom-call(s32[32]{0:T(128)} %copy-done.18, bf16[2,512,256]{2,1,0:T(8,128)(2,1)} %pad_maximum_fusion.1.parts_ref, bf16[32,256,128]{2,1,0:T(8,128)(2,1)} %fusion.5.hits_ref, bf16[32,256,256]{2,1,0:T(8,128)(2,1)} %slice.9.weights_ref, f32[16,256]{1,0:T(8,128)} %bitcast.75), custom_call_target="tpu_custom_call" | custom-call | flops 738197504 | bytes 2621440 | tf_op jit(solution)/shard_map/pallas_call | solution.py:103
  143.2 1.6 collective-permute-start.6
  144.8 3.3 collective-permute-start.7
  148.9 8.4 %shard_map.68 = f32[16,16,256]{2,1,0:T(8,128)} custom-call(s32[32]{0:T(128)} %copy-done.18, bf16[2,512,256]{2,1,0:T(8,128)(2,1)} %pad_maximum_fusion.1.parts_ref, bf16[32,256,128]{2,1,0:T(8,128)(2,1)} %fusion.5.hits_ref, bf16[32,256,256]{2,1,0:T(8,128)(2,1)} %slice.9.weights_ref, f32[16,256]{1,0:T(8,128)} %bitcast.76), custom_call_target="tpu_custom_call" | custom-call | flops 738197504 | bytes 2621440 | tf_op jit(solution)/shard_map/pallas_call | solution.py:103
  158.5 1.3 broadcast_in_dim.12
  159.8 10.1 %all-to-all-start.1 = ((f32[128,1,1]{2,1,0:T(1,128)}), f32[128,1,1]{2,1,0:T(1,128)S(1)}, u32[]{:S(2)}, u32[]{:S(2)}) async-start(f32[128,1,1]{2,1,0:T(1,128)} %broadcast_in_dim.12), calls=%async_computation.1 | async-start | bytes 131072 | tf_op jit(solution)/shard_map/all_to_all | solution.py:152
  170.0 3.5 collective-permute-start.5
  174.3 7.8 %shard_map.71 = f32[512,256]{1,0:T(8,128)} custom-call(s32[32]{0:T(128)} %copy-done.18, bf16[2,512,256]{2,1,0:T(8,128)(2,1)} %pad_maximum_fusion.1.parts_ref, bf16[32,256,128]{2,1,0:T(8,128)(2,1)} %fusion.5.hits_ref, s32[32,1,256]{2,1,0:T(1,128)} %copy-done.7, bf16[32,256,256]{2,1,0:T(8,128)(2,1)} %slice.9.weights_ref, ...), custom_call_target="tpu_custom_call" | custom-call | flops 1275068416 | bytes 3145728 | tf_op jit(solution)/shard_map/pallas_call | solution.py:120
  182.1 0.8 add_add_fusion.5.amp_ref
  182.9 7.8 %shard_map.69 = f32[512,256]{1,0:T(8,128)} custom-call(s32[32]{0:T(128)} %copy-done.18, bf16[2,512,256]{2,1,0:T(8,128)(2,1)} %pad_maximum_fusion.1.parts_ref, bf16[32,256,128]{2,1,0:T(8,128)(2,1)} %fusion.5.hits_ref, s32[32,1,256]{2,1,0:T(1,128)} %copy-done.7, bf16[32,256,256]{2,1,0:T(8,128)(2,1)} %slice.9.weights_ref, ...), custom_call_target="tpu_custom_call" | custom-call | flops 1275068416 | bytes 3145728 | tf_op jit(solution)/shard_map/pallas_call | solution.py:120
  190.7 1.8 fusion.14
  192.5 1.2 broadcast_in_dim.26
  193.7 7.6 %all-to-all-start.3 = ((f32[128,1,1]{2,1,0:T(1,128)}), f32[128,1,1]{2,1,0:T(1,128)S(1)}, u32[]{:S(2)}, u32[]{:S(2)}) async-start(f32[128,1,1]{2,1,0:T(1,128)} %broadcast_in_dim.26), calls=%async_computation.3 | async-start | bytes 131072 | tf_op jit(solution)/shard_map/all_to_all | solution.py:152
  202.1 8.9 %all-to-all-done.3 = f32[128,1,1]{2,1,0:T(1,128)S(1)} async-done(((f32[128,1,1]{2,1,0:T(1,128)}), f32[128,1,1]{2,1,0:T(1,128)S(1)}, u32[]{:S(2)}, u32[]{:S(2)}) %all-to-all-start.3) | async-done | bytes 544 | tf_op jit(solution)/shard_map/all_to_all | solution.py:152
  213.0 1.8 multiply_reduce_fusion.3
  214.8 0.8 pad_maximum_fusion.2.parts_ref
  215.7 8.4 %shard_map.74 = f32[16,16,256]{2,1,0:T(8,128)} custom-call(s32[32]{0:T(128)} %copy-done.18, bf16[2,512,256]{2,1,0:T(8,128)(2,1)} %pad_maximum_fusion.2.parts_ref, bf16[32,256,128]{2,1,0:T(8,128)(2,1)} %fusion.5.hits_ref, bf16[32,256,256]{2,1,0:T(8,128)(2,1)} %slice.9.weights_ref, f32[16,256]{1,0:T(8,128)} %bitcast.77), custom_call_target="tpu_custom_call" | custom-call | flops 738197504 | bytes 2621440 | tf_op jit(solution)/shard_map/pallas_call | solution.py:103
  224.6 1.4 collective-permute-start.13
  226.1 1.2 collective-permute-start.14
  227.3 1.2 broadcast_in_dim.27
  228.5 6.0 %all-to-all-start.4 = ((f32[128,1,1]{2,1,0:T(1,128)}), f32[128,1,1]{2,1,0:T(1,128)S(1)}, u32[]{:S(2)}, u32[]{:S(2)}) async-start(f32[128,1,1]{2,1,0:T(1,128)} %broadcast_in_dim.27), calls=%async_computation.4 | async-start | bytes 131072 | tf_op jit(solution)/shard_map/all_to_all | solution.py:152
  234.4 8.4 %shard_map.72 = f32[16,16,256]{2,1,0:T(8,128)} custom-call(s32[32]{0:T(128)} %copy-done.18, bf16[2,512,256]{2,1,0:T(8,128)(2,1)} %pad_maximum_fusion.2.parts_ref, bf16[32,256,128]{2,1,0:T(8,128)(2,1)} %fusion.5.hits_ref, bf16[32,256,256]{2,1,0:T(8,128)(2,1)} %slice.9.weights_ref, f32[16,256]{1,0:T(8,128)} %bitcast.78), custom_call_target="tpu_custom_call" | custom-call | flops 738197504 | bytes 2621440 | tf_op jit(solution)/shard_map/pallas_call | solution.py:103
  242.9 3.3 collective-permute-start.10
  248.7 1.3 collective-permute-start.9
  250.8 7.8 %shard_map.75 = f32[512,256]{1,0:T(8,128)} custom-call(s32[32]{0:T(128)} %copy-done.18, bf16[2,512,256]{2,1,0:T(8,128)(2,1)} %pad_maximum_fusion.2.parts_ref, bf16[32,256,128]{2,1,0:T(8,128)(2,1)} %fusion.5.hits_ref, s32[32,1,256]{2,1,0:T(1,128)} %copy-done.7, bf16[32,256,256]{2,1,0:T(8,128)(2,1)} %slice.9.weights_ref, ...), custom_call_target="tpu_custom_call" | custom-call | flops 1275068416 | bytes 3145728 | tf_op jit(solution)/shard_map/pallas_call | solution.py:120
  258.7 1.9 add_add_fusion.3.amp_ref
  260.6 7.8 %shard_map.73 = f32[512,256]{1,0:T(8,128)} custom-call(s32[32]{0:T(128)} %copy-done.18, bf16[2,512,256]{2,1,0:T(8,128)(2,1)} %pad_maximum_fusion.2.parts_ref, bf16[32,256,128]{2,1,0:T(8,128)(2,1)} %fusion.5.hits_ref, s32[32,1,256]{2,1,0:T(1,128)} %copy-done.7, bf16[32,256,256]{2,1,0:T(8,128)(2,1)} %slice.9.weights_ref, ...), custom_call_target="tpu_custom_call" | custom-call | flops 1275068416 | bytes 3145728 | tf_op jit(solution)/shard_map/pallas_call | solution.py:120
  268.4 1.9 multiply_reduce_fusion.2
  270.9 19.2 %all_to_all.46 = f32[128,1,1]{2,1,0:T(1,128)S(1)} all-to-all(f32[128,1,1]{2,1,0:T(1,128)S(1)} %broadcast_in_dim.28), channel_id=1, replica_groups=mesh['tm'=32,'chan'=4] {'tm','chan'}, dimensions={0} | all-to-all | bytes 1024 | tf_op jit(solution)/shard_map/all_to_all | solution.py:152
  292.9 0.8 pad_maximum_fusion.3.parts_ref
  293.8 8.4 %shard_map.78 = f32[16,16,256]{2,1,0:T(8,128)} custom-call(s32[32]{0:T(128)} %copy-done.18, bf16[2,512,256]{2,1,0:T(8,128)(2,1)} %pad_maximum_fusion.3.parts_ref, bf16[32,256,128]{2,1,0:T(8,128)(2,1)} %fusion.5.hits_ref, bf16[32,256,256]{2,1,0:T(8,128)(2,1)} %slice.9.weights_ref, f32[16,256]{1,0:T(8,128)} %bitcast.79), custom_call_target="tpu_custom_call" | custom-call | flops 738197504 | bytes 2621440 | tf_op jit(solution)/shard_map/pallas_call | solution.py:103
  302.8 1.4 collective-permute-start.19
  304.2 1.2 collective-permute-start.20
  305.4 1.3 broadcast_in_dim.29
  306.7 6.0 %all-to-all-start.6 = ((f32[128,1,1]{2,1,0:T(1,128)}), f32[128,1,1]{2,1,0:T(1,128)S(1)}, u32[]{:S(2)}, u32[]{:S(2)}) async-start(f32[128,1,1]{2,1,0:T(1,128)} %broadcast_in_dim.29), calls=%async_computation.6 | async-start | bytes 131072 | tf_op jit(solution)/shard_map/all_to_all | solution.py:152
  312.7 8.4 %shard_map.76 = f32[16,16,256]{2,1,0:T(8,128)} custom-call(s32[32]{0:T(128)} %copy-done.18, bf16[2,512,256]{2,1,0:T(8,128)(2,1)} %pad_maximum_fusion.3.parts_ref, bf16[32,256,128]{2,1,0:T(8,128)(2,1)} %fusion.5.hits_ref, bf16[32,256,256]{2,1,0:T(8,128)(2,1)} %slice.9.weights_ref, f32[16,256]{1,0:T(8,128)} %bitcast.80), custom_call_target="tpu_custom_call" | custom-call | flops 738197504 | bytes 2621440 | tf_op jit(solution)/shard_map/pallas_call | solution.py:103
  321.1 1.5 collective-permute-start.15
  322.6 2.9 collective-permute-start.16
  327.4 1.2 collective-permute-start.17
  328.6 1.7 add_add_fusion.amp_ref
  330.3 7.8 %shard_map.79 = f32[512,256]{1,0:T(8,128)} custom-call(s32[32]{0:T(128)} %copy-done.18, bf16[2,512,256]{2,1,0:T(8,128)(2,1)} %pad_maximum_fusion.3.parts_ref, bf16[32,256,128]{2,1,0:T(8,128)(2,1)} %fusion.5.hits_ref, s32[32,1,256]{2,1,0:T(1,128)} %copy-done.7, bf16[32,256,256]{2,1,0:T(8,128)(2,1)} %slice.9.weights_ref, f32[16,16,256]{2,1,0:T(8,128)} %add_add_fusion.amp_ref, ...), custom_call_target="tpu_custom_call" | custom-call | flops 1275068416 | bytes 3145728 | tf_op jit(solution)/shard_map/pallas_call | solution.py:120
  338.2 1.9 add_add_fusion.1.amp_ref
  340.0 7.8 %shard_map.77 = f32[512,256]{1,0:T(8,128)} custom-call(s32[32]{0:T(128)} %copy-done.18, bf16[2,512,256]{2,1,0:T(8,128)(2,1)} %pad_maximum_fusion.3.parts_ref, bf16[32,256,128]{2,1,0:T(8,128)(2,1)} %fusion.5.hits_ref, s32[32,1,256]{2,1,0:T(1,128)} %copy-done.7, bf16[32,256,256]{2,1,0:T(8,128)(2,1)} %slice.9.weights_ref, ...), custom_call_target="tpu_custom_call" | custom-call | flops 1275068416 | bytes 3145728 | tf_op jit(solution)/shard_map/pallas_call | solution.py:120
  347.8 1.8 multiply_reduce_fusion
  350.4 18.3 %all_to_all.47 = f32[128,1,1]{2,1,0:T(1,128)S(1)} all-to-all(f32[128,1,1]{2,1,0:T(1,128)S(1)} %broadcast_in_dim.30), channel_id=1, replica_groups=mesh['tm'=32,'chan'=4] {'tm','chan'}, dimensions={0} | all-to-all | bytes 1024 | tf_op jit(solution)/shard_map/all_to_all | solution.py:152
  370.6 1.2 multiply_subtract_fusion
  (92 shorter events, 13.3 us)
Async XLA Ops:
  0.6 75.3 %copy-start = (s32[32,32]{1,0:T(8,128)S(1)}, s32[32,32]{1,0:T(8,128)}, u32[]{:S(2)}) copy-start(s32[32,32]{1,0:T(8,128)} %param.8) | copy-start | bytes 12292
  6.0 8.8 %copy-start.5 = (f32[256,16]{0,1:T(8,128)S(1)}, f32[256,16]{0,1:T(8,128)}, u32[]{:S(2)}) copy-start(f32[256,16]{0,1:T(8,128)} %param.9) | copy-start | bytes 49156
  6.0 62.4 %all-to-all-start.2 = ((bf16[32,257,256]{2,1,0:T(8,128)(2,1)}), bf16[32,257,256]{2,1,0:T(8,128)(2,1)}, u32[]{:S(2)}, u32[]{:S(2)}) async-start(bf16[32,257,256]{2,1,0:T(8,128)(2,1)} %pad_maximum_fusion), calls=%async_computation.2 | async-start | bytes 8650752 | tf_op jit(solution)/shard_map/all_to_all | solution.py:169
  14.8 16.4 %copy-start.17 = (s32[8192]{0:T(1024)S(1)}, s32[8192]{0:T(1024)}, u32[]{:S(2)}) copy-start(s32[8192]{0:T(1024)} %param.7) | copy-start | bytes 98308
  25.0 15.9 %collective-permute-start = (f32[16,32,256]{2,0,1:T(8,128)S(1)}, f32[16,32,256]{2,0,1:T(8,128)S(1)}, u32[]{:S(2)}, u32[]{:S(2)}) collective-permute-start(f32[16,32,256]{2,0,1:T(8,128)S(1)} %fusion.7), channel_id=1, source_target_pairs={{0,1},{1,2},{2,3},{3,0},{4,5},{5,6},{6,7},{7,4},{8,9},{9,10},{10,1... | collective-permute-start | bytes 1572872 | tf_op jit(solution)/shard_map/ppermute | solution.py:146
  26.7 26.4 %collective-permute-start.1 = (f32[16,32,256]{2,0,1:T(8,128)S(1)}, f32[16,32,256]{2,0,1:T(8,128)S(1)}, u32[]{:S(2)}, u32[]{:S(2)}) collective-permute-start(f32[16,32,256]{2,0,1:T(8,128)S(1)} %fusion.7), channel_id=1, source_target_pairs={{0,2},{1,3},{2,0},{3,1},{4,6},{5,7},{6,4},{7,5},{8,10},{9,11},{10,... | collective-permute-start | bytes 1572872 | tf_op jit(solution)/shard_map/ppermute | solution.py:146
  30.0 23.1 %collective-permute-start.2 = (f32[16,32,256]{2,0,1:T(8,128)S(1)}, f32[16,32,256]{2,0,1:T(8,128)S(1)}, u32[]{:S(2)}, u32[]{:S(2)}) collective-permute-start(f32[16,32,256]{2,0,1:T(8,128)S(1)} %fusion.7), channel_id=1, source_target_pairs={{0,3},{1,0},{2,1},{3,2},{4,7},{5,4},{6,5},{7,6},{8,11},{9,8},{10,9... | collective-permute-start | bytes 1572872 | tf_op jit(solution)/shard_map/ppermute | solution.py:146
  31.2 28.9 %copy-start.1 = (bf16[8192,256]{1,0:T(8,128)(2,1)S(1)}, bf16[8192,256]{1,0:T(8,128)(2,1)}, u32[]{:S(2)}) copy-start(bf16[8192,256]{1,0:T(8,128)(2,1)} %param.6) | copy-start | bytes 12582916
  31.2 28.9 %copy-start.2 = (bf16[8192,256]{1,0:T(8,128)(2,1)S(1)}, bf16[8192,256]{1,0:T(8,128)(2,1)}, u32[]{:S(2)}) copy-start(bf16[8192,256]{1,0:T(8,128)(2,1)} %param.5) | copy-start | bytes 12582916
  68.4 59.5 %all-to-all-start = ((f32[32,128,256]{2,1,0:T(8,128)}), f32[32,128,256]{2,1,0:T(8,128)}, u32[]{:S(2)}, u32[]{:S(2)}) async-start(f32[32,128,256]{2,1,0:T(8,128)} %fusion), calls=%async_computation | async-start | bytes 8388608 | tf_op jit(solution)/shard_map/all_to_all | solution.py:230
  76.2 51.7 %copy-start.18 = (s32[32]{0:T(128)}, s32[32]{0:T(128)S(1)}, u32[]{:S(2)}) copy-start(s32[32]{0:T(128)S(1)} %dynamic-slice_reduce_fusion.blocks_ref) | copy-start | bytes 388
  77.2 4.7 %copy-start.7 = (s32[32,1,256]{2,1,0:T(1,128)}, s32[32,1,256]{2,1,0:T(1,128)S(1)}, u32[]{:S(2)}) copy-start(s32[32,1,256]{2,1,0:T(1,128)S(1)} %slice_convert_fusion.rows_ref) | copy-start | bytes 98308
  133.9 15.0 %copy-start.6 = (f32[256,16]{0,1:T(8,128)S(1)}, f32[256,16]{0,1:T(8,128)}, u32[]{:S(2)}) copy-start(f32[256,16]{0,1:T(8,128)} %param.9) | copy-start | bytes 49156
  143.2 30.3 %copy-start.16 = (f32[16,16,256]{2,1,0:T(8,128)S(1)}, f32[16,16,256]{2,1,0:T(8,128)}, u32[]{:S(2)}) copy-start(f32[16,16,256]{2,1,0:T(8,128)} %shard_map.70) | copy-start | bytes 786436
  143.2 26.8 %collective-permute-start.6 = (f32[16,16,256]{2,1,0:T(8,128)}, f32[16,16,256]{2,1,0:T(8,128)S(1)}, u32[]{:S(2)}, u32[]{:S(2)}) collective-permute-start(f32[16,16,256]{2,1,0:T(8,128)} %shard_map.70), channel_id=1, source_target_pairs={{0,1},{1,2},{2,3},{3,0},{4,5},{5,6},{6,7},{7,4},{8,9},{9,10},{10,1... | collective-permute-start | bytes 786440 | tf_op jit(solution)/shard_map/ppermute | solution.py:146
  144.8 28.7 %collective-permute-start.7 = (f32[16,16,256]{2,1,0:T(8,128)}, f32[16,16,256]{2,1,0:T(8,128)S(1)}, u32[]{:S(2)}, u32[]{:S(2)}) collective-permute-start(f32[16,16,256]{2,1,0:T(8,128)} %shard_map.70), channel_id=1, source_target_pairs={{0,2},{1,3},{2,0},{3,1},{4,6},{5,7},{6,4},{7,5},{8,10},{9,11},{10,... | collective-permute-start | bytes 786440 | tf_op jit(solution)/shard_map/ppermute | solution.py:146
  148.1 25.4 %collective-permute-start.8 = (f32[16,16,256]{2,1,0:T(8,128)}, f32[16,16,256]{2,1,0:T(8,128)S(1)}, u32[]{:S(2)}, u32[]{:S(2)}) collective-permute-start(f32[16,16,256]{2,1,0:T(8,128)} %shard_map.70), channel_id=1, source_target_pairs={{0,3},{1,0},{2,1},{3,2},{4,7},{5,4},{6,5},{7,6},{8,11},{9,8},{10,9... | collective-permute-start | bytes 786440 | tf_op jit(solution)/shard_map/ppermute | solution.py:146
  148.8 25.4 %copy-start.10 = (bf16[96,256]{1,0:T(8,128)(2,1)}, bf16[96,256]{1,0:T(8,128)(2,1)S(1)}, u32[]{:S(2)}) copy-start(bf16[96,256]{1,0:T(8,128)(2,1)S(1)} %constant_dynamic-update-slice_fusion.stacked_ref) | copy-start | bytes 147460
  157.3 24.8 %collective-permute-start.3 = (f32[16,16,256]{2,1,0:T(8,128)}, f32[16,16,256]{2,1,0:T(8,128)S(1)}, u32[]{:S(2)}, u32[]{:S(2)}) collective-permute-start(f32[16,16,256]{2,1,0:T(8,128)} %shard_map.68), channel_id=1, source_target_pairs={{0,1},{1,2},{2,3},{3,0},{4,5},{5,6},{6,7},{7,4},{8,9},{9,10},{10,1... | collective-permute-start | bytes 786440 | tf_op jit(solution)/shard_map/ppermute | solution.py:146
  158.0 24.1 %collective-permute-start.4 = (f32[16,16,256]{2,1,0:T(8,128)}, f32[16,16,256]{2,1,0:T(8,128)S(1)}, u32[]{:S(2)}, u32[]{:S(2)}) collective-permute-start(f32[16,16,256]{2,1,0:T(8,128)} %shard_map.68), channel_id=1, source_target_pairs={{0,2},{1,3},{2,0},{3,1},{4,6},{5,7},{6,4},{7,5},{8,10},{9,11},{10,... | collective-permute-start | bytes 786440 | tf_op jit(solution)/shard_map/ppermute | solution.py:146
  159.8 32.7 %all-to-all-start.1 = ((f32[128,1,1]{2,1,0:T(1,128)}), f32[128,1,1]{2,1,0:T(1,128)S(1)}, u32[]{:S(2)}, u32[]{:S(2)}) async-start(f32[128,1,1]{2,1,0:T(1,128)} %broadcast_in_dim.12), calls=%async_computation.1 | async-start | bytes 131072 | tf_op jit(solution)/shard_map/all_to_all | solution.py:152
  169.9 12.2 %copy-start.15 = (f32[16,16,256]{2,1,0:T(8,128)S(1)}, f32[16,16,256]{2,1,0:T(8,128)}, u32[]{:S(2)}) copy-start(f32[16,16,256]{2,1,0:T(8,128)} %shard_map.68) | copy-start | bytes 786436
  170.0 12.2 %collective-permute-start.5 = (f32[16,16,256]{2,1,0:T(8,128)}, f32[16,16,256]{2,1,0:T(8,128)S(1)}, u32[]{:S(2)}, u32[]{:S(2)}) collective-permute-start(f32[16,16,256]{2,1,0:T(8,128)} %shard_map.68), channel_id=1, source_target_pairs={{0,3},{1,0},{2,1},{3,2},{4,7},{5,4},{6,5},{7,6},{8,11},{9,8},{10,9... | collective-permute-start | bytes 786440 | tf_op jit(solution)/shard_map/ppermute | solution.py:146
  182.1 8.6 %copy-start.3 = (f32[512,256]{1,0:T(8,128)S(1)}, f32[512,256]{1,0:T(8,128)}, u32[]{:S(2)}) copy-start(f32[512,256]{1,0:T(8,128)} %shard_map.71) | copy-start | bytes 1572868
  193.7 17.2 %all-to-all-start.3 = ((f32[128,1,1]{2,1,0:T(1,128)}), f32[128,1,1]{2,1,0:T(1,128)S(1)}, u32[]{:S(2)}, u32[]{:S(2)}) async-start(f32[128,1,1]{2,1,0:T(1,128)} %broadcast_in_dim.26), calls=%async_computation.3 | async-start | bytes 131072 | tf_op jit(solution)/shard_map/all_to_all | solution.py:152
  224.1 25.9 %copy-start.11 = (f32[16,16,256]{2,1,0:T(8,128)S(1)}, f32[16,16,256]{2,1,0:T(8,128)}, u32[]{:S(2)}) copy-start(f32[16,16,256]{2,1,0:T(8,128)} %shard_map.74) | copy-start | bytes 786436
  224.1 24.6 %collective-permute-start.12 = (f32[16,16,256]{2,1,0:T(8,128)}, f32[16,16,256]{2,1,0:T(8,128)S(1)}, u32[]{:S(2)}, u32[]{:S(2)}) collective-permute-start(f32[16,16,256]{2,1,0:T(8,128)} %shard_map.74), channel_id=1, source_target_pairs={{0,1},{1,2},{2,3},{3,0},{4,5},{5,6},{6,7},{7,4},{8,9},{9,10},{10,1... | collective-permute-start | bytes 786440 | tf_op jit(solution)/shard_map/ppermute | solution.py:146
  224.6 25.3 %collective-permute-start.13 = (f32[16,16,256]{2,1,0:T(8,128)}, f32[16,16,256]{2,1,0:T(8,128)S(1)}, u32[]{:S(2)}, u32[]{:S(2)}) collective-permute-start(f32[16,16,256]{2,1,0:T(8,128)} %shard_map.74), channel_id=1, source_target_pairs={{0,2},{1,3},{2,0},{3,1},{4,6},{5,7},{6,4},{7,5},{8,10},{9,11},{10,... | collective-permute-start | bytes 786440 | tf_op jit(solution)/shard_map/ppermute | solution.py:146
  226.1 23.9 %collective-permute-start.14 = (f32[16,16,256]{2,1,0:T(8,128)}, f32[16,16,256]{2,1,0:T(8,128)S(1)}, u32[]{:S(2)}, u32[]{:S(2)}) collective-permute-start(f32[16,16,256]{2,1,0:T(8,128)} %shard_map.74), channel_id=1, source_target_pairs={{0,3},{1,0},{2,1},{3,2},{4,7},{5,4},{6,5},{7,6},{8,11},{9,8},{10,9... | collective-permute-start | bytes 786440 | tf_op jit(solution)/shard_map/ppermute | solution.py:146
  228.5 18.3 %all-to-all-start.4 = ((f32[128,1,1]{2,1,0:T(1,128)}), f32[128,1,1]{2,1,0:T(1,128)S(1)}, u32[]{:S(2)}, u32[]{:S(2)}) async-start(f32[128,1,1]{2,1,0:T(1,128)} %broadcast_in_dim.27), calls=%async_computation.4 | async-start | bytes 131072 | tf_op jit(solution)/shard_map/all_to_all | solution.py:152
  242.9 15.7 %collective-permute-start.10 = (f32[16,16,256]{2,1,0:T(8,128)}, f32[16,16,256]{2,1,0:T(8,128)S(1)}, u32[]{:S(2)}, u32[]{:S(2)}) collective-permute-start(f32[16,16,256]{2,1,0:T(8,128)} %shard_map.72), channel_id=1, source_target_pairs={{0,2},{1,3},{2,0},{3,1},{4,6},{5,7},{6,4},{7,5},{8,10},{9,11},{10,... | collective-permute-start | bytes 786440 | tf_op jit(solution)/shard_map/ppermute | solution.py:146
  246.1 12.5 %collective-permute-start.11 = (f32[16,16,256]{2,1,0:T(8,128)}, f32[16,16,256]{2,1,0:T(8,128)}, u32[]{:S(2)}, u32[]{:S(2)}) collective-permute-start(f32[16,16,256]{2,1,0:T(8,128)} %shard_map.72), channel_id=1, source_target_pairs={{0,3},{1,0},{2,1},{3,2},{4,7},{5,4},{6,5},{7,6},{8,11},{9,8},{10,9... | collective-permute-start | bytes 786440 | tf_op jit(solution)/shard_map/ppermute | solution.py:146
  248.6 10.1 %copy-start.13 = (f32[16,16,256]{2,1,0:T(8,128)S(1)}, f32[16,16,256]{2,1,0:T(8,128)}, u32[]{:S(2)}) copy-start(f32[16,16,256]{2,1,0:T(8,128)} %shard_map.72) | copy-start | bytes 786436
  248.7 10.0 %collective-permute-start.9 = (f32[16,16,256]{2,1,0:T(8,128)}, f32[16,16,256]{2,1,0:T(8,128)}, u32[]{:S(2)}, u32[]{:S(2)}) collective-permute-start(f32[16,16,256]{2,1,0:T(8,128)} %shard_map.72), channel_id=1, source_target_pairs={{0,1},{1,2},{2,3},{3,0},{4,5},{5,6},{6,7},{7,4},{8,9},{9,10},{10,1... | collective-permute-start | bytes 786440 | tf_op jit(solution)/shard_map/ppermute | solution.py:146
  258.6 9.8 %copy-start.4 = (f32[512,256]{1,0:T(8,128)S(1)}, f32[512,256]{1,0:T(8,128)}, u32[]{:S(2)}) copy-start(f32[512,256]{1,0:T(8,128)} %shard_map.69) | copy-start | bytes 1572868
  258.6 9.8 %copy-start.9 = (f32[512,256]{1,0:T(8,128)S(1)}, f32[512,256]{1,0:T(8,128)}, u32[]{:S(2)}) copy-start(f32[512,256]{1,0:T(8,128)} %shard_map.75) | copy-start | bytes 1572868
  302.2 26.4 %copy-start.12 = (f32[16,16,256]{2,1,0:T(8,128)S(1)}, f32[16,16,256]{2,1,0:T(8,128)}, u32[]{:S(2)}) copy-start(f32[16,16,256]{2,1,0:T(8,128)} %shard_map.78) | copy-start | bytes 786436
  302.2 25.2 %collective-permute-start.18 = (f32[16,16,256]{2,1,0:T(8,128)}, f32[16,16,256]{2,1,0:T(8,128)S(1)}, u32[]{:S(2)}, u32[]{:S(2)}) collective-permute-start(f32[16,16,256]{2,1,0:T(8,128)} %shard_map.78), channel_id=1, source_target_pairs={{0,1},{1,2},{2,3},{3,0},{4,5},{5,6},{6,7},{7,4},{8,9},{9,10},{10,1... | collective-permute-start | bytes 786440 | tf_op jit(solution)/shard_map/ppermute | solution.py:146
  302.8 25.8 %collective-permute-start.19 = (f32[16,16,256]{2,1,0:T(8,128)}, f32[16,16,256]{2,1,0:T(8,128)S(1)}, u32[]{:S(2)}, u32[]{:S(2)}) collective-permute-start(f32[16,16,256]{2,1,0:T(8,128)} %shard_map.78), channel_id=1, source_target_pairs={{0,2},{1,3},{2,0},{3,1},{4,6},{5,7},{6,4},{7,5},{8,10},{9,11},{10,... | collective-permute-start | bytes 786440 | tf_op jit(solution)/shard_map/ppermute | solution.py:146
  304.2 24.4 %collective-permute-start.20 = (f32[16,16,256]{2,1,0:T(8,128)}, f32[16,16,256]{2,1,0:T(8,128)}, u32[]{:S(2)}, u32[]{:S(2)}) collective-permute-start(f32[16,16,256]{2,1,0:T(8,128)} %shard_map.78), channel_id=1, source_target_pairs={{0,3},{1,0},{2,1},{3,2},{4,7},{5,4},{6,5},{7,6},{8,11},{9,8},{10,9... | collective-permute-start | bytes 786440 | tf_op jit(solution)/shard_map/ppermute | solution.py:146
  306.7 18.8 %all-to-all-start.6 = ((f32[128,1,1]{2,1,0:T(1,128)}), f32[128,1,1]{2,1,0:T(1,128)S(1)}, u32[]{:S(2)}, u32[]{:S(2)}) async-start(f32[128,1,1]{2,1,0:T(1,128)} %broadcast_in_dim.29), calls=%async_computation.6 | async-start | bytes 131072 | tf_op jit(solution)/shard_map/all_to_all | solution.py:152
  321.1 17.1 %collective-permute-start.15 = (f32[16,16,256]{2,1,0:T(8,128)}, f32[16,16,256]{2,1,0:T(8,128)S(1)}, u32[]{:S(2)}, u32[]{:S(2)}) collective-permute-start(f32[16,16,256]{2,1,0:T(8,128)} %shard_map.76), channel_id=1, source_target_pairs={{0,1},{1,2},{2,3},{3,0},{4,5},{5,6},{6,7},{7,4},{8,9},{9,10},{10,1... | collective-permute-start | bytes 786440 | tf_op jit(solution)/shard_map/ppermute | solution.py:146
  322.6 15.6 %collective-permute-start.16 = (f32[16,16,256]{2,1,0:T(8,128)}, f32[16,16,256]{2,1,0:T(8,128)}, u32[]{:S(2)}, u32[]{:S(2)}) collective-permute-start(f32[16,16,256]{2,1,0:T(8,128)} %shard_map.76), channel_id=1, source_target_pairs={{0,2},{1,3},{2,0},{3,1},{4,6},{5,7},{6,4},{7,5},{8,10},{9,11},{10,... | collective-permute-start | bytes 786440 | tf_op jit(solution)/shard_map/ppermute | solution.py:146
  327.4 10.8 %copy-start.14 = (f32[16,16,256]{2,1,0:T(8,128)S(1)}, f32[16,16,256]{2,1,0:T(8,128)}, u32[]{:S(2)}) copy-start(f32[16,16,256]{2,1,0:T(8,128)} %shard_map.76) | copy-start | bytes 786436
  327.4 10.7 %collective-permute-start.17 = (f32[16,16,256]{2,1,0:T(8,128)}, f32[16,16,256]{2,1,0:T(8,128)}, u32[]{:S(2)}, u32[]{:S(2)}) collective-permute-start(f32[16,16,256]{2,1,0:T(8,128)} %shard_map.76), channel_id=1, source_target_pairs={{0,3},{1,0},{2,1},{3,2},{4,7},{5,4},{6,5},{7,6},{8,11},{9,8},{10,9... | collective-permute-start | bytes 786440 | tf_op jit(solution)/shard_map/ppermute | solution.py:146
  338.1 9.7 %copy-start.8 = (f32[512,256]{1,0:T(8,128)S(1)}, f32[512,256]{1,0:T(8,128)}, u32[]{:S(2)}) copy-start(f32[512,256]{1,0:T(8,128)} %shard_map.79) | copy-start | bytes 1572868

commit v12 on v11

--- a/solution.py
+++ b/solution.py
@@ -93,7 +93,7 @@
     gather_flops = groups * 2 * 2 * run_length * BLK * channels
     m_high, m_middle, m_low = split3(modes_t)
     stacked = jnp.concatenate([m_high, m_high, m_high, m_middle, m_middle, m_low], axis=0)
-    halves = 2 if steps % 2 == 0 else 1
+    halves = 4 if steps % 4 == 0 else (2 if steps % 2 == 0 else 1)
     span = steps // halves
     binned = None
     for half in range(halves):

time: 378 us -> 455 us (1.20); the launches traced: 372 us -> 455 us
  Pallas kernels: 97.4 us -> 133 us
  starting transfers between devices: 79.6 us -> 109 us
  waiting for transfers between devices: 77 us -> 92 us
    pallas_call x6 -> x12, Pallas kernels: 46.8 us -> 64.5 us  [owner_operator(): pl.pallas_call(functools.partial(bin_kernel, offset), grid_spec=pltpu.Pre...]
    ppermute x21 -> x39, waiting for transfers between devices: 21.9 us -> 39.4 us  [chan_sum(): total = total + lax.ppermute(value, 'chan', pairs)]
    pallas_call x6 -> x12, Pallas kernels: 50.6 us -> 68 us  [owner_operator(): pl.pallas_call(functools.partial(amp_kernel, offset), grid_spec=pltpu.Pre...]
    ppermute x21 -> x39, starting transfers between devices: 33.7 us -> 49.1 us  [chan_sum(): total = total + lax.ppermute(value, 'chan', pairs)]
    all_to_all x1, starting transfers between devices: 7.53 us -> 18.5 us  [per_device(): arrived = lax.all_to_all(local_partial, 'tm', 0, 0, tiled=True)]
    add x6 -> x12, other arithmetic: 7.86 us -> 9.35 us  [chan_sum(): total = total + lax.ppermute(value, 'chan', pairs)]
  transfers between devices with their start and end apart: 27 -> 45, of which waited for: 6 -> 11; matrix products, arithmetic and copies ran while one was open for 12% -> 10% of each run, Pallas kernels for 15% -> 23%
where the time goes in v12:
time: 455 us
  Pallas kernels  133 us (29%)
  starting transfers between devices  109 us (24%)
  waiting for transfers between devices  92 us (20%)
  blocking collectives  37.2 us (8%)
  other arithmetic  36.1 us (8%)
  matrix products  28.5 us (6%)
  local copies, waits for them, and re-layouts  11.6 us (3%)
  between operations  7.89 us (2%)
    pallas_call x12, Pallas kernels, owner_operator(): pl.pallas_call(functools.partial(amp_kernel, offset), grid_spec=pltpu.Pre...  68 us
    pallas_call x12, Pallas kernels, owner_operator(): pl.pallas_call(functools.partial(bin_kernel, offset), grid_spec=pltpu.Pre...  64.5 us
    ppermute x39, starting transfers between devices, chan_sum(): total = total + lax.ppermute(value, 'chan', pairs)  49.1 us
    all_to_all x1, waiting for transfers between devices, per_device(): arrived = lax.all_to_all(local_partial, 'tm', 0, 0, tiled=True)  43.4 us
    ppermute x39, waiting for transfers between devices, chan_sum(): total = total + lax.ppermute(value, 'chan', pairs)  39.4 us
    all_to_all x2, blocking collectives, global_sum(): lax.all_to_all(jnp.broadcast_to(value, (everyone, 1)), ('tm', 'chan'), 0,...  37.2 us
    all_to_all x4, starting transfers between devices, global_sum(): lax.all_to_all(jnp.broadcast_to(value, (everyone, 1)), ('tm', 'chan'), 0,...  32.4 us
    all_to_all x1, starting transfers between devices, per_device(): arrived = lax.all_to_all(local_partial, 'tm', 0, 0, tiled=True)  18.5 us
  transfers between devices with their start and end apart: 45, of which 11 were waited for; matrix products, arithmetic and copies ran while one was open for 10% of the time, Pallas kernels for 23%

profile of v12, /device:TPU:1, one launch (start us, length us, event | category | flops | bytes accessed | tf_op | source)
XLA Modules:
  0.0 454.7 jit_solution(1299597640822367484)
XLA Ops:
  1.4 4.6 %pad_maximum_fusion = bf16[32,257,256]{2,1,0:T(8,128)(2,1)} fusion(bf16[32,1,256]{2,1,0:T(2,128)(2,1)S(1)} %convert_element_type.99, bf16[32,256,256]{2,1,0:T(8,128)(2,1)} %bitcast.63), kind=kLoop, calls=%fused_computation.5 | loop fusion | flops 8421376 | bytes 8421376 | tf_op jit(solution)/shard_map/concatenate | solution.py:168
  6.0 8.8 %all-to-all-start.2 = ((bf16[32,257,256]{2,1,0:T(8,128)(2,1)}), bf16[32,257,256]{2,1,0:T(8,128)(2,1)}, u32[]{:S(2)}, u32[]{:S(2)}) async-start(bf16[32,257,256]{2,1,0:T(8,128)(2,1)} %pad_maximum_fusion), calls=%async_computation.2 | async-start | bytes 8650752 | tf_op jit(solution)/shard_map/all_to_all | solution.py:169
  14.8 10.2 %fusion.7 = f32[16,32,256]{2,0,1:T(8,128)S(1)} fusion(bf16[32,256,256]{2,1,0:T(8,128)(2,1)} %bitcast.64, bf16[32,256,256]{2,1,0:T(8,128)(2,1)} %bitcast.67, f32[256,16]{0,1:T(8,128)S(1)} %copy-done.4), kind=kOutput, calls=%fused_computation.12 | convolution fusion | flops 408944640 | bytes 8929280 | tf_op jit(solution)/shard_map/csk,km->mcs/dot_general | solution.py:187
  25.0 3.8 collective-permute-start.2
  29.9 21.1 %collective-permute-done.2 = f32[16,32,256]{2,0,1:T(8,128)S(1)} collective-permute-done((f32[16,32,256]{2,0,1:T(8,128)S(1)}, f32[16,32,256]{2,0,1:T(8,128)S(1)}, u32[]{:S(2)}, u32[]{:S(2)}) %collective-permute-start.2) | collective-permute-done | bytes 524320 | tf_op jit(solution)/shard_map/ppermute | solution.py:146
  51.0 4.5 collective-permute-done
  55.5 7.0 %fusion.18 = f32[32,256,256]{2,1,0:T(8,128)S(1)} fusion(f32[16,32,256]{2,0,1:T(8,128)S(1)} %collective-permute-done.2, f32[16,32,256]{2,0,1:T(8,128)S(1)} %collective-permute-done.1, f32[16,32,256]{2,0,1:T(8,128)S(1)} %fusion.7, f32[16,32,256]{2,0,1:T(8,128)S(1)} %collective-permute-done, f32[256,16]{0,1:T(8,128)S(1)} %copy-done.4), kind=kOutput, calls=%fused_computation.47 | convolution fusion | flops 403046400 | bytes 10502144 | tf_op jit(solution)/shard_map/mcs,km->csk/dot_general | solution.py:190
  62.5 5.5 %fusion = f32[32,128,256]{2,1,0:T(8,128)} fusion(bf16[32,256,256]{2,1,0:T(8,128)(2,1)S(1)} %bitcast.65, f32[32,256,256]{2,1,0:T(8,128)S(1)} %fusion.18, bf16[32,256,256]{2,1,0:T(8,128)(2,1)S(1)} %bitcast.68, s32[32,256]{1,0:T(8,128)S(1)} %eq.47), kind=kOutput, calls=%fused_computation.2 | convolution fusion | flops 1622147072 | bytes 21004288 | tf_op jit(solution)/shard_map/csp,csk->cpk/dot_general | solution.py:229
  68.4 18.5 %all-to-all-start = ((f32[32,128,256]{2,1,0:T(8,128)}), f32[32,128,256]{2,1,0:T(8,128)}, u32[]{:S(2)}, u32[]{:S(2)}) async-start(f32[32,128,256]{2,1,0:T(8,128)} %fusion), calls=%async_computation | async-start | bytes 8388608 | tf_op jit(solution)/shard_map/all_to_all | solution.py:230
  88.2 4.6 %slice.9.weights_ref = bf16[32,256,256]{2,1,0:T(8,128)(2,1)} slice(bf16[32,257,256]{2,1,0:T(8,128)(2,1)} %all-to-all-done.2), slice={[0:32], [0:256], [0:256]} | slice | bytes 8388608 | tf_op jit(solution)/shard_map/slice | solution.py:170
  92.8 2.6 fusion.5.hits_ref
  95.4 43.4 %all-to-all-done = f32[32,128,256]{2,1,0:T(8,128)} async-done(((f32[32,128,256]{2,1,0:T(8,128)}), f32[32,128,256]{2,1,0:T(8,128)}, u32[]{:S(2)}, u32[]{:S(2)}) %all-to-all-start) | async-done | bytes 4194336 | tf_op jit(solution)/shard_map/all_to_all | solution.py:230
  138.9 5.8 %multiply_reduce_fusion.4 = (f32[]{:T(128)}, f32[4,128,256]{2,0,1:T(4,128)S(1)}) fusion(f32[32,128,256]{2,1,0:T(8,128)} %all-to-all-done, s32[32]{0:T(128)S(1)} %dynamic-slice_reduce_fusion.blocks_ref), kind=kOutput, calls=%fused_computation.46 | convolution fusion | flops 25428096 | bytes 4718724 | tf_op jit(solution)/shard_map/cb,cpk->bpk/dot_general | solution.py:231
  145.7 5.6 %shard_map.74 = f32[8,16,256]{2,1,0:T(8,128)} custom-call(s32[32]{0:T(128)} %copy-done.26, bf16[2,512,256]{2,1,0:T(8,128)(2,1)} %pad_maximum_fusion.1.parts_ref, bf16[32,256,128]{2,1,0:T(8,128)(2,1)} %fusion.5.hits_ref, bf16[32,256,256]{2,1,0:T(8,128)(2,1)} %slice.9.weights_ref, f32[16,256]{1,0:T(8,128)} %bitcast.69), custom_call_target="tpu_custom_call" | custom-call | flops 369098752 | bytes 1572864 | tf_op jit(solution)/shard_map/pallas_call | solution.py:103
  151.3 3.8 collective-permute-start.14
  155.8 5.6 %shard_map.72 = f32[8,16,256]{2,1,0:T(8,128)} custom-call(s32[32]{0:T(128)} %copy-done.26, bf16[2,512,256]{2,1,0:T(8,128)(2,1)} %pad_maximum_fusion.1.parts_ref, bf16[32,256,128]{2,1,0:T(8,128)(2,1)} %fusion.5.hits_ref, bf16[32,256,256]{2,1,0:T(8,128)(2,1)} %slice.9.weights_ref, f32[16,256]{1,0:T(8,128)} %bitcast.70), custom_call_target="tpu_custom_call" | custom-call | flops 369098752 | bytes 1572864 | tf_op jit(solution)/shard_map/pallas_call | solution.py:103
  161.4 2.0 collective-permute-start.11
  163.4 1.8 collective-permute-start.10
  166.5 8.5 %all-to-all-start.1 = ((f32[128,1,1]{2,1,0:T(1,128)}), f32[128,1,1]{2,1,0:T(1,128)S(1)}, u32[]{:S(2)}, u32[]{:S(2)}) async-start(f32[128,1,1]{2,1,0:T(1,128)} %broadcast_in_dim.12), calls=%async_computation.1 | async-start | bytes 131072 | tf_op jit(solution)/shard_map/all_to_all | solution.py:152
  175.0 5.6 %shard_map.68 = f32[8,16,256]{2,1,0:T(8,128)} custom-call(s32[32]{0:T(128)} %copy-done.26, bf16[2,512,256]{2,1,0:T(8,128)(2,1)} %pad_maximum_fusion.1.parts_ref, bf16[32,256,128]{2,1,0:T(8,128)(2,1)} %fusion.5.hits_ref, bf16[32,256,256]{2,1,0:T(8,128)(2,1)} %slice.9.weights_ref, f32[16,256]{1,0:T(8,128)} %bitcast.71), custom_call_target="tpu_custom_call" | custom-call | flops 369098752 | bytes 1572864 | tf_op jit(solution)/shard_map/pallas_call | solution.py:103
  180.7 5.8 %shard_map.70 = f32[8,16,256]{2,1,0:T(8,128)} custom-call(s32[32]{0:T(128)} %copy-done.26, bf16[2,512,256]{2,1,0:T(8,128)(2,1)} %pad_maximum_fusion.1.parts_ref, bf16[32,256,128]{2,1,0:T(8,128)(2,1)} %fusion.5.hits_ref, bf16[32,256,256]{2,1,0:T(8,128)(2,1)} %slice.9.weights_ref, f32[16,256]{1,0:T(8,128)} %bitcast.72), custom_call_target="tpu_custom_call" | custom-call | flops 369098752 | bytes 1572864 | tf_op jit(solution)/shard_map/pallas_call | solution.py:103
  188.0 1.8 collective-permute-start.5
  192.5 2.1 collective-permute-start.8
  196.9 3.9 collective-permute-done.3
  201.5 5.3 %shard_map.75 = f32[512,256]{1,0:T(8,128)} custom-call(s32[32]{0:T(128)} %copy-done.26, bf16[2,512,256]{2,1,0:T(8,128)(2,1)} %pad_maximum_fusion.1.parts_ref, bf16[32,256,128]{2,1,0:T(8,128)(2,1)} %fusion.5.hits_ref, s32[32,1,256]{2,1,0:T(1,128)} %copy-done.6, bf16[32,256,256]{2,1,0:T(8,128)(2,1)} %slice.9.weights_ref, f32[8,16,256]{2,1,0:T(8,128)} %add_add_fusion.8.amp_ref, ...), custom_call_target="tpu_custom_call" | custom-call | flops 637534208 | bytes 2097152 | tf_op jit(solution)/shard_map/pallas_call | solution.py:120
  206.8 5.3 %shard_map.73 = f32[512,256]{1,0:T(8,128)} custom-call(s32[32]{0:T(128)} %copy-done.26, bf16[2,512,256]{2,1,0:T(8,128)(2,1)} %pad_maximum_fusion.1.parts_ref, bf16[32,256,128]{2,1,0:T(8,128)(2,1)} %fusion.5.hits_ref, s32[32,1,256]{2,1,0:T(1,128)} %copy-done.6, bf16[32,256,256]{2,1,0:T(8,128)(2,1)} %slice.9.weights_ref, f32[8,16,256]{2,1,0:T(8,128)} %add_add_fusion.9.amp_ref, ...), custom_call_target="tpu_custom_call" | custom-call | flops 637534208 | bytes 2097152 | tf_op jit(solution)/shard_map/pallas_call | solution.py:120
  212.2 5.5 %shard_map.69 = f32[512,256]{1,0:T(8,128)} custom-call(s32[32]{0:T(128)} %copy-done.26, bf16[2,512,256]{2,1,0:T(8,128)(2,1)} %pad_maximum_fusion.1.parts_ref, bf16[32,256,128]{2,1,0:T(8,128)(2,1)} %fusion.5.hits_ref, s32[32,1,256]{2,1,0:T(1,128)} %copy-done.6, bf16[32,256,256]{2,1,0:T(8,128)(2,1)} %slice.9.weights_ref, ...), custom_call_target="tpu_custom_call" | custom-call | flops 637534208 | bytes 2097152 | tf_op jit(solution)/shard_map/pallas_call | solution.py:120
  218.4 5.3 %shard_map.71 = f32[512,256]{1,0:T(8,128)} custom-call(s32[32]{0:T(128)} %copy-done.26, bf16[2,512,256]{2,1,0:T(8,128)(2,1)} %pad_maximum_fusion.1.parts_ref, bf16[32,256,128]{2,1,0:T(8,128)(2,1)} %fusion.5.hits_ref, s32[32,1,256]{2,1,0:T(1,128)} %copy-done.6, bf16[32,256,256]{2,1,0:T(8,128)(2,1)} %slice.9.weights_ref, ...), custom_call_target="tpu_custom_call" | custom-call | flops 637534208 | bytes 2097152 | tf_op jit(solution)/shard_map/pallas_call | solution.py:120
  223.7 1.8 fusion.14
  226.9 9.1 %all-to-all-start.3 = ((f32[128,1,1]{2,1,0:T(1,128)}), f32[128,1,1]{2,1,0:T(1,128)S(1)}, u32[]{:S(2)}, u32[]{:S(2)}) async-start(f32[128,1,1]{2,1,0:T(1,128)} %broadcast_in_dim.26), calls=%async_computation.3 | async-start | bytes 131072 | tf_op jit(solution)/shard_map/all_to_all | solution.py:152
  236.8 8.8 %all-to-all-done.3 = f32[128,1,1]{2,1,0:T(1,128)S(1)} async-done(((f32[128,1,1]{2,1,0:T(1,128)}), f32[128,1,1]{2,1,0:T(1,128)S(1)}, u32[]{:S(2)}, u32[]{:S(2)}) %all-to-all-start.3) | async-done | bytes 544 | tf_op jit(solution)/shard_map/all_to_all | solution.py:152
  249.4 5.6 %shard_map.82 = f32[8,16,256]{2,1,0:T(8,128)} custom-call(s32[32]{0:T(128)} %copy-done.26, bf16[2,512,256]{2,1,0:T(8,128)(2,1)} %pad_maximum_fusion.2.parts_ref, bf16[32,256,128]{2,1,0:T(8,128)(2,1)} %fusion.5.hits_ref, bf16[32,256,256]{2,1,0:T(8,128)(2,1)} %slice.9.weights_ref, f32[16,256]{1,0:T(8,128)} %bitcast.73), custom_call_target="tpu_custom_call" | custom-call | flops 369098752 | bytes 1572864 | tf_op jit(solution)/shard_map/pallas_call | solution.py:103
  255.8 1.6 collective-permute-start.25
  257.5 5.6 %shard_map.80 = f32[8,16,256]{2,1,0:T(8,128)} custom-call(s32[32]{0:T(128)} %copy-done.26, bf16[2,512,256]{2,1,0:T(8,128)(2,1)} %pad_maximum_fusion.2.parts_ref, bf16[32,256,128]{2,1,0:T(8,128)(2,1)} %fusion.5.hits_ref, bf16[32,256,256]{2,1,0:T(8,128)(2,1)} %slice.9.weights_ref, f32[16,256]{1,0:T(8,128)} %bitcast.74), custom_call_target="tpu_custom_call" | custom-call | flops 369098752 | bytes 1572864 | tf_op jit(solution)/shard_map/pallas_call | solution.py:103
  263.1 2.7 collective-permute-start.23
  267.3 7.4 %all-to-all-start.4 = ((f32[128,1,1]{2,1,0:T(1,128)}), f32[128,1,1]{2,1,0:T(1,128)S(1)}, u32[]{:S(2)}, u32[]{:S(2)}) async-start(f32[128,1,1]{2,1,0:T(1,128)} %broadcast_in_dim.27), calls=%async_computation.4 | async-start | bytes 131072 | tf_op jit(solution)/shard_map/all_to_all | solution.py:152
  274.7 5.6 %shard_map.76 = f32[8,16,256]{2,1,0:T(8,128)} custom-call(s32[32]{0:T(128)} %copy-done.26, bf16[2,512,256]{2,1,0:T(8,128)(2,1)} %pad_maximum_fusion.2.parts_ref, bf16[32,256,128]{2,1,0:T(8,128)(2,1)} %fusion.5.hits_ref, bf16[32,256,256]{2,1,0:T(8,128)(2,1)} %slice.9.weights_ref, f32[16,256]{1,0:T(8,128)} %bitcast.75), custom_call_target="tpu_custom_call" | custom-call | flops 369098752 | bytes 1572864 | tf_op jit(solution)/shard_map/pallas_call | solution.py:103
  280.4 5.8 %shard_map.78 = f32[8,16,256]{2,1,0:T(8,128)} custom-call(s32[32]{0:T(128)} %copy-done.26, bf16[2,512,256]{2,1,0:T(8,128)(2,1)} %pad_maximum_fusion.2.parts_ref, bf16[32,256,128]{2,1,0:T(8,128)(2,1)} %fusion.5.hits_ref, bf16[32,256,256]{2,1,0:T(8,128)(2,1)} %slice.9.weights_ref, f32[16,256]{1,0:T(8,128)} %bitcast.76), custom_call_target="tpu_custom_call" | custom-call | flops 369098752 | bytes 1572864 | tf_op jit(solution)/shard_map/pallas_call | solution.py:103
  289.8 1.8 collective-permute-start.17
  294.3 2.1 collective-permute-start.20
  298.8 3.9 collective-permute-done.15
  303.3 5.3 %shard_map.83 = f32[512,256]{1,0:T(8,128)} custom-call(s32[32]{0:T(128)} %copy-done.26, bf16[2,512,256]{2,1,0:T(8,128)(2,1)} %pad_maximum_fusion.2.parts_ref, bf16[32,256,128]{2,1,0:T(8,128)(2,1)} %fusion.5.hits_ref, s32[32,1,256]{2,1,0:T(1,128)} %copy-done.6, bf16[32,256,256]{2,1,0:T(8,128)(2,1)} %slice.9.weights_ref, f32[8,16,256]{2,1,0:T(8,128)} %add_add_fusion.4.amp_ref, ...), custom_call_target="tpu_custom_call" | custom-call | flops 637534208 | bytes 2097152 | tf_op jit(solution)/shard_map/pallas_call | solution.py:120
  308.7 5.3 %shard_map.81 = f32[512,256]{1,0:T(8,128)} custom-call(s32[32]{0:T(128)} %copy-done.26, bf16[2,512,256]{2,1,0:T(8,128)(2,1)} %pad_maximum_fusion.2.parts_ref, bf16[32,256,128]{2,1,0:T(8,128)(2,1)} %fusion.5.hits_ref, s32[32,1,256]{2,1,0:T(1,128)} %copy-done.6, bf16[32,256,256]{2,1,0:T(8,128)(2,1)} %slice.9.weights_ref, f32[8,16,256]{2,1,0:T(8,128)} %add_add_fusion.5.amp_ref, ...), custom_call_target="tpu_custom_call" | custom-call | flops 637534208 | bytes 2097152 | tf_op jit(solution)/shard_map/pallas_call | solution.py:120
  314.0 5.5 %shard_map.77 = f32[512,256]{1,0:T(8,128)} custom-call(s32[32]{0:T(128)} %copy-done.26, bf16[2,512,256]{2,1,0:T(8,128)(2,1)} %pad_maximum_fusion.2.parts_ref, bf16[32,256,128]{2,1,0:T(8,128)(2,1)} %fusion.5.hits_ref, s32[32,1,256]{2,1,0:T(1,128)} %copy-done.6, bf16[32,256,256]{2,1,0:T(8,128)(2,1)} %slice.9.weights_ref, f32[8,16,256]{2,1,0:T(8,128)} %add_add_fusion.7.amp_ref, ...), custom_call_target="tpu_custom_call" | custom-call | flops 637534208 | bytes 2097152 | tf_op jit(solution)/shard_map/pallas_call | solution.py:120
  320.2 5.3 %shard_map.79 = f32[512,256]{1,0:T(8,128)} custom-call(s32[32]{0:T(128)} %copy-done.26, bf16[2,512,256]{2,1,0:T(8,128)(2,1)} %pad_maximum_fusion.2.parts_ref, bf16[32,256,128]{2,1,0:T(8,128)(2,1)} %fusion.5.hits_ref, s32[32,1,256]{2,1,0:T(1,128)} %copy-done.6, bf16[32,256,256]{2,1,0:T(8,128)(2,1)} %slice.9.weights_ref, f32[8,16,256]{2,1,0:T(8,128)} %add_add_fusion.6.amp_ref, ...), custom_call_target="tpu_custom_call" | custom-call | flops 637534208 | bytes 2097152 | tf_op jit(solution)/shard_map/pallas_call | solution.py:120
  325.6 2.0 multiply_reduce_fusion.2
  328.3 18.6 %all_to_all.46 = f32[128,1,1]{2,1,0:T(1,128)S(1)} all-to-all(f32[128,1,1]{2,1,0:T(1,128)S(1)} %broadcast_in_dim.28), channel_id=1, replica_groups=mesh['tm'=32,'chan'=4] {'tm','chan'}, dimensions={0} | all-to-all | bytes 1024 | tf_op jit(solution)/shard_map/all_to_all | solution.py:152
  350.7 5.6 %shard_map.90 = f32[8,16,256]{2,1,0:T(8,128)} custom-call(s32[32]{0:T(128)} %copy-done.26, bf16[2,512,256]{2,1,0:T(8,128)(2,1)} %pad_maximum_fusion.3.parts_ref, bf16[32,256,128]{2,1,0:T(8,128)(2,1)} %fusion.5.hits_ref, bf16[32,256,256]{2,1,0:T(8,128)(2,1)} %slice.9.weights_ref, f32[16,256]{1,0:T(8,128)} %bitcast.77), custom_call_target="tpu_custom_call" | custom-call | flops 369098752 | bytes 1572864 | tf_op jit(solution)/shard_map/pallas_call | solution.py:103
  359.1 5.6 %shard_map.88 = f32[8,16,256]{2,1,0:T(8,128)} custom-call(s32[32]{0:T(128)} %copy-done.26, bf16[2,512,256]{2,1,0:T(8,128)(2,1)} %pad_maximum_fusion.3.parts_ref, bf16[32,256,128]{2,1,0:T(8,128)(2,1)} %fusion.5.hits_ref, bf16[32,256,256]{2,1,0:T(8,128)(2,1)} %slice.9.weights_ref, f32[16,256]{1,0:T(8,128)} %bitcast.78), custom_call_target="tpu_custom_call" | custom-call | flops 369098752 | bytes 1572864 | tf_op jit(solution)/shard_map/pallas_call | solution.py:103
  364.7 2.7 collective-permute-start.35
  368.9 7.4 %all-to-all-start.6 = ((f32[128,1,1]{2,1,0:T(1,128)}), f32[128,1,1]{2,1,0:T(1,128)S(1)}, u32[]{:S(2)}, u32[]{:S(2)}) async-start(f32[128,1,1]{2,1,0:T(1,128)} %broadcast_in_dim.29), calls=%async_computation.6 | async-start | bytes 131072 | tf_op jit(solution)/shard_map/all_to_all | solution.py:152
  376.3 5.6 %shard_map.84 = f32[8,16,256]{2,1,0:T(8,128)} custom-call(s32[32]{0:T(128)} %copy-done.26, bf16[2,512,256]{2,1,0:T(8,128)(2,1)} %pad_maximum_fusion.3.parts_ref, bf16[32,256,128]{2,1,0:T(8,128)(2,1)} %fusion.5.hits_ref, bf16[32,256,256]{2,1,0:T(8,128)(2,1)} %slice.9.weights_ref, f32[16,256]{1,0:T(8,128)} %bitcast.79), custom_call_target="tpu_custom_call" | custom-call | flops 369098752 | bytes 1572864 | tf_op jit(solution)/shard_map/pallas_call | solution.py:103
  382.0 5.8 %shard_map.86 = f32[8,16,256]{2,1,0:T(8,128)} custom-call(s32[32]{0:T(128)} %copy-done.26, bf16[2,512,256]{2,1,0:T(8,128)(2,1)} %pad_maximum_fusion.3.parts_ref, bf16[32,256,128]{2,1,0:T(8,128)(2,1)} %fusion.5.hits_ref, bf16[32,256,256]{2,1,0:T(8,128)(2,1)} %slice.9.weights_ref, f32[16,256]{1,0:T(8,128)} %bitcast.80), custom_call_target="tpu_custom_call" | custom-call | flops 369098752 | bytes 1572864 | tf_op jit(solution)/shard_map/pallas_call | solution.py:103
  391.4 1.8 collective-permute-start.29
  395.9 2.1 collective-permute-start.32
  400.4 3.9 collective-permute-done.27
  404.9 5.3 %shard_map.91 = f32[512,256]{1,0:T(8,128)} custom-call(s32[32]{0:T(128)} %copy-done.26, bf16[2,512,256]{2,1,0:T(8,128)(2,1)} %pad_maximum_fusion.3.parts_ref, bf16[32,256,128]{2,1,0:T(8,128)(2,1)} %fusion.5.hits_ref, s32[32,1,256]{2,1,0:T(1,128)} %copy-done.6, bf16[32,256,256]{2,1,0:T(8,128)(2,1)} %slice.9.weights_ref, f32[8,16,256]{2,1,0:T(8,128)} %add_add_fusion.amp_ref, ...), custom_call_target="tpu_custom_call" | custom-call | flops 637534208 | bytes 2097152 | tf_op jit(solution)/shard_map/pallas_call | solution.py:120
  410.3 5.3 %shard_map.89 = f32[512,256]{1,0:T(8,128)} custom-call(s32[32]{0:T(128)} %copy-done.26, bf16[2,512,256]{2,1,0:T(8,128)(2,1)} %pad_maximum_fusion.3.parts_ref, bf16[32,256,128]{2,1,0:T(8,128)(2,1)} %fusion.5.hits_ref, s32[32,1,256]{2,1,0:T(1,128)} %copy-done.6, bf16[32,256,256]{2,1,0:T(8,128)(2,1)} %slice.9.weights_ref, f32[8,16,256]{2,1,0:T(8,128)} %add_add_fusion.1.amp_ref, ...), custom_call_target="tpu_custom_call" | custom-call | flops 637534208 | bytes 2097152 | tf_op jit(solution)/shard_map/pallas_call | solution.py:120
  415.6 5.5 %shard_map.85 = f32[512,256]{1,0:T(8,128)} custom-call(s32[32]{0:T(128)} %copy-done.26, bf16[2,512,256]{2,1,0:T(8,128)(2,1)} %pad_maximum_fusion.3.parts_ref, bf16[32,256,128]{2,1,0:T(8,128)(2,1)} %fusion.5.hits_ref, s32[32,1,256]{2,1,0:T(1,128)} %copy-done.6, bf16[32,256,256]{2,1,0:T(8,128)(2,1)} %slice.9.weights_ref, f32[8,16,256]{2,1,0:T(8,128)} %add_add_fusion.3.amp_ref, ...), custom_call_target="tpu_custom_call" | custom-call | flops 637534208 | bytes 2097152 | tf_op jit(solution)/shard_map/pallas_call | solution.py:120
  421.1 1.7 add_add_fusion.2.amp_ref
  422.8 5.3 %shard_map.87 = f32[512,256]{1,0:T(8,128)} custom-call(s32[32]{0:T(128)} %copy-done.26, bf16[2,512,256]{2,1,0:T(8,128)(2,1)} %pad_maximum_fusion.3.parts_ref, bf16[32,256,128]{2,1,0:T(8,128)(2,1)} %fusion.5.hits_ref, s32[32,1,256]{2,1,0:T(1,128)} %copy-done.6, bf16[32,256,256]{2,1,0:T(8,128)(2,1)} %slice.9.weights_ref, f32[8,16,256]{2,1,0:T(8,128)} %add_add_fusion.2.amp_ref, ...), custom_call_target="tpu_custom_call" | custom-call | flops 637534208 | bytes 2097152 | tf_op jit(solution)/shard_map/pallas_call | solution.py:120
  428.2 2.8 multiply_reduce_fusion
  431.7 18.6 %all_to_all.47 = f32[128,1,1]{2,1,0:T(1,128)S(1)} all-to-all(f32[128,1,1]{2,1,0:T(1,128)S(1)} %broadcast_in_dim.30), channel_id=1, replica_groups=mesh['tm'=32,'chan'=4] {'tm','chan'}, dimensions={0} | all-to-all | bytes 1024 | tf_op jit(solution)/shard_map/all_to_all | solution.py:152
  452.3 2.2 multiply_subtract_fusion
  (164 shorter events, 46.9 us)
Async XLA Ops:
  0.6 86.3 %copy-start = (s32[32,32]{1,0:T(8,128)S(1)}, s32[32,32]{1,0:T(8,128)}, u32[]{:S(2)}) copy-start(s32[32,32]{1,0:T(8,128)} %param.8) | copy-start | bytes 12292
  6.0 8.8 %copy-start.4 = (f32[256,16]{0,1:T(8,128)S(1)}, f32[256,16]{0,1:T(8,128)}, u32[]{:S(2)}) copy-start(f32[256,16]{0,1:T(8,128)} %param.9) | copy-start | bytes 49156
  6.0 62.4 %all-to-all-start.2 = ((bf16[32,257,256]{2,1,0:T(8,128)(2,1)}), bf16[32,257,256]{2,1,0:T(8,128)(2,1)}, u32[]{:S(2)}, u32[]{:S(2)}) async-start(bf16[32,257,256]{2,1,0:T(8,128)(2,1)} %pad_maximum_fusion), calls=%async_computation.2 | async-start | bytes 8650752 | tf_op jit(solution)/shard_map/all_to_all | solution.py:169
  14.8 15.1 %copy-start.27 = (s32[8192]{0:T(1024)S(1)}, s32[8192]{0:T(1024)}, u32[]{:S(2)}) copy-start(s32[8192]{0:T(1024)} %param.7) | copy-start | bytes 98308
  25.0 26.0 %collective-permute-start.2 = (f32[16,32,256]{2,0,1:T(8,128)S(1)}, f32[16,32,256]{2,0,1:T(8,128)S(1)}, u32[]{:S(2)}, u32[]{:S(2)}) collective-permute-start(f32[16,32,256]{2,0,1:T(8,128)S(1)} %fusion.7), channel_id=1, source_target_pairs={{0,3},{1,0},{2,1},{3,2},{4,7},{5,4},{6,5},{7,6},{8,11},{9,8},{10,9... | collective-permute-start | bytes 1572872 | tf_op jit(solution)/shard_map/ppermute | solution.py:146
  28.8 22.2 %collective-permute-start.1 = (f32[16,32,256]{2,0,1:T(8,128)S(1)}, f32[16,32,256]{2,0,1:T(8,128)S(1)}, u32[]{:S(2)}, u32[]{:S(2)}) collective-permute-start(f32[16,32,256]{2,0,1:T(8,128)S(1)} %fusion.7), channel_id=1, source_target_pairs={{0,2},{1,3},{2,0},{3,1},{4,6},{5,7},{6,4},{7,5},{8,10},{9,11},{10,... | collective-permute-start | bytes 1572872 | tf_op jit(solution)/shard_map/ppermute | solution.py:146
  28.8 26.7 %collective-permute-start = (f32[16,32,256]{2,0,1:T(8,128)S(1)}, f32[16,32,256]{2,0,1:T(8,128)S(1)}, u32[]{:S(2)}, u32[]{:S(2)}) collective-permute-start(f32[16,32,256]{2,0,1:T(8,128)S(1)} %fusion.7), channel_id=1, source_target_pairs={{0,1},{1,2},{2,3},{3,0},{4,5},{5,6},{6,7},{7,4},{8,9},{9,10},{10,1... | collective-permute-start | bytes 1572872 | tf_op jit(solution)/shard_map/ppermute | solution.py:146
  29.9 32.7 %copy-start.1 = (bf16[8192,256]{1,0:T(8,128)(2,1)S(1)}, bf16[8192,256]{1,0:T(8,128)(2,1)}, u32[]{:S(2)}) copy-start(bf16[8192,256]{1,0:T(8,128)(2,1)} %param.6) | copy-start | bytes 12582916
  29.9 32.7 %copy-start.2 = (bf16[8192,256]{1,0:T(8,128)(2,1)S(1)}, bf16[8192,256]{1,0:T(8,128)(2,1)}, u32[]{:S(2)}) copy-start(bf16[8192,256]{1,0:T(8,128)(2,1)} %param.5) | copy-start | bytes 12582916
  68.4 70.4 %all-to-all-start = ((f32[32,128,256]{2,1,0:T(8,128)}), f32[32,128,256]{2,1,0:T(8,128)}, u32[]{:S(2)}, u32[]{:S(2)}) async-start(f32[32,128,256]{2,1,0:T(8,128)} %fusion), calls=%async_computation | async-start | bytes 8388608 | tf_op jit(solution)/shard_map/all_to_all | solution.py:230
  87.1 51.7 %copy-start.26 = (s32[32]{0:T(128)}, s32[32]{0:T(128)S(1)}, u32[]{:S(2)}) copy-start(s32[32]{0:T(128)S(1)} %dynamic-slice_reduce_fusion.blocks_ref) | copy-start | bytes 388
  144.8 10.9 %copy-start.5 = (f32[256,16]{0,1:T(8,128)S(1)}, f32[256,16]{0,1:T(8,128)}, u32[]{:S(2)}) copy-start(f32[256,16]{0,1:T(8,128)} %param.9) | copy-start | bytes 49156
  151.3 35.1 %collective-permute-start.14 = (f32[8,16,256]{2,1,0:T(8,128)}, f32[8,16,256]{2,1,0:T(8,128)S(1)}, u32[]{:S(2)}, u32[]{:S(2)}) collective-permute-start(f32[8,16,256]{2,1,0:T(8,128)} %shard_map.74), channel_id=1, source_target_pairs={{0,3},{1,0},{2,1},{3,2},{4,7},{5,4},{6,5},{7,6},{8,11},{9,8},{10,9... | collective-permute-start | bytes 393224 | tf_op jit(solution)/shard_map/ppermute | solution.py:146
  155.1 32.9 %collective-permute-start.13 = (f32[8,16,256]{2,1,0:T(8,128)}, f32[8,16,256]{2,1,0:T(8,128)S(1)}, u32[]{:S(2)}, u32[]{:S(2)}) collective-permute-start(f32[8,16,256]{2,1,0:T(8,128)} %shard_map.74), channel_id=1, source_target_pairs={{0,2},{1,3},{2,0},{3,1},{4,6},{5,7},{6,4},{7,5},{8,10},{9,11},{10,... | collective-permute-start | bytes 393224 | tf_op jit(solution)/shard_map/ppermute | solution.py:146
  155.1 34.7 %collective-permute-start.12 = (f32[8,16,256]{2,1,0:T(8,128)}, f32[8,16,256]{2,1,0:T(8,128)S(1)}, u32[]{:S(2)}, u32[]{:S(2)}) collective-permute-start(f32[8,16,256]{2,1,0:T(8,128)} %shard_map.74), channel_id=1, source_target_pairs={{0,1},{1,2},{2,3},{3,0},{4,5},{5,6},{6,7},{7,4},{8,9},{9,10},{10,1... | collective-permute-start | bytes 393224 | tf_op jit(solution)/shard_map/ppermute | solution.py:146
  155.8 24.9 %copy-start.3 = (bf16[96,256]{1,0:T(8,128)(2,1)}, bf16[96,256]{1,0:T(8,128)(2,1)S(1)}, u32[]{:S(2)}) copy-start(bf16[96,256]{1,0:T(8,128)(2,1)S(1)} %constant_dynamic-update-slice_fusion.stacked_ref) | copy-start | bytes 147460
  161.4 30.5 %collective-permute-start.11 = (f32[8,16,256]{2,1,0:T(8,128)}, f32[8,16,256]{2,1,0:T(8,128)S(1)}, u32[]{:S(2)}, u32[]{:S(2)}) collective-permute-start(f32[8,16,256]{2,1,0:T(8,128)} %shard_map.72), channel_id=1, source_target_pairs={{0,3},{1,0},{2,1},{3,2},{4,7},{5,4},{6,5},{7,6},{8,11},{9,8},{10,9... | collective-permute-start | bytes 393224 | tf_op jit(solution)/shard_map/ppermute | solution.py:146
  163.4 29.0 %collective-permute-start.10 = (f32[8,16,256]{2,1,0:T(8,128)}, f32[8,16,256]{2,1,0:T(8,128)S(1)}, u32[]{:S(2)}, u32[]{:S(2)}) collective-permute-start(f32[8,16,256]{2,1,0:T(8,128)} %shard_map.72), channel_id=1, source_target_pairs={{0,2},{1,3},{2,0},{3,1},{4,6},{5,7},{6,4},{7,5},{8,10},{9,11},{10,... | collective-permute-start | bytes 393224 | tf_op jit(solution)/shard_map/ppermute | solution.py:146
  166.5 59.1 %all-to-all-start.1 = ((f32[128,1,1]{2,1,0:T(1,128)}), f32[128,1,1]{2,1,0:T(1,128)S(1)}, u32[]{:S(2)}, u32[]{:S(2)}) async-start(f32[128,1,1]{2,1,0:T(1,128)} %broadcast_in_dim.12), calls=%async_computation.1 | async-start | bytes 131072 | tf_op jit(solution)/shard_map/all_to_all | solution.py:152
  180.7 7.3 %copy-start.21 = (f32[8,16,256]{2,1,0:T(8,128)S(1)}, f32[8,16,256]{2,1,0:T(8,128)}, u32[]{:S(2)}) copy-start(f32[8,16,256]{2,1,0:T(8,128)} %shard_map.68) | copy-start | bytes 393220
  180.7 10.5 %copy-start.25 = (f32[8,16,256]{2,1,0:T(8,128)S(1)}, f32[8,16,256]{2,1,0:T(8,128)}, u32[]{:S(2)}) copy-start(f32[8,16,256]{2,1,0:T(8,128)} %shard_map.74) | copy-start | bytes 393220
  186.5 8.1 %collective-permute-start.9 = (f32[8,16,256]{2,1,0:T(8,128)S(1)}, f32[8,16,256]{2,1,0:T(8,128)S(1)}, u32[]{:S(2)}, u32[]{:S(2)}) collective-permute-start(f32[8,16,256]{2,1,0:T(8,128)S(1)} %copy-done.22), channel_id=1, source_target_pairs={{0,1},{1,2},{2,3},{3,0},{4,5},{5,6},{6,7},{7,4},{8,9},{9,10},{10,1... | collective-permute-start | bytes 393224 | tf_op jit(solution)/shard_map/ppermute | solution.py:146
  188.0 7.7 %collective-permute-start.5 = (f32[8,16,256]{2,1,0:T(8,128)S(1)}, f32[8,16,256]{2,1,0:T(8,128)S(1)}, u32[]{:S(2)}, u32[]{:S(2)}) collective-permute-start(f32[8,16,256]{2,1,0:T(8,128)S(1)} %copy-done.21), channel_id=1, source_target_pairs={{0,3},{1,0},{2,1},{3,2},{4,7},{5,4},{6,5},{7,6},{8,11},{9,8},{10,9... | collective-permute-start | bytes 393224 | tf_op jit(solution)/shard_map/ppermute | solution.py:146
  189.8 7.1 %collective-permute-start.4 = (f32[8,16,256]{2,1,0:T(8,128)S(1)}, f32[8,16,256]{2,1,0:T(8,128)S(1)}, u32[]{:S(2)}, u32[]{:S(2)}) collective-permute-start(f32[8,16,256]{2,1,0:T(8,128)S(1)} %copy-done.21), channel_id=1, source_target_pairs={{0,2},{1,3},{2,0},{3,1},{4,6},{5,7},{6,4},{7,5},{8,10},{9,11},{10,... | collective-permute-start | bytes 393224 | tf_op jit(solution)/shard_map/ppermute | solution.py:146
  191.9 8.9 %collective-permute-start.3 = (f32[8,16,256]{2,1,0:T(8,128)S(1)}, f32[8,16,256]{2,1,0:T(8,128)S(1)}, u32[]{:S(2)}, u32[]{:S(2)}) collective-permute-start(f32[8,16,256]{2,1,0:T(8,128)S(1)} %copy-done.21), channel_id=1, source_target_pairs={{0,1},{1,2},{2,3},{3,0},{4,5},{5,6},{6,7},{7,4},{8,9},{9,10},{10,1... | collective-permute-start | bytes 393224 | tf_op jit(solution)/shard_map/ppermute | solution.py:146
  192.5 25.2 %collective-permute-start.8 = (f32[8,16,256]{2,1,0:T(8,128)}, f32[8,16,256]{2,1,0:T(8,128)S(1)}, u32[]{:S(2)}, u32[]{:S(2)}) collective-permute-start(f32[8,16,256]{2,1,0:T(8,128)} %shard_map.70), channel_id=1, source_target_pairs={{0,3},{1,0},{2,1},{3,2},{4,7},{5,4},{6,5},{7,6},{8,11},{9,8},{10,9... | collective-permute-start | bytes 393224 | tf_op jit(solution)/shard_map/ppermute | solution.py:146
  194.6 23.1 %collective-permute-start.7 = (f32[8,16,256]{2,1,0:T(8,128)}, f32[8,16,256]{2,1,0:T(8,128)S(1)}, u32[]{:S(2)}, u32[]{:S(2)}) collective-permute-start(f32[8,16,256]{2,1,0:T(8,128)} %shard_map.70), channel_id=1, source_target_pairs={{0,2},{1,3},{2,0},{3,1},{4,6},{5,7},{6,4},{7,5},{8,10},{9,11},{10,... | collective-permute-start | bytes 393224 | tf_op jit(solution)/shard_map/ppermute | solution.py:146
  195.7 22.0 %collective-permute-start.6 = (f32[8,16,256]{2,1,0:T(8,128)}, f32[8,16,256]{2,1,0:T(8,128)S(1)}, u32[]{:S(2)}, u32[]{:S(2)}) collective-permute-start(f32[8,16,256]{2,1,0:T(8,128)} %shard_map.70), channel_id=1, source_target_pairs={{0,1},{1,2},{2,3},{3,0},{4,5},{5,6},{6,7},{7,4},{8,9},{9,10},{10,1... | collective-permute-start | bytes 393224 | tf_op jit(solution)/shard_map/ppermute | solution.py:146
  217.6 6.1 %copy-start.11 = (f32[512,256]{1,0:T(8,128)S(1)}, f32[512,256]{1,0:T(8,128)}, u32[]{:S(2)}) copy-start(f32[512,256]{1,0:T(8,128)} %shard_map.69) | copy-start | bytes 1572868
  226.9 18.7 %all-to-all-start.3 = ((f32[128,1,1]{2,1,0:T(1,128)}), f32[128,1,1]{2,1,0:T(1,128)S(1)}, u32[]{:S(2)}, u32[]{:S(2)}) async-start(f32[128,1,1]{2,1,0:T(1,128)} %broadcast_in_dim.26), calls=%async_computation.3 | async-start | bytes 131072 | tf_op jit(solution)/shard_map/all_to_all | solution.py:152
  255.0 33.2 %collective-permute-start.26 = (f32[8,16,256]{2,1,0:T(8,128)}, f32[8,16,256]{2,1,0:T(8,128)S(1)}, u32[]{:S(2)}, u32[]{:S(2)}) collective-permute-start(f32[8,16,256]{2,1,0:T(8,128)} %shard_map.82), channel_id=1, source_target_pairs={{0,3},{1,0},{2,1},{3,2},{4,7},{5,4},{6,5},{7,6},{8,11},{9,8},{10,9... | collective-permute-start | bytes 393224 | tf_op jit(solution)/shard_map/ppermute | solution.py:146
  255.8 34.0 %collective-permute-start.25 = (f32[8,16,256]{2,1,0:T(8,128)}, f32[8,16,256]{2,1,0:T(8,128)S(1)}, u32[]{:S(2)}, u32[]{:S(2)}) collective-permute-start(f32[8,16,256]{2,1,0:T(8,128)} %shard_map.82), channel_id=1, source_target_pairs={{0,2},{1,3},{2,0},{3,1},{4,6},{5,7},{6,4},{7,5},{8,10},{9,11},{10,... | collective-permute-start | bytes 393224 | tf_op jit(solution)/shard_map/ppermute | solution.py:146
  257.4 34.3 %collective-permute-start.24 = (f32[8,16,256]{2,1,0:T(8,128)}, f32[8,16,256]{2,1,0:T(8,128)S(1)}, u32[]{:S(2)}, u32[]{:S(2)}) collective-permute-start(f32[8,16,256]{2,1,0:T(8,128)} %shard_map.82), channel_id=1, source_target_pairs={{0,1},{1,2},{2,3},{3,0},{4,5},{5,6},{6,7},{7,4},{8,9},{9,10},{10,1... | collective-permute-start | bytes 393224 | tf_op jit(solution)/shard_map/ppermute | solution.py:146
  263.1 30.6 %collective-permute-start.23 = (f32[8,16,256]{2,1,0:T(8,128)}, f32[8,16,256]{2,1,0:T(8,128)S(1)}, u32[]{:S(2)}, u32[]{:S(2)}) collective-permute-start(f32[8,16,256]{2,1,0:T(8,128)} %shard_map.80), channel_id=1, source_target_pairs={{0,3},{1,0},{2,1},{3,2},{4,7},{5,4},{6,5},{7,6},{8,11},{9,8},{10,9... | collective-permute-start | bytes 393224 | tf_op jit(solution)/shard_map/ppermute | solution.py:146
  265.8 28.5 %collective-permute-start.22 = (f32[8,16,256]{2,1,0:T(8,128)}, f32[8,16,256]{2,1,0:T(8,128)S(1)}, u32[]{:S(2)}, u32[]{:S(2)}) collective-permute-start(f32[8,16,256]{2,1,0:T(8,128)} %shard_map.80), channel_id=1, source_target_pairs={{0,2},{1,3},{2,0},{3,1},{4,6},{5,7},{6,4},{7,5},{8,10},{9,11},{10,... | collective-permute-start | bytes 393224 | tf_op jit(solution)/shard_map/ppermute | solution.py:146
  267.3 18.9 %all-to-all-start.4 = ((f32[128,1,1]{2,1,0:T(1,128)}), f32[128,1,1]{2,1,0:T(1,128)S(1)}, u32[]{:S(2)}, u32[]{:S(2)}) async-start(f32[128,1,1]{2,1,0:T(1,128)} %broadcast_in_dim.27), calls=%async_computation.4 | async-start | bytes 131072 | tf_op jit(solution)/shard_map/all_to_all | solution.py:152
  280.4 7.9 %copy-start.19 = (f32[8,16,256]{2,1,0:T(8,128)S(1)}, f32[8,16,256]{2,1,0:T(8,128)}, u32[]{:S(2)}) copy-start(f32[8,16,256]{2,1,0:T(8,128)} %shard_map.80) | copy-start | bytes 393220
  280.4 9.5 %copy-start.17 = (f32[8,16,256]{2,1,0:T(8,128)S(1)}, f32[8,16,256]{2,1,0:T(8,128)}, u32[]{:S(2)}) copy-start(f32[8,16,256]{2,1,0:T(8,128)} %shard_map.76) | copy-start | bytes 393220
  280.4 12.7 %copy-start.23 = (f32[8,16,256]{2,1,0:T(8,128)S(1)}, f32[8,16,256]{2,1,0:T(8,128)}, u32[]{:S(2)}) copy-start(f32[8,16,256]{2,1,0:T(8,128)} %shard_map.82) | copy-start | bytes 393220
  288.3 8.2 %collective-permute-start.21 = (f32[8,16,256]{2,1,0:T(8,128)S(1)}, f32[8,16,256]{2,1,0:T(8,128)S(1)}, u32[]{:S(2)}, u32[]{:S(2)}) collective-permute-start(f32[8,16,256]{2,1,0:T(8,128)S(1)} %copy-done.19), channel_id=1, source_target_pairs={{0,1},{1,2},{2,3},{3,0},{4,5},{5,6},{6,7},{7,4},{8,9},{9,10},{10,1... | collective-permute-start | bytes 393224 | tf_op jit(solution)/shard_map/ppermute | solution.py:146
  289.8 7.7 %collective-permute-start.17 = (f32[8,16,256]{2,1,0:T(8,128)S(1)}, f32[8,16,256]{2,1,0:T(8,128)S(1)}, u32[]{:S(2)}, u32[]{:S(2)}) collective-permute-start(f32[8,16,256]{2,1,0:T(8,128)S(1)} %copy-done.17), channel_id=1, source_target_pairs={{0,3},{1,0},{2,1},{3,2},{4,7},{5,4},{6,5},{7,6},{8,11},{9,8},{10,9... | collective-permute-start | bytes 393224 | tf_op jit(solution)/shard_map/ppermute | solution.py:146
  291.7 7.1 %collective-permute-start.16 = (f32[8,16,256]{2,1,0:T(8,128)S(1)}, f32[8,16,256]{2,1,0:T(8,128)S(1)}, u32[]{:S(2)}, u32[]{:S(2)}) collective-permute-start(f32[8,16,256]{2,1,0:T(8,128)S(1)} %copy-done.17), channel_id=1, source_target_pairs={{0,2},{1,3},{2,0},{3,1},{4,6},{5,7},{6,4},{7,5},{8,10},{9,11},{10,... | collective-permute-start | bytes 393224 | tf_op jit(solution)/shard_map/ppermute | solution.py:146
  293.8 8.9 %collective-permute-start.15 = (f32[8,16,256]{2,1,0:T(8,128)S(1)}, f32[8,16,256]{2,1,0:T(8,128)S(1)}, u32[]{:S(2)}, u32[]{:S(2)}) collective-permute-start(f32[8,16,256]{2,1,0:T(8,128)S(1)} %copy-done.17), channel_id=1, source_target_pairs={{0,1},{1,2},{2,3},{3,0},{4,5},{5,6},{6,7},{7,4},{8,9},{9,10},{10,1... | collective-permute-start | bytes 393224 | tf_op jit(solution)/shard_map/ppermute | solution.py:146
  294.3 25.2 %collective-permute-start.20 = (f32[8,16,256]{2,1,0:T(8,128)}, f32[8,16,256]{2,1,0:T(8,128)S(1)}, u32[]{:S(2)}, u32[]{:S(2)}) collective-permute-start(f32[8,16,256]{2,1,0:T(8,128)} %shard_map.78), channel_id=1, source_target_pairs={{0,3},{1,0},{2,1},{3,2},{4,7},{5,4},{6,5},{7,6},{8,11},{9,8},{10,9... | collective-permute-start | bytes 393224 | tf_op jit(solution)/shard_map/ppermute | solution.py:146
  296.5 23.1 %collective-permute-start.19 = (f32[8,16,256]{2,1,0:T(8,128)}, f32[8,16,256]{2,1,0:T(8,128)S(1)}, u32[]{:S(2)}, u32[]{:S(2)}) collective-permute-start(f32[8,16,256]{2,1,0:T(8,128)} %shard_map.78), channel_id=1, source_target_pairs={{0,2},{1,3},{2,0},{3,1},{4,6},{5,7},{6,4},{7,5},{8,10},{9,11},{10,... | collective-permute-start | bytes 393224 | tf_op jit(solution)/shard_map/ppermute | solution.py:146
  297.5 22.0 %collective-permute-start.18 = (f32[8,16,256]{2,1,0:T(8,128)}, f32[8,16,256]{2,1,0:T(8,128)S(1)}, u32[]{:S(2)}, u32[]{:S(2)}) collective-permute-start(f32[8,16,256]{2,1,0:T(8,128)} %shard_map.78), channel_id=1, source_target_pairs={{0,1},{1,2},{2,3},{3,0},{4,5},{5,6},{6,7},{7,4},{8,9},{9,10},{10,1... | collective-permute-start | bytes 393224 | tf_op jit(solution)/shard_map/ppermute | solution.py:146
  356.3 33.5 %collective-permute-start.38 = (f32[8,16,256]{2,1,0:T(8,128)}, f32[8,16,256]{2,1,0:T(8,128)S(1)}, u32[]{:S(2)}, u32[]{:S(2)}) collective-permute-start(f32[8,16,256]{2,1,0:T(8,128)} %shard_map.90), channel_id=1, source_target_pairs={{0,3},{1,0},{2,1},{3,2},{4,7},{5,4},{6,5},{7,6},{8,11},{9,8},{10,9... | collective-permute-start | bytes 393224 | tf_op jit(solution)/shard_map/ppermute | solution.py:146
  357.1 34.3 %collective-permute-start.37 = (f32[8,16,256]{2,1,0:T(8,128)}, f32[8,16,256]{2,1,0:T(8,128)S(1)}, u32[]{:S(2)}, u32[]{:S(2)}) collective-permute-start(f32[8,16,256]{2,1,0:T(8,128)} %shard_map.90), channel_id=1, source_target_pairs={{0,2},{1,3},{2,0},{3,1},{4,6},{5,7},{6,4},{7,5},{8,10},{9,11},{10,... | collective-permute-start | bytes 393224 | tf_op jit(solution)/shard_map/ppermute | solution.py:146
  358.7 34.6 %collective-permute-start.36 = (f32[8,16,256]{2,1,0:T(8,128)}, f32[8,16,256]{2,1,0:T(8,128)S(1)}, u32[]{:S(2)}, u32[]{:S(2)}) collective-permute-start(f32[8,16,256]{2,1,0:T(8,128)} %shard_map.90), channel_id=1, source_target_pairs={{0,1},{1,2},{2,3},{3,0},{4,5},{5,6},{6,7},{7,4},{8,9},{9,10},{10,1... | collective-permute-start | bytes 393224 | tf_op jit(solution)/shard_map/ppermute | solution.py:146
  364.7 30.6 %collective-permute-start.35 = (f32[8,16,256]{2,1,0:T(8,128)}, f32[8,16,256]{2,1,0:T(8,128)S(1)}, u32[]{:S(2)}, u32[]{:S(2)}) collective-permute-start(f32[8,16,256]{2,1,0:T(8,128)} %shard_map.88), channel_id=1, source_target_pairs={{0,3},{1,0},{2,1},{3,2},{4,7},{5,4},{6,5},{7,6},{8,11},{9,8},{10,9... | collective-permute-start | bytes 393224 | tf_op jit(solution)/shard_map/ppermute | solution.py:146
  367.4 28.5 %collective-permute-start.34 = (f32[8,16,256]{2,1,0:T(8,128)}, f32[8,16,256]{2,1,0:T(8,128)S(1)}, u32[]{:S(2)}, u32[]{:S(2)}) collective-permute-start(f32[8,16,256]{2,1,0:T(8,128)} %shard_map.88), channel_id=1, source_target_pairs={{0,2},{1,3},{2,0},{3,1},{4,6},{5,7},{6,4},{7,5},{8,10},{9,11},{10,... | collective-permute-start | bytes 393224 | tf_op jit(solution)/shard_map/ppermute | solution.py:146
  368.9 18.9 %all-to-all-start.6 = ((f32[128,1,1]{2,1,0:T(1,128)}), f32[128,1,1]{2,1,0:T(1,128)S(1)}, u32[]{:S(2)}, u32[]{:S(2)}) async-start(f32[128,1,1]{2,1,0:T(1,128)} %broadcast_in_dim.29), calls=%async_computation.6 | async-start | bytes 131072 | tf_op jit(solution)/shard_map/all_to_all | solution.py:152
  381.9 7.9 %copy-start.20 = (f32[8,16,256]{2,1,0:T(8,128)S(1)}, f32[8,16,256]{2,1,0:T(8,128)}, u32[]{:S(2)}) copy-start(f32[8,16,256]{2,1,0:T(8,128)} %shard_map.88) | copy-start | bytes 393220
  381.9 9.5 %copy-start.18 = (f32[8,16,256]{2,1,0:T(8,128)S(1)}, f32[8,16,256]{2,1,0:T(8,128)}, u32[]{:S(2)}) copy-start(f32[8,16,256]{2,1,0:T(8,128)} %shard_map.84) | copy-start | bytes 393220
  381.9 12.7 %copy-start.24 = (f32[8,16,256]{2,1,0:T(8,128)S(1)}, f32[8,16,256]{2,1,0:T(8,128)}, u32[]{:S(2)}) copy-start(f32[8,16,256]{2,1,0:T(8,128)} %shard_map.90) | copy-start | bytes 393220
  389.9 8.2 %collective-permute-start.33 = (f32[8,16,256]{2,1,0:T(8,128)S(1)}, f32[8,16,256]{2,1,0:T(8,128)S(1)}, u32[]{:S(2)}, u32[]{:S(2)}) collective-permute-start(f32[8,16,256]{2,1,0:T(8,128)S(1)} %copy-done.20), channel_id=1, source_target_pairs={{0,1},{1,2},{2,3},{3,0},{4,5},{5,6},{6,7},{7,4},{8,9},{9,10},{10,1... | collective-permute-start | bytes 393224 | tf_op jit(solution)/shard_map/ppermute | solution.py:146
  391.4 7.7 %collective-permute-start.29 = (f32[8,16,256]{2,1,0:T(8,128)S(1)}, f32[8,16,256]{2,1,0:T(8,128)S(1)}, u32[]{:S(2)}, u32[]{:S(2)}) collective-permute-start(f32[8,16,256]{2,1,0:T(8,128)S(1)} %copy-done.18), channel_id=1, source_target_pairs={{0,3},{1,0},{2,1},{3,2},{4,7},{5,4},{6,5},{7,6},{8,11},{9,8},{10,9... | collective-permute-start | bytes 393224 | tf_op jit(solution)/shard_map/ppermute | solution.py:146
  393.3 7.1 %collective-permute-start.28 = (f32[8,16,256]{2,1,0:T(8,128)S(1)}, f32[8,16,256]{2,1,0:T(8,128)S(1)}, u32[]{:S(2)}, u32[]{:S(2)}) collective-permute-start(f32[8,16,256]{2,1,0:T(8,128)S(1)} %copy-done.18), channel_id=1, source_target_pairs={{0,2},{1,3},{2,0},{3,1},{4,6},{5,7},{6,4},{7,5},{8,10},{9,11},{10,... | collective-permute-start | bytes 393224 | tf_op jit(solution)/shard_map/ppermute | solution.py:146
  395.4 8.9 %collective-permute-start.27 = (f32[8,16,256]{2,1,0:T(8,128)S(1)}, f32[8,16,256]{2,1,0:T(8,128)S(1)}, u32[]{:S(2)}, u32[]{:S(2)}) collective-permute-start(f32[8,16,256]{2,1,0:T(8,128)S(1)} %copy-done.18), channel_id=1, source_target_pairs={{0,1},{1,2},{2,3},{3,0},{4,5},{5,6},{6,7},{7,4},{8,9},{9,10},{10,1... | collective-permute-start | bytes 393224 | tf_op jit(solution)/shard_map/ppermute | solution.py:146
  395.9 25.2 %collective-permute-start.32 = (f32[8,16,256]{2,1,0:T(8,128)}, f32[8,16,256]{2,1,0:T(8,128)S(1)}, u32[]{:S(2)}, u32[]{:S(2)}) collective-permute-start(f32[8,16,256]{2,1,0:T(8,128)} %shard_map.86), channel_id=1, source_target_pairs={{0,3},{1,0},{2,1},{3,2},{4,7},{5,4},{6,5},{7,6},{8,11},{9,8},{10,9... | collective-permute-start | bytes 393224 | tf_op jit(solution)/shard_map/ppermute | solution.py:146
  398.0 23.1 %collective-permute-start.31 = (f32[8,16,256]{2,1,0:T(8,128)}, f32[8,16,256]{2,1,0:T(8,128)S(1)}, u32[]{:S(2)}, u32[]{:S(2)}) collective-permute-start(f32[8,16,256]{2,1,0:T(8,128)} %shard_map.86), channel_id=1, source_target_pairs={{0,2},{1,3},{2,0},{3,1},{4,6},{5,7},{6,4},{7,5},{8,10},{9,11},{10,... | collective-permute-start | bytes 393224 | tf_op jit(solution)/shard_map/ppermute | solution.py:146
  399.1 22.0 %collective-permute-start.30 = (f32[8,16,256]{2,1,0:T(8,128)}, f32[8,16,256]{2,1,0:T(8,128)}, u32[]{:S(2)}, u32[]{:S(2)}) collective-permute-start(f32[8,16,256]{2,1,0:T(8,128)} %shard_map.86), channel_id=1, source_target_pairs={{0,1},{1,2},{2,3},{3,0},{4,5},{5,6},{6,7},{7,4},{8,9},{9,10},{10,1... | collective-permute-start | bytes 393224 | tf_op jit(solution)/shard_map/ppermute | solution.py:146
  421.1 7.1 %copy-start.12 = (f32[512,256]{1,0:T(8,128)S(1)}, f32[512,256]{1,0:T(8,128)}, u32[]{:S(2)}) copy-start(f32[512,256]{1,0:T(8,128)} %shard_map.91) | copy-start | bytes 1572868
  421.1 7.1 %copy-start.13 = (f32[512,256]{1,0:T(8,128)S(1)}, f32[512,256]{1,0:T(8,128)}, u32[]{:S(2)}) copy-start(f32[512,256]{1,0:T(8,128)} %shard_map.89) | copy-start | bytes 1572868
  (9 other events, 51.4 us)
